TPU v7x, 32 devices: a whole 2x2x4 slice. The times are simulated.
32 devices in a mesh: grp: 4 (over y, x), mem: 2 (over core), row: 4 (over z).
Axes of the slice: x: 2, y: 2, z: 4, core: 2. Of those that a mesh axis runs over, the one named last changes fastest.
Arguments:
- field: bfloat16 [4, 512, 16384], P(None, ('grp', 'mem', 'row')), may hold values from -60 to 60
- counts: int32 [32], P(('grp', 'mem', 'row')), may hold values from 1 to 6, as said below
- kappa_rows: float32 [512], P(('grp', 'mem', 'row')), may hold values from 0.7 to 1
- kappa_cols: bfloat16 [16384], replicated, may hold values from 0.69921875 to 1
- drift_rows: float32 [2, 512], P(None, ('grp', 'mem', 'row')), may hold values from -0.95 to 0.95
- drift_cols: bfloat16 [2, 16384], replicated, may hold values from -0.94921875 to 0.94921875
- assign: int32 [32], replicated, may hold values from 0 to 3
- buffer: bfloat16 [4, 32, 4, 1024], P('grp', 'mem'), may hold values from -30 to 30
- lift_weight: bfloat16 [4, 32], replicated, may hold values from -3 to 3
- lift_bias: float32 [32], replicated, may hold values from -3 to 3
- point_weight: bfloat16 [32, 32], P(None, 'row'), may hold values from -1 to 1
- point_bias: float32 [32], P('row'), may hold values from -3 to 3
- spectral_weight: bfloat16 [2, 32, 32, 32, 16], P(None, None, 'row'), may hold values from -1 to 1
- cotangent: bfloat16 [4, 32, 32, 1024], P('grp', 'mem', 'row'), may hold values from -6 to 6
Outputs:
- fresh_sample: float32 [32, 4, 1024], P(('grp', 'mem', 'row'))
- layer_out: bfloat16 [4, 32, 32, 1024], P('grp', 'mem', 'row')
- grad_spectral: float32 [2, 32, 32, 32, 16], P(None, 'mem', 'row', 'grp')
Inputs may be any that keep to these rules, and one draw needn't show every extreme that they name: The counts sum to 96, and a quarter of the slabs take exactly 6.
All inputs are finite; a program needn't handle non-finite values.
Results may differ from a plain program's by a relative error of at most 0.0049.
Values may be sent and summed in bfloat16 or wider, within the bound.
No kernel may reach another device: no remote copies, remote signals or barrier semaphores. Data moves between devices by JAX's collectives and lax.ppermute only.
A program may use at most 64 MiB of HBM per device.

v0:
```python
import math

import jax
import jax.numpy as jnp
from jax import lax
from jax.sharding import PartitionSpec as P

C = 4
SW = 1024
FACTOR = 16
HID = 32
MODES = 16


window_time = 0.24


def with_halo(block, sides, width):
    for axis, dim in sides:
        count = lax.axis_size(axis)
        forward = [(i, i + 1) for i in range(count - 1)]
        forward.append((count - 1, 0))
        backward = [(target, source) for source, target in forward]
        low = lax.ppermute(
            lax.slice_in_dim(block, block.shape[dim] - width, None, axis=dim), axis, forward
        )
        high = lax.ppermute(lax.slice_in_dim(block, 0, width, axis=dim), axis, backward)
        block = jnp.concatenate([low, block, high], axis=dim)
    return block


def slab_solve(
    slab_rows, above_row, below_row, substeps, kappa_row, drift_row, kappa_col, drift_col
):
    diffusion = kappa_row[:, None] * kappa_col[None, :]
    drift_along = drift_row[0][:, None] * drift_col[0][None, :]
    drift_across = drift_row[1][:, None] * drift_col[1][None, :]
    step_size = window_time / substeps.astype(jnp.float32)

    def advance(number, current):
        stacked = jnp.concatenate([above_row, current, below_row], axis=1)
        upper_rows = stacked[:, :-2]
        lower_rows = stacked[:, 2:]
        right_cells = jnp.roll(current, -1, axis=2)
        left_cells = jnp.roll(current, 1, axis=2)
        change = diffusion * (right_cells + left_cells + upper_rows + lower_rows - 4.0 * current)
        change = (
            change
            - 0.5 * drift_along * (right_cells - left_cells)
            - 0.5 * drift_across * (lower_rows - upper_rows)
        )
        return current + step_size * change

    return lax.fori_loop(jnp.zeros((), jnp.int32), substeps, advance, slab_rows)


def coarsen(stepped):
    return stepped.reshape(C, FACTOR, SW, FACTOR).mean(axis=(1, 3))


def column_table():
    columns = jnp.arange(SW, dtype=jnp.int32)
    orders = jnp.arange(MODES, dtype=jnp.int32)
    phase_angle = 2.0 * math.pi / SW * (columns[:, None] * orders[None, :] % SW).astype(jnp.float32)
    return jnp.concatenate([jnp.cos(phase_angle), -jnp.sin(phase_angle)], axis=1).astype(
        jnp.bfloat16
    )


def inverse_table():
    columns = jnp.arange(SW, dtype=jnp.int32)
    orders = jnp.arange(MODES, dtype=jnp.int32)
    phase_angle = 2.0 * math.pi / SW * (orders[:, None] * columns[None, :] % SW).astype(jnp.float32)
    weights = jnp.where(orders == 0, 1.0, 2.0).astype(jnp.float32)[:, None]
    return jnp.concatenate(
        [weights * jnp.cos(phase_angle), -weights * jnp.sin(phase_angle)], axis=0
    )


def row_tables(row_ids, total_rows):
    orders = jnp.arange(2 * MODES, dtype=jnp.int32)
    wave_numbers = jnp.where(orders < MODES, orders, total_rows - 2 * MODES + orders)
    phase_angle = (
        2.0
        * math.pi
        / total_rows
        * (wave_numbers[:, None] * row_ids[None, :] % total_rows).astype(jnp.float32)
    )
    return (jnp.cos(phase_angle), jnp.sin(phase_angle))


def rows_forward(part_real, part_imag, cosine_table, sine_table):
    highest = lax.Precision.HIGHEST
    real_part = jnp.einsum("jy,yhl->hjl", cosine_table, part_real, precision=highest) + jnp.einsum(
        "jy,yhl->hjl", sine_table, part_imag, precision=highest
    )
    imag_part = jnp.einsum("jy,yhl->hjl", cosine_table, part_imag, precision=highest) - jnp.einsum(
        "jy,yhl->hjl", sine_table, part_real, precision=highest
    )
    return (real_part, imag_part)


def rows_inverse(mixed_real, mixed_imag, cosine_table, sine_table):
    highest = lax.Precision.HIGHEST
    rows_real = jnp.einsum("jy,ojl->yol", cosine_table, mixed_real, precision=highest) - jnp.einsum(
        "jy,ojl->yol", sine_table, mixed_imag, precision=highest
    )
    rows_imag = jnp.einsum("jy,ojl->yol", sine_table, mixed_real, precision=highest) + jnp.einsum(
        "jy,ojl->yol", cosine_table, mixed_imag, precision=highest
    )
    return jnp.concatenate([rows_real, rows_imag], axis=2)


def mix_modes(spectral, mode_real, mode_imag):
    highest = lax.Precision.HIGHEST
    mixed_real = jnp.einsum(
        "hojl,hjl->ojl", spectral[0], mode_real, precision=highest
    ) - jnp.einsum("hojl,hjl->ojl", spectral[1], mode_imag, precision=highest)
    mixed_imag = jnp.einsum(
        "hojl,hjl->ojl", spectral[0], mode_imag, precision=highest
    ) + jnp.einsum("hojl,hjl->ojl", spectral[1], mode_real, precision=highest)
    return (mixed_real, mixed_imag)


def gelu_slope(pre_act):
    normal_cdf = 0.5 * (1.0 + lax.erf(pre_act * (1.0 / math.sqrt(2.0))))
    density = jnp.exp(-0.5 * pre_act * pre_act) * (1.0 / math.sqrt(2.0 * math.pi))
    return normal_cdf + pre_act * density


def weight_grads(back_real, back_imag, mode_real, mode_imag):
    highest = lax.Precision.HIGHEST
    grad_real = jnp.einsum("ojl,hjl->hojl", back_real, mode_real, precision=highest) + jnp.einsum(
        "ojl,hjl->hojl", back_imag, mode_imag, precision=highest
    )
    grad_imag = jnp.einsum("ojl,hjl->hojl", back_imag, mode_real, precision=highest) - jnp.einsum(
        "ojl,hjl->hojl", back_real, mode_imag, precision=highest
    )
    return jnp.stack([grad_real, grad_imag])


def lift_rows(sample, lift_weight, lift_bias):
    lifted = jnp.einsum("ycx,ch->yhx", sample, lift_weight, preferred_element_type=jnp.float32)
    return (lifted + lift_bias[None, :, None]).astype(jnp.bfloat16)


def body(
    field,
    counts,
    kappa_rows,
    kappa_cols,
    drift_rows,
    drift_cols,
    assign,
    buffer,
    lift_weight,
    lift_bias,
    point_weight,
    point_bias,
    spectral_weight,
    cotangent,
):
    padded = with_halo(field, ((("grp", "mem", "row"), 1),), 1)
    stepped = slab_solve(
        padded[:, 1:-1].astype(jnp.float32),
        padded[:, :1].astype(jnp.float32),
        padded[:, -1:].astype(jnp.float32),
        counts[0],
        kappa_rows,
        drift_rows,
        kappa_cols.astype(jnp.float32),
        drift_cols.astype(jnp.float32),
    )
    coarse_rows = coarsen(stepped)[None]
    coarse_low = coarse_rows.astype(jnp.bfloat16)
    member = lax.axis_index("mem")
    member_rows = buffer.shape[1]
    total_rows = member_rows * lax.axis_size("mem")
    row_ids = member * member_rows + jnp.arange(member_rows, dtype=jnp.int32)
    owners = lax.dynamic_slice_in_dim(assign, member * member_rows, member_rows, 0)
    chosen = (owners == lax.axis_index("grp"))[:, None, None]
    forward_table = column_table()
    every_row = lax.all_gather(coarse_low, ("grp", "mem", "row"), axis=0, tiled=True)
    fresh_rows = lax.dynamic_slice_in_dim(every_row, member * member_rows, member_rows, 0)
    sample = jnp.where(chosen, fresh_rows, buffer[0])
    hidden = lift_rows(sample, lift_weight, lift_bias)
    column_part = jnp.einsum(
        "yhx,xk->yhk", hidden, forward_table, preferred_element_type=jnp.float32
    )
    norm_scale = 1.0 / math.sqrt(total_rows * SW)
    cosine_table, sine_table = row_tables(row_ids, total_rows)
    part_real, part_imag = rows_forward(
        column_part[:, :, :MODES], column_part[:, :, MODES:], cosine_table, sine_table
    )
    mode_real, mode_imag = lax.psum((part_real * norm_scale, part_imag * norm_scale), "mem")
    mixed_real, mixed_imag = mix_modes(spectral_weight.astype(jnp.float32), mode_real, mode_imag)
    spatial = (
        jnp.einsum(
            "yok,kx->yox",
            rows_inverse(mixed_real, mixed_imag, cosine_table, sine_table),
            inverse_table(),
            precision=lax.Precision.HIGHEST,
        )
        * norm_scale
    )
    pre_act = (
        spatial
        + jnp.einsum("yhx,ho->yox", hidden, point_weight, preferred_element_type=jnp.float32)
        + point_bias[None, :, None]
    )
    layer_rows = jax.nn.gelu(pre_act, approximate=False).astype(jnp.bfloat16)[None]
    back_signal = (cotangent[0].astype(jnp.float32) * gelu_slope(pre_act)).astype(jnp.bfloat16)
    back_part = jnp.einsum(
        "yox,xk->yok", back_signal, forward_table, preferred_element_type=jnp.float32
    )
    back_real, back_imag = rows_forward(
        back_part[:, :, :MODES], back_part[:, :, MODES:], cosine_table, sine_table
    )
    weights_mode = jnp.where(jnp.arange(MODES) == 0, 1.0, 2.0).astype(jnp.float32) * norm_scale
    back_real, back_imag = lax.psum((back_real * weights_mode, back_imag * weights_mode), "mem")
    block_size = HID // lax.axis_size("mem")
    block_real = lax.dynamic_slice_in_dim(mode_real, member * block_size, block_size, 0)
    block_imag = lax.dynamic_slice_in_dim(mode_imag, member * block_size, block_size, 0)
    grad_terms = weight_grads(back_real, back_imag, block_real, block_imag)
    summed = lax.psum_scatter(grad_terms, "grp", scatter_dimension=3, tiled=True)
    return (coarse_rows, layer_rows, summed / lax.axis_size("grp"))


def solution(mesh):
    in_specs = (
        P(None, ("grp", "mem", "row"), None),
        P(("grp", "mem", "row")),
        P(("grp", "mem", "row")),
        P(),
        P(None, ("grp", "mem", "row")),
        P(),
        P(),
        P("grp", "mem", None, None),
        P(),
        P(),
        P(None, "row"),
        P("row"),
        P(None, None, "row", None, None),
        P("grp", "mem", "row", None),
    )
    out_specs = (
        P(("grp", "mem", "row"), None, None),
        P("grp", "mem", "row", None),
        P(None, "mem", "row", "grp", None),
    )
    return jax.shard_map(body, mesh=mesh, in_specs=in_specs, out_specs=out_specs, check_vma=False)
```

profile of v0, /device:TPU:0, one launch (start us, length us, event | category | flops | bytes accessed | tf_op | source)
XLA Modules:
  0.0 263.5 jit_solution(3023545381430888745)
XLA Ops:
  7.2 2.0 fusion.171
  9.2 3.1 %collective-permute-start = (bf16[4,1,16384]{2,1,0:T(2,128)(2,1)S(1)}, bf16[4,1,16384]{2,1,0:T(2,128)(2,1)S(1)}, u32[]{:S(2)}, u32[]{:S(2)}) collective-permute-start(bf16[4,1,16384]{2,1,0:T(2,128)(2,1)S(1)} %get-tuple-element.130), channel_id=1, source_target_pairs={{0,1},{1,2},{2,3},{3,4},{4,5},{5,6},{6,7},{7,8},{8,9},{9,10},{10,1... | collective-permute-start | bytes 393224 | tf_op jit(solution)/shard_map/ppermute | solution.py:24
  12.3 3.4 %collective-permute-start.1 = (bf16[4,1,16384]{2,1,0:T(2,128)(2,1)S(1)}, bf16[4,1,16384]{2,1,0:T(2,128)(2,1)S(1)}, u32[]{:S(2)}, u32[]{:S(2)}) collective-permute-start(bf16[4,1,16384]{2,1,0:T(2,128)(2,1)S(1)} %get-tuple-element.129), channel_id=1, source_target_pairs={{1,0},{2,1},{3,2},{4,3},{5,4},{6,5},{7,6},{8,7},{9,8},{10,9},{11,1... | collective-permute-start | bytes 393224 | tf_op jit(solution)/shard_map/ppermute | solution.py:27
  15.7 0.3 negate_convert_fusion
  16.0 1.0 fusion.174
  17.0 0.8 slice_bitcast_fusion
  17.8 0.3 sine_multiply_fusion
  18.0 0.7 dynamic-slice_compare_fusion
  18.8 3.8 %convert_element_type.62 = f32[4,16,16384]{2,1,0:T(8,128)} convert(bf16[4,16,16384]{2,1,0:T(8,128)(2,1)} %param.16) | non-fusion elementwise | flops 1048576 | bytes 6291456 | tf_op jit(solution)/shard_map/convert_element_type | solution.py:165
  23.6 0.3 convert_element_type.65
  23.9 1.8 collective-permute-done.1
  25.7 0.3 convert_element_type.66
  26.0 65.0 %while.11 = (s32[]{:T(128)}, f32[4,16,16384]{2,1,0:T(8,128)}, s32[]{:T(128)}, f32[]{:T(128)}, f32[4,1,16384]{2,1,0:T(1,128)S(1)}, /*index=5*/f32[4,1,16384]{2,1,...) while((s32[]{:T(128)}, f32[4,16,16384]{2,1,0:T(8,128)}, ...), condition=%wide.region_1.2_spmd.clone, body=%wide.region_0.1_spmd.clone.sunk | while | flops 20185088 | bytes 48955712 | solution.py:54
  26.6 2.2 copy.107
  28.8 1.4 fusion.183
  30.7 6.0 %multiply_add_fusion.2 = f32[4,16,16384]{2,1,0:T(8,128)} fusion(f32[4,16,16384]{2,1,0:T(8,128)S(1)} %copy.107, f32[4,1,16384]{2,1,0:T(1,128)S(1)} %get-tuple-element.262, f32[4,1,16384]{2,1,0:T(1,128)S(1)} %get-tuple-element.261, f32[4,16,16383]{2,1,0:T(8,128)S(1)} %get-tuple-element.225, f32[4,16,1]{2,1,0:T(8,128)S(1)} %get-tuple-element.226, ...), kind=kLoop, calls=%fused_computation.7.clone.1 | loop fusion | flops 18874368 | bytes 20447236 | tf_op jit(solution)/shard_map/while/body/add | solution.py:52
  37.3 2.2 copy.107
  39.5 1.4 fusion.183
  41.4 6.0 %multiply_add_fusion.2 = f32[4,16,16384]{2,1,0:T(8,128)} fusion(f32[4,16,16384]{2,1,0:T(8,128)S(1)} %copy.107, f32[4,1,16384]{2,1,0:T(1,128)S(1)} %get-tuple-element.262, f32[4,1,16384]{2,1,0:T(1,128)S(1)} %get-tuple-element.261, f32[4,16,16383]{2,1,0:T(8,128)S(1)} %get-tuple-element.225, f32[4,16,1]{2,1,0:T(8,128)S(1)} %get-tuple-element.226, ...), kind=kLoop, calls=%fused_computation.7.clone.1 | loop fusion | flops 18874368 | bytes 20447236 | tf_op jit(solution)/shard_map/while/body/add | solution.py:52
  48.1 2.2 copy.107
  50.2 1.4 fusion.183
  52.1 6.0 %multiply_add_fusion.2 = f32[4,16,16384]{2,1,0:T(8,128)} fusion(f32[4,16,16384]{2,1,0:T(8,128)S(1)} %copy.107, f32[4,1,16384]{2,1,0:T(1,128)S(1)} %get-tuple-element.262, f32[4,1,16384]{2,1,0:T(1,128)S(1)} %get-tuple-element.261, f32[4,16,16383]{2,1,0:T(8,128)S(1)} %get-tuple-element.225, f32[4,16,1]{2,1,0:T(8,128)S(1)} %get-tuple-element.226, ...), kind=kLoop, calls=%fused_computation.7.clone.1 | loop fusion | flops 18874368 | bytes 20447236 | tf_op jit(solution)/shard_map/while/body/add | solution.py:52
  58.8 2.2 copy.107
  61.0 1.4 fusion.183
  62.8 6.0 %multiply_add_fusion.2 = f32[4,16,16384]{2,1,0:T(8,128)} fusion(f32[4,16,16384]{2,1,0:T(8,128)S(1)} %copy.107, f32[4,1,16384]{2,1,0:T(1,128)S(1)} %get-tuple-element.262, f32[4,1,16384]{2,1,0:T(1,128)S(1)} %get-tuple-element.261, f32[4,16,16383]{2,1,0:T(8,128)S(1)} %get-tuple-element.225, f32[4,16,1]{2,1,0:T(8,128)S(1)} %get-tuple-element.226, ...), kind=kLoop, calls=%fused_computation.7.clone.1 | loop fusion | flops 18874368 | bytes 20447236 | tf_op jit(solution)/shard_map/while/body/add | solution.py:52
  69.5 2.2 copy.107
  71.7 1.4 fusion.183
  73.5 6.0 %multiply_add_fusion.2 = f32[4,16,16384]{2,1,0:T(8,128)} fusion(f32[4,16,16384]{2,1,0:T(8,128)S(1)} %copy.107, f32[4,1,16384]{2,1,0:T(1,128)S(1)} %get-tuple-element.262, f32[4,1,16384]{2,1,0:T(1,128)S(1)} %get-tuple-element.261, f32[4,16,16383]{2,1,0:T(8,128)S(1)} %get-tuple-element.225, f32[4,16,1]{2,1,0:T(8,128)S(1)} %get-tuple-element.226, ...), kind=kLoop, calls=%fused_computation.7.clone.1 | loop fusion | flops 18874368 | bytes 20447236 | tf_op jit(solution)/shard_map/while/body/add | solution.py:52
  80.2 2.2 copy.107
  82.4 1.4 fusion.183
  84.3 6.0 %multiply_add_fusion.2 = f32[4,16,16384]{2,1,0:T(8,128)} fusion(f32[4,16,16384]{2,1,0:T(8,128)S(1)} %copy.107, f32[4,1,16384]{2,1,0:T(1,128)S(1)} %get-tuple-element.262, f32[4,1,16384]{2,1,0:T(1,128)S(1)} %get-tuple-element.261, f32[4,16,16383]{2,1,0:T(8,128)S(1)} %get-tuple-element.225, f32[4,16,1]{2,1,0:T(8,128)S(1)} %get-tuple-element.226, ...), kind=kLoop, calls=%fused_computation.7.clone.1 | loop fusion | flops 18874368 | bytes 20447236 | tf_op jit(solution)/shard_map/while/body/add | solution.py:52
  91.0 2.9 %reduce_sum.10 = f32[4,16384]{1,0:T(4,128)S(1)} reduce(f32[4,16,16384]{2,1,0:T(8,128)} %get-tuple-element.51, f32[]{:T(128)} %constant.55.clone.1), dimensions={1}, to_apply=%region_2.3 | reduce | flops 983040 | bytes 4456452 | tf_op jit(solution)/shard_map/reduce_sum | solution.py:58
  93.9 0.7 reduce_sum.14
  94.6 0.6 reduce_sum.18
  95.2 0.6 fusion.168
  95.8 65.9 %all_gather.3 = bf16[32,4,1024]{2,1,0:T(4,128)(2,1)S(1)} all-gather(bf16[1,4,1024]{2,1,0:T(4,128)(2,1)S(1)} %get-tuple-element.121), channel_id=1, replica_groups=mesh['grp'=4,'mem'=2,'row'=4] {'grp','mem','row'}, dimensions={0}, use_global_device_ids=true | all-gather | bytes 270336 | tf_op jit(solution)/shard_map/all_gather | solution.py:183
  161.7 0.5 fusion.10
  162.3 0.9 fusion.69
  163.2 0.7 fusion.48
  163.9 0.7 fusion.44
  164.5 1.4 fusion.16
  165.9 1.4 fusion.14
  167.5 0.3 cosine_multiply_fusion
  167.8 16.1 %all-reduce.4.cloned.1.call-done = (f32[32,32,16]{1,0,2:T(8,128)}, f32[32,32,16]{1,0,2:T(8,128)}) async-done(((f32[32,32,16]{1,0,2:T(8,128)}, f32[32,32,16]{1,0,2:T(8,128)}), (f32[32,32,16]{1,0,2:T(8,128)}, f32[32,32,16]{1,0,2:T(8,128)})) %all-reduce.4.cloned.1.call-update) | async-done | bytes 131088 | tf_op jit(solution)/shard_map/psum | solution.py:195
  183.8 1.2 copy.82
  185.0 1.1 copy.83
  186.1 1.0 fusion.9
  187.1 0.6 fusion.58
  187.8 0.7 fusion.60
  188.5 0.6 convolution_add_fusion.2
  189.1 0.7 convolution_subtract_fusion.2
  189.9 0.6 convolution_multiply_fusion
  190.5 0.3 fusion.12
  190.8 0.3 fusion.38
  191.3 0.3 fusion.83
  191.7 0.3 fusion.85
  192.0 0.3 fusion.18
  192.4 0.3 fusion.20
  192.7 3.8 %all-reduce = (f32[32,16,8]{0,1,2:T(8,128)S(1)}, f32[32,16,8]{0,1,2:T(8,128)S(1)}) all-reduce(f32[32,16,8]{0,1,2:T(8,128)S(1)} %fusion.18, f32[32,16,8]{0,1,2:T(8,128)S(1)} %fusion.20), channel_id=1, replica_groups=mesh['grp'=4,'mem'=2,'row'=4] {'mem'}, use_global_device_ids=true, to_apply=%region_7.8 | all-reduce | flops 8192 | bytes 65536 | tf_op jit(solution)/shard_map/psum | solution.py:220
  197.0 0.6 add_bitcast_fusion
  197.6 2.6 pad_maximum_fusion.4
  200.3 1.8 fusion.37
  202.1 52.2 %reduce-scatter.2.cloned.1.call-done = f32[2,16,8,8,16]{4,3,2,1,0:T(8,128)} async-done(((f32[2,16,8,32,16]{4,3,2,1,0:T(8,128)}), f32[2,16,8,8,16]{4,3,2,1,0:T(8,128)}) %reduce-scatter.2.cloned.1.call-update) | async-done | bytes 131088 | tf_op jit(solution)/shard_map/reduce_scatter | solution.py:225
  254.4 2.3 broadcast_multiply_fusion.1
  (60 shorter events, 4.1 us)
Async XLA Ops:
  7.2 183.3 %copy-start = (bf16[32,8]{0,1:T(8,128)(2,1)S(1)}, bf16[32,8]{0,1:T(8,128)(2,1)}, u32[]{:S(2)}) copy-start(bf16[32,8]{0,1:T(8,128)(2,1)} %param.26) | copy-start | bytes 1540
  7.2 16.1 %copy-start.5 = (bf16[16384]{0:T(1024)(128)(2,1)S(1)}, bf16[16384]{0:T(1024)(128)(2,1)}, u32[]{:S(2)}) copy-start(bf16[16384]{0:T(1024)(128)(2,1)} %param.19) | copy-start | bytes 98308
  7.2 176.7 %all-reduce.4.cloned.1.call-start = ((), (), s32[]{:S(2)}) async-start(), calls=%async_computation.2 | async-start | bytes 1048576 | tf_op jit(solution)/shard_map/psum | solution.py:195
  9.2 16.8 %copy-start.6 = (f32[16]{0:T(128)S(1)}, f32[16]{0:T(128)}, u32[]{:S(2)}) copy-start(f32[16]{0:T(128)} %param.18) | copy-start | bytes 196
  9.2 14.4 %collective-permute-start = (bf16[4,1,16384]{2,1,0:T(2,128)(2,1)S(1)}, bf16[4,1,16384]{2,1,0:T(2,128)(2,1)S(1)}, u32[]{:S(2)}, u32[]{:S(2)}) collective-permute-start(bf16[4,1,16384]{2,1,0:T(2,128)(2,1)S(1)} %get-tuple-element.130), channel_id=1, source_target_pairs={{0,1},{1,2},{2,3},{3,4},{4,5},{5,6},{6,7},{7,8},{8,9},{9,10},{10,1... | collective-permute-start | bytes 393224 | tf_op jit(solution)/shard_map/ppermute | solution.py:24
  12.3 13.4 %collective-permute-start.1 = (bf16[4,1,16384]{2,1,0:T(2,128)(2,1)S(1)}, bf16[4,1,16384]{2,1,0:T(2,128)(2,1)S(1)}, u32[]{:S(2)}, u32[]{:S(2)}) collective-permute-start(bf16[4,1,16384]{2,1,0:T(2,128)(2,1)S(1)} %get-tuple-element.129), channel_id=1, source_target_pairs={{1,0},{2,1},{3,2},{4,3},{5,4},{6,5},{7,6},{8,7},{9,8},{10,9},{11,1... | collective-permute-start | bytes 393224 | tf_op jit(solution)/shard_map/ppermute | solution.py:27
  90.9 70.8 %copy-start.4 = (bf16[1,16,4,1024]{3,2,1,0:T(4,128)(2,1)S(1)}, bf16[1,16,4,1024]{3,2,1,0:T(4,128)(2,1)}, u32[]{:S(2)}) copy-start(bf16[1,16,4,1024]{3,2,1,0:T(4,128)(2,1)} %param.23) | copy-start | bytes 393220
  90.9 70.8 %copy-start.7 = (bf16[4,32]{1,0:T(4,128)(2,1)S(1)}, bf16[4,32]{1,0:T(4,128)(2,1)}, u32[]{:S(2)}) copy-start(bf16[4,32]{1,0:T(4,128)(2,1)} %param.24) | copy-start | bytes 772
  91.0 70.8 %copy-start.8 = (f32[32]{0:T(128)S(1)}, f32[32]{0:T(128)}, u32[]{:S(2)}) copy-start(f32[32]{0:T(128)} %param.25) | copy-start | bytes 388
  95.2 90.9 %copy-start.1 = (bf16[2,32,8,32,16]{3,4,2,1,0:T(8,128)(2,1)S(1)}, bf16[2,32,8,32,16]{3,4,2,1,0:T(8,128)(2,1)}, u32[]{:S(2)}) copy-start(bf16[2,32,8,32,16]{3,4,2,1,0:T(8,128)(2,1)} %param.28) | copy-start | bytes 1572868
  164.5 26.0 %copy-start.9 = (f32[8]{0:T(128)S(1)}, f32[8]{0:T(128)}, u32[]{:S(2)}) copy-start(f32[8]{0:T(128)} %param.27) | copy-start | bytes 100
  167.3 87.1 %reduce-scatter.2.cloned.1.call-start = ((), (), s32[]{:S(2)}) async-start(), calls=%async_computation.1 | async-start | bytes 5242880 | tf_op jit(solution)/shard_map/reduce_scatter | solution.py:225
  183.8 4.6 %copy-start.2 = (f32[32,32,16]{1,0,2:T(8,128)S(1)}, f32[32,32,16]{1,0,2:T(8,128)}, u32[]{:S(2)}) copy-start(f32[32,32,16]{1,0,2:T(8,128)} %get-tuple-element.119) | copy-start | bytes 196612
  183.8 4.6 %copy-start.3 = (f32[32,32,16]{1,0,2:T(8,128)S(1)}, f32[32,32,16]{1,0,2:T(8,128)}, u32[]{:S(2)}) copy-start(f32[32,32,16]{1,0,2:T(8,128)} %get-tuple-element.120) | copy-start | bytes 196612
  183.8 6.9 %copy-start.10 = (bf16[1,16,8,1024]{3,2,1,0:T(8,128)(2,1)S(1)}, bf16[1,16,8,1024]{3,2,1,0:T(8,128)(2,1)}, u32[]{:S(2)}) copy-start(bf16[1,16,8,1024]{3,2,1,0:T(8,128)(2,1)} %param.29) | copy-start | bytes 786436
Sparse Core Ops, SparseCore 0:
  167.4 16.3 all-reduce.3
  200.4 53.8 reduce-scatter.1
where the time goes:
time: 265 us; the launch traced here: 264 us
  waiting for transfers between devices  70.1 us (26%)
  blocking collectives  69.7 us (26%)
  other arithmetic  57 us (22%)
  local copies, waits for them, and re-layouts  29.6 us (11%)
  between operations  15.1 us (6%)
  matrix products  10.5 us (4%)
  starting transfers between devices  6.76 us (3%)
  loops' own time  4.74 us (2%)
    all_gather x1, blocking collectives, body(): lax.all_gather(coarse_low, ('grp', 'mem', 'row'), axis=0, tiled=True)  65.9 us
    reduce_scatter x1, waiting for transfers between devices, body(): lax.psum_scatter(grad_terms, 'grp', scatter_dimension=3, tiled=True)  52.2 us
    add x6, other arithmetic, advance(): return current + step_size * change  36.1 us
    psum x1, waiting for transfers between devices, body(): lax.psum((part_real * norm_scale, part_imag * norm_scale), 'mem')  16.1 us
    while x6, local copies, waits for them, and re-layouts  13.1 us
    slice x12, local copies, waits for them, and re-layouts, advance(): right_cells = jnp.roll(current, -1, axis=2)  8.89 us
  transfers between devices with their start and end apart: 4, of which 3 were waited for; matrix products, arithmetic and copies ran while one was open for 4% of the time, Pallas kernels for 0%

commit v1 on v0

--- a/solution.py
+++ b/solution.py
@@ -142,6 +142,50 @@
 def lift_rows(sample, lift_weight, lift_bias):
     lifted = jnp.einsum("ycx,ch->yhx", sample, lift_weight, preferred_element_type=jnp.float32)
     return (lifted + lift_bias[None, :, None]).astype(jnp.bfloat16)
+
+
+def gather_along(block, axis):
+    count = lax.axis_size(axis)
+    index = lax.axis_index(axis)
+    gathered = jnp.zeros((count,) + block.shape, block.dtype)
+    for shift in range(count):
+        if shift == 0:
+            piece = block
+        else:
+            piece = lax.ppermute(block, axis, [(i, (i + shift) % count) for i in range(count)])
+        gathered = lax.dynamic_update_index_in_dim(gathered, piece, (index - shift) % count, 0)
+    return gathered
+
+
+def gather_rows(block, axes):
+    for axis in reversed(axes):
+        block = gather_along(block, axis)
+    return block.reshape((-1,) + block.shape[len(axes):])
+
+
+def pair_sum(values, axis):
+    if lax.axis_size(axis) != 2:
+        return lax.psum(values, axis)
+    other = lax.ppermute(values, axis, [(0, 1), (1, 0)])
+    return jax.tree.map(lambda mine, theirs: mine + theirs, values, other)
+
+
+def group_grads(back_real, back_imag, mode_real, mode_imag, axis):
+    count = lax.axis_size(axis)
+    index = lax.axis_index(axis)
+    block = mode_real.shape[1] // count
+    total = None
+    for shift in range(count):
+        target = (index + shift) % count
+        piece = tuple(
+            lax.dynamic_slice_in_dim(part, target * block, block, 1)
+            for part in (back_real, back_imag, mode_real, mode_imag)
+        )
+        if shift:
+            piece = lax.ppermute(piece, axis, [(i, (i + shift) % count) for i in range(count)])
+        term = weight_grads(*piece)
+        total = term if total is None else total + term
+    return total
 
 
 def body(
@@ -180,7 +224,7 @@
     owners = lax.dynamic_slice_in_dim(assign, member * member_rows, member_rows, 0)
     chosen = (owners == lax.axis_index("grp"))[:, None, None]
     forward_table = column_table()
-    every_row = lax.all_gather(coarse_low, ("grp", "mem", "row"), axis=0, tiled=True)
+    every_row = gather_rows(coarse_low[0], ("grp", "mem", "row"))
     fresh_rows = lax.dynamic_slice_in_dim(every_row, member * member_rows, member_rows, 0)
     sample = jnp.where(chosen, fresh_rows, buffer[0])
     hidden = lift_rows(sample, lift_weight, lift_bias)
@@ -192,7 +236,7 @@
     part_real, part_imag = rows_forward(
         column_part[:, :, :MODES], column_part[:, :, MODES:], cosine_table, sine_table
     )
-    mode_real, mode_imag = lax.psum((part_real * norm_scale, part_imag * norm_scale), "mem")
+    mode_real, mode_imag = pair_sum((part_real * norm_scale, part_imag * norm_scale), "mem")
     mixed_real, mixed_imag = mix_modes(spectral_weight.astype(jnp.float32), mode_real, mode_imag)
     spatial = (
         jnp.einsum(
@@ -217,12 +261,11 @@
         back_part[:, :, :MODES], back_part[:, :, MODES:], cosine_table, sine_table
     )
     weights_mode = jnp.where(jnp.arange(MODES) == 0, 1.0, 2.0).astype(jnp.float32) * norm_scale
-    back_real, back_imag = lax.psum((back_real * weights_mode, back_imag * weights_mode), "mem")
+    back_real, back_imag = pair_sum((back_real * weights_mode, back_imag * weights_mode), "mem")
     block_size = HID // lax.axis_size("mem")
     block_real = lax.dynamic_slice_in_dim(mode_real, member * block_size, block_size, 0)
     block_imag = lax.dynamic_slice_in_dim(mode_imag, member * block_size, block_size, 0)
-    grad_terms = weight_grads(back_real, back_imag, block_real, block_imag)
-    summed = lax.psum_scatter(grad_terms, "grp", scatter_dimension=3, tiled=True)
+    summed = group_grads(back_real, back_imag, block_real, block_imag, "grp")
     return (coarse_rows, layer_rows, summed / lax.axis_size("grp"))
 
 

time: 265 us -> 158 us (0.60)
  blocking collectives: 69.7 us -> 0 us
  waiting for transfers between devices: 70.1 us -> 11.6 us
  starting transfers between devices: 6.76 us -> 52.2 us
  other arithmetic: 57 us -> 41.4 us
  between operations: 15.1 us -> 2.03 us
  matrix products: 10.5 us -> 17.1 us
    all_gather x1 -> x0, blocking collectives: 65.9 us -> none  [body(): lax.all_gather(coarse_low, ('grp', 'mem', 'row'), axis=0, tiled=True)]
    reduce_scatter x1 -> x0, waiting for transfers between devices: 52.2 us -> none  [body(): lax.psum_scatter(grad_terms, 'grp', scatter_dimension=3, tiled=True)]
    ppermute x0 -> x23, starting transfers between devices: none -> 45.8 us  [the longest x7 30.2 us: gather_along(): lax.ppermute(block, axis, [(i, (i + shift) % count) for i in range(count)])]
    psum x1 -> x0, waiting for transfers between devices: 16.1 us -> none  [body(): lax.psum((part_real * norm_scale, part_imag * norm_scale), 'mem')]
    add x6 -> x4, other arithmetic: 36.1 us -> 23.9 us  [advance(): return current + step_size * change]
    ppermute x0 -> x23, waiting for transfers between devices: none -> 11.6 us  [the longest x12 6.7 us: group_grads(): lax.ppermute(piece, axis, [(i, (i + shift) % count) for i in range(count)])]
    dot_general x0 -> x4, matrix products: none -> 7.26 us  [the longest x1 1.82 us: mix_modes(): jnp.einsum('hojl,hjl->ojl', spectral[0], mode_real, precision=highest)]
    squeeze x0 -> x3, local copies, waits for them, and re-layouts: none -> 7.2 us  [the longest x2 4.21 us: mix_modes(): spectral[1]]
  transfers between devices with their start and end apart: 4 -> 25, of which waited for: 3 -> 12; matrix products, arithmetic and copies ran while one was open for 4% -> 14% of each run, Pallas kernels for 0% -> 0%
where the time goes in v1:
time: 158 us
  starting transfers between devices  52.2 us (33%)
  other arithmetic  41.4 us (26%)
  local copies, waits for them, and re-layouts  30.1 us (19%)
  matrix products  17.1 us (11%)
  waiting for transfers between devices  11.6 us (7%)
  loops' own time  3.38 us (2%)
  between operations  2.03 us (1%)
    ppermute x7, starting transfers between devices, gather_along(): lax.ppermute(block, axis, [(i, (i + shift) % count) for i in range(count)])  30.2 us
    add x4, other arithmetic, advance(): return current + step_size * change  23.9 us
    ppermute x12, starting transfers between devices, group_grads(): lax.ppermute(piece, axis, [(i, (i + shift) % count) for i in range(count)])  14.8 us
    while x4, local copies, waits for them, and re-layouts  8.76 us
    ppermute x12, waiting for transfers between devices, group_grads(): lax.ppermute(piece, axis, [(i, (i + shift) % count) for i in range(count)])  6.7 us
    slice x8, local copies, waits for them, and re-layouts, advance(): right_cells = jnp.roll(current, -1, axis=2)  5.93 us
    ppermute x7, waiting for transfers between devices, gather_along(): lax.ppermute(block, axis, [(i, (i + shift) % count) for i in range(count)])  4.51 us
    squeeze x2, local copies, waits for them, and re-layouts, mix_modes(): spectral[1]  4.21 us
  transfers between devices with their start and end apart: 25, of which 12 were waited for; matrix products, arithmetic and copies ran while one was open for 14% of the time, Pallas kernels for 0%

profile of v1, /device:TPU:0, one launch (start us, length us, event | category | flops | bytes accessed | tf_op | source)
XLA Modules:
  0.0 157.8 jit_solution(4108788901877914138)
XLA Ops:
  0.7 2.8 %fusion.161 = (bf16[4,1,16384]{2,1,0:T(2,128)(2,1)}, bf16[4,1,16384]{2,1,0:T(2,128)(2,1)}) fusion(bf16[4,16,16384]{2,1,0:T(8,128)(2,1)} %param.16), kind=kLoop, calls=%fused_computation.235 | loop fusion | bytes 524288 | tf_op jit(solution)/shard_map/slice | solution.py:27
  3.4 3.0 %collective-permute-start = (bf16[4,1,16384]{2,1,0:T(2,128)(2,1)}, bf16[4,1,16384]{2,1,0:T(2,128)(2,1)}, u32[]{:S(2)}, u32[]{:S(2)}) collective-permute-start(bf16[4,1,16384]{2,1,0:T(2,128)(2,1)} %get-tuple-element.122), channel_id=1, source_target_pairs={{0,1},{1,2},{2,3},{3,4},{4,5},{5,6},{6,7},{7,8},{8,9},{9,10},{10,1... | collective-permute-start | bytes 393224 | tf_op jit(solution)/shard_map/ppermute | solution.py:24
  6.4 3.4 %collective-permute-start.1 = (bf16[4,1,16384]{2,1,0:T(2,128)(2,1)}, bf16[4,1,16384]{2,1,0:T(2,128)(2,1)}, u32[]{:S(2)}, u32[]{:S(2)}) collective-permute-start(bf16[4,1,16384]{2,1,0:T(2,128)(2,1)} %get-tuple-element.121), channel_id=1, source_target_pairs={{1,0},{2,1},{3,2},{4,3},{5,4},{6,5},{7,6},{8,7},{9,8},{10,9},{11,1... | collective-permute-start | bytes 393224 | tf_op jit(solution)/shard_map/ppermute | solution.py:27
  9.8 1.0 fusion.164
  10.8 0.8 slice_bitcast_fusion.2
  11.6 1.9 %slice_bitcast_fusion = (bf16[32,8,32,16]{2,3,1,0:T(8,128)(2,1)S(1)}, bf16[32,8,32,16]{2,3,1,0:T(8,128)(2,1)S(1)}) fusion(bf16[2,32,8,32,16]{3,4,2,1,0:T(8,128)(2,1)} %param.28), kind=kLoop, calls=%fused_computation.33 | loop fusion | bytes 1048576 | tf_op jit(solution)/shard_map/squeeze | solution.py:118
  14.1 3.8 %convert_element_type.65 = f32[4,16,16384]{2,1,0:T(8,128)} convert(bf16[4,16,16384]{2,1,0:T(8,128)(2,1)} %param.16) | non-fusion elementwise | flops 1048576 | bytes 6291456 | tf_op jit(solution)/shard_map/convert_element_type | solution.py:209
  18.6 2.3 %copy.69 = bf16[32,8,32,16]{0,1,3,2:T(8,128)(2,1)S(1)} copy(bf16[32,8,32,16]{2,3,1,0:T(8,128)(2,1)S(1)} %get-tuple-element.119) | data formatting | bytes 524288 | tf_op jit(solution)/shard_map/squeeze | solution.py:118
  20.9 3.0 %copy.66 = bf16[32,8,32,16]{0,1,3,2:T(8,128)(2,1)} copy(bf16[32,8,32,16]{2,3,1,0:T(8,128)(2,1)S(1)} %get-tuple-element.120) | data formatting | bytes 524288 | tf_op jit(solution)/shard_map/squeeze | solution.py:117
  24.0 0.9 negate_convert_fusion
  24.9 1.2 convert_element_type.68
  26.2 1.2 convert_element_type.69
  27.4 43.4 %while.11 = (s32[]{:T(128)}, f32[4,16,16384]{2,1,0:T(8,128)}, s32[]{:T(128)}, f32[]{:T(128)}, f32[4,1,16384]{2,1,0:T(1,128)S(1)}, /*index=5*/f32[4,1,16384]{2,1,...) while((s32[]{:T(128)}, f32[4,16,16384]{2,1,0:T(8,128)}, ...), condition=%wide.region_1.2_spmd.clone, body=%wide.region_0.1_spmd.clone.sunk | while | flops 20185088 | bytes 48955712 | solution.py:54
  28.3 2.2 %copy.118 = f32[4,16,16384]{2,1,0:T(8,128)S(1)} copy(f32[4,16,16384]{2,1,0:T(8,128)} %get-tuple-element.259) | data formatting | bytes 8388608 | tf_op jit(solution)/shard_map/while
  30.5 1.4 fusion.193
  32.1 6.0 %multiply_add_fusion.2 = f32[4,16,16384]{2,1,0:T(8,128)} fusion(f32[4,16,16384]{2,1,0:T(8,128)S(1)} %copy.118, f32[4,1,16384]{2,1,0:T(1,128)S(1)} %get-tuple-element.276, f32[4,1,16384]{2,1,0:T(1,128)S(1)} %get-tuple-element.275, f32[4,16,16383]{2,1,0:T(8,128)S(1)} %get-tuple-element.239, f32[4,16,1]{2,1,0:T(8,128)S(1)} %get-tuple-element.240, ...), kind=kLoop, calls=%fused_computation.7.clone.1 | loop fusion | flops 18874368 | bytes 20447236 | tf_op jit(solution)/shard_map/while/body/add | solution.py:52
  39.0 2.2 %copy.118 = f32[4,16,16384]{2,1,0:T(8,128)S(1)} copy(f32[4,16,16384]{2,1,0:T(8,128)} %get-tuple-element.259) | data formatting | bytes 8388608 | tf_op jit(solution)/shard_map/while
  41.2 1.4 fusion.193
  42.8 6.0 %multiply_add_fusion.2 = f32[4,16,16384]{2,1,0:T(8,128)} fusion(f32[4,16,16384]{2,1,0:T(8,128)S(1)} %copy.118, f32[4,1,16384]{2,1,0:T(1,128)S(1)} %get-tuple-element.276, f32[4,1,16384]{2,1,0:T(1,128)S(1)} %get-tuple-element.275, f32[4,16,16383]{2,1,0:T(8,128)S(1)} %get-tuple-element.239, f32[4,16,1]{2,1,0:T(8,128)S(1)} %get-tuple-element.240, ...), kind=kLoop, calls=%fused_computation.7.clone.1 | loop fusion | flops 18874368 | bytes 20447236 | tf_op jit(solution)/shard_map/while/body/add | solution.py:52
  49.7 2.2 %copy.118 = f32[4,16,16384]{2,1,0:T(8,128)S(1)} copy(f32[4,16,16384]{2,1,0:T(8,128)} %get-tuple-element.259) | data formatting | bytes 8388608 | tf_op jit(solution)/shard_map/while
  51.9 1.4 fusion.193
  53.5 6.0 %multiply_add_fusion.2 = f32[4,16,16384]{2,1,0:T(8,128)} fusion(f32[4,16,16384]{2,1,0:T(8,128)S(1)} %copy.118, f32[4,1,16384]{2,1,0:T(1,128)S(1)} %get-tuple-element.276, f32[4,1,16384]{2,1,0:T(1,128)S(1)} %get-tuple-element.275, f32[4,16,16383]{2,1,0:T(8,128)S(1)} %get-tuple-element.239, f32[4,16,1]{2,1,0:T(8,128)S(1)} %get-tuple-element.240, ...), kind=kLoop, calls=%fused_computation.7.clone.1 | loop fusion | flops 18874368 | bytes 20447236 | tf_op jit(solution)/shard_map/while/body/add | solution.py:52
  60.4 2.2 %copy.118 = f32[4,16,16384]{2,1,0:T(8,128)S(1)} copy(f32[4,16,16384]{2,1,0:T(8,128)} %get-tuple-element.259) | data formatting | bytes 8388608 | tf_op jit(solution)/shard_map/while
  62.5 1.4 fusion.193
  64.2 6.0 %multiply_add_fusion.2 = f32[4,16,16384]{2,1,0:T(8,128)} fusion(f32[4,16,16384]{2,1,0:T(8,128)S(1)} %copy.118, f32[4,1,16384]{2,1,0:T(1,128)S(1)} %get-tuple-element.276, f32[4,1,16384]{2,1,0:T(1,128)S(1)} %get-tuple-element.275, f32[4,16,16383]{2,1,0:T(8,128)S(1)} %get-tuple-element.239, f32[4,16,1]{2,1,0:T(8,128)S(1)} %get-tuple-element.240, ...), kind=kLoop, calls=%fused_computation.7.clone.1 | loop fusion | flops 18874368 | bytes 20447236 | tf_op jit(solution)/shard_map/while/body/add | solution.py:52
  70.8 2.9 %reduce_sum.10 = f32[4,16384]{1,0:T(4,128)S(1)} reduce(f32[4,16,16384]{2,1,0:T(8,128)} %get-tuple-element.51, f32[]{:T(128)} %constant.322.clone.1), dimensions={1}, to_apply=%region_2.3 | reduce | flops 983040 | bytes 4456452 | tf_op jit(solution)/shard_map/reduce_sum | solution.py:58
  73.7 0.7 reduce_sum.14
  74.4 0.6 reduce_sum.18
  75.2 3.7 %collective-permute-start.4 = (bf16[4,1024]{1,0:T(4,128)(2,1)S(1)}, bf16[4,1024]{1,0:T(4,128)(2,1)S(1)}, u32[]{:S(2)}, u32[]{:S(2)}) collective-permute-start(bf16[4,1024]{1,0:T(4,128)(2,1)S(1)} %multiply_convert_fusion), channel_id=1, source_target_pairs={{0,3},{1,0},{2,1},{3,2},{4,7},{5,4},{6,5},{7,6},{8,11},{9,8},{10,9... | collective-permute-start | bytes 24584 | tf_op jit(solution)/shard_map/ppermute | solution.py:155
  79.0 0.6 convert_dynamic-update-slice_fusion
  79.6 1.0 collective-permute-done.2
  81.3 1.1 collective-permute-done.5
  82.5 22.4 %collective-permute-start.6 = (bf16[2,4,4,1024]{3,2,1,0:T(4,128)(2,1)S(1)}, bf16[2,4,4,1024]{3,2,1,0:T(4,128)(2,1)S(1)}, u32[]{:S(2)}, u32[]{:S(2)}) collective-permute-start(bf16[2,4,4,1024]{3,2,1,0:T(4,128)(2,1)S(1)} %bitcast_dynamic-update-slice_fusion.4), channel_id=1, source_target_pairs={{0,8},{8,16},{16,24},{24,0},{1,9},{9,17},{17,25},{25,1},{2,10},{10... | collective-permute-start | bytes 196616 | tf_op jit(solution)/shard_map/ppermute | solution.py:155
  104.9 1.0 collective-permute-start.7
  105.9 2.8 %collective-permute-start.8 = (bf16[2,4,4,1024]{3,2,1,0:T(4,128)(2,1)S(1)}, bf16[2,4,4,1024]{3,2,1,0:T(4,128)(2,1)S(1)}, u32[]{:S(2)}, u32[]{:S(2)}) collective-permute-start(bf16[2,4,4,1024]{3,2,1,0:T(4,128)(2,1)S(1)} %bitcast_dynamic-update-slice_fusion.4), channel_id=1, source_target_pairs={{0,24},{8,0},{16,8},{24,16},{1,25},{9,1},{17,9},{25,17},{2,26},{10... | collective-permute-start | bytes 196616 | tf_op jit(solution)/shard_map/ppermute | solution.py:155
  109.2 1.6 %collective-permute-done.8 = bf16[2,4,4,1024]{3,2,1,0:T(4,128)(2,1)S(1)} collective-permute-done((bf16[2,4,4,1024]{3,2,1,0:T(4,128)(2,1)S(1)}, bf16[2,4,4,1024]{3,2,1,0:T(4,128)(2,1)S(1)}, u32[]{:S(2)}, u32[]{:S(2)}) %collective-permute-start.8) | collective-permute-done | bytes 65568 | tf_op jit(solution)/shard_map/ppermute | solution.py:155
  110.9 1.4 fusion.6
  112.3 0.9 fusion.72
  114.3 0.5 fusion.10
  115.5 0.6 collective-permute-start.9
  116.5 1.8 %fusion.41 = f32[32,16,1,8]{3,2,1,0:T(1,128)S(1)} fusion(bf16[32,8,32,16]{0,1,3,2:T(8,128)(2,1)S(1)} %copy.69, f32[32,32,16,1]{0,1,2,3:T(8,128)S(1)} %bitcast.180), kind=kOutput, calls=%fused_computation.75 | convolution fusion | flops 1572864 | bytes 344064 | tf_op jit(solution)/shard_map/hojl,hjl->ojl/dot_general | solution.py:118
  118.4 1.8 %fusion.43 = f32[32,16,1,8]{3,2,1,0:T(1,128)S(1)} fusion(bf16[32,8,32,16]{0,1,3,2:T(8,128)(2,1)S(1)} %copy.69, f32[32,32,16,1]{0,1,2,3:T(8,128)S(1)} %bitcast.182), kind=kOutput, calls=%fused_computation.77 | convolution fusion | flops 1572864 | bytes 344064 | tf_op jit(solution)/shard_map/hojl,hjl->ojl/dot_general | solution.py:121
  120.3 1.8 %fusion.45 = f32[32,16,1,8]{3,2,1,0:T(1,128)S(1)} fusion(bf16[32,8,32,16]{0,1,3,2:T(8,128)(2,1)S(1)} %copy-done.1, f32[32,32,16,1]{0,1,2,3:T(8,128)S(1)} %bitcast.183), kind=kOutput, calls=%fused_computation.79 | convolution fusion | flops 1572864 | bytes 344064 | tf_op jit(solution)/shard_map/hojl,hjl->ojl/dot_general | solution.py:116
  122.1 1.8 %fusion.39 = f32[32,16,1,8]{3,2,1,0:T(1,128)S(1)} fusion(bf16[32,8,32,16]{0,1,3,2:T(8,128)(2,1)S(1)} %copy-done.1, f32[32,32,16,1]{0,1,2,3:T(8,128)S(1)} %bitcast.181), kind=kOutput, calls=%fused_computation.73 | convolution fusion | flops 1572864 | bytes 344064 | tf_op jit(solution)/shard_map/hojl,hjl->ojl/dot_general | solution.py:119
  124.1 0.6 fusion.90
  124.8 0.7 fusion.78
  125.7 0.6 fusion.80
  126.3 0.7 fusion.88
  127.4 0.9 convolution_multiply_fusion
  128.6 1.8 %fusion.36 = bf16[1,16,8,1024]{3,2,1,0:T(8,128)(2,1)} fusion(f32[16,8,1024]{2,1,0:T(8,128)S(1)} %fusion.8), kind=kLoop, calls=%fused_computation.71 | loop fusion | flops 8519680 | bytes 786432 | tf_op jit(solution)/shard_map/broadcast_in_dim | solution.py:255
  131.4 3.1 %collective-permute-start.21 = (f32[16,8,16]{0,1,2:T(8,128)S(1)}, f32[16,8,16]{0,1,2:T(8,128)S(1)}, u32[]{:S(2)}, u32[]{:S(2)}) collective-permute-start(f32[16,8,16]{0,1,2:T(8,128)S(1)} %get-tuple-element.123), channel_id=1, source_target_pairs={{0,24},{8,0},{16,8},{24,16},{1,25},{9,1},{17,9},{25,17},{2,26},{10... | collective-permute-start | bytes 24584 | tf_op jit(solution)/shard_map/ppermute | solution.py:185
  135.7 1.7 %collective-permute-start.19 = (f32[16,8,16]{0,1,2:T(8,128)S(1)}, f32[16,8,16]{0,1,2:T(8,128)S(1)}, u32[]{:S(2)}, u32[]{:S(2)}) collective-permute-start(f32[16,8,16]{0,1,2:T(8,128)S(1)} %get-tuple-element.128), channel_id=1, source_target_pairs={{0,16},{8,24},{16,0},{24,8},{1,17},{9,25},{17,1},{25,9},{2,18},{10... | collective-permute-start | bytes 24584 | tf_op jit(solution)/shard_map/ppermute | solution.py:185
  137.4 2.0 %collective-permute-start.13 = (f32[16,8,16]{0,1,2:T(8,128)S(1)}, f32[16,8,16]{0,1,2:T(8,128)S(1)}, u32[]{:S(2)}, u32[]{:S(2)}) collective-permute-start(f32[16,8,16]{0,1,2:T(8,128)S(1)} %get-tuple-element.125), channel_id=1, source_target_pairs={{0,8},{8,16},{16,24},{24,0},{1,9},{9,17},{17,25},{25,1},{2,10},{10... | collective-permute-start | bytes 24584 | tf_op jit(solution)/shard_map/ppermute | solution.py:185
  140.7 2.5 %collective-permute-done.19 = f32[16,8,16]{0,1,2:T(8,128)S(1)} collective-permute-done((f32[16,8,16]{0,1,2:T(8,128)S(1)}, f32[16,8,16]{0,1,2:T(8,128)S(1)}, u32[]{:S(2)}, u32[]{:S(2)}) %collective-permute-start.19) | collective-permute-done | bytes 8224 | tf_op jit(solution)/shard_map/ppermute | solution.py:185
  143.5 1.0 collective-permute-done.15
  144.8 0.8 collective-permute-start.22
  145.8 2.2 %collective-permute-start.24 = (f32[8,8,16]{1,2,0:T(8,128)S(1)}, f32[8,8,16]{1,2,0:T(8,128)S(1)}, u32[]{:S(2)}, u32[]{:S(2)}) collective-permute-start(f32[8,8,16]{1,2,0:T(8,128)S(1)} %get-tuple-element.145), channel_id=1, source_target_pairs={{0,24},{8,0},{16,8},{24,16},{1,25},{9,1},{17,9},{25,17},{2,26},{10... | collective-permute-start | bytes 12296 | tf_op jit(solution)/shard_map/ppermute | solution.py:185
  148.0 0.6 collective-permute-start.18
  148.5 1.5 collective-permute-start.20
  150.1 2.0 %collective-permute-start.16 = (f32[8,8,16]{1,2,0:T(8,128)S(1)}, f32[8,8,16]{1,2,0:T(8,128)S(1)}, u32[]{:S(2)}, u32[]{:S(2)}) collective-permute-start(f32[8,8,16]{1,2,0:T(8,128)S(1)} %get-tuple-element.147), channel_id=1, source_target_pairs={{0,8},{8,16},{16,24},{24,0},{1,9},{9,17},{17,25},{25,1},{2,10},{10... | collective-permute-start | bytes 12296 | tf_op jit(solution)/shard_map/ppermute | solution.py:185
  152.9 0.6 collective-permute-done.20
  153.6 1.6 %collective-permute-done.14 = f32[8,8,16]{1,2,0:T(8,128)S(1)} collective-permute-done((f32[8,8,16]{1,2,0:T(8,128)S(1)}, f32[8,8,16]{1,2,0:T(8,128)S(1)}, u32[]{:S(2)}, u32[]{:S(2)}) %collective-permute-start.14) | collective-permute-done | bytes 4128 | tf_op jit(solution)/shard_map/ppermute | solution.py:185
  155.2 0.6 collective-permute-done.16
  156.4 1.4 fusion.19
  (128 shorter events, 12.6 us)
Async XLA Ops:
  0.6 127.7 %copy-start = (bf16[32,8]{0,1:T(8,128)(2,1)S(1)}, bf16[32,8]{0,1:T(8,128)(2,1)}, u32[]{:S(2)}) copy-start(bf16[32,8]{0,1:T(8,128)(2,1)} %param.26) | copy-start | bytes 1540
  0.6 13.4 %copy-start.8 = (s32[32]{0:T(128)S(1)}, s32[32]{0:T(128)}, u32[]{:S(2)}) copy-start(s32[32]{0:T(128)} %param.22) | copy-start | bytes 388
  3.4 21.5 %collective-permute-start = (bf16[4,1,16384]{2,1,0:T(2,128)(2,1)}, bf16[4,1,16384]{2,1,0:T(2,128)(2,1)}, u32[]{:S(2)}, u32[]{:S(2)}) collective-permute-start(bf16[4,1,16384]{2,1,0:T(2,128)(2,1)} %get-tuple-element.122), channel_id=1, source_target_pairs={{0,1},{1,2},{2,3},{3,4},{4,5},{5,6},{6,7},{7,8},{8,9},{9,10},{10,1... | collective-permute-start | bytes 393224 | tf_op jit(solution)/shard_map/ppermute | solution.py:24
  6.4 19.7 %collective-permute-start.1 = (bf16[4,1,16384]{2,1,0:T(2,128)(2,1)}, bf16[4,1,16384]{2,1,0:T(2,128)(2,1)}, u32[]{:S(2)}, u32[]{:S(2)}) collective-permute-start(bf16[4,1,16384]{2,1,0:T(2,128)(2,1)} %get-tuple-element.121), channel_id=1, source_target_pairs={{1,0},{2,1},{3,2},{4,3},{5,4},{6,5},{7,6},{8,7},{9,8},{10,9},{11,1... | collective-permute-start | bytes 393224 | tf_op jit(solution)/shard_map/ppermute | solution.py:27
  13.5 4.5 %copy-start.6 = (bf16[16384]{0:T(1024)(128)(2,1)S(1)}, bf16[16384]{0:T(1024)(128)(2,1)}, u32[]{:S(2)}) copy-start(bf16[16384]{0:T(1024)(128)(2,1)} %param.19) | copy-start | bytes 98308
  18.0 9.4 %copy-start.7 = (f32[16]{0:T(128)S(1)}, f32[16]{0:T(128)}, u32[]{:S(2)}) copy-start(f32[16]{0:T(128)} %param.18) | copy-start | bytes 196
  74.4 37.9 %copy-start.2 = (bf16[1024,16]{0,1:T(8,128)(2,1)S(1)}, bf16[1024,16]{0,1:T(8,128)(2,1)}, u32[]{:S(2)}) copy-start(bf16[1024,16]{0,1:T(8,128)(2,1)} %get-tuple-element.157) | copy-start | bytes 98308
  74.4 37.9 %copy-start.4 = (bf16[1024,16]{0,1:T(8,128)(2,1)S(1)}, bf16[1024,16]{0,1:T(8,128)(2,1)}, u32[]{:S(2)}) copy-start(bf16[1024,16]{0,1:T(8,128)(2,1)} %get-tuple-element.158) | copy-start | bytes 98308
  75.1 5.5 %collective-permute-start.2 = (bf16[4,1024]{1,0:T(4,128)(2,1)S(1)}, bf16[4,1024]{1,0:T(4,128)(2,1)S(1)}, u32[]{:S(2)}, u32[]{:S(2)}) collective-permute-start(bf16[4,1024]{1,0:T(4,128)(2,1)S(1)} %multiply_convert_fusion), channel_id=1, source_target_pairs={{0,1},{1,2},{2,3},{3,0},{4,5},{5,6},{6,7},{7,4},{8,9},{9,10},{10,1... | collective-permute-start | bytes 24584 | tf_op jit(solution)/shard_map/ppermute | solution.py:155
  75.1 5.5 %collective-permute-start.3 = (bf16[4,1024]{1,0:T(4,128)(2,1)S(1)}, bf16[4,1024]{1,0:T(4,128)(2,1)S(1)}, u32[]{:S(2)}, u32[]{:S(2)}) collective-permute-start(bf16[4,1024]{1,0:T(4,128)(2,1)S(1)} %multiply_convert_fusion), channel_id=1, source_target_pairs={{0,2},{1,3},{2,0},{3,1},{4,6},{5,7},{6,4},{7,5},{8,10},{9,11},{10,... | collective-permute-start | bytes 24584 | tf_op jit(solution)/shard_map/ppermute | solution.py:155
  75.2 5.9 %collective-permute-start.4 = (bf16[4,1024]{1,0:T(4,128)(2,1)S(1)}, bf16[4,1024]{1,0:T(4,128)(2,1)S(1)}, u32[]{:S(2)}, u32[]{:S(2)}) collective-permute-start(bf16[4,1024]{1,0:T(4,128)(2,1)S(1)} %multiply_convert_fusion), channel_id=1, source_target_pairs={{0,3},{1,0},{2,1},{3,2},{4,7},{5,4},{6,5},{7,6},{8,11},{9,8},{10,9... | collective-permute-start | bytes 24584 | tf_op jit(solution)/shard_map/ppermute | solution.py:155
  81.2 1.3 collective-permute-start.5
  82.5 26.4 %collective-permute-start.6 = (bf16[2,4,4,1024]{3,2,1,0:T(4,128)(2,1)S(1)}, bf16[2,4,4,1024]{3,2,1,0:T(4,128)(2,1)S(1)}, u32[]{:S(2)}, u32[]{:S(2)}) collective-permute-start(bf16[2,4,4,1024]{3,2,1,0:T(4,128)(2,1)S(1)} %bitcast_dynamic-update-slice_fusion.4), channel_id=1, source_target_pairs={{0,8},{8,16},{16,24},{24,0},{1,9},{9,17},{17,25},{25,1},{2,10},{10... | collective-permute-start | bytes 196616 | tf_op jit(solution)/shard_map/ppermute | solution.py:155
  104.9 4.3 %collective-permute-start.7 = (bf16[2,4,4,1024]{3,2,1,0:T(4,128)(2,1)S(1)}, bf16[2,4,4,1024]{3,2,1,0:T(4,128)(2,1)S(1)}, u32[]{:S(2)}, u32[]{:S(2)}) collective-permute-start(bf16[2,4,4,1024]{3,2,1,0:T(4,128)(2,1)S(1)} %bitcast_dynamic-update-slice_fusion.4), channel_id=1, source_target_pairs={{0,16},{8,24},{16,0},{24,8},{1,17},{9,25},{17,1},{25,9},{2,18},{10... | collective-permute-start | bytes 196616 | tf_op jit(solution)/shard_map/ppermute | solution.py:155
  105.9 4.9 %collective-permute-start.8 = (bf16[2,4,4,1024]{3,2,1,0:T(4,128)(2,1)S(1)}, bf16[2,4,4,1024]{3,2,1,0:T(4,128)(2,1)S(1)}, u32[]{:S(2)}, u32[]{:S(2)}) collective-permute-start(bf16[2,4,4,1024]{3,2,1,0:T(4,128)(2,1)S(1)} %bitcast_dynamic-update-slice_fusion.4), channel_id=1, source_target_pairs={{0,24},{8,0},{16,8},{24,16},{1,25},{9,1},{17,9},{25,17},{2,26},{10... | collective-permute-start | bytes 196616 | tf_op jit(solution)/shard_map/ppermute | solution.py:155
  113.2 7.0 %copy-start.1 = (bf16[32,8,32,16]{0,1,3,2:T(8,128)(2,1)S(1)}, bf16[32,8,32,16]{0,1,3,2:T(8,128)(2,1)}, u32[]{:S(2)}) copy-start(bf16[32,8,32,16]{0,1,3,2:T(8,128)(2,1)} %copy.66) | copy-start | bytes 786436
  114.9 1.6 %collective-permute-start.10 = (f32[32,32,16]{0,1,2:T(8,128)S(1)}, f32[32,32,16]{0,1,2:T(8,128)S(1)}, u32[]{:S(2)}, u32[]{:S(2)}) collective-permute-start(f32[32,32,16]{0,1,2:T(8,128)S(1)} %fusion.10), channel_id=1, source_target_pairs={{0,4},{4,0},{1,5},{5,1},{2,6},{6,2},{3,7},{7,3},{8,12},{12,8},{9,1... | collective-permute-start | bytes 196616 | tf_op jit(solution)/shard_map/ppermute | solution.py:169
  115.5 2.8 %collective-permute-start.9 = (f32[32,32,16]{0,1,2:T(8,128)S(1)}, f32[32,32,16]{0,1,2:T(8,128)S(1)}, u32[]{:S(2)}, u32[]{:S(2)}) collective-permute-start(f32[32,32,16]{0,1,2:T(8,128)S(1)} %fusion.12), channel_id=1, source_target_pairs={{0,4},{4,0},{1,5},{5,1},{2,6},{6,2},{3,7},{7,3},{8,12},{12,8},{9,1... | collective-permute-start | bytes 196616 | tf_op jit(solution)/shard_map/ppermute | solution.py:169
  120.2 8.1 %copy-start.9 = (f32[8]{0:T(128)S(1)}, f32[8]{0:T(128)}, u32[]{:S(2)}) copy-start(f32[8]{0:T(128)} %param.27) | copy-start | bytes 100
  123.9 6.5 %copy-start.3 = (bf16[1024,16]{0,1:T(8,128)(2,1)S(1)}, bf16[1024,16]{0,1:T(8,128)(2,1)}, u32[]{:S(2)}) copy-start(bf16[1024,16]{0,1:T(8,128)(2,1)} %get-tuple-element.157) | copy-start | bytes 98308
  123.9 6.5 %copy-start.5 = (bf16[1024,16]{0,1:T(8,128)(2,1)S(1)}, bf16[1024,16]{0,1:T(8,128)(2,1)}, u32[]{:S(2)}) copy-start(bf16[1024,16]{0,1:T(8,128)(2,1)} %get-tuple-element.158) | copy-start | bytes 98308
  123.9 6.5 %copy-start.10 = (bf16[1,16,8,1024]{3,2,1,0:T(8,128)(2,1)S(1)}, bf16[1,16,8,1024]{3,2,1,0:T(8,128)(2,1)}, u32[]{:S(2)}) copy-start(bf16[1,16,8,1024]{3,2,1,0:T(8,128)(2,1)} %param.29) | copy-start | bytes 786436
  131.4 6.0 %collective-permute-start.21 = (f32[16,8,16]{0,1,2:T(8,128)S(1)}, f32[16,8,16]{0,1,2:T(8,128)S(1)}, u32[]{:S(2)}, u32[]{:S(2)}) collective-permute-start(f32[16,8,16]{0,1,2:T(8,128)S(1)} %get-tuple-element.123), channel_id=1, source_target_pairs={{0,24},{8,0},{16,8},{24,16},{1,25},{9,1},{17,9},{25,17},{2,26},{10... | collective-permute-start | bytes 24584 | tf_op jit(solution)/shard_map/ppermute | solution.py:185
  134.5 4.8 %collective-permute-start.23 = (f32[16,8,16]{0,1,2:T(8,128)S(1)}, f32[16,8,16]{0,1,2:T(8,128)S(1)}, u32[]{:S(2)}, u32[]{:S(2)}) collective-permute-start(f32[16,8,16]{0,1,2:T(8,128)S(1)} %get-tuple-element.127), channel_id=1, source_target_pairs={{0,24},{8,0},{16,8},{24,16},{1,25},{9,1},{17,9},{25,17},{2,26},{10... | collective-permute-start | bytes 24584 | tf_op jit(solution)/shard_map/ppermute | solution.py:185
  135.2 9.4 %collective-permute-start.11 = (f32[8,32,16]{1,2,0:T(8,128)S(1)}, f32[8,32,16]{1,2,0:T(8,128)S(1)}, u32[]{:S(2)}, u32[]{:S(2)}) collective-permute-start(f32[8,32,16]{1,2,0:T(8,128)S(1)} %fusion.16), channel_id=1, source_target_pairs={{0,4},{4,0},{1,5},{5,1},{2,6},{6,2},{3,7},{7,3},{8,12},{12,8},{9,1... | collective-permute-start | bytes 49160 | tf_op jit(solution)/shard_map/ppermute | solution.py:169
  135.3 5.3 %collective-permute-start.17 = (f32[16,8,16]{0,1,2:T(8,128)S(1)}, f32[16,8,16]{0,1,2:T(8,128)S(1)}, u32[]{:S(2)}, u32[]{:S(2)}) collective-permute-start(f32[16,8,16]{0,1,2:T(8,128)S(1)} %get-tuple-element.124), channel_id=1, source_target_pairs={{0,16},{8,24},{16,0},{24,8},{1,17},{9,25},{17,1},{25,9},{2,18},{10... | collective-permute-start | bytes 24584 | tf_op jit(solution)/shard_map/ppermute | solution.py:185
  135.7 7.6 %collective-permute-start.19 = (f32[16,8,16]{0,1,2:T(8,128)S(1)}, f32[16,8,16]{0,1,2:T(8,128)S(1)}, u32[]{:S(2)}, u32[]{:S(2)}) collective-permute-start(f32[16,8,16]{0,1,2:T(8,128)S(1)} %get-tuple-element.128), channel_id=1, source_target_pairs={{0,16},{8,24},{16,0},{24,8},{1,17},{9,25},{17,1},{25,9},{2,18},{10... | collective-permute-start | bytes 24584 | tf_op jit(solution)/shard_map/ppermute | solution.py:185
  137.4 6.0 %collective-permute-start.13 = (f32[16,8,16]{0,1,2:T(8,128)S(1)}, f32[16,8,16]{0,1,2:T(8,128)S(1)}, u32[]{:S(2)}, u32[]{:S(2)}) collective-permute-start(f32[16,8,16]{0,1,2:T(8,128)S(1)} %get-tuple-element.125), channel_id=1, source_target_pairs={{0,8},{8,16},{16,24},{24,0},{1,9},{9,17},{17,25},{25,1},{2,10},{10... | collective-permute-start | bytes 24584 | tf_op jit(solution)/shard_map/ppermute | solution.py:185
  139.3 5.2 %collective-permute-start.15 = (f32[16,8,16]{0,1,2:T(8,128)S(1)}, f32[16,8,16]{0,1,2:T(8,128)S(1)}, u32[]{:S(2)}, u32[]{:S(2)}) collective-permute-start(f32[16,8,16]{0,1,2:T(8,128)S(1)} %get-tuple-element.129), channel_id=1, source_target_pairs={{0,8},{8,16},{16,24},{24,0},{1,9},{9,17},{17,25},{25,1},{2,10},{10... | collective-permute-start | bytes 24584 | tf_op jit(solution)/shard_map/ppermute | solution.py:185
  140.6 5.0 %collective-permute-start.12 = (f32[8,32,16]{1,2,0:T(8,128)S(1)}, f32[8,32,16]{1,2,0:T(8,128)S(1)}, u32[]{:S(2)}, u32[]{:S(2)}) collective-permute-start(f32[8,32,16]{1,2,0:T(8,128)S(1)} %fusion.14), channel_id=1, source_target_pairs={{0,4},{4,0},{1,5},{5,1},{2,6},{6,2},{3,7},{7,3},{8,12},{12,8},{9,1... | collective-permute-start | bytes 49160 | tf_op jit(solution)/shard_map/ppermute | solution.py:169
  144.8 5.4 %collective-permute-start.22 = (f32[8,8,16]{1,2,0:T(8,128)S(1)}, f32[8,8,16]{1,2,0:T(8,128)S(1)}, u32[]{:S(2)}, u32[]{:S(2)}) collective-permute-start(f32[8,8,16]{1,2,0:T(8,128)S(1)} %get-tuple-element.141), channel_id=1, source_target_pairs={{0,24},{8,0},{16,8},{24,16},{1,25},{9,1},{17,9},{25,17},{2,26},{10... | collective-permute-start | bytes 12296 | tf_op jit(solution)/shard_map/ppermute | solution.py:185
  145.8 6.6 %collective-permute-start.24 = (f32[8,8,16]{1,2,0:T(8,128)S(1)}, f32[8,8,16]{1,2,0:T(8,128)S(1)}, u32[]{:S(2)}, u32[]{:S(2)}) collective-permute-start(f32[8,8,16]{1,2,0:T(8,128)S(1)} %get-tuple-element.145), channel_id=1, source_target_pairs={{0,24},{8,0},{16,8},{24,16},{1,25},{9,1},{17,9},{25,17},{2,26},{10... | collective-permute-start | bytes 12296 | tf_op jit(solution)/shard_map/ppermute | solution.py:185
  148.0 4.8 %collective-permute-start.18 = (f32[8,8,16]{1,2,0:T(8,128)S(1)}, f32[8,8,16]{1,2,0:T(8,128)S(1)}, u32[]{:S(2)}, u32[]{:S(2)}) collective-permute-start(f32[8,8,16]{1,2,0:T(8,128)S(1)} %get-tuple-element.142), channel_id=1, source_target_pairs={{0,16},{8,24},{16,0},{24,8},{1,17},{9,25},{17,1},{25,9},{2,18},{10... | collective-permute-start | bytes 12296 | tf_op jit(solution)/shard_map/ppermute | solution.py:185
  148.5 5.0 %collective-permute-start.20 = (f32[8,8,16]{1,2,0:T(8,128)S(1)}, f32[8,8,16]{1,2,0:T(8,128)S(1)}, u32[]{:S(2)}, u32[]{:S(2)}) collective-permute-start(f32[8,8,16]{1,2,0:T(8,128)S(1)} %get-tuple-element.146), channel_id=1, source_target_pairs={{0,16},{8,24},{16,0},{24,8},{1,17},{9,25},{17,1},{25,9},{2,18},{10... | collective-permute-start | bytes 12296 | tf_op jit(solution)/shard_map/ppermute | solution.py:185
  150.0 5.2 %collective-permute-start.14 = (f32[8,8,16]{1,2,0:T(8,128)S(1)}, f32[8,8,16]{1,2,0:T(8,128)S(1)}, u32[]{:S(2)}, u32[]{:S(2)}) collective-permute-start(f32[8,8,16]{1,2,0:T(8,128)S(1)} %get-tuple-element.143), channel_id=1, source_target_pairs={{0,8},{8,16},{16,24},{24,0},{1,9},{9,17},{17,25},{25,1},{2,10},{10... | collective-permute-start | bytes 12296 | tf_op jit(solution)/shard_map/ppermute | solution.py:185
  150.1 5.7 %collective-permute-start.16 = (f32[8,8,16]{1,2,0:T(8,128)S(1)}, f32[8,8,16]{1,2,0:T(8,128)S(1)}, u32[]{:S(2)}, u32[]{:S(2)}) collective-permute-start(f32[8,8,16]{1,2,0:T(8,128)S(1)} %get-tuple-element.147), channel_id=1, source_target_pairs={{0,8},{8,16},{16,24},{24,0},{1,9},{9,17},{17,25},{25,1},{2,10},{10... | collective-permute-start | bytes 12296 | tf_op jit(solution)/shard_map/ppermute | solution.py:185

commit v2 on v1

--- a/solution.py
+++ b/solution.py
@@ -3,6 +3,8 @@
 import jax
 import jax.numpy as jnp
 from jax import lax
+from jax.experimental import pallas as pl
+from jax.experimental.pallas import tpu as pltpu
 from jax.sharding import PartitionSpec as P
 
 C = 4
@@ -27,6 +29,15 @@
         high = lax.ppermute(lax.slice_in_dim(block, 0, width, axis=dim), axis, backward)
         block = jnp.concatenate([low, block, high], axis=dim)
     return block
+
+
+def halo_rows(block, axis):
+    count = lax.axis_size(axis)
+    forward = [(i, (i + 1) % count) for i in range(count)]
+    backward = [((i + 1) % count, i) for i in range(count)]
+    above = lax.ppermute(block[:, -1:], axis, forward)
+    below = lax.ppermute(block[:, :1], axis, backward)
+    return above, below
 
 
 def slab_solve(
@@ -52,6 +63,111 @@
         return current + step_size * change
 
     return lax.fori_loop(jnp.zeros((), jnp.int32), substeps, advance, slab_rows)
+
+
+CHUNK = 512
+
+
+def solve_kernel(
+    step_ref, count_ref, field_ref, above_ref, below_ref, krow_ref, drow_ref, kcol_ref, dcol_ref,
+    out_ref, state_ref, coef_ref,
+):
+    tracers, rows, width = field_ref.shape
+    chunks = width // CHUNK
+
+    def chunk_at(index):
+        return pl.ds(pl.multiple_of(index * CHUNK, CHUNK), CHUNK)
+
+    def prepare(index, carry):
+        cols = chunk_at(index)
+        coef_ref[0, :, cols] = krow_ref[...] * kcol_ref[:, cols].astype(jnp.float32)
+        coef_ref[1, :, cols] = 0.5 * (drow_ref[0] * dcol_ref[0, :, cols].astype(jnp.float32))
+        coef_ref[2, :, cols] = 0.5 * (drow_ref[1] * dcol_ref[1, :, cols].astype(jnp.float32))
+        for tracer in range(tracers):
+            state_ref[0, tracer, :, cols] = field_ref[tracer, :, cols].astype(jnp.float32)
+        return carry
+
+    lax.fori_loop(0, chunks, prepare, 0)
+    step = step_ref[0]
+    row_ids = lax.broadcasted_iota(jnp.int32, (rows, CHUNK), 0)
+
+    def substep(number, carry):
+        source = number % 2
+        target = 1 - source
+
+        def update(index, inner):
+            tracer = index // chunks
+            column = index % chunks
+            cols = chunk_at(column)
+            before = pl.ds(pl.multiple_of(((column * CHUNK - 128) % width), 128), 128)
+            after = pl.ds(pl.multiple_of((((column + 1) * CHUNK) % width), 128), 128)
+            current = state_ref[source, tracer, :, cols]
+            extended = jnp.concatenate(
+                [state_ref[source, tracer, :, before], current, state_ref[source, tracer, :, after]],
+                axis=1,
+            )
+            span = CHUNK + 256
+            right_cells = pltpu.roll(extended, span - 1, 1)[:, 128 : 128 + CHUNK]
+            left_cells = pltpu.roll(extended, 1, 1)[:, 128 : 128 + CHUNK]
+            upper_rows = jnp.where(
+                row_ids == 0, above_ref[tracer, :, cols], pltpu.roll(current, 1, 0)
+            )
+            lower_rows = jnp.where(
+                row_ids == rows - 1, below_ref[tracer, :, cols], pltpu.roll(current, rows - 1, 0)
+            )
+            change = coef_ref[0, :, cols] * (
+                right_cells + left_cells + upper_rows + lower_rows - 4.0 * current
+            )
+            change = (
+                change
+                - coef_ref[1, :, cols] * (right_cells - left_cells)
+                - coef_ref[2, :, cols] * (lower_rows - upper_rows)
+            )
+            state_ref[target, tracer, :, cols] = current + step * change
+            return inner
+
+        lax.fori_loop(0, tracers * chunks, update, 0)
+        return carry
+
+    total = count_ref[0]
+    lax.fori_loop(0, total, substep, 0)
+    final = total % 2
+
+    def collect(index, carry):
+        tracer = index // chunks
+        cols = chunk_at(index % chunks)
+        out_ref[tracer, :, cols] = jnp.sum(state_ref[final, tracer, :, cols], axis=0, keepdims=True)
+        return carry
+
+    lax.fori_loop(0, tracers * chunks, collect, 0)
+
+
+def solve_rows(field, above_row, below_row, substeps, kappa_row, drift_row, kappa_col, drift_col):
+    tracers, rows, width = field.shape
+    step = (window_time / substeps.astype(jnp.float32)).reshape(1)
+    smem = pl.BlockSpec(memory_space=pltpu.SMEM)
+    vmem = pl.BlockSpec(memory_space=pltpu.VMEM)
+    return pl.pallas_call(
+        solve_kernel,
+        out_shape=jax.ShapeDtypeStruct((tracers, 1, width), jnp.float32),
+        in_specs=[smem, smem] + [vmem] * 7,
+        out_specs=vmem,
+        scratch_shapes=[
+            pltpu.VMEM((2, tracers, rows, width), jnp.float32),
+            pltpu.VMEM((3, rows, width), jnp.float32),
+        ],
+        compiler_params=pltpu.CompilerParams(vmem_limit_bytes=56 * 1024 * 1024),
+    )(
+        step,
+        substeps.reshape(1),
+        field,
+        above_row.astype(jnp.float32),
+        below_row.astype(jnp.float32),
+        kappa_row.reshape(rows, 1),
+        drift_row.reshape(2, rows, 1),
+        kappa_col.reshape(1, width),
+        drift_col.reshape(2, 1, width),
+    )
 
 
 def coarsen(stepped):
@@ -204,18 +320,18 @@
     spectral_weight,
     cotangent,
 ):
-    padded = with_halo(field, ((("grp", "mem", "row"), 1),), 1)
-    stepped = slab_solve(
-        padded[:, 1:-1].astype(jnp.float32),
-        padded[:, :1].astype(jnp.float32),
-        padded[:, -1:].astype(jnp.float32),
+    above_row, below_row = halo_rows(field, ("grp", "mem", "row"))
+    row_sums = solve_rows(
+        field,
+        above_row,
+        below_row,
         counts[0],
         kappa_rows,
         drift_rows,
-        kappa_cols.astype(jnp.float32),
-        drift_cols.astype(jnp.float32),
-    )
-    coarse_rows = coarsen(stepped)[None]
+        kappa_cols,
+        drift_cols,
+    )
+    coarse_rows = (row_sums.reshape(C, SW, FACTOR).sum(axis=2) * (1.0 / (FACTOR * FACTOR)))[None]
     coarse_low = coarse_rows.astype(jnp.bfloat16)
     member = lax.axis_index("mem")
     member_rows = buffer.shape[1]

time: 158 us -> 180 us (1.14)
  Pallas kernels: 0 us -> 34.7 us
  other arithmetic: 41.4 us -> 11.4 us
  starting transfers between devices: 52.2 us -> 79.9 us
  local copies, waits for them, and re-layouts: 30.1 us -> 17.8 us
  waiting for transfers between devices: 11.6 us -> 17.4 us
  loops' own time: 3.38 us -> 0 us
    pallas_call x0 -> x1, Pallas kernels: none -> 34.7 us  [solve_rows(): pl.pallas_call(solve_kernel, out_shape=jax.ShapeDtypeStruct((tracers, 1,...]
    ppermute x7, starting transfers between devices: 30.2 us -> 60 us  [gather_along(): lax.ppermute(block, axis, [(i, (i + shift) % count) for i in range(count)])]
    add x4 -> x0, other arithmetic: 23.9 us -> none  [advance(): return current + step_size * change]
    while x4 -> x0, local copies, waits for them, and re-layouts: 8.76 us -> none
    slice x10 -> x1, local copies, waits for them, and re-layouts: 9.71 us -> 2.74 us  [halo_rows(): below = lax.ppermute(block[:, :1], axis, backward)]
    ppermute x7, waiting for transfers between devices: 4.51 us -> 9.85 us  [gather_along(): lax.ppermute(block, axis, [(i, (i + shift) % count) for i in range(count)])]
    reshape x0 -> x5, local copies, waits for them, and re-layouts: none -> 3.45 us  [the longest x1 0.76 us: solve_rows(): drift_col.reshape(2, 1, width)]
    convert_element_type x4 -> x2, other arithmetic: 6.28 us -> 2.9 us  [the longest x1 1.92 us: solve_rows(): below_row.astype(jnp.float32)]
  transfers between devices with their start and end apart: 25 -> 25, of which waited for: 12 -> 9; matrix products, arithmetic and copies ran while one was open for 14% -> 12% of each run, Pallas kernels for 0% -> 0%
where the time goes in v2:
time: 180 us
  starting transfers between devices  79.9 us (44%)
  Pallas kernels  34.7 us (19%)
  local copies, waits for them, and re-layouts  17.8 us (10%)
  waiting for transfers between devices  17.4 us (10%)
  matrix products  16.6 us (9%)
  other arithmetic  11.4 us (6%)
  between operations  2.26 us (1%)
    ppermute x7, starting transfers between devices, gather_along(): lax.ppermute(block, axis, [(i, (i + shift) % count) for i in range(count)])  60 us
    pallas_call x1, Pallas kernels, solve_rows(): pl.pallas_call(solve_kernel, out_shape=jax.ShapeDtypeStruct((tracers, 1,...  34.7 us
    ppermute x12, starting transfers between devices, group_grads(): lax.ppermute(piece, axis, [(i, (i + shift) % count) for i in range(count)])  12.3 us
    ppermute x7, waiting for transfers between devices, gather_along(): lax.ppermute(block, axis, [(i, (i + shift) % count) for i in range(count)])  9.85 us
    ppermute x12, waiting for transfers between devices, group_grads(): lax.ppermute(piece, axis, [(i, (i + shift) % count) for i in range(count)])  7.14 us
    ppermute x1, starting transfers between devices, halo_rows(): below = lax.ppermute(block[:, :1], axis, backward)  6.37 us
    squeeze x2, local copies, waits for them, and re-layouts, mix_modes(): spectral[1]  4.92 us
  transfers between devices with their start and end apart: 25, of which 9 were waited for; matrix products, arithmetic and copies ran while one was open for 12% of the time, Pallas kernels for 0%

profile of v2, /device:TPU:0, one launch (start us, length us, event | category | flops | bytes accessed | tf_op | source)
XLA Modules:
  0.0 180.1 jit_solution(5340030907572448021)
XLA Ops:
  0.6 2.7 %fusion.153 = (bf16[4,1,16384]{2,1,0:T(2,128)(2,1)}, bf16[4,1,16384]{2,1,0:T(2,128)(2,1)}) fusion(bf16[4,16,16384]{2,1,0:T(8,128)(2,1)} %field_ref.1), kind=kLoop, calls=%fused_computation.220 | loop fusion | bytes 524288 | tf_op jit(solution)/shard_map/slice | solution.py:39
  3.4 6.4 %collective-permute-start.1 = (bf16[4,1,16384]{2,1,0:T(2,128)(2,1)}, bf16[4,1,16384]{2,1,0:T(2,128)(2,1)}, u32[]{:S(2)}, u32[]{:S(2)}) collective-permute-start(bf16[4,1,16384]{2,1,0:T(2,128)(2,1)} %get-tuple-element.7), channel_id=1, source_target_pairs={{1,0},{2,1},{3,2},{4,3},{5,4},{6,5},{7,6},{8,7},{9,8},{10,9},{11,1... | collective-permute-start | bytes 393224 | tf_op jit(solution)/shard_map/ppermute | solution.py:39
  10.4 1.9 %slice_bitcast_fusion = (bf16[32,8,32,16]{2,3,1,0:T(8,128)(2,1)S(1)}, bf16[32,8,32,16]{2,3,1,0:T(8,128)(2,1)S(1)}) fusion(bf16[2,32,8,32,16]{3,4,2,1,0:T(8,128)(2,1)} %param.26), kind=kLoop, calls=%fused_computation.22 | loop fusion | bytes 1048576 | tf_op jit(solution)/shard_map/squeeze | solution.py:234
  13.3 0.7 copy.43.krow_ref
  13.9 0.7 copy.44.drow_ref
  14.6 0.7 reshape.72.kcol_ref
  15.3 0.8 copy.45.dcol_ref
  16.0 3.0 %copy.74 = bf16[32,8,32,16]{0,1,3,2:T(8,128)(2,1)} copy(bf16[32,8,32,16]{2,3,1,0:T(8,128)(2,1)S(1)} %get-tuple-element.5) | data formatting | bytes 524288 | tf_op jit(solution)/shard_map/squeeze | solution.py:234
  19.0 2.3 %copy.71 = bf16[32,8,32,16]{0,1,3,2:T(8,128)(2,1)S(1)} copy(bf16[32,8,32,16]{2,3,1,0:T(8,128)(2,1)S(1)} %get-tuple-element.6) | data formatting | bytes 524288 | tf_op jit(solution)/shard_map/squeeze | solution.py:233
  21.4 0.9 negate_convert_fusion
  22.3 1.9 %convert_element_type.59.below_ref = f32[4,1,16384]{2,1,0:T(1,128)} convert(bf16[4,1,16384]{2,1,0:T(2,128)(2,1)} %collective-permute-done.1) | non-fusion elementwise | flops 65536 | bytes 393216 | tf_op jit(solution)/shard_map/convert_element_type | solution.py:165
  24.3 1.0 convert_element_type.58.above_ref
  25.2 34.7 %shard_map.157 = f32[4,1,16384]{2,1,0:T(1,128)} custom-call(f32[1]{0:T(128)S(6)} %div.10.step_ref, s32[1]{0:T(128)S(6)} %copy.114.count_ref, bf16[4,16,16384]{2,1,0:T(8,128)(2,1)} %field_ref.1, f32[4,1,16384]{2,1,0:T(1,128)} %convert_element_type.58.above_ref, f32[4,1,16384]{2,1,0:T(1,128)} %convert_element_type.59.below_ref, f32[16,1]{1,0:T(8,128)} %copy.43.krow_ref, ...), custom_call_target="tpu_custom_call" | custom-call | tf_op jit(solution)/shard_map/pallas_call | solution.py:150
  59.9 1.6 reduce
  61.6 0.7 reshape.74
  62.3 0.6 reduce_sum.9
  62.9 2.3 %collective-permute-start.4 = (bf16[4,1024]{1,0:T(4,128)(2,1)S(1)}, bf16[4,1024]{1,0:T(4,128)(2,1)S(1)}, u32[]{:S(2)}, u32[]{:S(2)}) collective-permute-start(bf16[4,1024]{1,0:T(4,128)(2,1)S(1)} %multiply_convert_fusion), channel_id=1, source_target_pairs={{0,3},{1,0},{2,1},{3,2},{4,7},{5,4},{6,5},{7,6},{8,11},{9,8},{10,9... | collective-permute-start | bytes 24584 | tf_op jit(solution)/shard_map/ppermute | solution.py:271
  65.2 0.6 collective-permute-start.2
  65.8 0.6 convert_dynamic-update-slice_fusion
  66.4 4.2 %collective-permute-done.2 = bf16[4,1024]{1,0:T(4,128)(2,1)S(1)} collective-permute-done((bf16[4,1024]{1,0:T(4,128)(2,1)S(1)}, bf16[4,1024]{1,0:T(4,128)(2,1)S(1)}, u32[]{:S(2)}, u32[]{:S(2)}) %collective-permute-start.2) | collective-permute-done | bytes 8224 | tf_op jit(solution)/shard_map/ppermute | solution.py:271
  70.7 49.6 %collective-permute-start.5 = (bf16[4,4,1024]{2,1,0:T(4,128)(2,1)S(1)}, bf16[4,4,1024]{2,1,0:T(4,128)(2,1)S(1)}, u32[]{:S(2)}, u32[]{:S(2)}) collective-permute-start(bf16[4,4,1024]{2,1,0:T(4,128)(2,1)S(1)} %bitcast_dynamic-update-slice_fusion.6), channel_id=1, source_target_pairs={{0,4},{4,0},{1,5},{5,1},{2,6},{6,2},{3,7},{7,3},{8,12},{12,8},{9,1... | collective-permute-start | bytes 98312 | tf_op jit(solution)/shard_map/ppermute | solution.py:271
  120.3 0.8 collective-permute-done.5
  121.2 6.9 %collective-permute-start.8 = (bf16[2,4,4,1024]{3,2,1,0:T(4,128)(2,1)S(1)}, bf16[2,4,4,1024]{3,2,1,0:T(4,128)(2,1)S(1)}, u32[]{:S(2)}, u32[]{:S(2)}) collective-permute-start(bf16[2,4,4,1024]{3,2,1,0:T(4,128)(2,1)S(1)} %bitcast_dynamic-update-slice_fusion.4), channel_id=1, source_target_pairs={{0,24},{8,0},{16,8},{24,16},{1,25},{9,1},{17,9},{25,17},{2,26},{10... | collective-permute-start | bytes 196616 | tf_op jit(solution)/shard_map/ppermute | solution.py:271
  128.1 0.6 collective-permute-start.6
  128.8 4.5 %collective-permute-done.6 = bf16[2,4,4,1024]{3,2,1,0:T(4,128)(2,1)S(1)} collective-permute-done((bf16[2,4,4,1024]{3,2,1,0:T(4,128)(2,1)S(1)}, bf16[2,4,4,1024]{3,2,1,0:T(4,128)(2,1)S(1)}, u32[]{:S(2)}, u32[]{:S(2)}) %collective-permute-start.6) | collective-permute-done | bytes 65568 | tf_op jit(solution)/shard_map/ppermute | solution.py:271
  133.3 0.4 collective-permute-done.7
  133.8 1.2 fusion
  135.1 0.9 fusion.66
  136.0 0.5 fusion.49
  136.6 0.5 fusion.45
  137.1 0.5 fusion.4
  137.7 0.5 fusion.6
  138.3 0.6 collective-permute-start.9
  138.8 0.4 collective-permute-done.10
  139.3 0.8 constant_dynamic-slice_fusion.1
  140.2 0.8 constant_dynamic-slice_fusion.3
  141.0 1.8 %fusion.37 = f32[32,16,1,8]{3,2,1,0:T(1,128)S(1)} fusion(bf16[32,8,32,16]{0,1,3,2:T(8,128)(2,1)S(1)} %copy-done.1, f32[32,32,16,1]{0,1,2,3:T(8,128)S(1)} %bitcast.175), kind=kOutput, calls=%fused_computation.66 | convolution fusion | flops 1572864 | bytes 344064 | tf_op jit(solution)/shard_map/hojl,hjl->ojl/dot_general | solution.py:237
  142.8 1.8 %fusion.35 = f32[32,16,1,8]{3,2,1,0:T(1,128)S(1)} fusion(bf16[32,8,32,16]{0,1,3,2:T(8,128)(2,1)S(1)} %copy-done.1, f32[32,32,16,1]{0,1,2,3:T(8,128)S(1)} %bitcast.173), kind=kOutput, calls=%fused_computation.64 | convolution fusion | flops 1572864 | bytes 344064 | tf_op jit(solution)/shard_map/hojl,hjl->ojl/dot_general | solution.py:234
  144.6 1.8 %fusion.33 = f32[32,16,1,8]{3,2,1,0:T(1,128)S(1)} fusion(bf16[32,8,32,16]{0,1,3,2:T(8,128)(2,1)S(1)} %copy.71, f32[32,32,16,1]{0,1,2,3:T(8,128)S(1)} %bitcast.174), kind=kOutput, calls=%fused_computation.62 | convolution fusion | flops 1572864 | bytes 344064 | tf_op jit(solution)/shard_map/hojl,hjl->ojl/dot_general | solution.py:235
  146.5 1.8 %fusion.39 = f32[32,16,1,8]{3,2,1,0:T(1,128)S(1)} fusion(bf16[32,8,32,16]{0,1,3,2:T(8,128)(2,1)S(1)} %copy.71, f32[32,32,16,1]{0,1,2,3:T(8,128)S(1)} %bitcast.176), kind=kOutput, calls=%fused_computation.68 | convolution fusion | flops 1572864 | bytes 344064 | tf_op jit(solution)/shard_map/hojl,hjl->ojl/dot_general | solution.py:232
  148.6 0.6 fusion.82
  149.2 0.7 fusion.74
  150.1 0.6 fusion.72
  150.8 0.6 fusion.84
  151.6 1.5 collective-permute-start.19
  153.1 1.9 %collective-permute-start.15 = (f32[16,8,16]{0,1,2:T(8,128)S(1)}, f32[16,8,16]{0,1,2:T(8,128)S(1)}, u32[]{:S(2)}, u32[]{:S(2)}) collective-permute-start(f32[16,8,16]{0,1,2:T(8,128)S(1)} %copy-done.13), channel_id=1, source_target_pairs={{0,8},{8,16},{16,24},{24,0},{1,9},{9,17},{17,25},{25,1},{2,10},{10... | collective-permute-start | bytes 24584 | tf_op jit(solution)/shard_map/ppermute | solution.py:301
  155.1 1.0 collective-permute-start.21
  156.1 0.8 collective-permute-start.17
  156.9 0.6 convolution_multiply_fusion
  157.9 1.8 %fusion.30 = bf16[1,16,8,1024]{3,2,1,0:T(8,128)(2,1)} fusion(f32[16,8,1024]{2,1,0:T(8,128)S(1)} %fusion.2), kind=kLoop, calls=%fused_computation.60 | loop fusion | flops 8519680 | bytes 786432 | tf_op jit(solution)/shard_map/broadcast_in_dim | solution.py:371
  159.7 0.3 fusion.31
  160.3 0.3 fusion.78
  161.3 0.8 collective-permute-start.13
  162.9 0.6 collective-permute-start.11
  163.8 2.8 %collective-permute-done.13 = f32[16,8,16]{0,1,2:T(8,128)S(1)} collective-permute-done((f32[16,8,16]{0,1,2:T(8,128)S(1)}, f32[16,8,16]{0,1,2:T(8,128)S(1)}, u32[]{:S(2)}, u32[]{:S(2)}) %collective-permute-start.13) | collective-permute-done | bytes 8224 | tf_op jit(solution)/shard_map/ppermute | solution.py:301
  166.9 0.9 collective-permute-start.24
  167.7 0.5 collective-permute-start.20
  168.2 2.0 %collective-permute-start.16 = (f32[8,8,16]{1,2,0:T(8,128)S(1)}, f32[8,8,16]{1,2,0:T(8,128)S(1)}, u32[]{:S(2)}, u32[]{:S(2)}) collective-permute-start(f32[8,8,16]{1,2,0:T(8,128)S(1)} %get-tuple-element.33), channel_id=1, source_target_pairs={{0,8},{8,16},{16,24},{24,0},{1,9},{9,17},{17,25},{25,1},{2,10},{10... | collective-permute-start | bytes 12296 | tf_op jit(solution)/shard_map/ppermute | solution.py:301
  170.4 1.0 collective-permute-start.22
  171.4 1.5 collective-permute-start.18
  173.6 1.3 collective-permute-done.22
  174.9 0.7 collective-permute-done.18
  175.7 2.4 %collective-permute-done.14 = f32[8,8,16]{1,2,0:T(8,128)S(1)} collective-permute-done((f32[8,8,16]{1,2,0:T(8,128)S(1)}, f32[8,8,16]{1,2,0:T(8,128)S(1)}, u32[]{:S(2)}, u32[]{:S(2)}) %collective-permute-start.14) | collective-permute-done | bytes 4128 | tf_op jit(solution)/shard_map/ppermute | solution.py:301
  178.6 1.4 fusion.13
  (126 shorter events, 6.0 us)
Async XLA Ops:
  0.6 156.9 %copy-start = (bf16[32,8]{0,1:T(8,128)(2,1)S(1)}, bf16[32,8]{0,1:T(8,128)(2,1)}, u32[]{:S(2)}) copy-start(bf16[32,8]{0,1:T(8,128)(2,1)} %param.24) | copy-start | bytes 1540
  3.4 19.0 %collective-permute-start.1 = (bf16[4,1,16384]{2,1,0:T(2,128)(2,1)}, bf16[4,1,16384]{2,1,0:T(2,128)(2,1)}, u32[]{:S(2)}, u32[]{:S(2)}) collective-permute-start(bf16[4,1,16384]{2,1,0:T(2,128)(2,1)} %get-tuple-element.7), channel_id=1, source_target_pairs={{1,0},{2,1},{3,2},{4,3},{5,4},{6,5},{7,6},{8,7},{9,8},{10,9},{11,1... | collective-permute-start | bytes 393224 | tf_op jit(solution)/shard_map/ppermute | solution.py:39
  9.8 14.5 %collective-permute-start = (bf16[4,1,16384]{2,1,0:T(2,128)(2,1)}, bf16[4,1,16384]{2,1,0:T(2,128)(2,1)S(1)}, u32[]{:S(2)}, u32[]{:S(2)}) collective-permute-start(bf16[4,1,16384]{2,1,0:T(2,128)(2,1)} %get-tuple-element.8), channel_id=1, source_target_pairs={{0,1},{1,2},{2,3},{3,4},{4,5},{5,6},{6,7},{7,8},{8,9},{9,10},{10,1... | collective-permute-start | bytes 393224 | tf_op jit(solution)/shard_map/ppermute | solution.py:38
  10.3 2.0 %copy-start.19 = (s32[32]{0:T(128)S(1)}, s32[32]{0:T(128)}, u32[]{:S(2)}) copy-start(s32[32]{0:T(128)} %param.20) | copy-start | bytes 388
  10.3 2.9 %copy-start.18 = (f32[16]{0:T(128)S(1)}, f32[16]{0:T(128)}, u32[]{:S(2)}) copy-start(f32[16]{0:T(128)} %param.16) | copy-start | bytes 196
  10.3 3.6 %copy-start.17 = (f32[2,16]{1,0:T(2,128)S(1)}, f32[2,16]{1,0:T(2,128)}, u32[]{:S(2)}) copy-start(f32[2,16]{1,0:T(2,128)} %param.18) | copy-start | bytes 388
  10.4 4.3 %copy-start.16 = (bf16[16384]{0:T(1024)(128)(2,1)S(1)}, bf16[16384]{0:T(1024)(128)(2,1)}, u32[]{:S(2)}) copy-start(bf16[16384]{0:T(1024)(128)(2,1)} %param.17) | copy-start | bytes 98308
  10.4 4.9 %copy-start.9 = (bf16[2,16384]{1,0:T(2,128)(2,1)S(1)}, bf16[2,16384]{1,0:T(2,128)(2,1)}, u32[]{:S(2)}) copy-start(bf16[2,16384]{1,0:T(2,128)(2,1)} %param.19) | copy-start | bytes 196612
  62.2 71.6 %copy-start.4 = (bf16[1,16,4,1024]{3,2,1,0:T(4,128)(2,1)S(1)}, bf16[1,16,4,1024]{3,2,1,0:T(4,128)(2,1)}, u32[]{:S(2)}) copy-start(bf16[1,16,4,1024]{3,2,1,0:T(4,128)(2,1)} %param.21) | copy-start | bytes 393220
  62.2 72.8 %copy-start.5 = (bf16[1024,16]{0,1:T(8,128)(2,1)S(1)}, bf16[1024,16]{0,1:T(8,128)(2,1)}, u32[]{:S(2)}) copy-start(bf16[1024,16]{0,1:T(8,128)(2,1)} %get-tuple-element.39) | copy-start | bytes 98308
  62.3 72.8 %copy-start.7 = (bf16[1024,16]{0,1:T(8,128)(2,1)S(1)}, bf16[1024,16]{0,1:T(8,128)(2,1)}, u32[]{:S(2)}) copy-start(bf16[1024,16]{0,1:T(8,128)(2,1)} %get-tuple-element.40) | copy-start | bytes 98308
  62.9 7.8 %collective-permute-start.4 = (bf16[4,1024]{1,0:T(4,128)(2,1)S(1)}, bf16[4,1024]{1,0:T(4,128)(2,1)S(1)}, u32[]{:S(2)}, u32[]{:S(2)}) collective-permute-start(bf16[4,1024]{1,0:T(4,128)(2,1)S(1)} %multiply_convert_fusion), channel_id=1, source_target_pairs={{0,3},{1,0},{2,1},{3,2},{4,7},{5,4},{6,5},{7,6},{8,11},{9,8},{10,9... | collective-permute-start | bytes 24584 | tf_op jit(solution)/shard_map/ppermute | solution.py:271
  65.2 5.5 %collective-permute-start.3 = (bf16[4,1024]{1,0:T(4,128)(2,1)S(1)}, bf16[4,1024]{1,0:T(4,128)(2,1)S(1)}, u32[]{:S(2)}, u32[]{:S(2)}) collective-permute-start(bf16[4,1024]{1,0:T(4,128)(2,1)S(1)} %multiply_convert_fusion), channel_id=1, source_target_pairs={{0,2},{1,3},{2,0},{3,1},{4,6},{5,7},{6,4},{7,5},{8,10},{9,11},{10,... | collective-permute-start | bytes 24584 | tf_op jit(solution)/shard_map/ppermute | solution.py:271
  65.2 5.4 %collective-permute-start.2 = (bf16[4,1024]{1,0:T(4,128)(2,1)S(1)}, bf16[4,1024]{1,0:T(4,128)(2,1)S(1)}, u32[]{:S(2)}, u32[]{:S(2)}) collective-permute-start(bf16[4,1024]{1,0:T(4,128)(2,1)S(1)} %multiply_convert_fusion), channel_id=1, source_target_pairs={{0,1},{1,2},{2,3},{3,0},{4,5},{5,6},{6,7},{7,4},{8,9},{9,10},{10,1... | collective-permute-start | bytes 24584 | tf_op jit(solution)/shard_map/ppermute | solution.py:271
  70.7 50.5 %collective-permute-start.5 = (bf16[4,4,1024]{2,1,0:T(4,128)(2,1)S(1)}, bf16[4,4,1024]{2,1,0:T(4,128)(2,1)S(1)}, u32[]{:S(2)}, u32[]{:S(2)}) collective-permute-start(bf16[4,4,1024]{2,1,0:T(4,128)(2,1)S(1)} %bitcast_dynamic-update-slice_fusion.6), channel_id=1, source_target_pairs={{0,4},{4,0},{1,5},{5,1},{2,6},{6,2},{3,7},{7,3},{8,12},{12,8},{9,1... | collective-permute-start | bytes 98312 | tf_op jit(solution)/shard_map/ppermute | solution.py:271
  121.2 12.6 %collective-permute-start.8 = (bf16[2,4,4,1024]{3,2,1,0:T(4,128)(2,1)S(1)}, bf16[2,4,4,1024]{3,2,1,0:T(4,128)(2,1)S(1)}, u32[]{:S(2)}, u32[]{:S(2)}) collective-permute-start(bf16[2,4,4,1024]{3,2,1,0:T(4,128)(2,1)S(1)} %bitcast_dynamic-update-slice_fusion.4), channel_id=1, source_target_pairs={{0,24},{8,0},{16,8},{24,16},{1,25},{9,1},{17,9},{25,17},{2,26},{10... | collective-permute-start | bytes 196616 | tf_op jit(solution)/shard_map/ppermute | solution.py:271
  128.1 5.7 %collective-permute-start.7 = (bf16[2,4,4,1024]{3,2,1,0:T(4,128)(2,1)S(1)}, bf16[2,4,4,1024]{3,2,1,0:T(4,128)(2,1)S(1)}, u32[]{:S(2)}, u32[]{:S(2)}) collective-permute-start(bf16[2,4,4,1024]{3,2,1,0:T(4,128)(2,1)S(1)} %bitcast_dynamic-update-slice_fusion.4), channel_id=1, source_target_pairs={{0,16},{8,24},{16,0},{24,8},{1,17},{9,25},{17,1},{25,9},{2,18},{10... | collective-permute-start | bytes 196616 | tf_op jit(solution)/shard_map/ppermute | solution.py:271
  128.1 5.2 %collective-permute-start.6 = (bf16[2,4,4,1024]{3,2,1,0:T(4,128)(2,1)S(1)}, bf16[2,4,4,1024]{3,2,1,0:T(4,128)(2,1)S(1)}, u32[]{:S(2)}, u32[]{:S(2)}) collective-permute-start(bf16[2,4,4,1024]{3,2,1,0:T(4,128)(2,1)S(1)} %bitcast_dynamic-update-slice_fusion.4), channel_id=1, source_target_pairs={{0,8},{8,16},{16,24},{24,0},{1,9},{9,17},{17,25},{25,1},{2,10},{10... | collective-permute-start | bytes 196616 | tf_op jit(solution)/shard_map/ppermute | solution.py:271
  136.5 4.5 %copy-start.1 = (bf16[32,8,32,16]{0,1,3,2:T(8,128)(2,1)S(1)}, bf16[32,8,32,16]{0,1,3,2:T(8,128)(2,1)}, u32[]{:S(2)}) copy-start(bf16[32,8,32,16]{0,1,3,2:T(8,128)(2,1)} %copy.74) | copy-start | bytes 786436
  137.6 1.6 collective-permute-start.10
  138.3 1.9 %collective-permute-start.9 = (f32[32,32,16]{0,1,2:T(8,128)S(1)}, f32[32,32,16]{0,1,2:T(8,128)S(1)}, u32[]{:S(2)}, u32[]{:S(2)}) collective-permute-start(f32[32,32,16]{0,1,2:T(8,128)S(1)} %fusion.6), channel_id=1, source_target_pairs={{0,4},{4,0},{1,5},{5,1},{2,6},{6,2},{3,7},{7,3},{8,12},{12,8},{9,1... | collective-permute-start | bytes 196616 | tf_op jit(solution)/shard_map/ppermute | solution.py:285
  146.5 6.7 %copy-start.13 = (f32[16,8,16]{0,1,2:T(8,128)S(1)}, f32[16,8,16]{0,1,2:T(8,128)}, u32[]{:S(2)}) copy-start(f32[16,8,16]{0,1,2:T(8,128)} %get-tuple-element.15) | copy-start | bytes 24580
  146.5 8.6 %copy-start.12 = (f32[16,8,16]{0,1,2:T(8,128)S(1)}, f32[16,8,16]{0,1,2:T(8,128)}, u32[]{:S(2)}) copy-start(f32[16,8,16]{0,1,2:T(8,128)} %get-tuple-element.9) | copy-start | bytes 24580
  146.5 9.6 %copy-start.11 = (f32[16,8,16]{0,1,2:T(8,128)S(1)}, f32[16,8,16]{0,1,2:T(8,128)}, u32[]{:S(2)}) copy-start(f32[16,8,16]{0,1,2:T(8,128)} %get-tuple-element.10) | copy-start | bytes 24580
  148.3 3.1 %copy-start.15 = (f32[16,8,16]{0,1,2:T(8,128)S(1)}, f32[16,8,16]{0,1,2:T(8,128)}, u32[]{:S(2)}) copy-start(f32[16,8,16]{0,1,2:T(8,128)} %get-tuple-element.13) | copy-start | bytes 24580
  148.3 3.3 %copy-start.14 = (f32[16,8,16]{0,1,2:T(8,128)S(1)}, f32[16,8,16]{0,1,2:T(8,128)}, u32[]{:S(2)}) copy-start(f32[16,8,16]{0,1,2:T(8,128)} %get-tuple-element.14) | copy-start | bytes 24580
  148.3 9.2 %copy-start.20 = (f32[8]{0:T(128)S(1)}, f32[8]{0:T(128)}, u32[]{:S(2)}) copy-start(f32[8]{0:T(128)} %param.25) | copy-start | bytes 100
  150.7 9.0 %copy-start.6 = (bf16[1024,16]{0,1:T(8,128)(2,1)S(1)}, bf16[1024,16]{0,1:T(8,128)(2,1)}, u32[]{:S(2)}) copy-start(bf16[1024,16]{0,1:T(8,128)(2,1)} %get-tuple-element.39) | copy-start | bytes 98308
  150.7 9.0 %copy-start.8 = (bf16[1024,16]{0,1:T(8,128)(2,1)S(1)}, bf16[1024,16]{0,1:T(8,128)(2,1)}, u32[]{:S(2)}) copy-start(bf16[1024,16]{0,1:T(8,128)(2,1)} %get-tuple-element.40) | copy-start | bytes 98308
  150.7 9.0 %copy-start.21 = (bf16[1,16,8,1024]{3,2,1,0:T(8,128)(2,1)S(1)}, bf16[1,16,8,1024]{3,2,1,0:T(8,128)(2,1)}, u32[]{:S(2)}) copy-start(bf16[1,16,8,1024]{3,2,1,0:T(8,128)(2,1)} %param.27) | copy-start | bytes 786436
  151.4 9.9 %collective-permute-start.23 = (f32[16,8,16]{0,1,2:T(8,128)S(1)}, f32[16,8,16]{0,1,2:T(8,128)S(1)}, u32[]{:S(2)}, u32[]{:S(2)}) collective-permute-start(f32[16,8,16]{0,1,2:T(8,128)S(1)} %copy-done.15), channel_id=1, source_target_pairs={{0,24},{8,0},{16,8},{24,16},{1,25},{9,1},{17,9},{25,17},{2,26},{10... | collective-permute-start | bytes 24584 | tf_op jit(solution)/shard_map/ppermute | solution.py:301
  151.6 10.5 %collective-permute-start.19 = (f32[16,8,16]{0,1,2:T(8,128)S(1)}, f32[16,8,16]{0,1,2:T(8,128)S(1)}, u32[]{:S(2)}, u32[]{:S(2)}) collective-permute-start(f32[16,8,16]{0,1,2:T(8,128)S(1)} %copy-done.14), channel_id=1, source_target_pairs={{0,16},{8,24},{16,0},{24,8},{1,17},{9,25},{17,1},{25,9},{2,18},{10... | collective-permute-start | bytes 24584 | tf_op jit(solution)/shard_map/ppermute | solution.py:301
  153.1 9.7 %collective-permute-start.15 = (f32[16,8,16]{0,1,2:T(8,128)S(1)}, f32[16,8,16]{0,1,2:T(8,128)S(1)}, u32[]{:S(2)}, u32[]{:S(2)}) collective-permute-start(f32[16,8,16]{0,1,2:T(8,128)S(1)} %copy-done.13), channel_id=1, source_target_pairs={{0,8},{8,16},{16,24},{24,0},{1,9},{9,17},{17,25},{25,1},{2,10},{10... | collective-permute-start | bytes 24584 | tf_op jit(solution)/shard_map/ppermute | solution.py:301
  155.1 8.5 %collective-permute-start.21 = (f32[16,8,16]{0,1,2:T(8,128)S(1)}, f32[16,8,16]{0,1,2:T(8,128)S(1)}, u32[]{:S(2)}, u32[]{:S(2)}) collective-permute-start(f32[16,8,16]{0,1,2:T(8,128)S(1)} %copy-done.12), channel_id=1, source_target_pairs={{0,24},{8,0},{16,8},{24,16},{1,25},{9,1},{17,9},{25,17},{2,26},{10... | collective-permute-start | bytes 24584 | tf_op jit(solution)/shard_map/ppermute | solution.py:301
  156.1 7.6 %collective-permute-start.17 = (f32[16,8,16]{0,1,2:T(8,128)S(1)}, f32[16,8,16]{0,1,2:T(8,128)S(1)}, u32[]{:S(2)}, u32[]{:S(2)}) collective-permute-start(f32[16,8,16]{0,1,2:T(8,128)S(1)} %copy-done.11), channel_id=1, source_target_pairs={{0,16},{8,24},{16,0},{24,8},{1,17},{9,25},{17,1},{25,9},{2,18},{10... | collective-permute-start | bytes 24584 | tf_op jit(solution)/shard_map/ppermute | solution.py:301
  157.8 3.5 %copy-start.10 = (f32[16,8,16]{0,1,2:T(8,128)S(1)}, f32[16,8,16]{0,1,2:T(8,128)}, u32[]{:S(2)}) copy-start(f32[16,8,16]{0,1,2:T(8,128)} %get-tuple-element.11) | copy-start | bytes 24580
  157.8 4.6 %copy-start.2 = (f32[8,16,16]{2,0,1:T(8,128)S(1)}, f32[8,16,16]{2,0,1:T(8,128)}, u32[]{:S(2)}) copy-start(f32[8,16,16]{2,0,1:T(8,128)} %get-tuple-element.16) | copy-start | bytes 24580
  157.9 4.7 %copy-start.3 = (f32[8,16,16]{2,0,1:T(8,128)S(1)}, f32[8,16,16]{2,0,1:T(8,128)}, u32[]{:S(2)}) copy-start(f32[8,16,16]{2,0,1:T(8,128)} %get-tuple-element.12) | copy-start | bytes 24580
  161.3 5.2 %collective-permute-start.13 = (f32[16,8,16]{0,1,2:T(8,128)S(1)}, f32[16,8,16]{0,1,2:T(8,128)S(1)}, u32[]{:S(2)}, u32[]{:S(2)}) collective-permute-start(f32[16,8,16]{0,1,2:T(8,128)S(1)} %copy-done.10), channel_id=1, source_target_pairs={{0,8},{8,16},{16,24},{24,0},{1,9},{9,17},{17,25},{25,1},{2,10},{10... | collective-permute-start | bytes 24584 | tf_op jit(solution)/shard_map/ppermute | solution.py:301
  162.1 4.5 %collective-permute-start.12 = (f32[8,32,16]{1,2,0:T(8,128)S(1)}, f32[8,32,16]{1,2,0:T(8,128)S(1)}, u32[]{:S(2)}, u32[]{:S(2)}) collective-permute-start(f32[8,32,16]{1,2,0:T(8,128)S(1)} %fusion.8), channel_id=1, source_target_pairs={{0,4},{4,0},{1,5},{5,1},{2,6},{6,2},{3,7},{7,3},{8,12},{12,8},{9,1... | collective-permute-start | bytes 49160 | tf_op jit(solution)/shard_map/ppermute | solution.py:285
  162.9 7.4 %collective-permute-start.11 = (f32[8,32,16]{1,2,0:T(8,128)S(1)}, f32[8,32,16]{1,2,0:T(8,128)S(1)}, u32[]{:S(2)}, u32[]{:S(2)}) collective-permute-start(f32[8,32,16]{1,2,0:T(8,128)S(1)} %fusion.10), channel_id=1, source_target_pairs={{0,4},{4,0},{1,5},{5,1},{2,6},{6,2},{3,7},{7,3},{8,12},{12,8},{9,1... | collective-permute-start | bytes 49160 | tf_op jit(solution)/shard_map/ppermute | solution.py:285
  166.9 6.1 %collective-permute-start.24 = (f32[8,8,16]{1,2,0:T(8,128)S(1)}, f32[8,8,16]{1,2,0:T(8,128)S(1)}, u32[]{:S(2)}, u32[]{:S(2)}) collective-permute-start(f32[8,8,16]{1,2,0:T(8,128)S(1)} %get-tuple-element.31), channel_id=1, source_target_pairs={{0,24},{8,0},{16,8},{24,16},{1,25},{9,1},{17,9},{25,17},{2,26},{10... | collective-permute-start | bytes 12296 | tf_op jit(solution)/shard_map/ppermute | solution.py:301
  167.7 5.7 %collective-permute-start.20 = (f32[8,8,16]{1,2,0:T(8,128)S(1)}, f32[8,8,16]{1,2,0:T(8,128)S(1)}, u32[]{:S(2)}, u32[]{:S(2)}) collective-permute-start(f32[8,8,16]{1,2,0:T(8,128)S(1)} %get-tuple-element.32), channel_id=1, source_target_pairs={{0,16},{8,24},{16,0},{24,8},{1,17},{9,25},{17,1},{25,9},{2,18},{10... | collective-permute-start | bytes 12296 | tf_op jit(solution)/shard_map/ppermute | solution.py:301
  168.2 5.3 %collective-permute-start.16 = (f32[8,8,16]{1,2,0:T(8,128)S(1)}, f32[8,8,16]{1,2,0:T(8,128)S(1)}, u32[]{:S(2)}, u32[]{:S(2)}) collective-permute-start(f32[8,8,16]{1,2,0:T(8,128)S(1)} %get-tuple-element.33), channel_id=1, source_target_pairs={{0,8},{8,16},{16,24},{24,0},{1,9},{9,17},{17,25},{25,1},{2,10},{10... | collective-permute-start | bytes 12296 | tf_op jit(solution)/shard_map/ppermute | solution.py:301
  170.4 4.4 %collective-permute-start.22 = (f32[8,8,16]{1,2,0:T(8,128)S(1)}, f32[8,8,16]{1,2,0:T(8,128)S(1)}, u32[]{:S(2)}, u32[]{:S(2)}) collective-permute-start(f32[8,8,16]{1,2,0:T(8,128)S(1)} %get-tuple-element.27), channel_id=1, source_target_pairs={{0,24},{8,0},{16,8},{24,16},{1,25},{9,1},{17,9},{25,17},{2,26},{10... | collective-permute-start | bytes 12296 | tf_op jit(solution)/shard_map/ppermute | solution.py:301
  171.4 4.3 %collective-permute-start.18 = (f32[8,8,16]{1,2,0:T(8,128)S(1)}, f32[8,8,16]{1,2,0:T(8,128)S(1)}, u32[]{:S(2)}, u32[]{:S(2)}) collective-permute-start(f32[8,8,16]{1,2,0:T(8,128)S(1)} %get-tuple-element.28), channel_id=1, source_target_pairs={{0,16},{8,24},{16,0},{24,8},{1,17},{9,25},{17,1},{25,9},{2,18},{10... | collective-permute-start | bytes 12296 | tf_op jit(solution)/shard_map/ppermute | solution.py:301
  172.9 5.2 %collective-permute-start.14 = (f32[8,8,16]{1,2,0:T(8,128)S(1)}, f32[8,8,16]{1,2,0:T(8,128)S(1)}, u32[]{:S(2)}, u32[]{:S(2)}) collective-permute-start(f32[8,8,16]{1,2,0:T(8,128)S(1)} %get-tuple-element.29), channel_id=1, source_target_pairs={{0,8},{8,16},{16,24},{24,0},{1,9},{9,17},{17,25},{25,1},{2,10},{10... | collective-permute-start | bytes 12296 | tf_op jit(solution)/shard_map/ppermute | solution.py:301

commit v3 on v2

--- a/solution.py
+++ b/solution.py
@@ -66,11 +66,11 @@
 
 
 CHUNK = 512
+UNROLL = 4
 
 
 def solve_kernel(
-    step_ref, count_ref, field_ref, above_ref, below_ref, krow_ref, drow_ref, kcol_ref, dcol_ref,
-    out_ref, state_ref, coef_ref,
+    step_ref, count_ref, field_ref, above_ref, below_ref, coef_ref, out_ref, first_ref, second_ref
 ):
     tracers, rows, width = field_ref.shape
     chunks = width // CHUNK
@@ -80,31 +80,24 @@
 
     def prepare(index, carry):
         cols = chunk_at(index)
-        coef_ref[0, :, cols] = krow_ref[...] * kcol_ref[:, cols].astype(jnp.float32)
-        coef_ref[1, :, cols] = 0.5 * (drow_ref[0] * dcol_ref[0, :, cols].astype(jnp.float32))
-        coef_ref[2, :, cols] = 0.5 * (drow_ref[1] * dcol_ref[1, :, cols].astype(jnp.float32))
         for tracer in range(tracers):
-            state_ref[0, tracer, :, cols] = field_ref[tracer, :, cols].astype(jnp.float32)
+            first_ref[tracer, :, cols] = field_ref[tracer, :, cols].astype(jnp.float32)
         return carry
 
     lax.fori_loop(0, chunks, prepare, 0)
     step = step_ref[0]
     row_ids = lax.broadcasted_iota(jnp.int32, (rows, CHUNK), 0)
 
-    def substep(number, carry):
-        source = number % 2
-        target = 1 - source
-
+    def sweep(source_ref, target_ref):
         def update(index, inner):
             tracer = index // chunks
             column = index % chunks
             cols = chunk_at(column)
             before = pl.ds(pl.multiple_of(((column * CHUNK - 128) % width), 128), 128)
             after = pl.ds(pl.multiple_of((((column + 1) * CHUNK) % width), 128), 128)
-            current = state_ref[source, tracer, :, cols]
+            current = source_ref[tracer, :, cols]
             extended = jnp.concatenate(
-                [state_ref[source, tracer, :, before], current, state_ref[source, tracer, :, after]],
-                axis=1,
+                [source_ref[tracer, :, before], current, source_ref[tracer, :, after]], axis=1
             )
             span = CHUNK + 256
             right_cells = pltpu.roll(extended, span - 1, 1)[:, 128 : 128 + CHUNK]
@@ -123,38 +116,60 @@
                 - coef_ref[1, :, cols] * (right_cells - left_cells)
                 - coef_ref[2, :, cols] * (lower_rows - upper_rows)
             )
-            state_ref[target, tracer, :, cols] = current + step * change
+            target_ref[tracer, :, cols] = current + step * change
             return inner
 
-        lax.fori_loop(0, tracers * chunks, update, 0)
+        lax.fori_loop(0, tracers * chunks, update, 0, unroll=UNROLL)
+
+    def two_steps(number, carry):
+        sweep(first_ref, second_ref)
+        sweep(second_ref, first_ref)
         return carry
 
     total = count_ref[0]
-    lax.fori_loop(0, total, substep, 0)
-    final = total % 2
-
-    def collect(index, carry):
-        tracer = index // chunks
-        cols = chunk_at(index % chunks)
-        out_ref[tracer, :, cols] = jnp.sum(state_ref[final, tracer, :, cols], axis=0, keepdims=True)
-        return carry
-
-    lax.fori_loop(0, tracers * chunks, collect, 0)
+    lax.fori_loop(0, total // 2, two_steps, 0)
+
+    def collect(final_ref):
+        def store(index, carry):
+            tracer = index // chunks
+            cols = chunk_at(index % chunks)
+            out_ref[tracer, :, cols] = jnp.sum(final_ref[tracer, :, cols], axis=0, keepdims=True)
+            return carry
+
+        lax.fori_loop(0, tracers * chunks, store, 0)
+
+    @pl.when(total % 2 == 1)
+    def _():
+        sweep(first_ref, second_ref)
+        collect(second_ref)
+
+    @pl.when(total % 2 == 0)
+    def _():
+        collect(first_ref)
 
 
 def solve_rows(field, above_row, below_row, substeps, kappa_row, drift_row, kappa_col, drift_col):
     tracers, rows, width = field.shape
     step = (window_time / substeps.astype(jnp.float32)).reshape(1)
+    kappa_col = kappa_col.astype(jnp.float32)
+    drift_col = drift_col.astype(jnp.float32)
+    coefficients = jnp.stack(
+        [
+            kappa_row[:, None] * kappa_col[None, :],
+            0.5 * (drift_row[0][:, None] * drift_col[0][None, :]),
+            0.5 * (drift_row[1][:, None] * drift_col[1][None, :]),
+        ]
+    )
     smem = pl.BlockSpec(memory_space=pltpu.SMEM)
     vmem = pl.BlockSpec(memory_space=pltpu.VMEM)
     return pl.pallas_call(
         solve_kernel,
         out_shape=jax.ShapeDtypeStruct((tracers, 1, width), jnp.float32),
-        in_specs=[smem, smem] + [vmem] * 7,
+        in_specs=[smem, smem] + [vmem] * 4,
         out_specs=vmem,
         scratch_shapes=[
-            pltpu.VMEM((2, tracers, rows, width), jnp.float32),
-            pltpu.VMEM((3, rows, width), jnp.float32),
+            pltpu.VMEM((tracers, rows, width), jnp.float32),
+            pltpu.VMEM((tracers, rows, width), jnp.float32),
         ],
         compiler_params=pltpu.CompilerParams(vmem_limit_bytes=56 * 1024 * 1024),
     )(
@@ -163,10 +178,7 @@
         field,
         above_row.astype(jnp.float32),
         below_row.astype(jnp.float32),
-        kappa_row.reshape(rows, 1),
-        drift_row.reshape(2, rows, 1),
-        kappa_col.reshape(1, width),
-        drift_col.reshape(2, 1, width),
+        coefficients,
     )
 
 

time: 180 us -> 133 us (0.74)
  Pallas kernels: 34.7 us -> 12.4 us
  starting transfers between devices: 79.9 us -> 59.9 us
  waiting for transfers between devices: 17.4 us -> 10.5 us
  other arithmetic: 11.4 us -> 15.3 us
  local copies, waits for them, and re-layouts: 17.8 us -> 15.4 us
    pallas_call x1, Pallas kernels: 34.7 us -> 12.4 us  [solve_rows(): pl.pallas_call(solve_kernel, out_shape=jax.ShapeDtypeStruct((tracers, 1,...]
    ppermute x7, starting transfers between devices: 60 us -> 38 us  [gather_along(): lax.ppermute(block, axis, [(i, (i + shift) % count) for i in range(count)])]
    ppermute x7, waiting for transfers between devices: 9.85 us -> 3.34 us  [gather_along(): lax.ppermute(block, axis, [(i, (i + shift) % count) for i in range(count)])]
    ppermute x1, starting transfers between devices: 0.01 us -> 3.02 us  [halo_rows(): above = lax.ppermute(block[:, -1:], axis, forward)]
    ppermute x1, starting transfers between devices: 6.37 us -> 3.35 us  [halo_rows(): below = lax.ppermute(block[:, :1], axis, backward)]
    reshape x4 -> x0, local copies, waits for them, and re-layouts: 2.78 us -> none  [the longest x1 0.76 us: solve_rows(): drift_col.reshape(2, 1, width)]
    ppermute x12, starting transfers between devices: 12.3 us -> 14.8 us  [group_grads(): lax.ppermute(piece, axis, [(i, (i + shift) % count) for i in range(count)])]
    another operation x1 -> x2, other arithmetic: 0.91 us -> 2.75 us  [the longest x1 1.84 us: solve_rows(): jnp.stack([kappa_row[:, None] * kappa_col[None, :], 0.5 * (drift_row[0][:...]
  transfers between devices with their start and end apart: 25 -> 25, of which waited for: 9 -> 10; matrix products, arithmetic and copies ran while one was open for 12% -> 16% of each run, Pallas kernels for 0% -> 0%
where the time goes in v3:
time: 133 us; the launch traced here: 132 us
  starting transfers between devices  59.9 us (45%)
  matrix products  16.8 us (13%)
  local copies, waits for them, and re-layouts  15.4 us (12%)
  other arithmetic  15.3 us (12%)
  Pallas kernels  12.4 us (9%)
  waiting for transfers between devices  10.5 us (8%)
  between operations  2.16 us (2%)
    ppermute x7, starting transfers between devices, gather_along(): lax.ppermute(block, axis, [(i, (i + shift) % count) for i in range(count)])  38 us
    ppermute x12, starting transfers between devices, group_grads(): lax.ppermute(piece, axis, [(i, (i + shift) % count) for i in range(count)])  14.8 us
    pallas_call x1, Pallas kernels, solve_rows(): pl.pallas_call(solve_kernel, out_shape=jax.ShapeDtypeStruct((tracers, 1,...  12.4 us
    ppermute x12, waiting for transfers between devices, group_grads(): lax.ppermute(piece, axis, [(i, (i + shift) % count) for i in range(count)])  6.7 us
    squeeze x2, local copies, waits for them, and re-layouts, mix_modes(): spectral[1]  4.22 us
    ppermute x1, starting transfers between devices, halo_rows(): below = lax.ppermute(block[:, :1], axis, backward)  3.35 us
    ppermute x7, waiting for transfers between devices, gather_along(): lax.ppermute(block, axis, [(i, (i + shift) % count) for i in range(count)])  3.34 us
    ppermute x1, starting transfers between devices, halo_rows(): above = lax.ppermute(block[:, -1:], axis, forward)  3.02 us
  transfers between devices with their start and end apart: 25, of which 10 were waited for; matrix products, arithmetic and copies ran while one was open for 16% of the time, Pallas kernels for 0%

profile of v3, /device:TPU:0, one launch (start us, length us, event | category | flops | bytes accessed | tf_op | source)
XLA Modules:
  0.0 132.5 jit_solution(14924644693506703269)
XLA Ops:
  0.6 2.7 %fusion.153 = (bf16[4,1,16384]{2,1,0:T(2,128)(2,1)}, bf16[4,1,16384]{2,1,0:T(2,128)(2,1)}) fusion(bf16[4,16,16384]{2,1,0:T(8,128)(2,1)} %field_ref.1), kind=kLoop, calls=%fused_computation.226 | loop fusion | bytes 524288 | tf_op jit(solution)/shard_map/slice | solution.py:39
  3.4 3.0 %collective-permute-start = (bf16[4,1,16384]{2,1,0:T(2,128)(2,1)}, bf16[4,1,16384]{2,1,0:T(2,128)(2,1)}, u32[]{:S(2)}, u32[]{:S(2)}) collective-permute-start(bf16[4,1,16384]{2,1,0:T(2,128)(2,1)} %get-tuple-element.8), channel_id=1, source_target_pairs={{0,1},{1,2},{2,3},{3,4},{4,5},{5,6},{6,7},{7,8},{8,9},{9,10},{10,1... | collective-permute-start | bytes 393224 | tf_op jit(solution)/shard_map/ppermute | solution.py:38
  6.4 3.4 %collective-permute-start.1 = (bf16[4,1,16384]{2,1,0:T(2,128)(2,1)}, bf16[4,1,16384]{2,1,0:T(2,128)(2,1)}, u32[]{:S(2)}, u32[]{:S(2)}) collective-permute-start(bf16[4,1,16384]{2,1,0:T(2,128)(2,1)} %get-tuple-element.7), channel_id=1, source_target_pairs={{1,0},{2,1},{3,2},{4,3},{5,4},{6,5},{7,6},{8,7},{9,8},{10,9},{11,1... | collective-permute-start | bytes 393224 | tf_op jit(solution)/shard_map/ppermute | solution.py:39
  9.8 1.0 fusion.156
  10.8 0.8 slice_bitcast_fusion.3
  11.6 0.8 convert_element_type.66
  12.3 1.9 %slice_bitcast_fusion = (bf16[32,8,32,16]{2,3,1,0:T(8,128)(2,1)S(1)}, bf16[32,8,32,16]{2,3,1,0:T(8,128)(2,1)S(1)}) fusion(bf16[2,32,8,32,16]{3,4,2,1,0:T(8,128)(2,1)} %param.26), kind=kLoop, calls=%fused_computation.23 | loop fusion | bytes 1048576 | tf_op jit(solution)/shard_map/squeeze | solution.py:246
  15.2 1.8 %pad_maximum_fusion.coef_ref = f32[3,16,16384]{2,1,0:T(8,128)} fusion(f32[1,16,16384]{2,1,0:T(8,128)S(1)} %get-tuple-element.43, f32[1,16,16384]{2,1,0:T(8,128)S(1)} %get-tuple-element.44, f32[1,16,16384]{2,1,0:T(8,128)S(1)} %broadcast_multiply_fusion), kind=kLoop, calls=%fused_computation | loop fusion | flops 1572864 | bytes 6291456 | tf_op jit(solution)/shard_map/stack | solution.py:156
  17.9 2.3 %copy.69 = bf16[32,8,32,16]{0,1,3,2:T(8,128)(2,1)S(1)} copy(bf16[32,8,32,16]{2,3,1,0:T(8,128)(2,1)S(1)} %get-tuple-element.5) | data formatting | bytes 524288 | tf_op jit(solution)/shard_map/squeeze | solution.py:246
  20.2 3.0 %copy.66 = bf16[32,8,32,16]{0,1,3,2:T(8,128)(2,1)} copy(bf16[32,8,32,16]{2,3,1,0:T(8,128)(2,1)S(1)} %get-tuple-element.6) | data formatting | bytes 524288 | tf_op jit(solution)/shard_map/squeeze | solution.py:245
  23.3 0.9 negate_convert_fusion
  24.2 1.9 %convert_element_type.64.above_ref = f32[4,1,16384]{2,1,0:T(1,128)} convert(bf16[4,1,16384]{2,1,0:T(2,128)(2,1)} %collective-permute-done) | non-fusion elementwise | flops 65536 | bytes 393216 | tf_op jit(solution)/shard_map/convert_element_type | solution.py:179
  26.1 1.9 %convert_element_type.65.below_ref = f32[4,1,16384]{2,1,0:T(1,128)} convert(bf16[4,1,16384]{2,1,0:T(2,128)(2,1)} %collective-permute-done.1) | non-fusion elementwise | flops 65536 | bytes 393216 | tf_op jit(solution)/shard_map/convert_element_type | solution.py:180
  28.1 12.4 %shard_map.157 = f32[4,1,16384]{2,1,0:T(1,128)} custom-call(f32[1]{0:T(128)S(6)} %div.10.step_ref, s32[1]{0:T(128)S(6)} %copy.109.count_ref, bf16[4,16,16384]{2,1,0:T(8,128)(2,1)} %field_ref.1, f32[4,1,16384]{2,1,0:T(1,128)} %convert_element_type.64.above_ref, f32[4,1,16384]{2,1,0:T(1,128)} %convert_element_type.65.below_ref, ...), custom_call_target="tpu_custom_call" | custom-call | tf_op jit(solution)/shard_map/pallas_call | solution.py:165
  40.4 1.6 %reduce = f32[4,16384]{1,0:T(4,128)S(1)} reduce(f32[4,1,16384]{2,1,0:T(1,128)} %shard_map.157, f32[]{:T(128)} %constant.378), dimensions={1}, to_apply=%pallas_call.3.reduce_sub_computation | reduce | bytes 524292 | tf_op jit(solution)/shard_map/pallas_call | solution.py:165
  42.1 0.7 reshape.211
  42.8 0.6 reduce_sum.9
  43.4 4.2 %collective-permute-start.2 = (bf16[4,1024]{1,0:T(4,128)(2,1)S(1)}, bf16[4,1024]{1,0:T(4,128)(2,1)S(1)}, u32[]{:S(2)}, u32[]{:S(2)}) collective-permute-start(bf16[4,1024]{1,0:T(4,128)(2,1)S(1)} %multiply_convert_fusion), channel_id=1, source_target_pairs={{0,1},{1,2},{2,3},{3,0},{4,5},{5,6},{6,7},{7,4},{8,9},{9,10},{10,1... | collective-permute-start | bytes 24584 | tf_op jit(solution)/shard_map/ppermute | solution.py:283
  47.6 6.8 %collective-permute-start.3 = (bf16[4,1024]{1,0:T(4,128)(2,1)S(1)}, bf16[4,1024]{1,0:T(4,128)(2,1)S(1)}, u32[]{:S(2)}, u32[]{:S(2)}) collective-permute-start(bf16[4,1024]{1,0:T(4,128)(2,1)S(1)} %multiply_convert_fusion), channel_id=1, source_target_pairs={{0,2},{1,3},{2,0},{3,1},{4,6},{5,7},{6,4},{7,5},{8,10},{9,11},{10,... | collective-permute-start | bytes 24584 | tf_op jit(solution)/shard_map/ppermute | solution.py:283
  54.5 2.8 %collective-permute-start.4 = (bf16[4,1024]{1,0:T(4,128)(2,1)S(1)}, bf16[4,1024]{1,0:T(4,128)(2,1)S(1)}, u32[]{:S(2)}, u32[]{:S(2)}) collective-permute-start(bf16[4,1024]{1,0:T(4,128)(2,1)S(1)} %multiply_convert_fusion), channel_id=1, source_target_pairs={{0,3},{1,0},{2,1},{3,2},{4,7},{5,4},{6,5},{7,6},{8,11},{9,8},{10,9... | collective-permute-start | bytes 24584 | tf_op jit(solution)/shard_map/ppermute | solution.py:283
  57.3 0.6 convert_dynamic-update-slice_fusion
  58.0 0.7 collective-permute-done.4
  58.7 14.6 %collective-permute-start.5 = (bf16[4,4,1024]{2,1,0:T(4,128)(2,1)S(1)}, bf16[4,4,1024]{2,1,0:T(4,128)(2,1)S(1)}, u32[]{:S(2)}, u32[]{:S(2)}) collective-permute-start(bf16[4,4,1024]{2,1,0:T(4,128)(2,1)S(1)} %bitcast_dynamic-update-slice_fusion.6), channel_id=1, source_target_pairs={{0,4},{4,0},{1,5},{5,1},{2,6},{6,2},{3,7},{7,3},{8,12},{12,8},{9,1... | collective-permute-start | bytes 98312 | tf_op jit(solution)/shard_map/ppermute | solution.py:283
  73.3 0.8 collective-permute-done.5
  74.2 4.0 %collective-permute-start.6 = (bf16[2,4,4,1024]{3,2,1,0:T(4,128)(2,1)S(1)}, bf16[2,4,4,1024]{3,2,1,0:T(4,128)(2,1)S(1)}, u32[]{:S(2)}, u32[]{:S(2)}) collective-permute-start(bf16[2,4,4,1024]{3,2,1,0:T(4,128)(2,1)S(1)} %bitcast_dynamic-update-slice_fusion.4), channel_id=1, source_target_pairs={{0,8},{8,16},{16,24},{24,0},{1,9},{9,17},{17,25},{25,1},{2,10},{10... | collective-permute-start | bytes 196616 | tf_op jit(solution)/shard_map/ppermute | solution.py:283
  78.2 2.6 %collective-permute-start.7 = (bf16[2,4,4,1024]{3,2,1,0:T(4,128)(2,1)S(1)}, bf16[2,4,4,1024]{3,2,1,0:T(4,128)(2,1)S(1)}, u32[]{:S(2)}, u32[]{:S(2)}) collective-permute-start(bf16[2,4,4,1024]{3,2,1,0:T(4,128)(2,1)S(1)} %bitcast_dynamic-update-slice_fusion.4), channel_id=1, source_target_pairs={{0,16},{8,24},{16,0},{24,8},{1,17},{9,25},{17,1},{25,9},{2,18},{10... | collective-permute-start | bytes 196616 | tf_op jit(solution)/shard_map/ppermute | solution.py:283
  80.8 2.8 %collective-permute-start.8 = (bf16[2,4,4,1024]{3,2,1,0:T(4,128)(2,1)S(1)}, bf16[2,4,4,1024]{3,2,1,0:T(4,128)(2,1)S(1)}, u32[]{:S(2)}, u32[]{:S(2)}) collective-permute-start(bf16[2,4,4,1024]{3,2,1,0:T(4,128)(2,1)S(1)} %bitcast_dynamic-update-slice_fusion.4), channel_id=1, source_target_pairs={{0,24},{8,0},{16,8},{24,16},{1,25},{9,1},{17,9},{25,17},{2,26},{10... | collective-permute-start | bytes 196616 | tf_op jit(solution)/shard_map/ppermute | solution.py:283
  83.9 1.8 %collective-permute-done.8 = bf16[2,4,4,1024]{3,2,1,0:T(4,128)(2,1)S(1)} collective-permute-done((bf16[2,4,4,1024]{3,2,1,0:T(4,128)(2,1)S(1)}, bf16[2,4,4,1024]{3,2,1,0:T(4,128)(2,1)S(1)}, u32[]{:S(2)}, u32[]{:S(2)}) %collective-permute-start.8) | collective-permute-done | bytes 65568 | tf_op jit(solution)/shard_map/ppermute | solution.py:283
  85.8 1.2 fusion
  87.0 0.9 fusion.66
  87.9 0.5 fusion.45
  88.5 0.5 fusion.49
  89.0 0.5 fusion.4
  89.6 0.5 fusion.6
  90.2 0.6 collective-permute-start.9
  90.7 0.4 collective-permute-done.10
  91.2 1.8 %fusion.35 = f32[32,16,1,8]{3,2,1,0:T(1,128)S(1)} fusion(bf16[32,8,32,16]{0,1,3,2:T(8,128)(2,1)S(1)} %copy.69, f32[32,32,16,1]{0,1,2,3:T(8,128)S(1)} %bitcast.176), kind=kOutput, calls=%fused_computation.68 | convolution fusion | flops 1572864 | bytes 344064 | tf_op jit(solution)/shard_map/hojl,hjl->ojl/dot_general | solution.py:246
  93.1 1.8 %fusion.37 = f32[32,16,1,8]{3,2,1,0:T(1,128)S(1)} fusion(bf16[32,8,32,16]{0,1,3,2:T(8,128)(2,1)S(1)} %copy.69, f32[32,32,16,1]{0,1,2,3:T(8,128)S(1)} %bitcast.178), kind=kOutput, calls=%fused_computation.70 | convolution fusion | flops 1572864 | bytes 344064 | tf_op jit(solution)/shard_map/hojl,hjl->ojl/dot_general | solution.py:249
  94.9 1.8 %fusion.39 = f32[32,16,1,8]{3,2,1,0:T(1,128)S(1)} fusion(bf16[32,8,32,16]{0,1,3,2:T(8,128)(2,1)S(1)} %copy-done.1, f32[32,32,16,1]{0,1,2,3:T(8,128)S(1)} %bitcast.179), kind=kOutput, calls=%fused_computation.72 | convolution fusion | flops 1572864 | bytes 344064 | tf_op jit(solution)/shard_map/hojl,hjl->ojl/dot_general | solution.py:244
  96.7 1.8 %fusion.33 = f32[32,16,1,8]{3,2,1,0:T(1,128)S(1)} fusion(bf16[32,8,32,16]{0,1,3,2:T(8,128)(2,1)S(1)} %copy-done.1, f32[32,32,16,1]{0,1,2,3:T(8,128)S(1)} %bitcast.177), kind=kOutput, calls=%fused_computation.66 | convolution fusion | flops 1572864 | bytes 344064 | tf_op jit(solution)/shard_map/hojl,hjl->ojl/dot_general | solution.py:247
  98.8 0.6 fusion.84
  99.4 0.7 fusion.72
  100.3 0.6 fusion.74
  101.0 0.7 fusion.82
  102.1 0.9 convolution_multiply_fusion
  103.3 1.8 %fusion.30 = bf16[1,16,8,1024]{3,2,1,0:T(8,128)(2,1)} fusion(f32[16,8,1024]{2,1,0:T(8,128)S(1)} %fusion.2), kind=kLoop, calls=%fused_computation.64 | loop fusion | flops 8519680 | bytes 786432 | tf_op jit(solution)/shard_map/broadcast_in_dim | solution.py:383
  105.1 0.3 fusion.31
  105.6 0.3 fusion.80
  106.0 3.1 %collective-permute-start.21 = (f32[16,8,16]{0,1,2:T(8,128)S(1)}, f32[16,8,16]{0,1,2:T(8,128)S(1)}, u32[]{:S(2)}, u32[]{:S(2)}) collective-permute-start(f32[16,8,16]{0,1,2:T(8,128)S(1)} %get-tuple-element.9), channel_id=1, source_target_pairs={{0,24},{8,0},{16,8},{24,16},{1,25},{9,1},{17,9},{25,17},{2,26},{10... | collective-permute-start | bytes 24584 | tf_op jit(solution)/shard_map/ppermute | solution.py:313
  109.9 0.4 collective-permute-start.17
  110.4 1.7 %collective-permute-start.19 = (f32[16,8,16]{0,1,2:T(8,128)S(1)}, f32[16,8,16]{0,1,2:T(8,128)S(1)}, u32[]{:S(2)}, u32[]{:S(2)}) collective-permute-start(f32[16,8,16]{0,1,2:T(8,128)S(1)} %get-tuple-element.14), channel_id=1, source_target_pairs={{0,16},{8,24},{16,0},{24,8},{1,17},{9,25},{17,1},{25,9},{2,18},{10... | collective-permute-start | bytes 24584 | tf_op jit(solution)/shard_map/ppermute | solution.py:313
  112.0 2.0 %collective-permute-start.13 = (f32[16,8,16]{0,1,2:T(8,128)S(1)}, f32[16,8,16]{0,1,2:T(8,128)S(1)}, u32[]{:S(2)}, u32[]{:S(2)}) collective-permute-start(f32[16,8,16]{0,1,2:T(8,128)S(1)} %get-tuple-element.11), channel_id=1, source_target_pairs={{0,8},{8,16},{16,24},{24,0},{1,9},{9,17},{17,25},{25,1},{2,10},{10... | collective-permute-start | bytes 24584 | tf_op jit(solution)/shard_map/ppermute | solution.py:313
  114.0 0.5 collective-permute-start.15
  115.4 2.5 %collective-permute-done.19 = f32[16,8,16]{0,1,2:T(8,128)S(1)} collective-permute-done((f32[16,8,16]{0,1,2:T(8,128)S(1)}, f32[16,8,16]{0,1,2:T(8,128)S(1)}, u32[]{:S(2)}, u32[]{:S(2)}) %collective-permute-start.19) | collective-permute-done | bytes 8224 | tf_op jit(solution)/shard_map/ppermute | solution.py:313
  118.2 1.0 collective-permute-done.15
  119.4 0.8 collective-permute-start.22
  120.4 2.2 %collective-permute-start.24 = (f32[8,8,16]{1,2,0:T(8,128)S(1)}, f32[8,8,16]{1,2,0:T(8,128)S(1)}, u32[]{:S(2)}, u32[]{:S(2)}) collective-permute-start(f32[8,8,16]{1,2,0:T(8,128)S(1)} %get-tuple-element.31), channel_id=1, source_target_pairs={{0,24},{8,0},{16,8},{24,16},{1,25},{9,1},{17,9},{25,17},{2,26},{10... | collective-permute-start | bytes 12296 | tf_op jit(solution)/shard_map/ppermute | solution.py:313
  122.6 0.6 collective-permute-start.18
  123.2 1.5 %collective-permute-start.20 = (f32[8,8,16]{1,2,0:T(8,128)S(1)}, f32[8,8,16]{1,2,0:T(8,128)S(1)}, u32[]{:S(2)}, u32[]{:S(2)}) collective-permute-start(f32[8,8,16]{1,2,0:T(8,128)S(1)} %get-tuple-element.32), channel_id=1, source_target_pairs={{0,16},{8,24},{16,0},{24,8},{1,17},{9,25},{17,1},{25,9},{2,18},{10... | collective-permute-start | bytes 12296 | tf_op jit(solution)/shard_map/ppermute | solution.py:313
  124.8 2.0 %collective-permute-start.16 = (f32[8,8,16]{1,2,0:T(8,128)S(1)}, f32[8,8,16]{1,2,0:T(8,128)S(1)}, u32[]{:S(2)}, u32[]{:S(2)}) collective-permute-start(f32[8,8,16]{1,2,0:T(8,128)S(1)} %get-tuple-element.33), channel_id=1, source_target_pairs={{0,8},{8,16},{16,24},{24,0},{1,9},{9,17},{17,25},{25,1},{2,10},{10... | collective-permute-start | bytes 12296 | tf_op jit(solution)/shard_map/ppermute | solution.py:313
  127.5 0.6 collective-permute-done.20
  128.2 1.6 %collective-permute-done.14 = f32[8,8,16]{1,2,0:T(8,128)S(1)} collective-permute-done((f32[8,8,16]{1,2,0:T(8,128)S(1)}, f32[8,8,16]{1,2,0:T(8,128)S(1)}, u32[]{:S(2)}, u32[]{:S(2)}) %collective-permute-start.14) | collective-permute-done | bytes 4128 | tf_op jit(solution)/shard_map/ppermute | solution.py:313
  129.9 0.6 collective-permute-done.16
  131.1 1.4 %fusion.13 = f32[2,16,8,8,16]{4,3,2,1,0:T(8,128)} fusion(f32[1,16,8,8,16]{4,3,2,1,0:T(8,128)S(1)} %get-tuple-element.26, f32[1,16,8,8,16]{4,3,2,1,0:T(8,128)S(1)} %get-tuple-element.25, f32[1,16,8,8,16]{4,3,2,1,0:T(8,128)S(1)} %get-tuple-element.24, f32[1,16,8,8,16]{4,3,2,1,0:T(8,128)S(1)} %get-tuple-element.23, ...), kind=kLoop, calls=%fused_computation.22 | loop fusion | flops 262144 | bytes 655360 | tf_op jit(solution)/shard_map/div | solution.py:397
  (106 shorter events, 6.7 us)
Async XLA Ops:
  0.6 102.3 %copy-start = (bf16[32,8]{0,1:T(8,128)(2,1)S(1)}, bf16[32,8]{0,1:T(8,128)(2,1)}, u32[]{:S(2)}) copy-start(bf16[32,8]{0,1:T(8,128)(2,1)} %param.24) | copy-start | bytes 1540
  3.4 20.8 %collective-permute-start = (bf16[4,1,16384]{2,1,0:T(2,128)(2,1)}, bf16[4,1,16384]{2,1,0:T(2,128)(2,1)}, u32[]{:S(2)}, u32[]{:S(2)}) collective-permute-start(bf16[4,1,16384]{2,1,0:T(2,128)(2,1)} %get-tuple-element.8), channel_id=1, source_target_pairs={{0,1},{1,2},{2,3},{3,4},{4,5},{5,6},{6,7},{7,8},{8,9},{9,10},{10,1... | collective-permute-start | bytes 393224 | tf_op jit(solution)/shard_map/ppermute | solution.py:38
  6.4 19.7 %collective-permute-start.1 = (bf16[4,1,16384]{2,1,0:T(2,128)(2,1)}, bf16[4,1,16384]{2,1,0:T(2,128)(2,1)}, u32[]{:S(2)}, u32[]{:S(2)}) collective-permute-start(bf16[4,1,16384]{2,1,0:T(2,128)(2,1)} %get-tuple-element.7), channel_id=1, source_target_pairs={{1,0},{2,1},{3,2},{4,3},{5,4},{6,5},{7,6},{8,7},{9,8},{10,9},{11,1... | collective-permute-start | bytes 393224 | tf_op jit(solution)/shard_map/ppermute | solution.py:39
  12.3 2.5 %copy-start.7 = (f32[16]{0:T(128)S(1)}, f32[16]{0:T(128)}, u32[]{:S(2)}) copy-start(f32[16]{0:T(128)} %param.16) | copy-start | bytes 196
  15.2 1.9 %copy-start.8 = (s32[32]{0:T(128)S(1)}, s32[32]{0:T(128)}, u32[]{:S(2)}) copy-start(s32[32]{0:T(128)} %param.20) | copy-start | bytes 388
  42.7 43.0 %copy-start.2 = (bf16[1,16,4,1024]{3,2,1,0:T(4,128)(2,1)S(1)}, bf16[1,16,4,1024]{3,2,1,0:T(4,128)(2,1)}, u32[]{:S(2)}) copy-start(bf16[1,16,4,1024]{3,2,1,0:T(4,128)(2,1)} %param.21) | copy-start | bytes 393220
  42.8 44.2 %copy-start.3 = (bf16[1024,16]{0,1:T(8,128)(2,1)S(1)}, bf16[1024,16]{0,1:T(8,128)(2,1)}, u32[]{:S(2)}) copy-start(bf16[1024,16]{0,1:T(8,128)(2,1)} %get-tuple-element.45) | copy-start | bytes 98308
  42.8 44.2 %copy-start.5 = (bf16[1024,16]{0,1:T(8,128)(2,1)S(1)}, bf16[1024,16]{0,1:T(8,128)(2,1)}, u32[]{:S(2)}) copy-start(bf16[1024,16]{0,1:T(8,128)(2,1)} %get-tuple-element.46) | copy-start | bytes 98308
  43.4 14.5 %collective-permute-start.2 = (bf16[4,1024]{1,0:T(4,128)(2,1)S(1)}, bf16[4,1024]{1,0:T(4,128)(2,1)S(1)}, u32[]{:S(2)}, u32[]{:S(2)}) collective-permute-start(bf16[4,1024]{1,0:T(4,128)(2,1)S(1)} %multiply_convert_fusion), channel_id=1, source_target_pairs={{0,1},{1,2},{2,3},{3,0},{4,5},{5,6},{6,7},{7,4},{8,9},{9,10},{10,1... | collective-permute-start | bytes 24584 | tf_op jit(solution)/shard_map/ppermute | solution.py:283
  47.6 10.3 %collective-permute-start.3 = (bf16[4,1024]{1,0:T(4,128)(2,1)S(1)}, bf16[4,1024]{1,0:T(4,128)(2,1)S(1)}, u32[]{:S(2)}, u32[]{:S(2)}) collective-permute-start(bf16[4,1024]{1,0:T(4,128)(2,1)S(1)} %multiply_convert_fusion), channel_id=1, source_target_pairs={{0,2},{1,3},{2,0},{3,1},{4,6},{5,7},{6,4},{7,5},{8,10},{9,11},{10,... | collective-permute-start | bytes 24584 | tf_op jit(solution)/shard_map/ppermute | solution.py:283
  54.5 4.2 %collective-permute-start.4 = (bf16[4,1024]{1,0:T(4,128)(2,1)S(1)}, bf16[4,1024]{1,0:T(4,128)(2,1)S(1)}, u32[]{:S(2)}, u32[]{:S(2)}) collective-permute-start(bf16[4,1024]{1,0:T(4,128)(2,1)S(1)} %multiply_convert_fusion), channel_id=1, source_target_pairs={{0,3},{1,0},{2,1},{3,2},{4,7},{5,4},{6,5},{7,6},{8,11},{9,8},{10,9... | collective-permute-start | bytes 24584 | tf_op jit(solution)/shard_map/ppermute | solution.py:283
  58.7 15.5 %collective-permute-start.5 = (bf16[4,4,1024]{2,1,0:T(4,128)(2,1)S(1)}, bf16[4,4,1024]{2,1,0:T(4,128)(2,1)S(1)}, u32[]{:S(2)}, u32[]{:S(2)}) collective-permute-start(bf16[4,4,1024]{2,1,0:T(4,128)(2,1)S(1)} %bitcast_dynamic-update-slice_fusion.6), channel_id=1, source_target_pairs={{0,4},{4,0},{1,5},{5,1},{2,6},{6,2},{3,7},{7,3},{8,12},{12,8},{9,1... | collective-permute-start | bytes 98312 | tf_op jit(solution)/shard_map/ppermute | solution.py:283
  74.2 9.6 %collective-permute-start.6 = (bf16[2,4,4,1024]{3,2,1,0:T(4,128)(2,1)S(1)}, bf16[2,4,4,1024]{3,2,1,0:T(4,128)(2,1)S(1)}, u32[]{:S(2)}, u32[]{:S(2)}) collective-permute-start(bf16[2,4,4,1024]{3,2,1,0:T(4,128)(2,1)S(1)} %bitcast_dynamic-update-slice_fusion.4), channel_id=1, source_target_pairs={{0,8},{8,16},{16,24},{24,0},{1,9},{9,17},{17,25},{25,1},{2,10},{10... | collective-permute-start | bytes 196616 | tf_op jit(solution)/shard_map/ppermute | solution.py:283
  78.2 5.7 %collective-permute-start.7 = (bf16[2,4,4,1024]{3,2,1,0:T(4,128)(2,1)S(1)}, bf16[2,4,4,1024]{3,2,1,0:T(4,128)(2,1)S(1)}, u32[]{:S(2)}, u32[]{:S(2)}) collective-permute-start(bf16[2,4,4,1024]{3,2,1,0:T(4,128)(2,1)S(1)} %bitcast_dynamic-update-slice_fusion.4), channel_id=1, source_target_pairs={{0,16},{8,24},{16,0},{24,8},{1,17},{9,25},{17,1},{25,9},{2,18},{10... | collective-permute-start | bytes 196616 | tf_op jit(solution)/shard_map/ppermute | solution.py:283
  80.8 4.9 %collective-permute-start.8 = (bf16[2,4,4,1024]{3,2,1,0:T(4,128)(2,1)S(1)}, bf16[2,4,4,1024]{3,2,1,0:T(4,128)(2,1)S(1)}, u32[]{:S(2)}, u32[]{:S(2)}) collective-permute-start(bf16[2,4,4,1024]{3,2,1,0:T(4,128)(2,1)S(1)} %bitcast_dynamic-update-slice_fusion.4), channel_id=1, source_target_pairs={{0,24},{8,0},{16,8},{24,16},{1,25},{9,1},{17,9},{25,17},{2,26},{10... | collective-permute-start | bytes 196616 | tf_op jit(solution)/shard_map/ppermute | solution.py:283
  89.6 1.6 %collective-permute-start.10 = (f32[32,32,16]{0,1,2:T(8,128)S(1)}, f32[32,32,16]{0,1,2:T(8,128)S(1)}, u32[]{:S(2)}, u32[]{:S(2)}) collective-permute-start(f32[32,32,16]{0,1,2:T(8,128)S(1)} %fusion.4), channel_id=1, source_target_pairs={{0,4},{4,0},{1,5},{5,1},{2,6},{6,2},{3,7},{7,3},{8,12},{12,8},{9,1... | collective-permute-start | bytes 196616 | tf_op jit(solution)/shard_map/ppermute | solution.py:297
  90.2 2.9 %collective-permute-start.9 = (f32[32,32,16]{0,1,2:T(8,128)S(1)}, f32[32,32,16]{0,1,2:T(8,128)S(1)}, u32[]{:S(2)}, u32[]{:S(2)}) collective-permute-start(f32[32,32,16]{0,1,2:T(8,128)S(1)} %fusion.6), channel_id=1, source_target_pairs={{0,4},{4,0},{1,5},{5,1},{2,6},{6,2},{3,7},{7,3},{8,12},{12,8},{9,1... | collective-permute-start | bytes 196616 | tf_op jit(solution)/shard_map/ppermute | solution.py:297
  91.2 3.7 %copy-start.1 = (bf16[32,8,32,16]{0,1,3,2:T(8,128)(2,1)S(1)}, bf16[32,8,32,16]{0,1,3,2:T(8,128)(2,1)}, u32[]{:S(2)}) copy-start(bf16[32,8,32,16]{0,1,3,2:T(8,128)(2,1)} %copy.66) | copy-start | bytes 786436
  98.6 4.4 %copy-start.9 = (f32[8]{0:T(128)S(1)}, f32[8]{0:T(128)}, u32[]{:S(2)}) copy-start(f32[8]{0:T(128)} %param.25) | copy-start | bytes 100
  102.0 3.1 %copy-start.4 = (bf16[1024,16]{0,1:T(8,128)(2,1)S(1)}, bf16[1024,16]{0,1:T(8,128)(2,1)}, u32[]{:S(2)}) copy-start(bf16[1024,16]{0,1:T(8,128)(2,1)} %get-tuple-element.45) | copy-start | bytes 98308
  102.0 3.1 %copy-start.6 = (bf16[1024,16]{0,1:T(8,128)(2,1)S(1)}, bf16[1024,16]{0,1:T(8,128)(2,1)}, u32[]{:S(2)}) copy-start(bf16[1024,16]{0,1:T(8,128)(2,1)} %get-tuple-element.46) | copy-start | bytes 98308
  102.0 3.1 %copy-start.10 = (bf16[1,16,8,1024]{3,2,1,0:T(8,128)(2,1)S(1)}, bf16[1,16,8,1024]{3,2,1,0:T(8,128)(2,1)}, u32[]{:S(2)}) copy-start(bf16[1,16,8,1024]{3,2,1,0:T(8,128)(2,1)} %param.27) | copy-start | bytes 786436
  106.0 6.0 %collective-permute-start.21 = (f32[16,8,16]{0,1,2:T(8,128)S(1)}, f32[16,8,16]{0,1,2:T(8,128)S(1)}, u32[]{:S(2)}, u32[]{:S(2)}) collective-permute-start(f32[16,8,16]{0,1,2:T(8,128)S(1)} %get-tuple-element.9), channel_id=1, source_target_pairs={{0,24},{8,0},{16,8},{24,16},{1,25},{9,1},{17,9},{25,17},{2,26},{10... | collective-permute-start | bytes 24584 | tf_op jit(solution)/shard_map/ppermute | solution.py:313
  109.1 4.8 %collective-permute-start.23 = (f32[16,8,16]{0,1,2:T(8,128)S(1)}, f32[16,8,16]{0,1,2:T(8,128)S(1)}, u32[]{:S(2)}, u32[]{:S(2)}) collective-permute-start(f32[16,8,16]{0,1,2:T(8,128)S(1)} %get-tuple-element.13), channel_id=1, source_target_pairs={{0,24},{8,0},{16,8},{24,16},{1,25},{9,1},{17,9},{25,17},{2,26},{10... | collective-permute-start | bytes 24584 | tf_op jit(solution)/shard_map/ppermute | solution.py:313
  109.9 9.4 %collective-permute-start.11 = (f32[8,32,16]{1,2,0:T(8,128)S(1)}, f32[8,32,16]{1,2,0:T(8,128)S(1)}, u32[]{:S(2)}, u32[]{:S(2)}) collective-permute-start(f32[8,32,16]{1,2,0:T(8,128)S(1)} %fusion.10), channel_id=1, source_target_pairs={{0,4},{4,0},{1,5},{5,1},{2,6},{6,2},{3,7},{7,3},{8,12},{12,8},{9,1... | collective-permute-start | bytes 49160 | tf_op jit(solution)/shard_map/ppermute | solution.py:297
  109.9 5.3 %collective-permute-start.17 = (f32[16,8,16]{0,1,2:T(8,128)S(1)}, f32[16,8,16]{0,1,2:T(8,128)S(1)}, u32[]{:S(2)}, u32[]{:S(2)}) collective-permute-start(f32[16,8,16]{0,1,2:T(8,128)S(1)} %get-tuple-element.10), channel_id=1, source_target_pairs={{0,16},{8,24},{16,0},{24,8},{1,17},{9,25},{17,1},{25,9},{2,18},{10... | collective-permute-start | bytes 24584 | tf_op jit(solution)/shard_map/ppermute | solution.py:313
  110.4 7.6 %collective-permute-start.19 = (f32[16,8,16]{0,1,2:T(8,128)S(1)}, f32[16,8,16]{0,1,2:T(8,128)S(1)}, u32[]{:S(2)}, u32[]{:S(2)}) collective-permute-start(f32[16,8,16]{0,1,2:T(8,128)S(1)} %get-tuple-element.14), channel_id=1, source_target_pairs={{0,16},{8,24},{16,0},{24,8},{1,17},{9,25},{17,1},{25,9},{2,18},{10... | collective-permute-start | bytes 24584 | tf_op jit(solution)/shard_map/ppermute | solution.py:313
  112.0 6.0 %collective-permute-start.13 = (f32[16,8,16]{0,1,2:T(8,128)S(1)}, f32[16,8,16]{0,1,2:T(8,128)S(1)}, u32[]{:S(2)}, u32[]{:S(2)}) collective-permute-start(f32[16,8,16]{0,1,2:T(8,128)S(1)} %get-tuple-element.11), channel_id=1, source_target_pairs={{0,8},{8,16},{16,24},{24,0},{1,9},{9,17},{17,25},{25,1},{2,10},{10... | collective-permute-start | bytes 24584 | tf_op jit(solution)/shard_map/ppermute | solution.py:313
  114.0 5.2 %collective-permute-start.15 = (f32[16,8,16]{0,1,2:T(8,128)S(1)}, f32[16,8,16]{0,1,2:T(8,128)S(1)}, u32[]{:S(2)}, u32[]{:S(2)}) collective-permute-start(f32[16,8,16]{0,1,2:T(8,128)S(1)} %get-tuple-element.15), channel_id=1, source_target_pairs={{0,8},{8,16},{16,24},{24,0},{1,9},{9,17},{17,25},{25,1},{2,10},{10... | collective-permute-start | bytes 24584 | tf_op jit(solution)/shard_map/ppermute | solution.py:313
  115.2 5.0 %collective-permute-start.12 = (f32[8,32,16]{1,2,0:T(8,128)S(1)}, f32[8,32,16]{1,2,0:T(8,128)S(1)}, u32[]{:S(2)}, u32[]{:S(2)}) collective-permute-start(f32[8,32,16]{1,2,0:T(8,128)S(1)} %fusion.8), channel_id=1, source_target_pairs={{0,4},{4,0},{1,5},{5,1},{2,6},{6,2},{3,7},{7,3},{8,12},{12,8},{9,1... | collective-permute-start | bytes 49160 | tf_op jit(solution)/shard_map/ppermute | solution.py:297
  119.4 5.4 %collective-permute-start.22 = (f32[8,8,16]{1,2,0:T(8,128)S(1)}, f32[8,8,16]{1,2,0:T(8,128)S(1)}, u32[]{:S(2)}, u32[]{:S(2)}) collective-permute-start(f32[8,8,16]{1,2,0:T(8,128)S(1)} %get-tuple-element.27), channel_id=1, source_target_pairs={{0,24},{8,0},{16,8},{24,16},{1,25},{9,1},{17,9},{25,17},{2,26},{10... | collective-permute-start | bytes 12296 | tf_op jit(solution)/shard_map/ppermute | solution.py:313
  120.4 6.6 %collective-permute-start.24 = (f32[8,8,16]{1,2,0:T(8,128)S(1)}, f32[8,8,16]{1,2,0:T(8,128)S(1)}, u32[]{:S(2)}, u32[]{:S(2)}) collective-permute-start(f32[8,8,16]{1,2,0:T(8,128)S(1)} %get-tuple-element.31), channel_id=1, source_target_pairs={{0,24},{8,0},{16,8},{24,16},{1,25},{9,1},{17,9},{25,17},{2,26},{10... | collective-permute-start | bytes 12296 | tf_op jit(solution)/shard_map/ppermute | solution.py:313
  122.6 4.8 %collective-permute-start.18 = (f32[8,8,16]{1,2,0:T(8,128)S(1)}, f32[8,8,16]{1,2,0:T(8,128)S(1)}, u32[]{:S(2)}, u32[]{:S(2)}) collective-permute-start(f32[8,8,16]{1,2,0:T(8,128)S(1)} %get-tuple-element.28), channel_id=1, source_target_pairs={{0,16},{8,24},{16,0},{24,8},{1,17},{9,25},{17,1},{25,9},{2,18},{10... | collective-permute-start | bytes 12296 | tf_op jit(solution)/shard_map/ppermute | solution.py:313
  123.2 5.0 %collective-permute-start.20 = (f32[8,8,16]{1,2,0:T(8,128)S(1)}, f32[8,8,16]{1,2,0:T(8,128)S(1)}, u32[]{:S(2)}, u32[]{:S(2)}) collective-permute-start(f32[8,8,16]{1,2,0:T(8,128)S(1)} %get-tuple-element.32), channel_id=1, source_target_pairs={{0,16},{8,24},{16,0},{24,8},{1,17},{9,25},{17,1},{25,9},{2,18},{10... | collective-permute-start | bytes 12296 | tf_op jit(solution)/shard_map/ppermute | solution.py:313
  124.7 5.2 %collective-permute-start.14 = (f32[8,8,16]{1,2,0:T(8,128)S(1)}, f32[8,8,16]{1,2,0:T(8,128)S(1)}, u32[]{:S(2)}, u32[]{:S(2)}) collective-permute-start(f32[8,8,16]{1,2,0:T(8,128)S(1)} %get-tuple-element.29), channel_id=1, source_target_pairs={{0,8},{8,16},{16,24},{24,0},{1,9},{9,17},{17,25},{25,1},{2,10},{10... | collective-permute-start | bytes 12296 | tf_op jit(solution)/shard_map/ppermute | solution.py:313
  124.8 5.7 %collective-permute-start.16 = (f32[8,8,16]{1,2,0:T(8,128)S(1)}, f32[8,8,16]{1,2,0:T(8,128)S(1)}, u32[]{:S(2)}, u32[]{:S(2)}) collective-permute-start(f32[8,8,16]{1,2,0:T(8,128)S(1)} %get-tuple-element.33), channel_id=1, source_target_pairs={{0,8},{8,16},{16,24},{24,0},{1,9},{9,17},{17,25},{25,1},{2,10},{10... | collective-permute-start | bytes 12296 | tf_op jit(solution)/shard_map/ppermute | solution.py:313

commit v4 on v3

--- a/solution.py
+++ b/solution.py
@@ -240,13 +240,11 @@
 
 
 def mix_modes(spectral, mode_real, mode_imag):
-    highest = lax.Precision.HIGHEST
-    mixed_real = jnp.einsum(
-        "hojl,hjl->ojl", spectral[0], mode_real, precision=highest
-    ) - jnp.einsum("hojl,hjl->ojl", spectral[1], mode_imag, precision=highest)
-    mixed_imag = jnp.einsum(
-        "hojl,hjl->ojl", spectral[0], mode_imag, precision=highest
-    ) + jnp.einsum("hojl,hjl->ojl", spectral[1], mode_real, precision=highest)
+    real_weight, imag_weight = spectral[0], spectral[1]
+    mode_real = mode_real[:, None]
+    mode_imag = mode_imag[:, None]
+    mixed_real = jnp.sum(real_weight * mode_real - imag_weight * mode_imag, axis=0)
+    mixed_imag = jnp.sum(real_weight * mode_imag + imag_weight * mode_real, axis=0)
     return (mixed_real, mixed_imag)
 
 
@@ -291,11 +289,22 @@
     return block.reshape((-1,) + block.shape[len(axes):])
 
 
+def packed_ppermute(parts, axis, perm):
+    flat = jnp.concatenate([part.reshape(-1) for part in parts])
+    flat = lax.ppermute(flat, axis, perm)
+    result = []
+    offset = 0
+    for part in parts:
+        result.append(flat[offset : offset + part.size].reshape(part.shape))
+        offset += part.size
+    return tuple(result)
+
+
 def pair_sum(values, axis):
     if lax.axis_size(axis) != 2:
         return lax.psum(values, axis)
-    other = lax.ppermute(values, axis, [(0, 1), (1, 0)])
-    return jax.tree.map(lambda mine, theirs: mine + theirs, values, other)
+    other = packed_ppermute(values, axis, [(0, 1), (1, 0)])
+    return tuple(mine + theirs for mine, theirs in zip(values, other))
 
 
 def group_grads(back_real, back_imag, mode_real, mode_imag, axis):
@@ -310,7 +319,7 @@
             for part in (back_real, back_imag, mode_real, mode_imag)
         )
         if shift:
-            piece = lax.ppermute(piece, axis, [(i, (i + shift) % count) for i in range(count)])
+            piece = packed_ppermute(piece, axis, [(i, (i + shift) % count) for i in range(count)])
         term = weight_grads(*piece)
         total = term if total is None else total + term
     return total

time: 133 us -> 114 us (0.86)
  starting transfers between devices: 59.9 us -> 18.7 us
  Pallas kernels: 12.4 us -> 40.3 us
  matrix products: 16.8 us -> 8.61 us
  other arithmetic: 15.3 us -> 19.9 us
  local copies, waits for them, and re-layouts: 15.4 us -> 13.4 us
    ppermute x7, starting transfers between devices: 38 us -> 8.84 us  [gather_along(): lax.ppermute(block, axis, [(i, (i + shift) % count) for i in range(count)])]
    pallas_call x1, Pallas kernels: 12.4 us -> 40.3 us  [solve_rows(): pl.pallas_call(solve_kernel, out_shape=jax.ShapeDtypeStruct((tracers, 1,...]
    ppermute x16 -> x5, starting transfers between devices: 15.6 us -> 3.49 us  [packed_ppermute(): flat = lax.ppermute(flat, axis, perm)]
    dot_general x4 -> x0, matrix products: 7.26 us -> none  [the longest x1 1.82 us: mix_modes(): jnp.einsum('hojl,hjl->ojl', spectral[1], mode_real, precision=highest)]
    squeeze x3 -> x0, local copies, waits for them, and re-layouts: 7.21 us -> none  [the longest x2 4.22 us: mix_modes(): spectral[1]]
    reshape x0 -> x36, local copies, waits for them, and re-layouts: none -> 4.03 us  [the longest x20 2.48 us: packed_ppermute(): result.append(flat[offset:offset + part.size].reshape(part.shape))]
    reduce_sum x0 -> x1, other arithmetic: none -> 3.04 us  [mix_modes(): jnp.sum(real_weight * mode_imag + imag_weight * mode_real, axis=0)]
    convert_element_type x0 -> x1, other arithmetic: none -> 2.52 us  [body(): spectral_weight.astype(jnp.float32)]
  transfers between devices with their start and end apart: 25 -> 14, of which waited for: 10 -> 9; matrix products, arithmetic and copies ran while one was open for 16% -> 13% of each run, Pallas kernels for 0% -> 0%
where the time goes in v4:
time: 114 us; the launch traced here: 113 us
  Pallas kernels  40.3 us (35%)
  other arithmetic  19.9 us (17%)
  starting transfers between devices  18.7 us (16%)
  local copies, waits for them, and re-layouts  13.4 us (12%)
  waiting for transfers between devices  9.86 us (9%)
  matrix products  8.61 us (8%)
  between operations  2.31 us (2%)
    pallas_call x1, Pallas kernels, solve_rows(): pl.pallas_call(solve_kernel, out_shape=jax.ShapeDtypeStruct((tracers, 1,...  40.3 us
    ppermute x7, starting transfers between devices, gather_along(): lax.ppermute(block, axis, [(i, (i + shift) % count) for i in range(count)])  8.84 us
    ppermute x7, waiting for transfers between devices, gather_along(): lax.ppermute(block, axis, [(i, (i + shift) % count) for i in range(count)])  5.19 us
    ppermute x5, waiting for transfers between devices, packed_ppermute(): flat = lax.ppermute(flat, axis, perm)  4.67 us
    ppermute x5, starting transfers between devices, packed_ppermute(): flat = lax.ppermute(flat, axis, perm)  3.49 us
    ppermute x1, starting transfers between devices, halo_rows(): below = lax.ppermute(block[:, :1], axis, backward)  3.35 us
    reduce_sum x1, other arithmetic, mix_modes(): jnp.sum(real_weight * mode_imag + imag_weight * mode_real, axis=0)  3.04 us
    ppermute x1, starting transfers between devices, halo_rows(): above = lax.ppermute(block[:, -1:], axis, forward)  3.02 us
  transfers between devices with their start and end apart: 14, of which 9 were waited for; matrix products, arithmetic and copies ran while one was open for 13% of the time, Pallas kernels for 0%

profile of v4, /device:TPU:0, one launch (start us, length us, event | category | flops | bytes accessed | tf_op | source)
XLA Modules:
  0.0 113.2 jit_solution(8945433749720957054)
XLA Ops:
  0.6 2.7 %fusion.141 = (bf16[4,1,16384]{2,1,0:T(2,128)(2,1)}, bf16[4,1,16384]{2,1,0:T(2,128)(2,1)}) fusion(bf16[4,16,16384]{2,1,0:T(8,128)(2,1)} %field_ref.1), kind=kLoop, calls=%fused_computation.220 | loop fusion | bytes 524288 | tf_op jit(solution)/shard_map/slice | solution.py:39
  3.4 3.0 %collective-permute-start = (bf16[4,1,16384]{2,1,0:T(2,128)(2,1)}, bf16[4,1,16384]{2,1,0:T(2,128)(2,1)}, u32[]{:S(2)}, u32[]{:S(2)}) collective-permute-start(bf16[4,1,16384]{2,1,0:T(2,128)(2,1)} %get-tuple-element.8), channel_id=1, source_target_pairs={{0,1},{1,2},{2,3},{3,4},{4,5},{5,6},{6,7},{7,8},{8,9},{9,10},{10,1... | collective-permute-start | bytes 393224 | tf_op jit(solution)/shard_map/ppermute | solution.py:38
  6.4 3.4 %collective-permute-start.1 = (bf16[4,1,16384]{2,1,0:T(2,128)(2,1)}, bf16[4,1,16384]{2,1,0:T(2,128)(2,1)S(1)}, u32[]{:S(2)}, u32[]{:S(2)}) collective-permute-start(bf16[4,1,16384]{2,1,0:T(2,128)(2,1)} %get-tuple-element.7), channel_id=1, source_target_pairs={{1,0},{2,1},{3,2},{4,3},{5,4},{6,5},{7,6},{8,7},{9,8},{10,9},{11,1... | collective-permute-start | bytes 393224 | tf_op jit(solution)/shard_map/ppermute | solution.py:39
  9.8 1.0 fusion.145
  10.8 0.8 slice_bitcast_fusion.3
  11.6 0.8 convert_element_type.68
  12.3 0.3 cosine_multiply_fusion
  12.6 0.8 broadcast_multiply_fusion
  13.4 0.2 multiply_multiply_fusion
  13.6 1.9 %pad_maximum_fusion.coef_ref = f32[3,16,16384]{2,1,0:T(8,128)} fusion(f32[1,16,16384]{2,1,0:T(8,128)S(1)} %get-tuple-element.59, f32[1,16,16384]{2,1,0:T(8,128)S(1)} %get-tuple-element.60, f32[1,16,16384]{2,1,0:T(8,128)S(1)} %broadcast_multiply_fusion), kind=kLoop, calls=%fused_computation | loop fusion | flops 1572864 | bytes 6291456 | tf_op jit(solution)/shard_map/stack | solution.py:156
  16.4 2.5 %convert_element_type.71 = f32[2,32,8,32,16]{3,4,2,1,0:T(8,128)} convert(bf16[2,32,8,32,16]{3,4,2,1,0:T(8,128)(2,1)S(1)} %copy-done.1) | non-fusion elementwise | flops 262144 | bytes 1572864 | tf_op jit(solution)/shard_map/convert_element_type | solution.py:377
  19.0 0.3 negate_convert_fusion
  19.3 1.9 %convert_element_type.66.above_ref = f32[4,1,16384]{2,1,0:T(1,128)} convert(bf16[4,1,16384]{2,1,0:T(2,128)(2,1)} %collective-permute-done) | non-fusion elementwise | flops 65536 | bytes 393216 | tf_op jit(solution)/shard_map/convert_element_type | solution.py:179
  21.2 1.0 convert_element_type.67.below_ref
  22.2 40.3 %shard_map.157 = f32[4,1,16384]{2,1,0:T(1,128)} custom-call(f32[1]{0:T(128)S(6)} %div.10.step_ref, s32[1]{0:T(128)S(6)} %copy.120.count_ref, bf16[4,16,16384]{2,1,0:T(8,128)(2,1)} %field_ref.1, f32[4,1,16384]{2,1,0:T(1,128)} %convert_element_type.66.above_ref, f32[4,1,16384]{2,1,0:T(1,128)} %convert_element_type.67.below_ref, ...), custom_call_target="tpu_custom_call" | custom-call | tf_op jit(solution)/shard_map/pallas_call | solution.py:165
  62.5 1.6 %reduce = f32[4,16384]{1,0:T(4,128)S(1)} reduce(f32[4,1,16384]{2,1,0:T(1,128)} %shard_map.157, f32[]{:T(128)} %constant.378), dimensions={1}, to_apply=%pallas_call.3.reduce_sub_computation | reduce | bytes 524292 | tf_op jit(solution)/shard_map/pallas_call | solution.py:165
  64.2 0.7 reshape.461
  64.9 0.6 reduce_sum.27
  65.6 3.7 %collective-permute-start.4 = (bf16[4,1024]{1,0:T(4,128)(2,1)S(1)}, bf16[4,1024]{1,0:T(4,128)(2,1)S(1)}, u32[]{:S(2)}, u32[]{:S(2)}) collective-permute-start(bf16[4,1024]{1,0:T(4,128)(2,1)S(1)} %multiply_convert_fusion), channel_id=1, source_target_pairs={{0,3},{1,0},{2,1},{3,2},{4,7},{5,4},{6,5},{7,6},{8,11},{9,8},{10,9... | collective-permute-start | bytes 24584 | tf_op jit(solution)/shard_map/ppermute | solution.py:281
  69.4 0.6 convert_dynamic-update-slice_fusion
  70.0 1.0 collective-permute-done.2
  71.0 0.5 collective-permute-done.4
  71.7 1.1 %collective-permute-done.5 = bf16[4,4,1024]{2,1,0:T(4,128)(2,1)S(1)} collective-permute-done((bf16[4,4,1024]{2,1,0:T(4,128)(2,1)S(1)}, bf16[4,4,1024]{2,1,0:T(4,128)(2,1)S(1)}, u32[]{:S(2)}, u32[]{:S(2)}) %collective-permute-start.5) | collective-permute-done | bytes 32800 | tf_op jit(solution)/shard_map/ppermute | solution.py:281
  72.9 1.1 collective-permute-start.6
  73.9 2.3 %collective-permute-start.7 = (bf16[2,4,4,1024]{3,2,1,0:T(4,128)(2,1)S(1)}, bf16[2,4,4,1024]{3,2,1,0:T(4,128)(2,1)S(1)}, u32[]{:S(2)}, u32[]{:S(2)}) collective-permute-start(bf16[2,4,4,1024]{3,2,1,0:T(4,128)(2,1)S(1)} %bitcast_dynamic-update-slice_fusion.4), channel_id=1, source_target_pairs={{0,16},{8,24},{16,0},{24,8},{1,17},{9,25},{17,1},{25,9},{2,18},{10... | collective-permute-start | bytes 196616 | tf_op jit(solution)/shard_map/ppermute | solution.py:281
  76.3 1.5 %collective-permute-start.8 = (bf16[2,4,4,1024]{3,2,1,0:T(4,128)(2,1)S(1)}, bf16[2,4,4,1024]{3,2,1,0:T(4,128)(2,1)S(1)}, u32[]{:S(2)}, u32[]{:S(2)}) collective-permute-start(bf16[2,4,4,1024]{3,2,1,0:T(4,128)(2,1)S(1)} %bitcast_dynamic-update-slice_fusion.4), channel_id=1, source_target_pairs={{0,24},{8,0},{16,8},{24,16},{1,25},{9,1},{17,9},{25,17},{2,26},{10... | collective-permute-start | bytes 196616 | tf_op jit(solution)/shard_map/ppermute | solution.py:281
  77.9 0.3 collective-permute-done.6
  78.2 1.3 %collective-permute-done.7 = bf16[2,4,4,1024]{3,2,1,0:T(4,128)(2,1)S(1)} collective-permute-done((bf16[2,4,4,1024]{3,2,1,0:T(4,128)(2,1)S(1)}, bf16[2,4,4,1024]{3,2,1,0:T(4,128)(2,1)S(1)}, u32[]{:S(2)}, u32[]{:S(2)}) %collective-permute-start.7) | collective-permute-done | bytes 65568 | tf_op jit(solution)/shard_map/ppermute | solution.py:281
  79.5 1.0 collective-permute-done.8
  80.6 0.5 fusion
  81.1 0.9 fusion.56
  82.1 0.5 fusion.41
  82.6 0.5 fusion.37
  83.1 0.5 fusion.6
  83.7 0.5 copy.67
  84.2 0.2 reshape.463
  84.4 0.5 fusion.4
  84.9 0.5 copy.70
  85.4 0.2 reshape.464
  85.7 0.3 sine_multiply_fusion
  86.0 1.1 collective-permute-done.9
  87.1 0.2 reshape.465
  87.3 0.4 copy.71
  88.1 0.4 copy.73
  88.8 3.0 %add_reduce_fusion = (f32[8,32,16]{1,2,0:T(8,128)S(1)}, f32[8,32,16]{1,2,0:T(8,128)S(1)}) fusion(f32[2,32,8,32,16]{3,4,2,1,0:T(8,128)} %convert_element_type.71, f32[32,32,16]{1,2,0:T(8,128)S(1)} %copy.74, f32[32,32,16]{1,2,0:T(8,128)S(1)} %copy.72), kind=kLoop, calls=%fused_computation.3 | loop fusion | flops 1040384 | bytes 1212416 | tf_op jit(solution)/shard_map/reduce_sum | solution.py:247
  91.8 0.6 fusion.72
  92.5 0.7 fusion.62
  93.1 0.7 convolution_subtract_fusion.2
  93.8 0.7 convolution_add_fusion.2
  94.6 0.6 convolution_multiply_fusion
  95.2 0.3 fusion.2
  95.4 1.8 %fusion.30 = bf16[1,16,8,1024]{3,2,1,0:T(8,128)(2,1)} fusion(f32[16,8,1024]{2,1,0:T(8,128)S(1)} %fusion.2), kind=kLoop, calls=%fused_computation.66 | loop fusion | flops 8519680 | bytes 786432 | tf_op jit(solution)/shard_map/broadcast_in_dim | solution.py:392
  97.3 0.3 fusion.31
  97.8 0.3 fusion.69
  98.2 0.3 fusion.67
  98.5 0.3 fusion.10
  99.1 0.3 fusion.8
  99.6 0.2 collective-permute-start.10
  102.5 2.5 %collective-permute-start.13 = (f32[6144]{0:T(1024)S(1)}, f32[6144]{0:T(1024)S(1)}, u32[]{:S(2)}, u32[]{:S(2)}) collective-permute-start(f32[6144]{0:T(1024)S(1)} %pad_maximum_fusion.6), channel_id=1, source_target_pairs={{0,24},{8,0},{16,8},{24,16},{1,25},{9,1},{17,9},{25,17},{2,26},{10... | collective-permute-start | bytes 73736 | tf_op jit(solution)/shard_map/ppermute | solution.py:294
  105.4 0.5 collective-permute-start.12
  106.2 0.2 collective-permute-start.11
  106.7 2.5 %collective-permute-done.12 = f32[6144]{0:T(1024)S(1)} collective-permute-done((f32[6144]{0:T(1024)S(1)}, f32[6144]{0:T(1024)S(1)}, u32[]{:S(2)}, u32[]{:S(2)}) %collective-permute-start.12) | collective-permute-done | bytes 24608 | tf_op jit(solution)/shard_map/ppermute | solution.py:294
  109.9 1.1 collective-permute-done.11
  111.7 1.4 %fusion.13 = f32[2,16,8,8,16]{4,3,2,1,0:T(8,128)} fusion(f32[1,16,8,8,16]{4,3,2,1,0:T(8,128)S(1)} %get-tuple-element.26, f32[1,16,8,8,16]{4,3,2,1,0:T(8,128)S(1)} %get-tuple-element.25, f32[1,16,8,8,16]{4,3,2,1,0:T(8,128)S(1)} %get-tuple-element.24, f32[1,16,8,8,16]{4,3,2,1,0:T(8,128)S(1)} %get-tuple-element.23, ...), kind=kLoop, calls=%fused_computation.28 | loop fusion | flops 262144 | bytes 655360 | tf_op jit(solution)/shard_map/div | solution.py:406
  (123 shorter events, 7.0 us)
Async XLA Ops:
  0.6 94.5 %copy-start = (bf16[32,8]{0,1:T(8,128)(2,1)S(1)}, bf16[32,8]{0,1:T(8,128)(2,1)}, u32[]{:S(2)}) copy-start(bf16[32,8]{0,1:T(8,128)(2,1)} %param.24) | copy-start | bytes 1540
  3.4 15.9 %collective-permute-start = (bf16[4,1,16384]{2,1,0:T(2,128)(2,1)}, bf16[4,1,16384]{2,1,0:T(2,128)(2,1)}, u32[]{:S(2)}, u32[]{:S(2)}) collective-permute-start(bf16[4,1,16384]{2,1,0:T(2,128)(2,1)} %get-tuple-element.8), channel_id=1, source_target_pairs={{0,1},{1,2},{2,3},{3,4},{4,5},{5,6},{6,7},{7,8},{8,9},{9,10},{10,1... | collective-permute-start | bytes 393224 | tf_op jit(solution)/shard_map/ppermute | solution.py:38
  6.4 14.8 %collective-permute-start.1 = (bf16[4,1,16384]{2,1,0:T(2,128)(2,1)}, bf16[4,1,16384]{2,1,0:T(2,128)(2,1)S(1)}, u32[]{:S(2)}, u32[]{:S(2)}) collective-permute-start(bf16[4,1,16384]{2,1,0:T(2,128)(2,1)} %get-tuple-element.7), channel_id=1, source_target_pairs={{1,0},{2,1},{3,2},{4,3},{5,4},{6,5},{7,6},{8,7},{9,8},{10,9},{11,1... | collective-permute-start | bytes 393224 | tf_op jit(solution)/shard_map/ppermute | solution.py:39
  13.6 1.9 %copy-start.5 = (s32[32]{0:T(128)S(1)}, s32[32]{0:T(128)}, u32[]{:S(2)}) copy-start(s32[32]{0:T(128)} %param.20) | copy-start | bytes 388
  13.6 2.8 %copy-start.1 = (bf16[2,32,8,32,16]{3,4,2,1,0:T(8,128)(2,1)S(1)}, bf16[2,32,8,32,16]{3,4,2,1,0:T(8,128)(2,1)}, u32[]{:S(2)}) copy-start(bf16[2,32,8,32,16]{3,4,2,1,0:T(8,128)(2,1)} %param.26) | copy-start | bytes 1572868
  64.8 15.7 %copy-start.2 = (bf16[1,16,4,1024]{3,2,1,0:T(4,128)(2,1)S(1)}, bf16[1,16,4,1024]{3,2,1,0:T(4,128)(2,1)}, u32[]{:S(2)}) copy-start(bf16[1,16,4,1024]{3,2,1,0:T(4,128)(2,1)} %param.21) | copy-start | bytes 393220
  64.8 15.7 %copy-start.3 = (bf16[4,32]{1,0:T(4,128)(2,1)S(1)}, bf16[4,32]{1,0:T(4,128)(2,1)}, u32[]{:S(2)}) copy-start(bf16[4,32]{1,0:T(4,128)(2,1)} %param.22) | copy-start | bytes 772
  64.9 15.7 %copy-start.4 = (f32[32]{0:T(128)S(1)}, f32[32]{0:T(128)}, u32[]{:S(2)}) copy-start(f32[32]{0:T(128)} %param.23) | copy-start | bytes 388
  65.5 5.5 %collective-permute-start.2 = (bf16[4,1024]{1,0:T(4,128)(2,1)S(1)}, bf16[4,1024]{1,0:T(4,128)(2,1)S(1)}, u32[]{:S(2)}, u32[]{:S(2)}) collective-permute-start(bf16[4,1024]{1,0:T(4,128)(2,1)S(1)} %multiply_convert_fusion), channel_id=1, source_target_pairs={{0,1},{1,2},{2,3},{3,0},{4,5},{5,6},{6,7},{7,4},{8,9},{9,10},{10,1... | collective-permute-start | bytes 24584 | tf_op jit(solution)/shard_map/ppermute | solution.py:281
  65.6 5.5 %collective-permute-start.3 = (bf16[4,1024]{1,0:T(4,128)(2,1)S(1)}, bf16[4,1024]{1,0:T(4,128)(2,1)S(1)}, u32[]{:S(2)}, u32[]{:S(2)}) collective-permute-start(bf16[4,1024]{1,0:T(4,128)(2,1)S(1)} %multiply_convert_fusion), channel_id=1, source_target_pairs={{0,2},{1,3},{2,0},{3,1},{4,6},{5,7},{6,4},{7,5},{8,10},{9,11},{10,... | collective-permute-start | bytes 24584 | tf_op jit(solution)/shard_map/ppermute | solution.py:281
  65.6 5.9 %collective-permute-start.4 = (bf16[4,1024]{1,0:T(4,128)(2,1)S(1)}, bf16[4,1024]{1,0:T(4,128)(2,1)S(1)}, u32[]{:S(2)}, u32[]{:S(2)}) collective-permute-start(bf16[4,1024]{1,0:T(4,128)(2,1)S(1)} %multiply_convert_fusion), channel_id=1, source_target_pairs={{0,3},{1,0},{2,1},{3,2},{4,7},{5,4},{6,5},{7,6},{8,11},{9,8},{10,9... | collective-permute-start | bytes 24584 | tf_op jit(solution)/shard_map/ppermute | solution.py:281
  71.6 1.3 %collective-permute-start.5 = (bf16[4,4,1024]{2,1,0:T(4,128)(2,1)S(1)}, bf16[4,4,1024]{2,1,0:T(4,128)(2,1)S(1)}, u32[]{:S(2)}, u32[]{:S(2)}) collective-permute-start(bf16[4,4,1024]{2,1,0:T(4,128)(2,1)S(1)} %bitcast_dynamic-update-slice_fusion.6), channel_id=1, source_target_pairs={{0,4},{4,0},{1,5},{5,1},{2,6},{6,2},{3,7},{7,3},{8,12},{12,8},{9,1... | collective-permute-start | bytes 98312 | tf_op jit(solution)/shard_map/ppermute | solution.py:281
  72.9 5.3 %collective-permute-start.6 = (bf16[2,4,4,1024]{3,2,1,0:T(4,128)(2,1)S(1)}, bf16[2,4,4,1024]{3,2,1,0:T(4,128)(2,1)S(1)}, u32[]{:S(2)}, u32[]{:S(2)}) collective-permute-start(bf16[2,4,4,1024]{3,2,1,0:T(4,128)(2,1)S(1)} %bitcast_dynamic-update-slice_fusion.4), channel_id=1, source_target_pairs={{0,8},{8,16},{16,24},{24,0},{1,9},{9,17},{17,25},{25,1},{2,10},{10... | collective-permute-start | bytes 196616 | tf_op jit(solution)/shard_map/ppermute | solution.py:281
  73.9 5.6 %collective-permute-start.7 = (bf16[2,4,4,1024]{3,2,1,0:T(4,128)(2,1)S(1)}, bf16[2,4,4,1024]{3,2,1,0:T(4,128)(2,1)S(1)}, u32[]{:S(2)}, u32[]{:S(2)}) collective-permute-start(bf16[2,4,4,1024]{3,2,1,0:T(4,128)(2,1)S(1)} %bitcast_dynamic-update-slice_fusion.4), channel_id=1, source_target_pairs={{0,16},{8,24},{16,0},{24,8},{1,17},{9,25},{17,1},{25,9},{2,18},{10... | collective-permute-start | bytes 196616 | tf_op jit(solution)/shard_map/ppermute | solution.py:281
  76.3 4.3 %collective-permute-start.8 = (bf16[2,4,4,1024]{3,2,1,0:T(4,128)(2,1)S(1)}, bf16[2,4,4,1024]{3,2,1,0:T(4,128)(2,1)S(1)}, u32[]{:S(2)}, u32[]{:S(2)}) collective-permute-start(bf16[2,4,4,1024]{3,2,1,0:T(4,128)(2,1)S(1)} %bitcast_dynamic-update-slice_fusion.4), channel_id=1, source_target_pairs={{0,24},{8,0},{16,8},{24,16},{1,25},{9,1},{17,9},{25,17},{2,26},{10... | collective-permute-start | bytes 196616 | tf_op jit(solution)/shard_map/ppermute | solution.py:281
  85.7 1.4 %collective-permute-start.9 = (f32[32768]{0:T(1024)S(1)}, f32[32768]{0:T(1024)S(1)}, u32[]{:S(2)}, u32[]{:S(2)}) collective-permute-start(f32[32768]{0:T(1024)S(1)} %pad_maximum_fusion.1), channel_id=1, source_target_pairs={{0,4},{4,0},{1,5},{5,1},{2,6},{6,2},{3,7},{7,3},{8,12},{12,8},{9,1... | collective-permute-start | bytes 393224 | tf_op jit(solution)/shard_map/ppermute | solution.py:294
  88.8 6.4 %copy-start.6 = (f32[8]{0:T(128)S(1)}, f32[8]{0:T(128)}, u32[]{:S(2)}) copy-start(f32[8]{0:T(128)} %param.25) | copy-start | bytes 100
  93.1 4.1 %copy-start.7 = (bf16[1,16,8,1024]{3,2,1,0:T(8,128)(2,1)S(1)}, bf16[1,16,8,1024]{3,2,1,0:T(8,128)(2,1)}, u32[]{:S(2)}) copy-start(bf16[1,16,8,1024]{3,2,1,0:T(8,128)(2,1)} %param.27) | copy-start | bytes 786436
  99.6 1.9 %collective-permute-start.10 = (f32[8192]{0:T(1024)S(1)}, f32[8192]{0:T(1024)S(1)}, u32[]{:S(2)}, u32[]{:S(2)}) collective-permute-start(f32[8192]{0:T(1024)S(1)} %pad_maximum_fusion.3), channel_id=1, source_target_pairs={{0,4},{4,0},{1,5},{5,1},{2,6},{6,2},{3,7},{7,3},{8,12},{12,8},{9,1... | collective-permute-start | bytes 98312 | tf_op jit(solution)/shard_map/ppermute | solution.py:294
  102.5 4.2 %collective-permute-start.13 = (f32[6144]{0:T(1024)S(1)}, f32[6144]{0:T(1024)S(1)}, u32[]{:S(2)}, u32[]{:S(2)}) collective-permute-start(f32[6144]{0:T(1024)S(1)} %pad_maximum_fusion.6), channel_id=1, source_target_pairs={{0,24},{8,0},{16,8},{24,16},{1,25},{9,1},{17,9},{25,17},{2,26},{10... | collective-permute-start | bytes 73736 | tf_op jit(solution)/shard_map/ppermute | solution.py:294
  105.4 3.9 %collective-permute-start.12 = (f32[6144]{0:T(1024)S(1)}, f32[6144]{0:T(1024)S(1)}, u32[]{:S(2)}, u32[]{:S(2)}) collective-permute-start(f32[6144]{0:T(1024)S(1)} %pad_maximum_fusion.5), channel_id=1, source_target_pairs={{0,16},{8,24},{16,0},{24,8},{1,17},{9,25},{17,1},{25,9},{2,18},{10... | collective-permute-start | bytes 73736 | tf_op jit(solution)/shard_map/ppermute | solution.py:294
  106.2 4.8 %collective-permute-start.11 = (f32[6144]{0:T(1024)S(1)}, f32[6144]{0:T(1024)S(1)}, u32[]{:S(2)}, u32[]{:S(2)}) collective-permute-start(f32[6144]{0:T(1024)S(1)} %pad_maximum_fusion.4), channel_id=1, source_target_pairs={{0,8},{8,16},{16,24},{24,0},{1,9},{9,17},{17,25},{25,1},{2,10},{10... | collective-permute-start | bytes 73736 | tf_op jit(solution)/shard_map/ppermute | solution.py:294

commit v5 on v4

--- a/solution.py
+++ b/solution.py
@@ -65,8 +65,8 @@
     return lax.fori_loop(jnp.zeros((), jnp.int32), substeps, advance, slab_rows)
 
 
-CHUNK = 512
-UNROLL = 4
+CHUNK = 256
+UNROLL = 2
 
 
 def solve_kernel(
@@ -89,37 +89,39 @@
     row_ids = lax.broadcasted_iota(jnp.int32, (rows, CHUNK), 0)
 
     def sweep(source_ref, target_ref):
-        def update(index, inner):
-            tracer = index // chunks
-            column = index % chunks
+        def update(column, inner):
             cols = chunk_at(column)
             before = pl.ds(pl.multiple_of(((column * CHUNK - 128) % width), 128), 128)
             after = pl.ds(pl.multiple_of((((column + 1) * CHUNK) % width), 128), 128)
-            current = source_ref[tracer, :, cols]
-            extended = jnp.concatenate(
-                [source_ref[tracer, :, before], current, source_ref[tracer, :, after]], axis=1
-            )
-            span = CHUNK + 256
-            right_cells = pltpu.roll(extended, span - 1, 1)[:, 128 : 128 + CHUNK]
-            left_cells = pltpu.roll(extended, 1, 1)[:, 128 : 128 + CHUNK]
-            upper_rows = jnp.where(
-                row_ids == 0, above_ref[tracer, :, cols], pltpu.roll(current, 1, 0)
-            )
-            lower_rows = jnp.where(
-                row_ids == rows - 1, below_ref[tracer, :, cols], pltpu.roll(current, rows - 1, 0)
-            )
-            change = coef_ref[0, :, cols] * (
-                right_cells + left_cells + upper_rows + lower_rows - 4.0 * current
-            )
-            change = (
-                change
-                - coef_ref[1, :, cols] * (right_cells - left_cells)
-                - coef_ref[2, :, cols] * (lower_rows - upper_rows)
-            )
-            target_ref[tracer, :, cols] = current + step * change
+            diffusion = coef_ref[0, :, cols]
+            along = coef_ref[1, :, cols]
+            across = coef_ref[2, :, cols]
+            for tracer in range(tracers):
+                current = source_ref[tracer, :, cols]
+                extended = jnp.concatenate(
+                    [source_ref[tracer, :, before], current, source_ref[tracer, :, after]], axis=1
+                )
+                span = CHUNK + 256
+                right_cells = pltpu.roll(extended, span - 1, 1)[:, 128 : 128 + CHUNK]
+                left_cells = pltpu.roll(extended, 1, 1)[:, 128 : 128 + CHUNK]
+                upper_rows = jnp.where(
+                    row_ids == 0, above_ref[tracer, :, cols], pltpu.roll(current, 1, 0)
+                )
+                lower_rows = jnp.where(
+                    row_ids == rows - 1, below_ref[tracer, :, cols], pltpu.roll(current, rows - 1, 0)
+                )
+                change = diffusion * (
+                    right_cells + left_cells + upper_rows + lower_rows - 4.0 * current
+                )
+                change = (
+                    change
+                    - along * (right_cells - left_cells)
+                    - across * (lower_rows - upper_rows)
+                )
+                target_ref[tracer, :, cols] = current + step * change
             return inner
 
-        lax.fori_loop(0, tracers * chunks, update, 0, unroll=UNROLL)
+        lax.fori_loop(0, chunks, update, 0, unroll=UNROLL)
 
     def two_steps(number, carry):
         sweep(first_ref, second_ref)

time: 114 us -> 116 us (1.018); the launches traced: 113 us -> 117 us
  starting transfers between devices: 18.7 us -> 45.4 us
  Pallas kernels: 40.3 us -> 14 us
  waiting for transfers between devices: 9.86 us -> 13 us
    ppermute x7, starting transfers between devices: 8.84 us -> 35.7 us  [gather_along(): lax.ppermute(block, axis, [(i, (i + shift) % count) for i in range(count)])]
    pallas_call x1, Pallas kernels: 40.3 us -> 14 us  [solve_rows(): pl.pallas_call(solve_kernel, out_shape=jax.ShapeDtypeStruct((tracers, 1,...]
    ppermute x7, waiting for transfers between devices: 5.19 us -> 8.18 us  [gather_along(): lax.ppermute(block, axis, [(i, (i + shift) % count) for i in range(count)])]
  transfers between devices with their start and end apart: 14 -> 14, of which waited for: 9 -> 10; matrix products, arithmetic and copies ran while one was open for 13% -> 13% of each run, Pallas kernels for 0% -> 0%
where the time goes in v5:
time: 116 us; the launch traced here: 117 us
  starting transfers between devices  45.4 us (39%)
  other arithmetic  19.9 us (17%)
  Pallas kernels  14 us (12%)
  local copies, waits for them, and re-layouts  13.4 us (12%)
  waiting for transfers between devices  13 us (11%)
  matrix products  8.62 us (7%)
  between operations  2.29 us (2%)
    ppermute x7, starting transfers between devices, gather_along(): lax.ppermute(block, axis, [(i, (i + shift) % count) for i in range(count)])  35.7 us
    pallas_call x1, Pallas kernels, solve_rows(): pl.pallas_call(solve_kernel, out_shape=jax.ShapeDtypeStruct((tracers, 1,...  14 us
    ppermute x7, waiting for transfers between devices, gather_along(): lax.ppermute(block, axis, [(i, (i + shift) % count) for i in range(count)])  8.18 us
    ppermute x5, waiting for transfers between devices, packed_ppermute(): flat = lax.ppermute(flat, axis, perm)  4.8 us
    ppermute x1, starting transfers between devices, halo_rows(): below = lax.ppermute(block[:, :1], axis, backward)  3.35 us
    ppermute x5, starting transfers between devices, packed_ppermute(): flat = lax.ppermute(flat, axis, perm)  3.31 us
    reduce_sum x1, other arithmetic, mix_modes(): jnp.sum(real_weight * mode_imag + imag_weight * mode_real, axis=0)  3.04 us
    ppermute x1, starting transfers between devices, halo_rows(): above = lax.ppermute(block[:, -1:], axis, forward)  3.02 us
  transfers between devices with their start and end apart: 14, of which 10 were waited for; matrix products, arithmetic and copies ran while one was open for 13% of the time, Pallas kernels for 0%

profile of v5, /device:TPU:0, one launch (start us, length us, event | category | flops | bytes accessed | tf_op | source)
XLA Modules:
  0.0 116.7 jit_solution(13982489350097055926)
XLA Ops:
  0.6 2.7 %fusion.141 = (bf16[4,1,16384]{2,1,0:T(2,128)(2,1)}, bf16[4,1,16384]{2,1,0:T(2,128)(2,1)}) fusion(bf16[4,16,16384]{2,1,0:T(8,128)(2,1)} %field_ref.1), kind=kLoop, calls=%fused_computation.220 | loop fusion | bytes 524288 | tf_op jit(solution)/shard_map/slice | solution.py:39
  3.4 3.0 %collective-permute-start = (bf16[4,1,16384]{2,1,0:T(2,128)(2,1)}, bf16[4,1,16384]{2,1,0:T(2,128)(2,1)}, u32[]{:S(2)}, u32[]{:S(2)}) collective-permute-start(bf16[4,1,16384]{2,1,0:T(2,128)(2,1)} %get-tuple-element.8), channel_id=1, source_target_pairs={{0,1},{1,2},{2,3},{3,4},{4,5},{5,6},{6,7},{7,8},{8,9},{9,10},{10,1... | collective-permute-start | bytes 393224 | tf_op jit(solution)/shard_map/ppermute | solution.py:38
  6.4 3.4 %collective-permute-start.1 = (bf16[4,1,16384]{2,1,0:T(2,128)(2,1)}, bf16[4,1,16384]{2,1,0:T(2,128)(2,1)S(1)}, u32[]{:S(2)}, u32[]{:S(2)}) collective-permute-start(bf16[4,1,16384]{2,1,0:T(2,128)(2,1)} %get-tuple-element.7), channel_id=1, source_target_pairs={{1,0},{2,1},{3,2},{4,3},{5,4},{6,5},{7,6},{8,7},{9,8},{10,9},{11,1... | collective-permute-start | bytes 393224 | tf_op jit(solution)/shard_map/ppermute | solution.py:39
  9.8 1.0 fusion.145
  10.8 0.8 slice_bitcast_fusion.3
  11.6 0.8 convert_element_type.68
  12.3 0.3 cosine_multiply_fusion
  12.6 0.8 broadcast_multiply_fusion
  13.4 0.2 multiply_multiply_fusion
  13.6 1.9 %pad_maximum_fusion.coef_ref = f32[3,16,16384]{2,1,0:T(8,128)} fusion(f32[1,16,16384]{2,1,0:T(8,128)S(1)} %get-tuple-element.59, f32[1,16,16384]{2,1,0:T(8,128)S(1)} %get-tuple-element.60, f32[1,16,16384]{2,1,0:T(8,128)S(1)} %broadcast_multiply_fusion), kind=kLoop, calls=%fused_computation | loop fusion | flops 1572864 | bytes 6291456 | tf_op jit(solution)/shard_map/stack | solution.py:158
  16.4 2.5 %convert_element_type.71 = f32[2,32,8,32,16]{3,4,2,1,0:T(8,128)} convert(bf16[2,32,8,32,16]{3,4,2,1,0:T(8,128)(2,1)S(1)} %copy-done.1) | non-fusion elementwise | flops 262144 | bytes 1572864 | tf_op jit(solution)/shard_map/convert_element_type | solution.py:379
  19.0 0.3 negate_convert_fusion
  19.3 1.9 %convert_element_type.66.above_ref = f32[4,1,16384]{2,1,0:T(1,128)} convert(bf16[4,1,16384]{2,1,0:T(2,128)(2,1)} %collective-permute-done) | non-fusion elementwise | flops 65536 | bytes 393216 | tf_op jit(solution)/shard_map/convert_element_type | solution.py:181
  21.2 1.0 convert_element_type.67.below_ref
  22.2 14.0 %shard_map.157 = f32[4,1,16384]{2,1,0:T(1,128)} custom-call(f32[1]{0:T(128)S(6)} %div.10.step_ref, s32[1]{0:T(128)S(6)} %copy.120.count_ref, bf16[4,16,16384]{2,1,0:T(8,128)(2,1)} %field_ref.1, f32[4,1,16384]{2,1,0:T(1,128)} %convert_element_type.66.above_ref, f32[4,1,16384]{2,1,0:T(1,128)} %convert_element_type.67.below_ref, ...), custom_call_target="tpu_custom_call" | custom-call | tf_op jit(solution)/shard_map/pallas_call | solution.py:167
  36.2 1.6 %reduce = f32[4,16384]{1,0:T(4,128)S(1)} reduce(f32[4,1,16384]{2,1,0:T(1,128)} %shard_map.157, f32[]{:T(128)} %constant.378), dimensions={1}, to_apply=%pallas_call.3.reduce_sub_computation | reduce | bytes 524292 | tf_op jit(solution)/shard_map/pallas_call | solution.py:167
  37.8 0.7 reshape.461
  38.5 0.6 reduce_sum.27
  39.2 29.3 %collective-permute-start.2 = (bf16[4,1024]{1,0:T(4,128)(2,1)S(1)}, bf16[4,1024]{1,0:T(4,128)(2,1)S(1)}, u32[]{:S(2)}, u32[]{:S(2)}) collective-permute-start(bf16[4,1024]{1,0:T(4,128)(2,1)S(1)} %multiply_convert_fusion), channel_id=1, source_target_pairs={{0,1},{1,2},{2,3},{3,0},{4,5},{5,6},{6,7},{7,4},{8,9},{9,10},{10,1... | collective-permute-start | bytes 24584 | tf_op jit(solution)/shard_map/ppermute | solution.py:283
  68.4 3.3 %collective-permute-start.3 = (bf16[4,1024]{1,0:T(4,128)(2,1)S(1)}, bf16[4,1024]{1,0:T(4,128)(2,1)S(1)}, u32[]{:S(2)}, u32[]{:S(2)}) collective-permute-start(bf16[4,1024]{1,0:T(4,128)(2,1)S(1)} %multiply_convert_fusion), channel_id=1, source_target_pairs={{0,2},{1,3},{2,0},{3,1},{4,6},{5,7},{6,4},{7,5},{8,10},{9,11},{10,... | collective-permute-start | bytes 24584 | tf_op jit(solution)/shard_map/ppermute | solution.py:283
  71.8 0.6 convert_dynamic-update-slice_fusion
  72.4 0.4 collective-permute-done.2
  72.8 0.5 collective-permute-done.3
  73.4 2.0 %collective-permute-done.4 = bf16[4,1024]{1,0:T(4,128)(2,1)S(1)} collective-permute-done((bf16[4,1024]{1,0:T(4,128)(2,1)S(1)}, bf16[4,1024]{1,0:T(4,128)(2,1)S(1)}, u32[]{:S(2)}, u32[]{:S(2)}) %collective-permute-start.4) | collective-permute-done | bytes 8224 | tf_op jit(solution)/shard_map/ppermute | solution.py:283
  75.6 1.1 collective-permute-done.5
  76.7 1.5 %collective-permute-start.6 = (bf16[2,4,4,1024]{3,2,1,0:T(4,128)(2,1)S(1)}, bf16[2,4,4,1024]{3,2,1,0:T(4,128)(2,1)S(1)}, u32[]{:S(2)}, u32[]{:S(2)}) collective-permute-start(bf16[2,4,4,1024]{3,2,1,0:T(4,128)(2,1)S(1)} %bitcast_dynamic-update-slice_fusion.4), channel_id=1, source_target_pairs={{0,8},{8,16},{16,24},{24,0},{1,9},{9,17},{17,25},{25,1},{2,10},{10... | collective-permute-start | bytes 196616 | tf_op jit(solution)/shard_map/ppermute | solution.py:283
  78.3 1.5 %collective-permute-start.7 = (bf16[2,4,4,1024]{3,2,1,0:T(4,128)(2,1)S(1)}, bf16[2,4,4,1024]{3,2,1,0:T(4,128)(2,1)S(1)}, u32[]{:S(2)}, u32[]{:S(2)}) collective-permute-start(bf16[2,4,4,1024]{3,2,1,0:T(4,128)(2,1)S(1)} %bitcast_dynamic-update-slice_fusion.4), channel_id=1, source_target_pairs={{0,16},{8,24},{16,0},{24,8},{1,17},{9,25},{17,1},{25,9},{2,18},{10... | collective-permute-start | bytes 196616 | tf_op jit(solution)/shard_map/ppermute | solution.py:283
  79.9 2.1 %collective-permute-done.6 = bf16[2,4,4,1024]{3,2,1,0:T(4,128)(2,1)S(1)} collective-permute-done((bf16[2,4,4,1024]{3,2,1,0:T(4,128)(2,1)S(1)}, bf16[2,4,4,1024]{3,2,1,0:T(4,128)(2,1)S(1)}, u32[]{:S(2)}, u32[]{:S(2)}) %collective-permute-start.6) | collective-permute-done | bytes 65568 | tf_op jit(solution)/shard_map/ppermute | solution.py:283
  82.0 1.2 %collective-permute-done.7 = bf16[2,4,4,1024]{3,2,1,0:T(4,128)(2,1)S(1)} collective-permute-done((bf16[2,4,4,1024]{3,2,1,0:T(4,128)(2,1)S(1)}, bf16[2,4,4,1024]{3,2,1,0:T(4,128)(2,1)S(1)}, u32[]{:S(2)}, u32[]{:S(2)}) %collective-permute-start.7) | collective-permute-done | bytes 65568 | tf_op jit(solution)/shard_map/ppermute | solution.py:283
  83.3 0.8 collective-permute-done.8
  84.1 0.5 fusion
  84.6 0.9 fusion.56
  85.6 0.5 fusion.41
  86.1 0.5 fusion.37
  86.7 0.5 fusion.6
  87.2 0.5 copy.67
  87.7 0.2 reshape.463
  87.9 0.5 fusion.4
  88.5 0.5 copy.70
  89.0 0.2 reshape.464
  89.3 0.3 sine_multiply_fusion
  89.5 1.1 collective-permute-done.9
  90.6 0.2 reshape.465
  90.8 0.4 copy.71
  91.7 0.4 copy.73
  92.3 3.0 %add_reduce_fusion = (f32[8,32,16]{1,2,0:T(8,128)S(1)}, f32[8,32,16]{1,2,0:T(8,128)S(1)}) fusion(f32[2,32,8,32,16]{3,4,2,1,0:T(8,128)} %convert_element_type.71, f32[32,32,16]{1,2,0:T(8,128)S(1)} %copy.74, f32[32,32,16]{1,2,0:T(8,128)S(1)} %copy.72), kind=kLoop, calls=%fused_computation.3 | loop fusion | flops 1040384 | bytes 1212416 | tf_op jit(solution)/shard_map/reduce_sum | solution.py:249
  95.4 0.6 fusion.72
  96.0 0.7 fusion.62
  96.7 0.7 convolution_subtract_fusion.2
  97.3 0.7 convolution_add_fusion.2
  98.1 0.6 convolution_multiply_fusion
  98.7 0.3 fusion.2
  99.0 1.8 %fusion.30 = bf16[1,16,8,1024]{3,2,1,0:T(8,128)(2,1)} fusion(f32[16,8,1024]{2,1,0:T(8,128)S(1)} %fusion.2), kind=kLoop, calls=%fused_computation.66 | loop fusion | flops 8519680 | bytes 786432 | tf_op jit(solution)/shard_map/broadcast_in_dim | solution.py:394
  100.8 0.3 fusion.31
  101.3 0.3 fusion.69
  101.7 0.3 fusion.67
  102.1 0.3 fusion.10
  102.6 0.3 fusion.8
  103.1 0.2 collective-permute-start.10
  106.1 1.4 %collective-permute-start.13 = (f32[6144]{0:T(1024)S(1)}, f32[6144]{0:T(1024)S(1)}, u32[]{:S(2)}, u32[]{:S(2)}) collective-permute-start(f32[6144]{0:T(1024)S(1)} %pad_maximum_fusion.6), channel_id=1, source_target_pairs={{0,24},{8,0},{16,8},{24,16},{1,25},{9,1},{17,9},{25,17},{2,26},{10... | collective-permute-start | bytes 73736 | tf_op jit(solution)/shard_map/ppermute | solution.py:296
  107.8 1.6 %collective-permute-start.12 = (f32[6144]{0:T(1024)S(1)}, f32[6144]{0:T(1024)S(1)}, u32[]{:S(2)}, u32[]{:S(2)}) collective-permute-start(f32[6144]{0:T(1024)S(1)} %pad_maximum_fusion.5), channel_id=1, source_target_pairs={{0,16},{8,24},{16,0},{24,8},{1,17},{9,25},{17,1},{25,9},{2,18},{10... | collective-permute-start | bytes 73736 | tf_op jit(solution)/shard_map/ppermute | solution.py:296
  110.1 1.6 %collective-permute-done.12 = f32[6144]{0:T(1024)S(1)} collective-permute-done((f32[6144]{0:T(1024)S(1)}, f32[6144]{0:T(1024)S(1)}, u32[]{:S(2)}, u32[]{:S(2)}) %collective-permute-start.12) | collective-permute-done | bytes 24608 | tf_op jit(solution)/shard_map/ppermute | solution.py:296
  112.3 2.2 %collective-permute-done.11 = f32[6144]{0:T(1024)S(1)} collective-permute-done((f32[6144]{0:T(1024)S(1)}, f32[6144]{0:T(1024)S(1)}, u32[]{:S(2)}, u32[]{:S(2)}) %collective-permute-start.11) | collective-permute-done | bytes 24608 | tf_op jit(solution)/shard_map/ppermute | solution.py:296
  115.2 1.4 %fusion.13 = f32[2,16,8,8,16]{4,3,2,1,0:T(8,128)} fusion(f32[1,16,8,8,16]{4,3,2,1,0:T(8,128)S(1)} %get-tuple-element.26, f32[1,16,8,8,16]{4,3,2,1,0:T(8,128)S(1)} %get-tuple-element.25, f32[1,16,8,8,16]{4,3,2,1,0:T(8,128)S(1)} %get-tuple-element.24, f32[1,16,8,8,16]{4,3,2,1,0:T(8,128)S(1)} %get-tuple-element.23, ...), kind=kLoop, calls=%fused_computation.28 | loop fusion | flops 262144 | bytes 655360 | tf_op jit(solution)/shard_map/div | solution.py:408
  (123 shorter events, 7.0 us)
Async XLA Ops:
  0.6 98.0 %copy-start = (bf16[32,8]{0,1:T(8,128)(2,1)S(1)}, bf16[32,8]{0,1:T(8,128)(2,1)}, u32[]{:S(2)}) copy-start(bf16[32,8]{0,1:T(8,128)(2,1)} %param.24) | copy-start | bytes 1540
  3.4 15.9 %collective-permute-start = (bf16[4,1,16384]{2,1,0:T(2,128)(2,1)}, bf16[4,1,16384]{2,1,0:T(2,128)(2,1)}, u32[]{:S(2)}, u32[]{:S(2)}) collective-permute-start(bf16[4,1,16384]{2,1,0:T(2,128)(2,1)} %get-tuple-element.8), channel_id=1, source_target_pairs={{0,1},{1,2},{2,3},{3,4},{4,5},{5,6},{6,7},{7,8},{8,9},{9,10},{10,1... | collective-permute-start | bytes 393224 | tf_op jit(solution)/shard_map/ppermute | solution.py:38
  6.4 14.8 %collective-permute-start.1 = (bf16[4,1,16384]{2,1,0:T(2,128)(2,1)}, bf16[4,1,16384]{2,1,0:T(2,128)(2,1)S(1)}, u32[]{:S(2)}, u32[]{:S(2)}) collective-permute-start(bf16[4,1,16384]{2,1,0:T(2,128)(2,1)} %get-tuple-element.7), channel_id=1, source_target_pairs={{1,0},{2,1},{3,2},{4,3},{5,4},{6,5},{7,6},{8,7},{9,8},{10,9},{11,1... | collective-permute-start | bytes 393224 | tf_op jit(solution)/shard_map/ppermute | solution.py:39
  13.6 1.9 %copy-start.5 = (s32[32]{0:T(128)S(1)}, s32[32]{0:T(128)}, u32[]{:S(2)}) copy-start(s32[32]{0:T(128)} %param.20) | copy-start | bytes 388
  13.6 2.8 %copy-start.1 = (bf16[2,32,8,32,16]{3,4,2,1,0:T(8,128)(2,1)S(1)}, bf16[2,32,8,32,16]{3,4,2,1,0:T(8,128)(2,1)}, u32[]{:S(2)}) copy-start(bf16[2,32,8,32,16]{3,4,2,1,0:T(8,128)(2,1)} %param.26) | copy-start | bytes 1572868
  38.5 45.6 %copy-start.2 = (bf16[1,16,4,1024]{3,2,1,0:T(4,128)(2,1)S(1)}, bf16[1,16,4,1024]{3,2,1,0:T(4,128)(2,1)}, u32[]{:S(2)}) copy-start(bf16[1,16,4,1024]{3,2,1,0:T(4,128)(2,1)} %param.21) | copy-start | bytes 393220
  38.5 45.6 %copy-start.3 = (bf16[4,32]{1,0:T(4,128)(2,1)S(1)}, bf16[4,32]{1,0:T(4,128)(2,1)}, u32[]{:S(2)}) copy-start(bf16[4,32]{1,0:T(4,128)(2,1)} %param.22) | copy-start | bytes 772
  38.5 45.6 %copy-start.4 = (f32[32]{0:T(128)S(1)}, f32[32]{0:T(128)}, u32[]{:S(2)}) copy-start(f32[32]{0:T(128)} %param.23) | copy-start | bytes 388
  39.2 33.6 %collective-permute-start.2 = (bf16[4,1024]{1,0:T(4,128)(2,1)S(1)}, bf16[4,1024]{1,0:T(4,128)(2,1)S(1)}, u32[]{:S(2)}, u32[]{:S(2)}) collective-permute-start(bf16[4,1024]{1,0:T(4,128)(2,1)S(1)} %multiply_convert_fusion), channel_id=1, source_target_pairs={{0,1},{1,2},{2,3},{3,0},{4,5},{5,6},{6,7},{7,4},{8,9},{9,10},{10,1... | collective-permute-start | bytes 24584 | tf_op jit(solution)/shard_map/ppermute | solution.py:283
  68.4 5.0 %collective-permute-start.3 = (bf16[4,1024]{1,0:T(4,128)(2,1)S(1)}, bf16[4,1024]{1,0:T(4,128)(2,1)S(1)}, u32[]{:S(2)}, u32[]{:S(2)}) collective-permute-start(bf16[4,1024]{1,0:T(4,128)(2,1)S(1)} %multiply_convert_fusion), channel_id=1, source_target_pairs={{0,2},{1,3},{2,0},{3,1},{4,6},{5,7},{6,4},{7,5},{8,10},{9,11},{10,... | collective-permute-start | bytes 24584 | tf_op jit(solution)/shard_map/ppermute | solution.py:283
  71.8 3.7 %collective-permute-start.4 = (bf16[4,1024]{1,0:T(4,128)(2,1)S(1)}, bf16[4,1024]{1,0:T(4,128)(2,1)S(1)}, u32[]{:S(2)}, u32[]{:S(2)}) collective-permute-start(bf16[4,1024]{1,0:T(4,128)(2,1)S(1)} %multiply_convert_fusion), channel_id=1, source_target_pairs={{0,3},{1,0},{2,1},{3,2},{4,7},{5,4},{6,5},{7,6},{8,11},{9,8},{10,9... | collective-permute-start | bytes 24584 | tf_op jit(solution)/shard_map/ppermute | solution.py:283
  75.4 1.3 %collective-permute-start.5 = (bf16[4,4,1024]{2,1,0:T(4,128)(2,1)S(1)}, bf16[4,4,1024]{2,1,0:T(4,128)(2,1)S(1)}, u32[]{:S(2)}, u32[]{:S(2)}) collective-permute-start(bf16[4,4,1024]{2,1,0:T(4,128)(2,1)S(1)} %bitcast_dynamic-update-slice_fusion.6), channel_id=1, source_target_pairs={{0,4},{4,0},{1,5},{5,1},{2,6},{6,2},{3,7},{7,3},{8,12},{12,8},{9,1... | collective-permute-start | bytes 98312 | tf_op jit(solution)/shard_map/ppermute | solution.py:283
  76.7 5.3 %collective-permute-start.6 = (bf16[2,4,4,1024]{3,2,1,0:T(4,128)(2,1)S(1)}, bf16[2,4,4,1024]{3,2,1,0:T(4,128)(2,1)S(1)}, u32[]{:S(2)}, u32[]{:S(2)}) collective-permute-start(bf16[2,4,4,1024]{3,2,1,0:T(4,128)(2,1)S(1)} %bitcast_dynamic-update-slice_fusion.4), channel_id=1, source_target_pairs={{0,8},{8,16},{16,24},{24,0},{1,9},{9,17},{17,25},{25,1},{2,10},{10... | collective-permute-start | bytes 196616 | tf_op jit(solution)/shard_map/ppermute | solution.py:283
  78.3 5.0 %collective-permute-start.7 = (bf16[2,4,4,1024]{3,2,1,0:T(4,128)(2,1)S(1)}, bf16[2,4,4,1024]{3,2,1,0:T(4,128)(2,1)S(1)}, u32[]{:S(2)}, u32[]{:S(2)}) collective-permute-start(bf16[2,4,4,1024]{3,2,1,0:T(4,128)(2,1)S(1)} %bitcast_dynamic-update-slice_fusion.4), channel_id=1, source_target_pairs={{0,16},{8,24},{16,0},{24,8},{1,17},{9,25},{17,1},{25,9},{2,18},{10... | collective-permute-start | bytes 196616 | tf_op jit(solution)/shard_map/ppermute | solution.py:283
  79.8 4.3 %collective-permute-start.8 = (bf16[2,4,4,1024]{3,2,1,0:T(4,128)(2,1)S(1)}, bf16[2,4,4,1024]{3,2,1,0:T(4,128)(2,1)S(1)}, u32[]{:S(2)}, u32[]{:S(2)}) collective-permute-start(bf16[2,4,4,1024]{3,2,1,0:T(4,128)(2,1)S(1)} %bitcast_dynamic-update-slice_fusion.4), channel_id=1, source_target_pairs={{0,24},{8,0},{16,8},{24,16},{1,25},{9,1},{17,9},{25,17},{2,26},{10... | collective-permute-start | bytes 196616 | tf_op jit(solution)/shard_map/ppermute | solution.py:283
  89.2 1.4 %collective-permute-start.9 = (f32[32768]{0:T(1024)S(1)}, f32[32768]{0:T(1024)S(1)}, u32[]{:S(2)}, u32[]{:S(2)}) collective-permute-start(f32[32768]{0:T(1024)S(1)} %pad_maximum_fusion.1), channel_id=1, source_target_pairs={{0,4},{4,0},{1,5},{5,1},{2,6},{6,2},{3,7},{7,3},{8,12},{12,8},{9,1... | collective-permute-start | bytes 393224 | tf_op jit(solution)/shard_map/ppermute | solution.py:296
  92.3 6.4 %copy-start.6 = (f32[8]{0:T(128)S(1)}, f32[8]{0:T(128)}, u32[]{:S(2)}) copy-start(f32[8]{0:T(128)} %param.25) | copy-start | bytes 100
  96.7 4.1 %copy-start.7 = (bf16[1,16,8,1024]{3,2,1,0:T(8,128)(2,1)S(1)}, bf16[1,16,8,1024]{3,2,1,0:T(8,128)(2,1)}, u32[]{:S(2)}) copy-start(bf16[1,16,8,1024]{3,2,1,0:T(8,128)(2,1)} %param.27) | copy-start | bytes 786436
  103.1 1.9 %collective-permute-start.10 = (f32[8192]{0:T(1024)S(1)}, f32[8192]{0:T(1024)S(1)}, u32[]{:S(2)}, u32[]{:S(2)}) collective-permute-start(f32[8192]{0:T(1024)S(1)} %pad_maximum_fusion.3), channel_id=1, source_target_pairs={{0,4},{4,0},{1,5},{5,1},{2,6},{6,2},{3,7},{7,3},{8,12},{12,8},{9,1... | collective-permute-start | bytes 98312 | tf_op jit(solution)/shard_map/ppermute | solution.py:296
  106.1 4.0 %collective-permute-start.13 = (f32[6144]{0:T(1024)S(1)}, f32[6144]{0:T(1024)S(1)}, u32[]{:S(2)}, u32[]{:S(2)}) collective-permute-start(f32[6144]{0:T(1024)S(1)} %pad_maximum_fusion.6), channel_id=1, source_target_pairs={{0,24},{8,0},{16,8},{24,16},{1,25},{9,1},{17,9},{25,17},{2,26},{10... | collective-permute-start | bytes 73736 | tf_op jit(solution)/shard_map/ppermute | solution.py:296
  107.8 3.9 %collective-permute-start.12 = (f32[6144]{0:T(1024)S(1)}, f32[6144]{0:T(1024)S(1)}, u32[]{:S(2)}, u32[]{:S(2)}) collective-permute-start(f32[6144]{0:T(1024)S(1)} %pad_maximum_fusion.5), channel_id=1, source_target_pairs={{0,16},{8,24},{16,0},{24,8},{1,17},{9,25},{17,1},{25,9},{2,18},{10... | collective-permute-start | bytes 73736 | tf_op jit(solution)/shard_map/ppermute | solution.py:296
  109.7 4.8 %collective-permute-start.11 = (f32[6144]{0:T(1024)S(1)}, f32[6144]{0:T(1024)S(1)}, u32[]{:S(2)}, u32[]{:S(2)}) collective-permute-start(f32[6144]{0:T(1024)S(1)} %pad_maximum_fusion.4), channel_id=1, source_target_pairs={{0,8},{8,16},{16,24},{24,0},{1,9},{9,17},{17,25},{25,1},{2,10},{10... | collective-permute-start | bytes 73736 | tf_op jit(solution)/shard_map/ppermute | solution.py:296

commit v6 on v4

--- a/solution.py
+++ b/solution.py
@@ -103,10 +103,14 @@
             right_cells = pltpu.roll(extended, span - 1, 1)[:, 128 : 128 + CHUNK]
             left_cells = pltpu.roll(extended, 1, 1)[:, 128 : 128 + CHUNK]
             upper_rows = jnp.where(
-                row_ids == 0, above_ref[tracer, :, cols], pltpu.roll(current, 1, 0)
+                row_ids == 0,
+                above_ref[tracer, :, cols].astype(jnp.float32),
+                pltpu.roll(current, 1, 0),
             )
             lower_rows = jnp.where(
-                row_ids == rows - 1, below_ref[tracer, :, cols], pltpu.roll(current, rows - 1, 0)
+                row_ids == rows - 1,
+                below_ref[tracer, :, cols].astype(jnp.float32),
+                pltpu.roll(current, rows - 1, 0),
             )
             change = coef_ref[0, :, cols] * (
                 right_cells + left_cells + upper_rows + lower_rows - 4.0 * current
@@ -176,8 +180,8 @@
         step,
         substeps.reshape(1),
         field,
-        above_row.astype(jnp.float32),
-        below_row.astype(jnp.float32),
+        above_row,
+        below_row,
         coefficients,
     )
 
@@ -374,7 +378,7 @@
         column_part[:, :, :MODES], column_part[:, :, MODES:], cosine_table, sine_table
     )
     mode_real, mode_imag = pair_sum((part_real * norm_scale, part_imag * norm_scale), "mem")
-    mixed_real, mixed_imag = mix_modes(spectral_weight.astype(jnp.float32), mode_real, mode_imag)
+    mixed_real, mixed_imag = mix_modes(spectral_weight, mode_real, mode_imag)
     spatial = (
         jnp.einsum(
             "yok,kx->yox",

time: 114 us -> 111 us (0.974)
  starting transfers between devices: 18.7 us -> 41.8 us
  Pallas kernels: 40.3 us -> 17.9 us
  other arithmetic: 19.9 us -> 13.9 us
  waiting for transfers between devices: 9.86 us -> 13.2 us
    pallas_call x1, Pallas kernels: 40.3 us -> 17.9 us  [solve_rows(): pl.pallas_call(solve_kernel, out_shape=jax.ShapeDtypeStruct((tracers, 1,...]
    ppermute x7, starting transfers between devices: 8.84 us -> 30.8 us  [gather_along(): lax.ppermute(block, axis, [(i, (i + shift) % count) for i in range(count)])]
    convert_element_type x3 -> x0, other arithmetic: 5.42 us -> none  [the longest x1 2.52 us: body(): spectral_weight.astype(jnp.float32)]
    ppermute x1, waiting for transfers between devices: 0.01 us -> 3.01 us  [halo_rows(): below = lax.ppermute(block[:, :1], axis, backward)]
  transfers between devices with their start and end apart: 14 -> 14, of which waited for: 9 -> 8; matrix products, arithmetic and copies ran while one was open for 13% -> 9% of each run, Pallas kernels for 0% -> 0%
where the time goes in v6:
time: 111 us
  starting transfers between devices  41.8 us (38%)
  Pallas kernels  17.9 us (16%)
  other arithmetic  13.9 us (13%)
  local copies, waits for them, and re-layouts  13.4 us (12%)
  waiting for transfers between devices  13.2 us (12%)
  matrix products  8.62 us (8%)
  between operations  2.29 us (2%)
    ppermute x7, starting transfers between devices, gather_along(): lax.ppermute(block, axis, [(i, (i + shift) % count) for i in range(count)])  30.8 us
    pallas_call x1, Pallas kernels, solve_rows(): pl.pallas_call(solve_kernel, out_shape=jax.ShapeDtypeStruct((tracers, 1,...  17.9 us
    ppermute x7, waiting for transfers between devices, gather_along(): lax.ppermute(block, axis, [(i, (i + shift) % count) for i in range(count)])  5.38 us
    ppermute x5, waiting for transfers between devices, packed_ppermute(): flat = lax.ppermute(flat, axis, perm)  4.8 us
    ppermute x5, starting transfers between devices, packed_ppermute(): flat = lax.ppermute(flat, axis, perm)  4.53 us
    ppermute x1, starting transfers between devices, halo_rows(): below = lax.ppermute(block[:, :1], axis, backward)  3.42 us
    ppermute x1, starting transfers between devices, halo_rows(): above = lax.ppermute(block[:, -1:], axis, forward)  3.08 us
    ppermute x1, waiting for transfers between devices, halo_rows(): below = lax.ppermute(block[:, :1], axis, backward)  3.01 us
  transfers between devices with their start and end apart: 14, of which 8 were waited for; matrix products, arithmetic and copies ran while one was open for 9% of the time, Pallas kernels for 0%

profile of v6, /device:TPU:0, one launch (start us, length us, event | category | flops | bytes accessed | tf_op | source)
XLA Modules:
  0.0 111.0 jit_solution(10468859497156463023)
XLA Ops:
  0.6 2.0 %fusion.145 = (bf16[4,1,16384]{2,1,0:T(2,128)(2,1)S(1)}, bf16[4,1,16384]{2,1,0:T(2,128)(2,1)S(1)}) fusion(bf16[4,16,16384]{2,1,0:T(8,128)(2,1)} %field_ref.1), kind=kLoop, calls=%fused_computation.224 | loop fusion | bytes 524288 | tf_op jit(solution)/shard_map/slice | solution.py:39
  2.6 3.1 %collective-permute-start = (bf16[4,1,16384]{2,1,0:T(2,128)(2,1)S(1)}, bf16[4,1,16384]{2,1,0:T(2,128)(2,1)S(1)}, u32[]{:S(2)}, u32[]{:S(2)}) collective-permute-start(bf16[4,1,16384]{2,1,0:T(2,128)(2,1)S(1)} %get-tuple-element.8), channel_id=1, source_target_pairs={{0,1},{1,2},{2,3},{3,4},{4,5},{5,6},{6,7},{7,8},{8,9},{9,10},{10,1... | collective-permute-start | bytes 393224 | tf_op jit(solution)/shard_map/ppermute | solution.py:38
  5.7 3.4 %collective-permute-start.1 = (bf16[4,1,16384]{2,1,0:T(2,128)(2,1)S(1)}, bf16[4,1,16384]{2,1,0:T(2,128)(2,1)S(1)}, u32[]{:S(2)}, u32[]{:S(2)}) collective-permute-start(bf16[4,1,16384]{2,1,0:T(2,128)(2,1)S(1)} %get-tuple-element.7), channel_id=1, source_target_pairs={{1,0},{2,1},{3,2},{4,3},{5,4},{6,5},{7,6},{8,7},{9,8},{10,9},{11,1... | collective-permute-start | bytes 393224 | tf_op jit(solution)/shard_map/ppermute | solution.py:39
  9.1 1.0 fusion.149
  10.1 0.8 slice_bitcast_fusion.1
  10.9 0.8 convert_element_type.71
  11.7 0.3 cosine_multiply_fusion
  11.9 0.8 broadcast_multiply_fusion
  12.7 0.2 multiply_multiply_fusion
  13.0 1.8 %pad_maximum_fusion.coef_ref = f32[3,16,16384]{2,1,0:T(8,128)} fusion(f32[1,16,16384]{2,1,0:T(8,128)S(1)} %get-tuple-element.59, f32[1,16,16384]{2,1,0:T(8,128)S(1)} %get-tuple-element.60, f32[1,16,16384]{2,1,0:T(8,128)S(1)} %broadcast_multiply_fusion), kind=kLoop, calls=%fused_computation | loop fusion | flops 1572864 | bytes 6291456 | tf_op jit(solution)/shard_map/stack | solution.py:160
  15.8 0.3 negate_convert_fusion
  16.1 3.0 %collective-permute-done.1.below_ref = bf16[4,1,16384]{2,1,0:T(2,128)(2,1)S(1)} collective-permute-done((bf16[4,1,16384]{2,1,0:T(2,128)(2,1)S(1)}, bf16[4,1,16384]{2,1,0:T(2,128)(2,1)S(1)}, u32[]{:S(2)}, u32[]{:S(2)}) %collective-permute-start.1) | collective-permute-done | bytes 131104 | tf_op jit(solution)/shard_map/ppermute | solution.py:39
  19.1 0.7 copy-done.2
  19.8 17.9 %shard_map.157 = f32[4,1,16384]{2,1,0:T(1,128)} custom-call(f32[1]{0:T(128)S(6)} %div.10.step_ref, s32[1]{0:T(128)S(6)} %copy.120.count_ref, bf16[4,16,16384]{2,1,0:T(8,128)(2,1)} %field_ref.1, bf16[4,1,16384]{2,1,0:T(2,128)(2,1)} %copy-done.1, bf16[4,1,16384]{2,1,0:T(2,128)(2,1)} %copy-done.2, f32[3,16,16384]{2,1,0:T(8,128)} %pad_maximum_fusion.coef_ref), custom_call_target="tpu_custom_call" | custom-call | tf_op jit(solution)/shard_map/pallas_call | solution.py:169
  37.6 1.6 %reduce = f32[4,16384]{1,0:T(4,128)S(1)} reduce(f32[4,1,16384]{2,1,0:T(1,128)} %shard_map.157, f32[]{:T(128)} %constant.378), dimensions={1}, to_apply=%pallas_call.3.reduce_sub_computation | reduce | bytes 524292 | tf_op jit(solution)/shard_map/pallas_call | solution.py:169
  39.3 0.7 reshape.465
  40.0 0.6 reduce_sum.27
  40.7 26.0 %collective-permute-start.3 = (bf16[4,1024]{1,0:T(4,128)(2,1)S(1)}, bf16[4,1024]{1,0:T(4,128)(2,1)S(1)}, u32[]{:S(2)}, u32[]{:S(2)}) collective-permute-start(bf16[4,1024]{1,0:T(4,128)(2,1)S(1)} %multiply_convert_fusion), channel_id=1, source_target_pairs={{0,2},{1,3},{2,0},{3,1},{4,6},{5,7},{6,4},{7,5},{8,10},{9,11},{10,... | collective-permute-start | bytes 24584 | tf_op jit(solution)/shard_map/ppermute | solution.py:285
  66.7 1.3 %collective-permute-start.4 = (bf16[4,1024]{1,0:T(4,128)(2,1)S(1)}, bf16[4,1024]{1,0:T(4,128)(2,1)S(1)}, u32[]{:S(2)}, u32[]{:S(2)}) collective-permute-start(bf16[4,1024]{1,0:T(4,128)(2,1)S(1)} %multiply_convert_fusion), channel_id=1, source_target_pairs={{0,3},{1,0},{2,1},{3,2},{4,7},{5,4},{6,5},{7,6},{8,11},{9,8},{10,9... | collective-permute-start | bytes 24584 | tf_op jit(solution)/shard_map/ppermute | solution.py:285
  68.1 0.6 convert_dynamic-update-slice_fusion
  68.8 1.6 %collective-permute-done.4 = bf16[4,1024]{1,0:T(4,128)(2,1)S(1)} collective-permute-done((bf16[4,1024]{1,0:T(4,128)(2,1)S(1)}, bf16[4,1024]{1,0:T(4,128)(2,1)S(1)}, u32[]{:S(2)}, u32[]{:S(2)}) %collective-permute-start.4) | collective-permute-done | bytes 8224 | tf_op jit(solution)/shard_map/ppermute | solution.py:285
  70.5 1.1 %collective-permute-done.5 = bf16[4,4,1024]{2,1,0:T(4,128)(2,1)S(1)} collective-permute-done((bf16[4,4,1024]{2,1,0:T(4,128)(2,1)S(1)}, bf16[4,4,1024]{2,1,0:T(4,128)(2,1)S(1)}, u32[]{:S(2)}, u32[]{:S(2)}) %collective-permute-start.5) | collective-permute-done | bytes 32800 | tf_op jit(solution)/shard_map/ppermute | solution.py:285
  71.8 1.8 %collective-permute-start.7 = (bf16[2,4,4,1024]{3,2,1,0:T(4,128)(2,1)S(1)}, bf16[2,4,4,1024]{3,2,1,0:T(4,128)(2,1)S(1)}, u32[]{:S(2)}, u32[]{:S(2)}) collective-permute-start(bf16[2,4,4,1024]{3,2,1,0:T(4,128)(2,1)S(1)} %bitcast_dynamic-update-slice_fusion.4), channel_id=1, source_target_pairs={{0,16},{8,24},{16,0},{24,8},{1,17},{9,25},{17,1},{25,9},{2,18},{10... | collective-permute-start | bytes 196616 | tf_op jit(solution)/shard_map/ppermute | solution.py:285
  73.5 1.4 %collective-permute-start.8 = (bf16[2,4,4,1024]{3,2,1,0:T(4,128)(2,1)S(1)}, bf16[2,4,4,1024]{3,2,1,0:T(4,128)(2,1)S(1)}, u32[]{:S(2)}, u32[]{:S(2)}) collective-permute-start(bf16[2,4,4,1024]{3,2,1,0:T(4,128)(2,1)S(1)} %bitcast_dynamic-update-slice_fusion.4), channel_id=1, source_target_pairs={{0,24},{8,0},{16,8},{24,16},{1,25},{9,1},{17,9},{25,17},{2,26},{10... | collective-permute-start | bytes 196616 | tf_op jit(solution)/shard_map/ppermute | solution.py:285
  75.1 2.4 %collective-permute-done.6 = bf16[2,4,4,1024]{3,2,1,0:T(4,128)(2,1)S(1)} collective-permute-done((bf16[2,4,4,1024]{3,2,1,0:T(4,128)(2,1)S(1)}, bf16[2,4,4,1024]{3,2,1,0:T(4,128)(2,1)S(1)}, u32[]{:S(2)}, u32[]{:S(2)}) %collective-permute-start.6) | collective-permute-done | bytes 65568 | tf_op jit(solution)/shard_map/ppermute | solution.py:285
  77.6 0.2 collective-permute-done.8
  77.9 0.5 fusion.4
  78.4 0.9 fusion.60
  79.3 0.5 fusion.45
  79.9 0.5 fusion.41
  80.4 0.5 fusion.10
  81.0 0.5 copy.67
  81.5 0.2 reshape.467
  81.7 0.5 fusion.8
  82.2 0.5 copy.70
  82.7 0.2 reshape.468
  83.0 0.3 sine_multiply_fusion
  83.3 1.1 collective-permute-done.9
  84.4 0.2 reshape.469
  84.6 0.4 copy.71
  85.1 0.2 copy.72
  85.2 0.2 reshape.470
  85.4 0.4 copy.73
  85.9 0.2 copy.74
  86.1 2.4 %fusion.3 = (f32[8,32,16]{1,2,0:T(8,128)S(1)}, f32[8,32,16]{1,2,0:T(8,128)S(1)}) fusion(f32[32,32,16]{1,2,0:T(8,128)S(1)} %copy.74, f32[32,32,16]{1,2,0:T(8,128)S(1)} %copy.72, bf16[2,32,8,32,16]{3,4,2,1,0:T(8,128)(2,1)} %param.26), kind=kLoop, calls=%fused_computation.8 | loop fusion | flops 1302528 | bytes 688128 | tf_op jit(solution)/shard_map/reduce_sum | solution.py:251
  88.5 0.6 fusion.76
  89.1 0.7 fusion.66
  89.8 0.7 convolution_subtract_fusion.2
  90.5 0.7 convolution_add_fusion.2
  91.2 0.6 convolution_multiply_fusion
  91.8 0.3 fusion.6
  92.1 1.8 %fusion.34 = bf16[1,16,8,1024]{3,2,1,0:T(8,128)(2,1)} fusion(f32[16,8,1024]{2,1,0:T(8,128)S(1)} %fusion.6), kind=kLoop, calls=%fused_computation.70 | loop fusion | flops 8519680 | bytes 786432 | tf_op jit(solution)/shard_map/broadcast_in_dim | solution.py:396
  93.9 0.3 fusion.35
  94.4 0.3 fusion.73
  94.9 0.3 fusion.71
  95.2 0.3 fusion.14
  95.7 0.3 fusion.12
  96.3 0.2 collective-permute-start.10
  96.6 0.2 constant_dynamic-slice_fusion
  99.2 2.4 %collective-permute-start.13 = (f32[6144]{0:T(1024)S(1)}, f32[6144]{0:T(1024)S(1)}, u32[]{:S(2)}, u32[]{:S(2)}) collective-permute-start(f32[6144]{0:T(1024)S(1)} %pad_maximum_fusion.6), channel_id=1, source_target_pairs={{0,24},{8,0},{16,8},{24,16},{1,25},{9,1},{17,9},{25,17},{2,26},{10... | collective-permute-start | bytes 73736 | tf_op jit(solution)/shard_map/ppermute | solution.py:298
  102.0 1.7 %collective-permute-start.12 = (f32[6144]{0:T(1024)S(1)}, f32[6144]{0:T(1024)S(1)}, u32[]{:S(2)}, u32[]{:S(2)}) collective-permute-start(f32[6144]{0:T(1024)S(1)} %pad_maximum_fusion.5), channel_id=1, source_target_pairs={{0,16},{8,24},{16,0},{24,8},{1,17},{9,25},{17,1},{25,9},{2,18},{10... | collective-permute-start | bytes 73736 | tf_op jit(solution)/shard_map/ppermute | solution.py:298
  104.4 1.4 %collective-permute-done.12 = f32[6144]{0:T(1024)S(1)} collective-permute-done((f32[6144]{0:T(1024)S(1)}, f32[6144]{0:T(1024)S(1)}, u32[]{:S(2)}, u32[]{:S(2)}) %collective-permute-start.12) | collective-permute-done | bytes 24608 | tf_op jit(solution)/shard_map/ppermute | solution.py:298
  106.5 2.3 %collective-permute-done.11 = f32[6144]{0:T(1024)S(1)} collective-permute-done((f32[6144]{0:T(1024)S(1)}, f32[6144]{0:T(1024)S(1)}, u32[]{:S(2)}, u32[]{:S(2)}) %collective-permute-start.11) | collective-permute-done | bytes 24608 | tf_op jit(solution)/shard_map/ppermute | solution.py:298
  109.6 1.4 %fusion.17 = f32[2,16,8,8,16]{4,3,2,1,0:T(8,128)} fusion(f32[1,16,8,8,16]{4,3,2,1,0:T(8,128)S(1)} %get-tuple-element.26, f32[1,16,8,8,16]{4,3,2,1,0:T(8,128)S(1)} %get-tuple-element.25, f32[1,16,8,8,16]{4,3,2,1,0:T(8,128)S(1)} %get-tuple-element.24, f32[1,16,8,8,16]{4,3,2,1,0:T(8,128)S(1)} %get-tuple-element.23, ...), kind=kLoop, calls=%fused_computation.32 | loop fusion | flops 262144 | bytes 655360 | tf_op jit(solution)/shard_map/div | solution.py:410
  (122 shorter events, 6.4 us)
Async XLA Ops:
  0.6 91.2 %copy-start = (bf16[32,8]{0,1:T(8,128)(2,1)S(1)}, bf16[32,8]{0,1:T(8,128)(2,1)}, u32[]{:S(2)}) copy-start(bf16[32,8]{0,1:T(8,128)(2,1)} %param.24) | copy-start | bytes 1540
  2.6 13.4 %collective-permute-start = (bf16[4,1,16384]{2,1,0:T(2,128)(2,1)S(1)}, bf16[4,1,16384]{2,1,0:T(2,128)(2,1)S(1)}, u32[]{:S(2)}, u32[]{:S(2)}) collective-permute-start(bf16[4,1,16384]{2,1,0:T(2,128)(2,1)S(1)} %get-tuple-element.8), channel_id=1, source_target_pairs={{0,1},{1,2},{2,3},{3,4},{4,5},{5,6},{6,7},{7,8},{8,9},{9,10},{10,1... | collective-permute-start | bytes 393224 | tf_op jit(solution)/shard_map/ppermute | solution.py:38
  5.7 13.4 %collective-permute-start.1 = (bf16[4,1,16384]{2,1,0:T(2,128)(2,1)S(1)}, bf16[4,1,16384]{2,1,0:T(2,128)(2,1)S(1)}, u32[]{:S(2)}, u32[]{:S(2)}) collective-permute-start(bf16[4,1,16384]{2,1,0:T(2,128)(2,1)S(1)} %get-tuple-element.7), channel_id=1, source_target_pairs={{1,0},{2,1},{3,2},{4,3},{5,4},{6,5},{7,6},{8,7},{9,8},{10,9},{11,1... | collective-permute-start | bytes 393224 | tf_op jit(solution)/shard_map/ppermute | solution.py:39
  13.0 1.9 %copy-start.6 = (s32[32]{0:T(128)S(1)}, s32[32]{0:T(128)}, u32[]{:S(2)}) copy-start(s32[32]{0:T(128)} %param.20) | copy-start | bytes 388
  16.0 3.0 %copy-start.1 = (bf16[4,1,16384]{2,1,0:T(2,128)(2,1)}, bf16[4,1,16384]{2,1,0:T(2,128)(2,1)S(1)}, u32[]{:S(2)}) copy-start(bf16[4,1,16384]{2,1,0:T(2,128)(2,1)S(1)} %collective-permute-done.above_ref) | copy-start | bytes 393220
  19.1 0.7 copy-start.2
  39.9 37.9 %copy-start.3 = (bf16[1,16,4,1024]{3,2,1,0:T(4,128)(2,1)S(1)}, bf16[1,16,4,1024]{3,2,1,0:T(4,128)(2,1)}, u32[]{:S(2)}) copy-start(bf16[1,16,4,1024]{3,2,1,0:T(4,128)(2,1)} %param.21) | copy-start | bytes 393220
  40.0 37.9 %copy-start.4 = (bf16[4,32]{1,0:T(4,128)(2,1)S(1)}, bf16[4,32]{1,0:T(4,128)(2,1)}, u32[]{:S(2)}) copy-start(bf16[4,32]{1,0:T(4,128)(2,1)} %param.22) | copy-start | bytes 772
  40.0 37.9 %copy-start.5 = (f32[32]{0:T(128)S(1)}, f32[32]{0:T(128)}, u32[]{:S(2)}) copy-start(f32[32]{0:T(128)} %param.23) | copy-start | bytes 388
  40.6 28.1 %collective-permute-start.2 = (bf16[4,1024]{1,0:T(4,128)(2,1)S(1)}, bf16[4,1024]{1,0:T(4,128)(2,1)S(1)}, u32[]{:S(2)}, u32[]{:S(2)}) collective-permute-start(bf16[4,1024]{1,0:T(4,128)(2,1)S(1)} %multiply_convert_fusion), channel_id=1, source_target_pairs={{0,1},{1,2},{2,3},{3,0},{4,5},{5,6},{6,7},{7,4},{8,9},{9,10},{10,1... | collective-permute-start | bytes 24584 | tf_op jit(solution)/shard_map/ppermute | solution.py:285
  40.7 28.0 %collective-permute-start.3 = (bf16[4,1024]{1,0:T(4,128)(2,1)S(1)}, bf16[4,1024]{1,0:T(4,128)(2,1)S(1)}, u32[]{:S(2)}, u32[]{:S(2)}) collective-permute-start(bf16[4,1024]{1,0:T(4,128)(2,1)S(1)} %multiply_convert_fusion), channel_id=1, source_target_pairs={{0,2},{1,3},{2,0},{3,1},{4,6},{5,7},{6,4},{7,5},{8,10},{9,11},{10,... | collective-permute-start | bytes 24584 | tf_op jit(solution)/shard_map/ppermute | solution.py:285
  66.7 3.7 %collective-permute-start.4 = (bf16[4,1024]{1,0:T(4,128)(2,1)S(1)}, bf16[4,1024]{1,0:T(4,128)(2,1)S(1)}, u32[]{:S(2)}, u32[]{:S(2)}) collective-permute-start(bf16[4,1024]{1,0:T(4,128)(2,1)S(1)} %multiply_convert_fusion), channel_id=1, source_target_pairs={{0,3},{1,0},{2,1},{3,2},{4,7},{5,4},{6,5},{7,6},{8,11},{9,8},{10,9... | collective-permute-start | bytes 24584 | tf_op jit(solution)/shard_map/ppermute | solution.py:285
  70.4 1.3 %collective-permute-start.5 = (bf16[4,4,1024]{2,1,0:T(4,128)(2,1)S(1)}, bf16[4,4,1024]{2,1,0:T(4,128)(2,1)S(1)}, u32[]{:S(2)}, u32[]{:S(2)}) collective-permute-start(bf16[4,4,1024]{2,1,0:T(4,128)(2,1)S(1)} %bitcast_dynamic-update-slice_fusion.6), channel_id=1, source_target_pairs={{0,4},{4,0},{1,5},{5,1},{2,6},{6,2},{3,7},{7,3},{8,12},{12,8},{9,1... | collective-permute-start | bytes 98312 | tf_op jit(solution)/shard_map/ppermute | solution.py:285
  71.7 5.8 %collective-permute-start.6 = (bf16[2,4,4,1024]{3,2,1,0:T(4,128)(2,1)S(1)}, bf16[2,4,4,1024]{3,2,1,0:T(4,128)(2,1)S(1)}, u32[]{:S(2)}, u32[]{:S(2)}) collective-permute-start(bf16[2,4,4,1024]{3,2,1,0:T(4,128)(2,1)S(1)} %bitcast_dynamic-update-slice_fusion.4), channel_id=1, source_target_pairs={{0,8},{8,16},{16,24},{24,0},{1,9},{9,17},{17,25},{25,1},{2,10},{10... | collective-permute-start | bytes 196616 | tf_op jit(solution)/shard_map/ppermute | solution.py:285
  71.8 5.8 %collective-permute-start.7 = (bf16[2,4,4,1024]{3,2,1,0:T(4,128)(2,1)S(1)}, bf16[2,4,4,1024]{3,2,1,0:T(4,128)(2,1)S(1)}, u32[]{:S(2)}, u32[]{:S(2)}) collective-permute-start(bf16[2,4,4,1024]{3,2,1,0:T(4,128)(2,1)S(1)} %bitcast_dynamic-update-slice_fusion.4), channel_id=1, source_target_pairs={{0,16},{8,24},{16,0},{24,8},{1,17},{9,25},{17,1},{25,9},{2,18},{10... | collective-permute-start | bytes 196616 | tf_op jit(solution)/shard_map/ppermute | solution.py:285
  73.5 4.3 %collective-permute-start.8 = (bf16[2,4,4,1024]{3,2,1,0:T(4,128)(2,1)S(1)}, bf16[2,4,4,1024]{3,2,1,0:T(4,128)(2,1)S(1)}, u32[]{:S(2)}, u32[]{:S(2)}) collective-permute-start(bf16[2,4,4,1024]{3,2,1,0:T(4,128)(2,1)S(1)} %bitcast_dynamic-update-slice_fusion.4), channel_id=1, source_target_pairs={{0,24},{8,0},{16,8},{24,16},{1,25},{9,1},{17,9},{25,17},{2,26},{10... | collective-permute-start | bytes 196616 | tf_op jit(solution)/shard_map/ppermute | solution.py:285
  83.0 1.4 %collective-permute-start.9 = (f32[32768]{0:T(1024)S(1)}, f32[32768]{0:T(1024)S(1)}, u32[]{:S(2)}, u32[]{:S(2)}) collective-permute-start(f32[32768]{0:T(1024)S(1)} %pad_maximum_fusion.1), channel_id=1, source_target_pairs={{0,4},{4,0},{1,5},{5,1},{2,6},{6,2},{3,7},{7,3},{8,12},{12,8},{9,1... | collective-permute-start | bytes 393224 | tf_op jit(solution)/shard_map/ppermute | solution.py:298
  86.1 5.7 %copy-start.7 = (f32[8]{0:T(128)S(1)}, f32[8]{0:T(128)}, u32[]{:S(2)}) copy-start(f32[8]{0:T(128)} %param.25) | copy-start | bytes 100
  89.8 4.1 %copy-start.8 = (bf16[1,16,8,1024]{3,2,1,0:T(8,128)(2,1)S(1)}, bf16[1,16,8,1024]{3,2,1,0:T(8,128)(2,1)}, u32[]{:S(2)}) copy-start(bf16[1,16,8,1024]{3,2,1,0:T(8,128)(2,1)} %param.27) | copy-start | bytes 786436
  96.3 1.9 %collective-permute-start.10 = (f32[8192]{0:T(1024)S(1)}, f32[8192]{0:T(1024)S(1)}, u32[]{:S(2)}, u32[]{:S(2)}) collective-permute-start(f32[8192]{0:T(1024)S(1)} %pad_maximum_fusion.3), channel_id=1, source_target_pairs={{0,4},{4,0},{1,5},{5,1},{2,6},{6,2},{3,7},{7,3},{8,12},{12,8},{9,1... | collective-permute-start | bytes 98312 | tf_op jit(solution)/shard_map/ppermute | solution.py:298
  99.2 5.2 %collective-permute-start.13 = (f32[6144]{0:T(1024)S(1)}, f32[6144]{0:T(1024)S(1)}, u32[]{:S(2)}, u32[]{:S(2)}) collective-permute-start(f32[6144]{0:T(1024)S(1)} %pad_maximum_fusion.6), channel_id=1, source_target_pairs={{0,24},{8,0},{16,8},{24,16},{1,25},{9,1},{17,9},{25,17},{2,26},{10... | collective-permute-start | bytes 73736 | tf_op jit(solution)/shard_map/ppermute | solution.py:298
  102.0 3.9 %collective-permute-start.12 = (f32[6144]{0:T(1024)S(1)}, f32[6144]{0:T(1024)S(1)}, u32[]{:S(2)}, u32[]{:S(2)}) collective-permute-start(f32[6144]{0:T(1024)S(1)} %pad_maximum_fusion.5), channel_id=1, source_target_pairs={{0,16},{8,24},{16,0},{24,8},{1,17},{9,25},{17,1},{25,9},{2,18},{10... | collective-permute-start | bytes 73736 | tf_op jit(solution)/shard_map/ppermute | solution.py:298
  104.0 4.8 %collective-permute-start.11 = (f32[6144]{0:T(1024)S(1)}, f32[6144]{0:T(1024)S(1)}, u32[]{:S(2)}, u32[]{:S(2)}) collective-permute-start(f32[6144]{0:T(1024)S(1)} %pad_maximum_fusion.4), channel_id=1, source_target_pairs={{0,8},{8,16},{16,24},{24,0},{1,9},{9,17},{17,25},{25,1},{2,10},{10... | collective-permute-start | bytes 73736 | tf_op jit(solution)/shard_map/ppermute | solution.py:298

commit v7 on v6

--- a/solution.py
+++ b/solution.py
@@ -294,13 +294,12 @@
 
 
 def packed_ppermute(parts, axis, perm):
-    flat = jnp.concatenate([part.reshape(-1) for part in parts])
-    flat = lax.ppermute(flat, axis, perm)
+    packed = lax.ppermute(jnp.concatenate(parts, axis=0), axis, perm)
     result = []
     offset = 0
     for part in parts:
-        result.append(flat[offset : offset + part.size].reshape(part.shape))
-        offset += part.size
+        result.append(lax.slice_in_dim(packed, offset, offset + part.shape[0], axis=0))
+        offset += part.shape[0]
     return tuple(result)
 
 

time: 111 us -> 108 us (0.973)
  starting transfers between devices: 41.8 us -> 30.5 us
  Pallas kernels: 17.9 us -> 29.1 us
  local copies, waits for them, and re-layouts: 13.4 us -> 9.29 us
    pallas_call x1, Pallas kernels: 17.9 us -> 29.1 us  [solve_rows(): pl.pallas_call(solve_kernel, out_shape=jax.ShapeDtypeStruct((tracers, 1,...]
    ppermute x7, starting transfers between devices: 30.8 us -> 19.9 us  [gather_along(): lax.ppermute(block, axis, [(i, (i + shift) % count) for i in range(count)])]
    reshape x36 -> x0, local copies, waits for them, and re-layouts: 4.03 us -> none  [the longest x20 2.48 us: packed_ppermute(): result.append(flat[offset:offset + part.size].reshape(part.shape))]
    slice x8 -> x18, local copies, waits for them, and re-layouts: 0.03 us -> 1.68 us  [packed_ppermute(): lax.slice_in_dim(packed, offset, offset + part.shape[0], axis=0)]
    mul x4 -> x0, local copies, waits for them, and re-layouts: 1.2 us -> none  [the longest x1 0.51 us: body(): part_real * norm_scale]
  transfers between devices with their start and end apart: 14 -> 14, of which waited for: 8 -> 10; matrix products, arithmetic and copies ran while one was open for 9% -> 9% of each run, Pallas kernels for 0% -> 0%
where the time goes in v7:
time: 108 us; the launch traced here: 107 us
  starting transfers between devices  30.5 us (28%)
  Pallas kernels  29.1 us (27%)
  other arithmetic  14.4 us (13%)
  waiting for transfers between devices  13 us (12%)
  local copies, waits for them, and re-layouts  9.29 us (9%)
  matrix products  8.62 us (8%)
  between operations  2.05 us (2%)
    pallas_call x1, Pallas kernels, solve_rows(): pl.pallas_call(solve_kernel, out_shape=jax.ShapeDtypeStruct((tracers, 1,...  29.1 us
    ppermute x7, starting transfers between devices, gather_along(): lax.ppermute(block, axis, [(i, (i + shift) % count) for i in range(count)])  19.9 us
    ppermute x5, waiting for transfers between devices, packed_ppermute(): packed = lax.ppermute(jnp.concatenate(parts, axis=0), axis, perm)  5.54 us
    ppermute x7, waiting for transfers between devices, gather_along(): lax.ppermute(block, axis, [(i, (i + shift) % count) for i in range(count)])  4.48 us
    ppermute x5, starting transfers between devices, packed_ppermute(): packed = lax.ppermute(jnp.concatenate(parts, axis=0), axis, perm)  4.12 us
    ppermute x1, starting transfers between devices, halo_rows(): below = lax.ppermute(block[:, :1], axis, backward)  3.42 us
    ppermute x1, starting transfers between devices, halo_rows(): above = lax.ppermute(block[:, -1:], axis, forward)  3.08 us
    ppermute x1, waiting for transfers between devices, halo_rows(): below = lax.ppermute(block[:, :1], axis, backward)  3.01 us
  transfers between devices with their start and end apart: 14, of which 10 were waited for; matrix products, arithmetic and copies ran while one was open for 9% of the time, Pallas kernels for 0%

profile of v7, /device:TPU:0, one launch (start us, length us, event | category | flops | bytes accessed | tf_op | source)
XLA Modules:
  0.0 107.0 jit_solution(13040859203439207133)
XLA Ops:
  0.6 2.0 %fusion.145 = (bf16[4,1,16384]{2,1,0:T(2,128)(2,1)S(1)}, bf16[4,1,16384]{2,1,0:T(2,128)(2,1)S(1)}) fusion(bf16[4,16,16384]{2,1,0:T(8,128)(2,1)} %field_ref.1), kind=kLoop, calls=%fused_computation.240 | loop fusion | bytes 524288 | tf_op jit(solution)/shard_map/slice | solution.py:39
  2.6 3.1 %collective-permute-start = (bf16[4,1,16384]{2,1,0:T(2,128)(2,1)S(1)}, bf16[4,1,16384]{2,1,0:T(2,128)(2,1)S(1)}, u32[]{:S(2)}, u32[]{:S(2)}) collective-permute-start(bf16[4,1,16384]{2,1,0:T(2,128)(2,1)S(1)} %get-tuple-element.8), channel_id=1, source_target_pairs={{0,1},{1,2},{2,3},{3,4},{4,5},{5,6},{6,7},{7,8},{8,9},{9,10},{10,1... | collective-permute-start | bytes 393224 | tf_op jit(solution)/shard_map/ppermute | solution.py:38
  5.7 3.4 %collective-permute-start.1 = (bf16[4,1,16384]{2,1,0:T(2,128)(2,1)S(1)}, bf16[4,1,16384]{2,1,0:T(2,128)(2,1)S(1)}, u32[]{:S(2)}, u32[]{:S(2)}) collective-permute-start(bf16[4,1,16384]{2,1,0:T(2,128)(2,1)S(1)} %get-tuple-element.7), channel_id=1, source_target_pairs={{1,0},{2,1},{3,2},{4,3},{5,4},{6,5},{7,6},{8,7},{9,8},{10,9},{11,1... | collective-permute-start | bytes 393224 | tf_op jit(solution)/shard_map/ppermute | solution.py:39
  9.1 1.0 fusion.148
  10.1 0.8 slice_bitcast_fusion.13
  10.9 0.8 convert_element_type.71
  11.7 0.3 cosine_multiply_fusion
  11.9 0.8 broadcast_multiply_fusion
  12.7 0.2 multiply_multiply_fusion
  13.0 1.8 %pad_maximum_fusion.coef_ref = f32[3,16,16384]{2,1,0:T(8,128)} fusion(f32[1,16,16384]{2,1,0:T(8,128)S(1)} %get-tuple-element.59, f32[1,16,16384]{2,1,0:T(8,128)S(1)} %get-tuple-element.60, f32[1,16,16384]{2,1,0:T(8,128)S(1)} %broadcast_multiply_fusion), kind=kLoop, calls=%fused_computation | loop fusion | flops 1572864 | bytes 6291456 | tf_op jit(solution)/shard_map/stack | solution.py:160
  15.8 0.3 negate_convert_fusion
  16.1 3.0 %collective-permute-done.1.below_ref = bf16[4,1,16384]{2,1,0:T(2,128)(2,1)S(1)} collective-permute-done((bf16[4,1,16384]{2,1,0:T(2,128)(2,1)S(1)}, bf16[4,1,16384]{2,1,0:T(2,128)(2,1)S(1)}, u32[]{:S(2)}, u32[]{:S(2)}) %collective-permute-start.1) | collective-permute-done | bytes 131104 | tf_op jit(solution)/shard_map/ppermute | solution.py:39
  19.1 0.7 copy-done.2
  19.8 29.1 %shard_map.157 = f32[4,1,16384]{2,1,0:T(1,128)} custom-call(f32[1]{0:T(128)S(6)} %div.10.step_ref, s32[1]{0:T(128)S(6)} %copy.161.count_ref, bf16[4,16,16384]{2,1,0:T(8,128)(2,1)} %field_ref.1, bf16[4,1,16384]{2,1,0:T(2,128)(2,1)} %copy-done.1, bf16[4,1,16384]{2,1,0:T(2,128)(2,1)} %copy-done.2, f32[3,16,16384]{2,1,0:T(8,128)} %pad_maximum_fusion.coef_ref), custom_call_target="tpu_custom_call" | custom-call | tf_op jit(solution)/shard_map/pallas_call | solution.py:169
  48.9 1.6 %reduce = f32[4,16384]{1,0:T(4,128)S(1)} reduce(f32[4,1,16384]{2,1,0:T(1,128)} %shard_map.157, f32[]{:T(128)} %constant.378), dimensions={1}, to_apply=%pallas_call.3.reduce_sub_computation | reduce | bytes 524292 | tf_op jit(solution)/shard_map/pallas_call | solution.py:169
  50.5 0.7 reshape.217
  51.2 0.6 reduce_sum.27
  51.9 12.9 %collective-permute-start.2 = (bf16[4,1024]{1,0:T(4,128)(2,1)S(1)}, bf16[4,1024]{1,0:T(4,128)(2,1)S(1)}, u32[]{:S(2)}, u32[]{:S(2)}) collective-permute-start(bf16[4,1024]{1,0:T(4,128)(2,1)S(1)} %multiply_convert_fusion), channel_id=1, source_target_pairs={{0,1},{1,2},{2,3},{3,0},{4,5},{5,6},{6,7},{7,4},{8,9},{9,10},{10,1... | collective-permute-start | bytes 24584 | tf_op jit(solution)/shard_map/ppermute | solution.py:285
  64.7 2.4 %collective-permute-start.4 = (bf16[4,1024]{1,0:T(4,128)(2,1)S(1)}, bf16[4,1024]{1,0:T(4,128)(2,1)S(1)}, u32[]{:S(2)}, u32[]{:S(2)}) collective-permute-start(bf16[4,1024]{1,0:T(4,128)(2,1)S(1)} %multiply_convert_fusion), channel_id=1, source_target_pairs={{0,3},{1,0},{2,1},{3,2},{4,7},{5,4},{6,5},{7,6},{8,11},{9,8},{10,9... | collective-permute-start | bytes 24584 | tf_op jit(solution)/shard_map/ppermute | solution.py:285
  67.2 0.6 convert_dynamic-update-slice_fusion
  67.8 1.5 %collective-permute-done.3 = bf16[4,1024]{1,0:T(4,128)(2,1)S(1)} collective-permute-done((bf16[4,1024]{1,0:T(4,128)(2,1)S(1)}, bf16[4,1024]{1,0:T(4,128)(2,1)S(1)}, u32[]{:S(2)}, u32[]{:S(2)}) %collective-permute-start.3) | collective-permute-done | bytes 8224 | tf_op jit(solution)/shard_map/ppermute | solution.py:285
  69.5 1.1 %collective-permute-done.5 = bf16[4,4,1024]{2,1,0:T(4,128)(2,1)S(1)} collective-permute-done((bf16[4,4,1024]{2,1,0:T(4,128)(2,1)S(1)}, bf16[4,4,1024]{2,1,0:T(4,128)(2,1)S(1)}, u32[]{:S(2)}, u32[]{:S(2)}) %collective-permute-start.5) | collective-permute-done | bytes 32800 | tf_op jit(solution)/shard_map/ppermute | solution.py:285
  70.6 1.5 %collective-permute-start.6 = (bf16[2,4,4,1024]{3,2,1,0:T(4,128)(2,1)S(1)}, bf16[2,4,4,1024]{3,2,1,0:T(4,128)(2,1)S(1)}, u32[]{:S(2)}, u32[]{:S(2)}) collective-permute-start(bf16[2,4,4,1024]{3,2,1,0:T(4,128)(2,1)S(1)} %bitcast_dynamic-update-slice_fusion.4), channel_id=1, source_target_pairs={{0,8},{8,16},{16,24},{24,0},{1,9},{9,17},{17,25},{25,1},{2,10},{10... | collective-permute-start | bytes 196616 | tf_op jit(solution)/shard_map/ppermute | solution.py:285
  72.3 2.8 %collective-permute-start.8 = (bf16[2,4,4,1024]{3,2,1,0:T(4,128)(2,1)S(1)}, bf16[2,4,4,1024]{3,2,1,0:T(4,128)(2,1)S(1)}, u32[]{:S(2)}, u32[]{:S(2)}) collective-permute-start(bf16[2,4,4,1024]{3,2,1,0:T(4,128)(2,1)S(1)} %bitcast_dynamic-update-slice_fusion.4), channel_id=1, source_target_pairs={{0,24},{8,0},{16,8},{24,16},{1,25},{9,1},{17,9},{25,17},{2,26},{10... | collective-permute-start | bytes 196616 | tf_op jit(solution)/shard_map/ppermute | solution.py:285
  75.3 0.6 collective-permute-done.6
  75.9 1.2 %collective-permute-done.7 = bf16[2,4,4,1024]{3,2,1,0:T(4,128)(2,1)S(1)} collective-permute-done((bf16[2,4,4,1024]{3,2,1,0:T(4,128)(2,1)S(1)}, bf16[2,4,4,1024]{3,2,1,0:T(4,128)(2,1)S(1)}, u32[]{:S(2)}, u32[]{:S(2)}) %collective-permute-start.7) | collective-permute-done | bytes 65568 | tf_op jit(solution)/shard_map/ppermute | solution.py:285
  77.3 0.5 fusion.4
  77.8 0.9 fusion.60
  78.7 0.5 fusion.41
  79.3 0.5 fusion.45
  79.8 0.5 fusion.8
  80.4 0.5 fusion.10
  80.9 0.1 pad_maximum_fusion.1
  81.1 0.3 sine_multiply_fusion
  81.4 1.3 %collective-permute-done.9 = f32[64,32,16]{0,1,2:T(8,128)S(1)} collective-permute-done((f32[64,32,16]{0,1,2:T(8,128)S(1)}, f32[64,32,16]{0,1,2:T(8,128)S(1)}, u32[]{:S(2)}, u32[]{:S(2)}) %collective-permute-start.9) | collective-permute-done | bytes 131104 | tf_op jit(solution)/shard_map/ppermute | solution.py:297
  82.8 0.2 copy.112
  83.0 0.2 copy.113
  83.1 2.4 %fusion.3 = (f32[8,32,16]{1,2,0:T(8,128)S(1)}, f32[8,32,16]{1,2,0:T(8,128)S(1)}) fusion(f32[32,32,16]{1,2,0:T(8,128)S(1)} %copy.113, f32[32,32,16]{1,2,0:T(8,128)S(1)} %copy.112, bf16[2,32,8,32,16]{3,4,2,1,0:T(8,128)(2,1)} %param.26), kind=kLoop, calls=%fused_computation.8 | loop fusion | flops 1302528 | bytes 688128 | tf_op jit(solution)/shard_map/reduce_sum | solution.py:251
  85.5 0.6 fusion.76
  86.2 0.7 fusion.66
  86.8 0.7 convolution_subtract_fusion.2
  87.5 0.7 convolution_add_fusion.2
  88.3 0.6 convolution_multiply_fusion
  88.9 0.3 fusion.6
  89.1 1.8 %fusion.34 = bf16[1,16,8,1024]{3,2,1,0:T(8,128)(2,1)} fusion(f32[16,8,1024]{2,1,0:T(8,128)S(1)} %fusion.6), kind=kLoop, calls=%fused_computation.73 | loop fusion | flops 8519680 | bytes 786432 | tf_op jit(solution)/shard_map/broadcast_in_dim | solution.py:395
  91.0 0.3 fusion.35
  91.5 0.3 fusion.71
  91.9 0.3 fusion.73
  92.2 0.3 fusion.12
  92.6 0.3 fusion.14
  92.9 0.2 collective-permute-start.10
  93.1 0.2 constant_dynamic-slice_fusion
  93.3 0.2 constant_dynamic-slice_fusion.1
  93.7 0.7 collective-permute-done.10
  94.3 0.1 constant_dynamic-slice_fusion.3
  94.9 3.1 %collective-permute-start.13 = (f32[48,8,16]{0,1,2:T(8,128)S(1)}, f32[48,8,16]{0,1,2:T(8,128)S(1)}, u32[]{:S(2)}, u32[]{:S(2)}) collective-permute-start(f32[48,8,16]{0,1,2:T(8,128)S(1)} %pad_maximum_fusion.6), channel_id=1, source_target_pairs={{0,24},{8,0},{16,8},{24,16},{1,25},{9,1},{17,9},{25,17},{2,26},{10... | collective-permute-start | bytes 73736 | tf_op jit(solution)/shard_map/ppermute | solution.py:297
  98.4 0.6 collective-permute-start.12
  99.5 0.2 add_bitcast_fusion.3
  99.7 0.6 collective-permute-done.13
  100.5 2.9 %collective-permute-done.12 = f32[48,8,16]{0,1,2:T(8,128)S(1)} collective-permute-done((f32[48,8,16]{0,1,2:T(8,128)S(1)}, f32[48,8,16]{0,1,2:T(8,128)S(1)}, u32[]{:S(2)}, u32[]{:S(2)}) %collective-permute-start.12) | collective-permute-done | bytes 24608 | tf_op jit(solution)/shard_map/ppermute | solution.py:297
  105.1 0.1 add_bitcast_fusion
  105.2 0.1 add_bitcast_fusion.1
  105.4 0.1 add_bitcast_fusion.2
  105.5 1.4 %fusion.17 = f32[2,16,8,8,16]{4,3,2,1,0:T(8,128)} fusion(f32[1,16,8,8,16]{4,3,2,1,0:T(8,128)S(1)} %get-tuple-element.28, f32[1,16,8,8,16]{4,3,2,1,0:T(8,128)S(1)} %get-tuple-element.27, f32[1,16,8,8,16]{4,3,2,1,0:T(8,128)S(1)} %get-tuple-element.26, f32[1,16,8,8,16]{4,3,2,1,0:T(8,128)S(1)} %get-tuple-element.25, ...), kind=kLoop, calls=%fused_computation.32 | loop fusion | flops 262144 | bytes 655360 | tf_op jit(solution)/shard_map/div | solution.py:409
  (84 shorter events, 4.6 us)
Async XLA Ops:
  0.6 88.2 %copy-start = (bf16[32,8]{0,1:T(8,128)(2,1)S(1)}, bf16[32,8]{0,1:T(8,128)(2,1)}, u32[]{:S(2)}) copy-start(bf16[32,8]{0,1:T(8,128)(2,1)} %param.24) | copy-start | bytes 1540
  2.6 13.4 %collective-permute-start = (bf16[4,1,16384]{2,1,0:T(2,128)(2,1)S(1)}, bf16[4,1,16384]{2,1,0:T(2,128)(2,1)S(1)}, u32[]{:S(2)}, u32[]{:S(2)}) collective-permute-start(bf16[4,1,16384]{2,1,0:T(2,128)(2,1)S(1)} %get-tuple-element.8), channel_id=1, source_target_pairs={{0,1},{1,2},{2,3},{3,4},{4,5},{5,6},{6,7},{7,8},{8,9},{9,10},{10,1... | collective-permute-start | bytes 393224 | tf_op jit(solution)/shard_map/ppermute | solution.py:38
  5.7 13.4 %collective-permute-start.1 = (bf16[4,1,16384]{2,1,0:T(2,128)(2,1)S(1)}, bf16[4,1,16384]{2,1,0:T(2,128)(2,1)S(1)}, u32[]{:S(2)}, u32[]{:S(2)}) collective-permute-start(bf16[4,1,16384]{2,1,0:T(2,128)(2,1)S(1)} %get-tuple-element.7), channel_id=1, source_target_pairs={{1,0},{2,1},{3,2},{4,3},{5,4},{6,5},{7,6},{8,7},{9,8},{10,9},{11,1... | collective-permute-start | bytes 393224 | tf_op jit(solution)/shard_map/ppermute | solution.py:39
  13.0 1.9 %copy-start.6 = (s32[32]{0:T(128)S(1)}, s32[32]{0:T(128)}, u32[]{:S(2)}) copy-start(s32[32]{0:T(128)} %param.20) | copy-start | bytes 388
  16.0 3.0 %copy-start.1 = (bf16[4,1,16384]{2,1,0:T(2,128)(2,1)}, bf16[4,1,16384]{2,1,0:T(2,128)(2,1)S(1)}, u32[]{:S(2)}) copy-start(bf16[4,1,16384]{2,1,0:T(2,128)(2,1)S(1)} %collective-permute-done.above_ref) | copy-start | bytes 393220
  19.1 0.7 copy-start.2
  51.2 26.0 %copy-start.3 = (bf16[1,16,4,1024]{3,2,1,0:T(4,128)(2,1)S(1)}, bf16[1,16,4,1024]{3,2,1,0:T(4,128)(2,1)}, u32[]{:S(2)}) copy-start(bf16[1,16,4,1024]{3,2,1,0:T(4,128)(2,1)} %param.21) | copy-start | bytes 393220
  51.2 26.0 %copy-start.4 = (bf16[4,32]{1,0:T(4,128)(2,1)S(1)}, bf16[4,32]{1,0:T(4,128)(2,1)}, u32[]{:S(2)}) copy-start(bf16[4,32]{1,0:T(4,128)(2,1)} %param.22) | copy-start | bytes 772
  51.2 26.0 %copy-start.5 = (f32[32]{0:T(128)S(1)}, f32[32]{0:T(128)}, u32[]{:S(2)}) copy-start(f32[32]{0:T(128)} %param.23) | copy-start | bytes 388
  51.9 15.9 %collective-permute-start.2 = (bf16[4,1024]{1,0:T(4,128)(2,1)S(1)}, bf16[4,1024]{1,0:T(4,128)(2,1)S(1)}, u32[]{:S(2)}, u32[]{:S(2)}) collective-permute-start(bf16[4,1024]{1,0:T(4,128)(2,1)S(1)} %multiply_convert_fusion), channel_id=1, source_target_pairs={{0,1},{1,2},{2,3},{3,0},{4,5},{5,6},{6,7},{7,4},{8,9},{9,10},{10,1... | collective-permute-start | bytes 24584 | tf_op jit(solution)/shard_map/ppermute | solution.py:285
  64.7 4.5 %collective-permute-start.3 = (bf16[4,1024]{1,0:T(4,128)(2,1)S(1)}, bf16[4,1024]{1,0:T(4,128)(2,1)S(1)}, u32[]{:S(2)}, u32[]{:S(2)}) collective-permute-start(bf16[4,1024]{1,0:T(4,128)(2,1)S(1)} %multiply_convert_fusion), channel_id=1, source_target_pairs={{0,2},{1,3},{2,0},{3,1},{4,6},{5,7},{6,4},{7,5},{8,10},{9,11},{10,... | collective-permute-start | bytes 24584 | tf_op jit(solution)/shard_map/ppermute | solution.py:285
  64.7 4.6 %collective-permute-start.4 = (bf16[4,1024]{1,0:T(4,128)(2,1)S(1)}, bf16[4,1024]{1,0:T(4,128)(2,1)S(1)}, u32[]{:S(2)}, u32[]{:S(2)}) collective-permute-start(bf16[4,1024]{1,0:T(4,128)(2,1)S(1)} %multiply_convert_fusion), channel_id=1, source_target_pairs={{0,3},{1,0},{2,1},{3,2},{4,7},{5,4},{6,5},{7,6},{8,11},{9,8},{10,9... | collective-permute-start | bytes 24584 | tf_op jit(solution)/shard_map/ppermute | solution.py:285
  69.3 1.3 %collective-permute-start.5 = (bf16[4,4,1024]{2,1,0:T(4,128)(2,1)S(1)}, bf16[4,4,1024]{2,1,0:T(4,128)(2,1)S(1)}, u32[]{:S(2)}, u32[]{:S(2)}) collective-permute-start(bf16[4,4,1024]{2,1,0:T(4,128)(2,1)S(1)} %bitcast_dynamic-update-slice_fusion.6), channel_id=1, source_target_pairs={{0,4},{4,0},{1,5},{5,1},{2,6},{6,2},{3,7},{7,3},{8,12},{12,8},{9,1... | collective-permute-start | bytes 98312 | tf_op jit(solution)/shard_map/ppermute | solution.py:285
  70.6 5.3 %collective-permute-start.6 = (bf16[2,4,4,1024]{3,2,1,0:T(4,128)(2,1)S(1)}, bf16[2,4,4,1024]{3,2,1,0:T(4,128)(2,1)S(1)}, u32[]{:S(2)}, u32[]{:S(2)}) collective-permute-start(bf16[2,4,4,1024]{3,2,1,0:T(4,128)(2,1)S(1)} %bitcast_dynamic-update-slice_fusion.4), channel_id=1, source_target_pairs={{0,8},{8,16},{16,24},{24,0},{1,9},{9,17},{17,25},{25,1},{2,10},{10... | collective-permute-start | bytes 196616 | tf_op jit(solution)/shard_map/ppermute | solution.py:285
  72.2 5.0 %collective-permute-start.7 = (bf16[2,4,4,1024]{3,2,1,0:T(4,128)(2,1)S(1)}, bf16[2,4,4,1024]{3,2,1,0:T(4,128)(2,1)S(1)}, u32[]{:S(2)}, u32[]{:S(2)}) collective-permute-start(bf16[2,4,4,1024]{3,2,1,0:T(4,128)(2,1)S(1)} %bitcast_dynamic-update-slice_fusion.4), channel_id=1, source_target_pairs={{0,16},{8,24},{16,0},{24,8},{1,17},{9,25},{17,1},{25,9},{2,18},{10... | collective-permute-start | bytes 196616 | tf_op jit(solution)/shard_map/ppermute | solution.py:285
  72.3 4.9 %collective-permute-start.8 = (bf16[2,4,4,1024]{3,2,1,0:T(4,128)(2,1)S(1)}, bf16[2,4,4,1024]{3,2,1,0:T(4,128)(2,1)S(1)}, u32[]{:S(2)}, u32[]{:S(2)}) collective-permute-start(bf16[2,4,4,1024]{3,2,1,0:T(4,128)(2,1)S(1)} %bitcast_dynamic-update-slice_fusion.4), channel_id=1, source_target_pairs={{0,24},{8,0},{16,8},{24,16},{1,25},{9,1},{17,9},{25,17},{2,26},{10... | collective-permute-start | bytes 196616 | tf_op jit(solution)/shard_map/ppermute | solution.py:285
  81.0 1.6 %collective-permute-start.9 = (f32[64,32,16]{0,1,2:T(8,128)S(1)}, f32[64,32,16]{0,1,2:T(8,128)S(1)}, u32[]{:S(2)}, u32[]{:S(2)}) collective-permute-start(f32[64,32,16]{0,1,2:T(8,128)S(1)} %pad_maximum_fusion.1), channel_id=1, source_target_pairs={{0,4},{4,0},{1,5},{5,1},{2,6},{6,2},{3,7},{7,3},{8,12},{12,8},{9,1... | collective-permute-start | bytes 393224 | tf_op jit(solution)/shard_map/ppermute | solution.py:297
  83.1 5.7 %copy-start.7 = (f32[8]{0:T(128)S(1)}, f32[8]{0:T(128)}, u32[]{:S(2)}) copy-start(f32[8]{0:T(128)} %param.25) | copy-start | bytes 100
  86.8 4.1 %copy-start.8 = (bf16[1,16,8,1024]{3,2,1,0:T(8,128)(2,1)S(1)}, bf16[1,16,8,1024]{3,2,1,0:T(8,128)(2,1)}, u32[]{:S(2)}) copy-start(bf16[1,16,8,1024]{3,2,1,0:T(8,128)(2,1)} %param.27) | copy-start | bytes 786436
  92.9 1.4 %collective-permute-start.10 = (f32[16,32,16]{1,2,0:T(8,128)S(1)}, f32[16,32,16]{1,2,0:T(8,128)S(1)}, u32[]{:S(2)}, u32[]{:S(2)}) collective-permute-start(f32[16,32,16]{1,2,0:T(8,128)S(1)} %pad_maximum_fusion.2), channel_id=1, source_target_pairs={{0,4},{4,0},{1,5},{5,1},{2,6},{6,2},{3,7},{7,3},{8,12},{12,8},{9,1... | collective-permute-start | bytes 98312 | tf_op jit(solution)/shard_map/ppermute | solution.py:297
  94.9 5.4 %collective-permute-start.13 = (f32[48,8,16]{0,1,2:T(8,128)S(1)}, f32[48,8,16]{0,1,2:T(8,128)S(1)}, u32[]{:S(2)}, u32[]{:S(2)}) collective-permute-start(f32[48,8,16]{0,1,2:T(8,128)S(1)} %pad_maximum_fusion.6), channel_id=1, source_target_pairs={{0,24},{8,0},{16,8},{24,16},{1,25},{9,1},{17,9},{25,17},{2,26},{10... | collective-permute-start | bytes 73736 | tf_op jit(solution)/shard_map/ppermute | solution.py:297
  98.4 5.0 %collective-permute-start.12 = (f32[48,8,16]{0,1,2:T(8,128)S(1)}, f32[48,8,16]{0,1,2:T(8,128)S(1)}, u32[]{:S(2)}, u32[]{:S(2)}) collective-permute-start(f32[48,8,16]{0,1,2:T(8,128)S(1)} %pad_maximum_fusion.5), channel_id=1, source_target_pairs={{0,16},{8,24},{16,0},{24,8},{1,17},{9,25},{17,1},{25,9},{2,18},{10... | collective-permute-start | bytes 73736 | tf_op jit(solution)/shard_map/ppermute | solution.py:297
  99.3 5.2 %collective-permute-start.11 = (f32[48,8,16]{0,1,2:T(8,128)S(1)}, f32[48,8,16]{0,1,2:T(8,128)S(1)}, u32[]{:S(2)}, u32[]{:S(2)}) collective-permute-start(f32[48,8,16]{0,1,2:T(8,128)S(1)} %pad_maximum_fusion.4), channel_id=1, source_target_pairs={{0,8},{8,16},{16,24},{24,0},{1,9},{9,17},{17,25},{25,1},{2,10},{10... | collective-permute-start | bytes 73736 | tf_op jit(solution)/shard_map/ppermute | solution.py:297

commit v8 on v7

--- a/solution.py
+++ b/solution.py
@@ -65,8 +65,8 @@
     return lax.fori_loop(jnp.zeros((), jnp.int32), substeps, advance, slab_rows)
 
 
-CHUNK = 512
-UNROLL = 4
+CHUNK = 1024
+UNROLL = 8
 
 
 def solve_kernel(

time: 108 us -> 95.8 us (0.89); the launches traced: 107 us -> 95.9 us
  Pallas kernels: 29.1 us -> 12.9 us
  starting transfers between devices: 30.5 us -> 34.5 us
  waiting for transfers between devices: 13 us -> 14.1 us
    pallas_call x1, Pallas kernels: 29.1 us -> 12.9 us  [solve_rows(): pl.pallas_call(solve_kernel, out_shape=jax.ShapeDtypeStruct((tracers, 1,...]
    ppermute x7, starting transfers between devices: 19.9 us -> 23.9 us  [gather_along(): lax.ppermute(block, axis, [(i, (i + shift) % count) for i in range(count)])]
    ppermute x7, waiting for transfers between devices: 4.48 us -> 5.64 us  [gather_along(): lax.ppermute(block, axis, [(i, (i + shift) % count) for i in range(count)])]
  transfers between devices with their start and end apart: 14 -> 14, of which waited for: 10 -> 10; matrix products, arithmetic and copies ran while one was open for 9% -> 10% of each run, Pallas kernels for 0% -> 0%
where the time goes in v8:
time: 95.8 us; the launch traced here: 95.9 us
  starting transfers between devices  34.5 us (36%)
  other arithmetic  14.4 us (15%)
  waiting for transfers between devices  14.1 us (15%)
  Pallas kernels  12.9 us (13%)
  local copies, waits for them, and re-layouts  9.3 us (10%)
  matrix products  8.62 us (9%)
  between operations  2.05 us (2%)
    ppermute x7, starting transfers between devices, gather_along(): lax.ppermute(block, axis, [(i, (i + shift) % count) for i in range(count)])  23.9 us
    pallas_call x1, Pallas kernels, solve_rows(): pl.pallas_call(solve_kernel, out_shape=jax.ShapeDtypeStruct((tracers, 1,...  12.9 us
    ppermute x7, waiting for transfers between devices, gather_along(): lax.ppermute(block, axis, [(i, (i + shift) % count) for i in range(count)])  5.64 us
    ppermute x5, waiting for transfers between devices, packed_ppermute(): packed = lax.ppermute(jnp.concatenate(parts, axis=0), axis, perm)  5.47 us
    ppermute x5, starting transfers between devices, packed_ppermute(): packed = lax.ppermute(jnp.concatenate(parts, axis=0), axis, perm)  4.12 us
    ppermute x1, starting transfers between devices, halo_rows(): below = lax.ppermute(block[:, :1], axis, backward)  3.42 us
    ppermute x1, starting transfers between devices, halo_rows(): above = lax.ppermute(block[:, -1:], axis, forward)  3.08 us
    ppermute x1, waiting for transfers between devices, halo_rows(): below = lax.ppermute(block[:, :1], axis, backward)  3.01 us
  transfers between devices with their start and end apart: 14, of which 10 were waited for; matrix products, arithmetic and copies ran while one was open for 10% of the time, Pallas kernels for 0%

profile of v8, /device:TPU:0, one launch (start us, length us, event | category | flops | bytes accessed | tf_op | source)
XLA Modules:
  0.0 95.9 jit_solution(17520449840766357846)
XLA Ops:
  0.6 2.0 %fusion.145 = (bf16[4,1,16384]{2,1,0:T(2,128)(2,1)S(1)}, bf16[4,1,16384]{2,1,0:T(2,128)(2,1)S(1)}) fusion(bf16[4,16,16384]{2,1,0:T(8,128)(2,1)} %field_ref.1), kind=kLoop, calls=%fused_computation.240 | loop fusion | bytes 524288 | tf_op jit(solution)/shard_map/slice | solution.py:39
  2.6 3.1 %collective-permute-start = (bf16[4,1,16384]{2,1,0:T(2,128)(2,1)S(1)}, bf16[4,1,16384]{2,1,0:T(2,128)(2,1)S(1)}, u32[]{:S(2)}, u32[]{:S(2)}) collective-permute-start(bf16[4,1,16384]{2,1,0:T(2,128)(2,1)S(1)} %get-tuple-element.8), channel_id=1, source_target_pairs={{0,1},{1,2},{2,3},{3,4},{4,5},{5,6},{6,7},{7,8},{8,9},{9,10},{10,1... | collective-permute-start | bytes 393224 | tf_op jit(solution)/shard_map/ppermute | solution.py:38
  5.7 3.4 %collective-permute-start.1 = (bf16[4,1,16384]{2,1,0:T(2,128)(2,1)S(1)}, bf16[4,1,16384]{2,1,0:T(2,128)(2,1)S(1)}, u32[]{:S(2)}, u32[]{:S(2)}) collective-permute-start(bf16[4,1,16384]{2,1,0:T(2,128)(2,1)S(1)} %get-tuple-element.7), channel_id=1, source_target_pairs={{1,0},{2,1},{3,2},{4,3},{5,4},{6,5},{7,6},{8,7},{9,8},{10,9},{11,1... | collective-permute-start | bytes 393224 | tf_op jit(solution)/shard_map/ppermute | solution.py:39
  9.1 1.0 %fusion.148 = (f32[1,16384]{1,0:T(1,128)S(1)}, f32[1,16384]{1,0:T(1,128)S(1)}) fusion(bf16[2,16384]{1,0:T(2,128)(2,1)} %param.19), kind=kLoop, calls=%fused_computation.243 | loop fusion | bytes 262144 | tf_op jit(solution)/shard_map/slice | solution.py:163
  10.1 0.8 slice_bitcast_fusion.13
  10.9 0.8 convert_element_type.71
  11.7 0.3 cosine_multiply_fusion
  11.9 0.8 broadcast_multiply_fusion
  12.7 0.2 multiply_multiply_fusion
  13.0 1.8 %pad_maximum_fusion.coef_ref = f32[3,16,16384]{2,1,0:T(8,128)} fusion(f32[1,16,16384]{2,1,0:T(8,128)S(1)} %get-tuple-element.59, f32[1,16,16384]{2,1,0:T(8,128)S(1)} %get-tuple-element.60, f32[1,16,16384]{2,1,0:T(8,128)S(1)} %broadcast_multiply_fusion), kind=kLoop, calls=%fused_computation | loop fusion | flops 1572864 | bytes 6291456 | tf_op jit(solution)/shard_map/stack | solution.py:160
  15.8 0.3 negate_convert_fusion
  16.1 3.0 %collective-permute-done.1.below_ref = bf16[4,1,16384]{2,1,0:T(2,128)(2,1)S(1)} collective-permute-done((bf16[4,1,16384]{2,1,0:T(2,128)(2,1)S(1)}, bf16[4,1,16384]{2,1,0:T(2,128)(2,1)S(1)}, u32[]{:S(2)}, u32[]{:S(2)}) %collective-permute-start.1) | collective-permute-done | bytes 131104 | tf_op jit(solution)/shard_map/ppermute | solution.py:39
  19.1 0.7 copy-done.2
  19.8 12.9 %shard_map.157 = f32[4,1,16384]{2,1,0:T(1,128)} custom-call(f32[1]{0:T(128)S(6)} %div.10.step_ref, s32[1]{0:T(128)S(6)} %copy.161.count_ref, bf16[4,16,16384]{2,1,0:T(8,128)(2,1)} %field_ref.1, bf16[4,1,16384]{2,1,0:T(2,128)(2,1)} %copy-done.1, bf16[4,1,16384]{2,1,0:T(2,128)(2,1)} %copy-done.2, f32[3,16,16384]{2,1,0:T(8,128)} %pad_maximum_fusion.coef_ref), custom_call_target="tpu_custom_call" | custom-call | tf_op jit(solution)/shard_map/pallas_call | solution.py:169
  32.7 1.6 %reduce = f32[4,16384]{1,0:T(4,128)S(1)} reduce(f32[4,1,16384]{2,1,0:T(1,128)} %shard_map.157, f32[]{:T(128)} %constant.378), dimensions={1}, to_apply=%pallas_call.3.reduce_sub_computation | reduce | bytes 524292 | tf_op jit(solution)/shard_map/pallas_call | solution.py:169
  34.4 0.7 reshape.217
  35.1 0.6 reduce_sum.27
  35.7 1.6 %collective-permute-start.2 = (bf16[4,1024]{1,0:T(4,128)(2,1)S(1)}, bf16[4,1024]{1,0:T(4,128)(2,1)S(1)}, u32[]{:S(2)}, u32[]{:S(2)}) collective-permute-start(bf16[4,1024]{1,0:T(4,128)(2,1)S(1)} %multiply_convert_fusion), channel_id=1, source_target_pairs={{0,1},{1,2},{2,3},{3,0},{4,5},{5,6},{6,7},{7,4},{8,9},{9,10},{10,1... | collective-permute-start | bytes 24584 | tf_op jit(solution)/shard_map/ppermute | solution.py:285
  37.3 9.7 %collective-permute-start.3 = (bf16[4,1024]{1,0:T(4,128)(2,1)S(1)}, bf16[4,1024]{1,0:T(4,128)(2,1)S(1)}, u32[]{:S(2)}, u32[]{:S(2)}) collective-permute-start(bf16[4,1024]{1,0:T(4,128)(2,1)S(1)} %multiply_convert_fusion), channel_id=1, source_target_pairs={{0,2},{1,3},{2,0},{3,1},{4,6},{5,7},{6,4},{7,5},{8,10},{9,11},{10,... | collective-permute-start | bytes 24584 | tf_op jit(solution)/shard_map/ppermute | solution.py:285
  47.0 0.6 convert_dynamic-update-slice_fusion
  47.6 0.4 collective-permute-done.2
  48.1 0.5 collective-permute-done.3
  48.6 2.0 %collective-permute-done.4 = bf16[4,1024]{1,0:T(4,128)(2,1)S(1)} collective-permute-done((bf16[4,1024]{1,0:T(4,128)(2,1)S(1)}, bf16[4,1024]{1,0:T(4,128)(2,1)S(1)}, u32[]{:S(2)}, u32[]{:S(2)}) %collective-permute-start.4) | collective-permute-done | bytes 8224 | tf_op jit(solution)/shard_map/ppermute | solution.py:285
  50.7 5.2 %collective-permute-start.5 = (bf16[4,4,1024]{2,1,0:T(4,128)(2,1)S(1)}, bf16[4,4,1024]{2,1,0:T(4,128)(2,1)S(1)}, u32[]{:S(2)}, u32[]{:S(2)}) collective-permute-start(bf16[4,4,1024]{2,1,0:T(4,128)(2,1)S(1)} %bitcast_dynamic-update-slice_fusion.6), channel_id=1, source_target_pairs={{0,4},{4,0},{1,5},{5,1},{2,6},{6,2},{3,7},{7,3},{8,12},{12,8},{9,1... | collective-permute-start | bytes 98312 | tf_op jit(solution)/shard_map/ppermute | solution.py:285
  55.9 0.8 collective-permute-done.5
  56.8 3.2 %collective-permute-start.6 = (bf16[2,4,4,1024]{3,2,1,0:T(4,128)(2,1)S(1)}, bf16[2,4,4,1024]{3,2,1,0:T(4,128)(2,1)S(1)}, u32[]{:S(2)}, u32[]{:S(2)}) collective-permute-start(bf16[2,4,4,1024]{3,2,1,0:T(4,128)(2,1)S(1)} %bitcast_dynamic-update-slice_fusion.4), channel_id=1, source_target_pairs={{0,8},{8,16},{16,24},{24,0},{1,9},{9,17},{17,25},{25,1},{2,10},{10... | collective-permute-start | bytes 196616 | tf_op jit(solution)/shard_map/ppermute | solution.py:285
  60.0 1.3 %collective-permute-start.7 = (bf16[2,4,4,1024]{3,2,1,0:T(4,128)(2,1)S(1)}, bf16[2,4,4,1024]{3,2,1,0:T(4,128)(2,1)S(1)}, u32[]{:S(2)}, u32[]{:S(2)}) collective-permute-start(bf16[2,4,4,1024]{3,2,1,0:T(4,128)(2,1)S(1)} %bitcast_dynamic-update-slice_fusion.4), channel_id=1, source_target_pairs={{0,16},{8,24},{16,0},{24,8},{1,17},{9,25},{17,1},{25,9},{2,18},{10... | collective-permute-start | bytes 196616 | tf_op jit(solution)/shard_map/ppermute | solution.py:285
  61.3 2.8 %collective-permute-start.8 = (bf16[2,4,4,1024]{3,2,1,0:T(4,128)(2,1)S(1)}, bf16[2,4,4,1024]{3,2,1,0:T(4,128)(2,1)S(1)}, u32[]{:S(2)}, u32[]{:S(2)}) collective-permute-start(bf16[2,4,4,1024]{3,2,1,0:T(4,128)(2,1)S(1)} %bitcast_dynamic-update-slice_fusion.4), channel_id=1, source_target_pairs={{0,24},{8,0},{16,8},{24,16},{1,25},{9,1},{17,9},{25,17},{2,26},{10... | collective-permute-start | bytes 196616 | tf_op jit(solution)/shard_map/ppermute | solution.py:285
  64.4 1.8 %collective-permute-done.8 = bf16[2,4,4,1024]{3,2,1,0:T(4,128)(2,1)S(1)} collective-permute-done((bf16[2,4,4,1024]{3,2,1,0:T(4,128)(2,1)S(1)}, bf16[2,4,4,1024]{3,2,1,0:T(4,128)(2,1)S(1)}, u32[]{:S(2)}, u32[]{:S(2)}) %collective-permute-start.8) | collective-permute-done | bytes 65568 | tf_op jit(solution)/shard_map/ppermute | solution.py:285
  66.3 0.5 fusion.4
  66.8 0.9 fusion.60
  67.8 0.5 fusion.41
  68.3 0.5 fusion.45
  68.8 0.5 fusion.8
  69.4 0.5 fusion.10
  70.1 0.3 sine_multiply_fusion
  70.4 1.3 %collective-permute-done.9 = f32[64,32,16]{0,1,2:T(8,128)S(1)} collective-permute-done((f32[64,32,16]{0,1,2:T(8,128)S(1)}, f32[64,32,16]{0,1,2:T(8,128)S(1)}, u32[]{:S(2)}, u32[]{:S(2)}) %collective-permute-start.9) | collective-permute-done | bytes 131104 | tf_op jit(solution)/shard_map/ppermute | solution.py:297
  71.8 0.2 copy.112
  72.0 0.2 copy.113
  72.2 2.4 %fusion.3 = (f32[8,32,16]{1,2,0:T(8,128)S(1)}, f32[8,32,16]{1,2,0:T(8,128)S(1)}) fusion(f32[32,32,16]{1,2,0:T(8,128)S(1)} %copy.113, f32[32,32,16]{1,2,0:T(8,128)S(1)} %copy.112, bf16[2,32,8,32,16]{3,4,2,1,0:T(8,128)(2,1)} %param.26), kind=kLoop, calls=%fused_computation.8 | loop fusion | flops 1302528 | bytes 688128 | tf_op jit(solution)/shard_map/reduce_sum | solution.py:251
  74.5 0.6 fusion.76
  75.2 0.7 fusion.66
  75.9 0.7 convolution_subtract_fusion.2
  76.5 0.7 convolution_add_fusion.2
  77.3 0.6 convolution_multiply_fusion
  77.9 0.3 fusion.6
  78.2 1.8 %fusion.34 = bf16[1,16,8,1024]{3,2,1,0:T(8,128)(2,1)} fusion(f32[16,8,1024]{2,1,0:T(8,128)S(1)} %fusion.6), kind=kLoop, calls=%fused_computation.73 | loop fusion | flops 8519680 | bytes 786432 | tf_op jit(solution)/shard_map/broadcast_in_dim | solution.py:395
  80.0 0.3 fusion.35
  80.5 0.3 fusion.71
  80.9 0.3 fusion.73
  81.3 0.3 fusion.12
  81.6 0.3 fusion.14
  81.9 0.2 collective-permute-start.10
  82.1 0.2 constant_dynamic-slice_fusion
  82.3 0.2 constant_dynamic-slice_fusion.1
  82.7 0.7 collective-permute-done.10
  83.9 3.1 %collective-permute-start.13 = (f32[48,8,16]{0,1,2:T(8,128)S(1)}, f32[48,8,16]{0,1,2:T(8,128)S(1)}, u32[]{:S(2)}, u32[]{:S(2)}) collective-permute-start(f32[48,8,16]{0,1,2:T(8,128)S(1)} %pad_maximum_fusion.6), channel_id=1, source_target_pairs={{0,24},{8,0},{16,8},{24,16},{1,25},{9,1},{17,9},{25,17},{2,26},{10... | collective-permute-start | bytes 73736 | tf_op jit(solution)/shard_map/ppermute | solution.py:297
  87.4 0.4 collective-permute-start.12
  88.1 0.3 collective-permute-start.11
  88.6 0.2 add_bitcast_fusion.3
  88.7 0.6 collective-permute-done.13
  89.5 2.9 %collective-permute-done.12 = f32[48,8,16]{0,1,2:T(8,128)S(1)} collective-permute-done((f32[48,8,16]{0,1,2:T(8,128)S(1)}, f32[48,8,16]{0,1,2:T(8,128)S(1)}, u32[]{:S(2)}, u32[]{:S(2)}) %collective-permute-start.12) | collective-permute-done | bytes 24608 | tf_op jit(solution)/shard_map/ppermute | solution.py:297
  94.0 0.1 add_bitcast_fusion
  94.5 1.4 %fusion.17 = f32[2,16,8,8,16]{4,3,2,1,0:T(8,128)} fusion(f32[1,16,8,8,16]{4,3,2,1,0:T(8,128)S(1)} %get-tuple-element.28, f32[1,16,8,8,16]{4,3,2,1,0:T(8,128)S(1)} %get-tuple-element.27, f32[1,16,8,8,16]{4,3,2,1,0:T(8,128)S(1)} %get-tuple-element.26, f32[1,16,8,8,16]{4,3,2,1,0:T(8,128)S(1)} %get-tuple-element.25, ...), kind=kLoop, calls=%fused_computation.32 | loop fusion | flops 262144 | bytes 655360 | tf_op jit(solution)/shard_map/div | solution.py:409
  (84 shorter events, 4.8 us)
Async XLA Ops:
  0.6 77.2 %copy-start = (bf16[32,8]{0,1:T(8,128)(2,1)S(1)}, bf16[32,8]{0,1:T(8,128)(2,1)}, u32[]{:S(2)}) copy-start(bf16[32,8]{0,1:T(8,128)(2,1)} %param.24) | copy-start | bytes 1540
  2.6 13.4 %collective-permute-start = (bf16[4,1,16384]{2,1,0:T(2,128)(2,1)S(1)}, bf16[4,1,16384]{2,1,0:T(2,128)(2,1)S(1)}, u32[]{:S(2)}, u32[]{:S(2)}) collective-permute-start(bf16[4,1,16384]{2,1,0:T(2,128)(2,1)S(1)} %get-tuple-element.8), channel_id=1, source_target_pairs={{0,1},{1,2},{2,3},{3,4},{4,5},{5,6},{6,7},{7,8},{8,9},{9,10},{10,1... | collective-permute-start | bytes 393224 | tf_op jit(solution)/shard_map/ppermute | solution.py:38
  5.7 13.4 %collective-permute-start.1 = (bf16[4,1,16384]{2,1,0:T(2,128)(2,1)S(1)}, bf16[4,1,16384]{2,1,0:T(2,128)(2,1)S(1)}, u32[]{:S(2)}, u32[]{:S(2)}) collective-permute-start(bf16[4,1,16384]{2,1,0:T(2,128)(2,1)S(1)} %get-tuple-element.7), channel_id=1, source_target_pairs={{1,0},{2,1},{3,2},{4,3},{5,4},{6,5},{7,6},{8,7},{9,8},{10,9},{11,1... | collective-permute-start | bytes 393224 | tf_op jit(solution)/shard_map/ppermute | solution.py:39
  13.0 1.9 %copy-start.6 = (s32[32]{0:T(128)S(1)}, s32[32]{0:T(128)}, u32[]{:S(2)}) copy-start(s32[32]{0:T(128)} %param.20) | copy-start | bytes 388
  16.0 3.0 %copy-start.1 = (bf16[4,1,16384]{2,1,0:T(2,128)(2,1)}, bf16[4,1,16384]{2,1,0:T(2,128)(2,1)S(1)}, u32[]{:S(2)}) copy-start(bf16[4,1,16384]{2,1,0:T(2,128)(2,1)S(1)} %collective-permute-done.above_ref) | copy-start | bytes 393220
  19.1 0.7 copy-start.2
  35.0 31.2 %copy-start.3 = (bf16[1,16,4,1024]{3,2,1,0:T(4,128)(2,1)S(1)}, bf16[1,16,4,1024]{3,2,1,0:T(4,128)(2,1)}, u32[]{:S(2)}) copy-start(bf16[1,16,4,1024]{3,2,1,0:T(4,128)(2,1)} %param.21) | copy-start | bytes 393220
  35.0 31.2 %copy-start.4 = (bf16[4,32]{1,0:T(4,128)(2,1)S(1)}, bf16[4,32]{1,0:T(4,128)(2,1)}, u32[]{:S(2)}) copy-start(bf16[4,32]{1,0:T(4,128)(2,1)} %param.22) | copy-start | bytes 772
  35.1 31.2 %copy-start.5 = (f32[32]{0:T(128)S(1)}, f32[32]{0:T(128)}, u32[]{:S(2)}) copy-start(f32[32]{0:T(128)} %param.23) | copy-start | bytes 388
  35.7 12.4 %collective-permute-start.2 = (bf16[4,1024]{1,0:T(4,128)(2,1)S(1)}, bf16[4,1024]{1,0:T(4,128)(2,1)S(1)}, u32[]{:S(2)}, u32[]{:S(2)}) collective-permute-start(bf16[4,1024]{1,0:T(4,128)(2,1)S(1)} %multiply_convert_fusion), channel_id=1, source_target_pairs={{0,1},{1,2},{2,3},{3,0},{4,5},{5,6},{6,7},{7,4},{8,9},{9,10},{10,1... | collective-permute-start | bytes 24584 | tf_op jit(solution)/shard_map/ppermute | solution.py:285
  37.3 11.3 %collective-permute-start.3 = (bf16[4,1024]{1,0:T(4,128)(2,1)S(1)}, bf16[4,1024]{1,0:T(4,128)(2,1)S(1)}, u32[]{:S(2)}, u32[]{:S(2)}) collective-permute-start(bf16[4,1024]{1,0:T(4,128)(2,1)S(1)} %multiply_convert_fusion), channel_id=1, source_target_pairs={{0,2},{1,3},{2,0},{3,1},{4,6},{5,7},{6,4},{7,5},{8,10},{9,11},{10,... | collective-permute-start | bytes 24584 | tf_op jit(solution)/shard_map/ppermute | solution.py:285
  47.0 3.7 %collective-permute-start.4 = (bf16[4,1024]{1,0:T(4,128)(2,1)S(1)}, bf16[4,1024]{1,0:T(4,128)(2,1)S(1)}, u32[]{:S(2)}, u32[]{:S(2)}) collective-permute-start(bf16[4,1024]{1,0:T(4,128)(2,1)S(1)} %multiply_convert_fusion), channel_id=1, source_target_pairs={{0,3},{1,0},{2,1},{3,2},{4,7},{5,4},{6,5},{7,6},{8,11},{9,8},{10,9... | collective-permute-start | bytes 24584 | tf_op jit(solution)/shard_map/ppermute | solution.py:285
  50.7 6.1 %collective-permute-start.5 = (bf16[4,4,1024]{2,1,0:T(4,128)(2,1)S(1)}, bf16[4,4,1024]{2,1,0:T(4,128)(2,1)S(1)}, u32[]{:S(2)}, u32[]{:S(2)}) collective-permute-start(bf16[4,4,1024]{2,1,0:T(4,128)(2,1)S(1)} %bitcast_dynamic-update-slice_fusion.6), channel_id=1, source_target_pairs={{0,4},{4,0},{1,5},{5,1},{2,6},{6,2},{3,7},{7,3},{8,12},{12,8},{9,1... | collective-permute-start | bytes 98312 | tf_op jit(solution)/shard_map/ppermute | solution.py:285
  56.8 7.5 %collective-permute-start.6 = (bf16[2,4,4,1024]{3,2,1,0:T(4,128)(2,1)S(1)}, bf16[2,4,4,1024]{3,2,1,0:T(4,128)(2,1)S(1)}, u32[]{:S(2)}, u32[]{:S(2)}) collective-permute-start(bf16[2,4,4,1024]{3,2,1,0:T(4,128)(2,1)S(1)} %bitcast_dynamic-update-slice_fusion.4), channel_id=1, source_target_pairs={{0,8},{8,16},{16,24},{24,0},{1,9},{9,17},{17,25},{25,1},{2,10},{10... | collective-permute-start | bytes 196616 | tf_op jit(solution)/shard_map/ppermute | solution.py:285
  60.0 4.3 %collective-permute-start.7 = (bf16[2,4,4,1024]{3,2,1,0:T(4,128)(2,1)S(1)}, bf16[2,4,4,1024]{3,2,1,0:T(4,128)(2,1)S(1)}, u32[]{:S(2)}, u32[]{:S(2)}) collective-permute-start(bf16[2,4,4,1024]{3,2,1,0:T(4,128)(2,1)S(1)} %bitcast_dynamic-update-slice_fusion.4), channel_id=1, source_target_pairs={{0,16},{8,24},{16,0},{24,8},{1,17},{9,25},{17,1},{25,9},{2,18},{10... | collective-permute-start | bytes 196616 | tf_op jit(solution)/shard_map/ppermute | solution.py:285
  61.3 4.9 %collective-permute-start.8 = (bf16[2,4,4,1024]{3,2,1,0:T(4,128)(2,1)S(1)}, bf16[2,4,4,1024]{3,2,1,0:T(4,128)(2,1)S(1)}, u32[]{:S(2)}, u32[]{:S(2)}) collective-permute-start(bf16[2,4,4,1024]{3,2,1,0:T(4,128)(2,1)S(1)} %bitcast_dynamic-update-slice_fusion.4), channel_id=1, source_target_pairs={{0,24},{8,0},{16,8},{24,16},{1,25},{9,1},{17,9},{25,17},{2,26},{10... | collective-permute-start | bytes 196616 | tf_op jit(solution)/shard_map/ppermute | solution.py:285
  70.1 1.6 %collective-permute-start.9 = (f32[64,32,16]{0,1,2:T(8,128)S(1)}, f32[64,32,16]{0,1,2:T(8,128)S(1)}, u32[]{:S(2)}, u32[]{:S(2)}) collective-permute-start(f32[64,32,16]{0,1,2:T(8,128)S(1)} %pad_maximum_fusion.1), channel_id=1, source_target_pairs={{0,4},{4,0},{1,5},{5,1},{2,6},{6,2},{3,7},{7,3},{8,12},{12,8},{9,1... | collective-permute-start | bytes 393224 | tf_op jit(solution)/shard_map/ppermute | solution.py:297
  72.1 5.7 %copy-start.7 = (f32[8]{0:T(128)S(1)}, f32[8]{0:T(128)}, u32[]{:S(2)}) copy-start(f32[8]{0:T(128)} %param.25) | copy-start | bytes 100
  75.9 4.1 %copy-start.8 = (bf16[1,16,8,1024]{3,2,1,0:T(8,128)(2,1)S(1)}, bf16[1,16,8,1024]{3,2,1,0:T(8,128)(2,1)}, u32[]{:S(2)}) copy-start(bf16[1,16,8,1024]{3,2,1,0:T(8,128)(2,1)} %param.27) | copy-start | bytes 786436
  81.9 1.4 %collective-permute-start.10 = (f32[16,32,16]{1,2,0:T(8,128)S(1)}, f32[16,32,16]{1,2,0:T(8,128)S(1)}, u32[]{:S(2)}, u32[]{:S(2)}) collective-permute-start(f32[16,32,16]{1,2,0:T(8,128)S(1)} %pad_maximum_fusion.2), channel_id=1, source_target_pairs={{0,4},{4,0},{1,5},{5,1},{2,6},{6,2},{3,7},{7,3},{8,12},{12,8},{9,1... | collective-permute-start | bytes 98312 | tf_op jit(solution)/shard_map/ppermute | solution.py:297
  83.9 5.4 %collective-permute-start.13 = (f32[48,8,16]{0,1,2:T(8,128)S(1)}, f32[48,8,16]{0,1,2:T(8,128)S(1)}, u32[]{:S(2)}, u32[]{:S(2)}) collective-permute-start(f32[48,8,16]{0,1,2:T(8,128)S(1)} %pad_maximum_fusion.6), channel_id=1, source_target_pairs={{0,24},{8,0},{16,8},{24,16},{1,25},{9,1},{17,9},{25,17},{2,26},{10... | collective-permute-start | bytes 73736 | tf_op jit(solution)/shard_map/ppermute | solution.py:297
  87.4 5.0 %collective-permute-start.12 = (f32[48,8,16]{0,1,2:T(8,128)S(1)}, f32[48,8,16]{0,1,2:T(8,128)S(1)}, u32[]{:S(2)}, u32[]{:S(2)}) collective-permute-start(f32[48,8,16]{0,1,2:T(8,128)S(1)} %pad_maximum_fusion.5), channel_id=1, source_target_pairs={{0,16},{8,24},{16,0},{24,8},{1,17},{9,25},{17,1},{25,9},{2,18},{10... | collective-permute-start | bytes 73736 | tf_op jit(solution)/shard_map/ppermute | solution.py:297
  88.1 5.3 %collective-permute-start.11 = (f32[48,8,16]{0,1,2:T(8,128)S(1)}, f32[48,8,16]{0,1,2:T(8,128)S(1)}, u32[]{:S(2)}, u32[]{:S(2)}) collective-permute-start(f32[48,8,16]{0,1,2:T(8,128)S(1)} %pad_maximum_fusion.4), channel_id=1, source_target_pairs={{0,8},{8,16},{16,24},{24,0},{1,9},{9,17},{17,25},{25,1},{2,10},{10... | collective-permute-start | bytes 73736 | tf_op jit(solution)/shard_map/ppermute | solution.py:297

commit v9 on v5

--- a/solution.py
+++ b/solution.py
@@ -65,8 +65,8 @@
     return lax.fori_loop(jnp.zeros((), jnp.int32), substeps, advance, slab_rows)
 
 
-CHUNK = 256
-UNROLL = 2
+CHUNK = 2048
+UNROLL = 4
 
 
 def solve_kernel(
@@ -105,10 +105,10 @@
                 right_cells = pltpu.roll(extended, span - 1, 1)[:, 128 : 128 + CHUNK]
                 left_cells = pltpu.roll(extended, 1, 1)[:, 128 : 128 + CHUNK]
                 upper_rows = jnp.where(
-                    row_ids == 0, above_ref[tracer, :, cols], pltpu.roll(current, 1, 0)
+                    row_ids == 0, above_ref[tracer, :, cols].astype(jnp.float32), pltpu.roll(current, 1, 0)
                 )
                 lower_rows = jnp.where(
-                    row_ids == rows - 1, below_ref[tracer, :, cols], pltpu.roll(current, rows - 1, 0)
+                    row_ids == rows - 1, below_ref[tracer, :, cols].astype(jnp.float32), pltpu.roll(current, rows - 1, 0)
                 )
                 change = diffusion * (
                     right_cells + left_cells + upper_rows + lower_rows - 4.0 * current
@@ -178,8 +178,8 @@
         step,
         substeps.reshape(1),
         field,
-        above_row.astype(jnp.float32),
-        below_row.astype(jnp.float32),
+        above_row,
+        below_row,
         coefficients,
     )
 
@@ -292,13 +292,12 @@
 
 
 def packed_ppermute(parts, axis, perm):
-    flat = jnp.concatenate([part.reshape(-1) for part in parts])
-    flat = lax.ppermute(flat, axis, perm)
+    packed = lax.ppermute(jnp.concatenate(parts, axis=0), axis, perm)
     result = []
     offset = 0
     for part in parts:
-        result.append(flat[offset : offset + part.size].reshape(part.shape))
-        offset += part.size
+        result.append(lax.slice_in_dim(packed, offset, offset + part.shape[0], axis=0))
+        offset += part.shape[0]
     return tuple(result)
 
 
@@ -376,7 +375,7 @@
         column_part[:, :, :MODES], column_part[:, :, MODES:], cosine_table, sine_table
     )
     mode_real, mode_imag = pair_sum((part_real * norm_scale, part_imag * norm_scale), "mem")
-    mixed_real, mixed_imag = mix_modes(spectral_weight.astype(jnp.float32), mode_real, mode_imag)
+    mixed_real, mixed_imag = mix_modes(spectral_weight, mode_real, mode_imag)
     spatial = (
         jnp.einsum(
             "yok,kx->yox",

time: 116 us -> 93.1 us (0.80)
  starting transfers between devices: 45.4 us -> 19.1 us
  Pallas kernels: 14 us -> 26.1 us
  other arithmetic: 19.9 us -> 14.4 us
  local copies, waits for them, and re-layouts: 13.4 us -> 9.29 us
    ppermute x7, starting transfers between devices: 35.7 us -> 8.63 us  [gather_along(): lax.ppermute(block, axis, [(i, (i + shift) % count) for i in range(count)])]
    pallas_call x1, Pallas kernels: 14 us -> 26.1 us  [solve_rows(): pl.pallas_call(solve_kernel, out_shape=jax.ShapeDtypeStruct((tracers, 1,...]
    convert_element_type x3 -> x0, other arithmetic: 5.42 us -> none  [the longest x1 2.52 us: body(): spectral_weight.astype(jnp.float32)]
    reshape x36 -> x0, local copies, waits for them, and re-layouts: 4.03 us -> none  [the longest x20 2.48 us: packed_ppermute(): result.append(flat[offset:offset + part.size].reshape(part.shape))]
    ppermute x1, waiting for transfers between devices: 0.01 us -> 3.01 us  [halo_rows(): below = lax.ppermute(block[:, :1], axis, backward)]
    ppermute x7, waiting for transfers between devices: 8.18 us -> 5.28 us  [gather_along(): lax.ppermute(block, axis, [(i, (i + shift) % count) for i in range(count)])]
    slice x8 -> x18, local copies, waits for them, and re-layouts: 0.03 us -> 1.68 us  [packed_ppermute(): lax.slice_in_dim(packed, offset, offset + part.shape[0], axis=0)]
    mul x4 -> x0, local copies, waits for them, and re-layouts: 1.2 us -> none  [the longest x1 0.51 us: body(): part_imag * norm_scale]
  transfers between devices with their start and end apart: 14 -> 14, of which waited for: 10 -> 11; matrix products, arithmetic and copies ran while one was open for 13% -> 10% of each run, Pallas kernels for 0% -> 0%
where the time goes in v9:
time: 93.1 us; the launch traced here: 92.7 us
  Pallas kernels  26.1 us (28%)
  starting transfers between devices  19.1 us (21%)
  other arithmetic  14.4 us (15%)
  waiting for transfers between devices  13.2 us (14%)
  local copies, waits for them, and re-layouts  9.29 us (10%)
  matrix products  8.62 us (9%)
  between operations  2.07 us (2%)
    pallas_call x1, Pallas kernels, solve_rows(): pl.pallas_call(solve_kernel, out_shape=jax.ShapeDtypeStruct((tracers, 1,...  26.1 us
    ppermute x7, starting transfers between devices, gather_along(): lax.ppermute(block, axis, [(i, (i + shift) % count) for i in range(count)])  8.63 us
    ppermute x7, waiting for transfers between devices, gather_along(): lax.ppermute(block, axis, [(i, (i + shift) % count) for i in range(count)])  5.28 us
    ppermute x5, waiting for transfers between devices, packed_ppermute(): packed = lax.ppermute(jnp.concatenate(parts, axis=0), axis, perm)  4.9 us
    ppermute x5, starting transfers between devices, packed_ppermute(): packed = lax.ppermute(jnp.concatenate(parts, axis=0), axis, perm)  3.98 us
    ppermute x1, starting transfers between devices, halo_rows(): below = lax.ppermute(block[:, :1], axis, backward)  3.42 us
    ppermute x1, starting transfers between devices, halo_rows(): above = lax.ppermute(block[:, -1:], axis, forward)  3.08 us
    ppermute x1, waiting for transfers between devices, halo_rows(): below = lax.ppermute(block[:, :1], axis, backward)  3.01 us
  transfers between devices with their start and end apart: 14, of which 11 were waited for; matrix products, arithmetic and copies ran while one was open for 10% of the time, Pallas kernels for 0%

profile of v9, /device:TPU:0, one launch (start us, length us, event | category | flops | bytes accessed | tf_op | source)
XLA Modules:
  0.0 92.7 jit_solution(5046901844121195335)
XLA Ops:
  0.6 2.0 %fusion.145 = (bf16[4,1,16384]{2,1,0:T(2,128)(2,1)S(1)}, bf16[4,1,16384]{2,1,0:T(2,128)(2,1)S(1)}) fusion(bf16[4,16,16384]{2,1,0:T(8,128)(2,1)} %field_ref.1), kind=kLoop, calls=%fused_computation.240 | loop fusion | bytes 524288 | tf_op jit(solution)/shard_map/slice | solution.py:39
  2.6 3.1 %collective-permute-start = (bf16[4,1,16384]{2,1,0:T(2,128)(2,1)S(1)}, bf16[4,1,16384]{2,1,0:T(2,128)(2,1)S(1)}, u32[]{:S(2)}, u32[]{:S(2)}) collective-permute-start(bf16[4,1,16384]{2,1,0:T(2,128)(2,1)S(1)} %get-tuple-element.8), channel_id=1, source_target_pairs={{0,1},{1,2},{2,3},{3,4},{4,5},{5,6},{6,7},{7,8},{8,9},{9,10},{10,1... | collective-permute-start | bytes 393224 | tf_op jit(solution)/shard_map/ppermute | solution.py:38
  5.7 3.4 %collective-permute-start.1 = (bf16[4,1,16384]{2,1,0:T(2,128)(2,1)S(1)}, bf16[4,1,16384]{2,1,0:T(2,128)(2,1)S(1)}, u32[]{:S(2)}, u32[]{:S(2)}) collective-permute-start(bf16[4,1,16384]{2,1,0:T(2,128)(2,1)S(1)} %get-tuple-element.7), channel_id=1, source_target_pairs={{1,0},{2,1},{3,2},{4,3},{5,4},{6,5},{7,6},{8,7},{9,8},{10,9},{11,1... | collective-permute-start | bytes 393224 | tf_op jit(solution)/shard_map/ppermute | solution.py:39
  9.1 1.0 %fusion.148 = (f32[1,16384]{1,0:T(1,128)S(1)}, f32[1,16384]{1,0:T(1,128)S(1)}) fusion(bf16[2,16384]{1,0:T(2,128)(2,1)} %param.19), kind=kLoop, calls=%fused_computation.243 | loop fusion | bytes 262144 | tf_op jit(solution)/shard_map/slice | solution.py:161
  10.1 0.8 slice_bitcast_fusion.13
  10.9 0.8 convert_element_type.71
  11.7 0.3 cosine_multiply_fusion
  11.9 0.8 broadcast_multiply_fusion
  12.7 0.2 multiply_multiply_fusion
  13.0 1.8 %pad_maximum_fusion.coef_ref = f32[3,16,16384]{2,1,0:T(8,128)} fusion(f32[1,16,16384]{2,1,0:T(8,128)S(1)} %get-tuple-element.59, f32[1,16,16384]{2,1,0:T(8,128)S(1)} %get-tuple-element.60, f32[1,16,16384]{2,1,0:T(8,128)S(1)} %broadcast_multiply_fusion), kind=kLoop, calls=%fused_computation | loop fusion | flops 1572864 | bytes 6291456 | tf_op jit(solution)/shard_map/stack | solution.py:158
  15.8 0.3 negate_convert_fusion
  16.1 3.0 %collective-permute-done.1.below_ref = bf16[4,1,16384]{2,1,0:T(2,128)(2,1)S(1)} collective-permute-done((bf16[4,1,16384]{2,1,0:T(2,128)(2,1)S(1)}, bf16[4,1,16384]{2,1,0:T(2,128)(2,1)S(1)}, u32[]{:S(2)}, u32[]{:S(2)}) %collective-permute-start.1) | collective-permute-done | bytes 131104 | tf_op jit(solution)/shard_map/ppermute | solution.py:39
  19.1 0.7 copy-done.2
  19.8 26.1 %shard_map.157 = f32[4,1,16384]{2,1,0:T(1,128)} custom-call(f32[1]{0:T(128)S(6)} %div.10.step_ref, s32[1]{0:T(128)S(6)} %copy.161.count_ref, bf16[4,16,16384]{2,1,0:T(8,128)(2,1)} %field_ref.1, bf16[4,1,16384]{2,1,0:T(2,128)(2,1)} %copy-done.1, bf16[4,1,16384]{2,1,0:T(2,128)(2,1)} %copy-done.2, f32[3,16,16384]{2,1,0:T(8,128)} %pad_maximum_fusion.coef_ref), custom_call_target="tpu_custom_call" | custom-call | tf_op jit(solution)/shard_map/pallas_call | solution.py:167
  45.8 1.6 %reduce = f32[4,16384]{1,0:T(4,128)S(1)} reduce(f32[4,1,16384]{2,1,0:T(1,128)} %shard_map.157, f32[]{:T(128)} %constant.378), dimensions={1}, to_apply=%pallas_call.3.reduce_sub_computation | reduce | bytes 524292 | tf_op jit(solution)/shard_map/pallas_call | solution.py:167
  47.5 0.7 reshape.217
  48.2 0.6 reduce_sum.27
  49.0 3.7 %collective-permute-start.4 = (bf16[4,1024]{1,0:T(4,128)(2,1)S(1)}, bf16[4,1024]{1,0:T(4,128)(2,1)S(1)}, u32[]{:S(2)}, u32[]{:S(2)}) collective-permute-start(bf16[4,1024]{1,0:T(4,128)(2,1)S(1)} %multiply_convert_fusion), channel_id=1, source_target_pairs={{0,3},{1,0},{2,1},{3,2},{4,7},{5,4},{6,5},{7,6},{8,11},{9,8},{10,9... | collective-permute-start | bytes 24584 | tf_op jit(solution)/shard_map/ppermute | solution.py:283
  52.7 0.6 convert_dynamic-update-slice_fusion
  53.3 1.0 %collective-permute-done.2 = bf16[4,1024]{1,0:T(4,128)(2,1)S(1)} collective-permute-done((bf16[4,1024]{1,0:T(4,128)(2,1)S(1)}, bf16[4,1024]{1,0:T(4,128)(2,1)S(1)}, u32[]{:S(2)}, u32[]{:S(2)}) %collective-permute-start.2) | collective-permute-done | bytes 8224 | tf_op jit(solution)/shard_map/ppermute | solution.py:283
  54.4 0.5 collective-permute-done.4
  55.0 1.1 %collective-permute-done.5 = bf16[4,4,1024]{2,1,0:T(4,128)(2,1)S(1)} collective-permute-done((bf16[4,4,1024]{2,1,0:T(4,128)(2,1)S(1)}, bf16[4,4,1024]{2,1,0:T(4,128)(2,1)S(1)}, u32[]{:S(2)}, u32[]{:S(2)}) %collective-permute-start.5) | collective-permute-done | bytes 32800 | tf_op jit(solution)/shard_map/ppermute | solution.py:283
  56.2 2.7 %collective-permute-start.6 = (bf16[2,4,4,1024]{3,2,1,0:T(4,128)(2,1)S(1)}, bf16[2,4,4,1024]{3,2,1,0:T(4,128)(2,1)S(1)}, u32[]{:S(2)}, u32[]{:S(2)}) collective-permute-start(bf16[2,4,4,1024]{3,2,1,0:T(4,128)(2,1)S(1)} %bitcast_dynamic-update-slice_fusion.4), channel_id=1, source_target_pairs={{0,8},{8,16},{16,24},{24,0},{1,9},{9,17},{17,25},{25,1},{2,10},{10... | collective-permute-start | bytes 196616 | tf_op jit(solution)/shard_map/ppermute | solution.py:283
  58.9 0.5 collective-permute-start.7
  59.5 1.4 %collective-permute-start.8 = (bf16[2,4,4,1024]{3,2,1,0:T(4,128)(2,1)S(1)}, bf16[2,4,4,1024]{3,2,1,0:T(4,128)(2,1)S(1)}, u32[]{:S(2)}, u32[]{:S(2)}) collective-permute-start(bf16[2,4,4,1024]{3,2,1,0:T(4,128)(2,1)S(1)} %bitcast_dynamic-update-slice_fusion.4), channel_id=1, source_target_pairs={{0,24},{8,0},{16,8},{24,16},{1,25},{9,1},{17,9},{25,17},{2,26},{10... | collective-permute-start | bytes 196616 | tf_op jit(solution)/shard_map/ppermute | solution.py:283
  61.0 0.4 collective-permute-done.6
  61.5 1.8 %collective-permute-done.7 = bf16[2,4,4,1024]{3,2,1,0:T(4,128)(2,1)S(1)} collective-permute-done((bf16[2,4,4,1024]{3,2,1,0:T(4,128)(2,1)S(1)}, bf16[2,4,4,1024]{3,2,1,0:T(4,128)(2,1)S(1)}, u32[]{:S(2)}, u32[]{:S(2)}) %collective-permute-start.7) | collective-permute-done | bytes 65568 | tf_op jit(solution)/shard_map/ppermute | solution.py:283
  63.2 0.5 collective-permute-done.8
  63.8 0.5 fusion.4
  64.3 0.9 fusion.60
  65.3 0.5 fusion.41
  65.8 0.5 fusion.45
  66.4 0.5 fusion.8
  66.9 0.5 fusion.10
  67.7 0.3 sine_multiply_fusion
  67.9 1.3 %collective-permute-done.9 = f32[64,32,16]{0,1,2:T(8,128)S(1)} collective-permute-done((f32[64,32,16]{0,1,2:T(8,128)S(1)}, f32[64,32,16]{0,1,2:T(8,128)S(1)}, u32[]{:S(2)}, u32[]{:S(2)}) %collective-permute-start.9) | collective-permute-done | bytes 131104 | tf_op jit(solution)/shard_map/ppermute | solution.py:295
  69.3 0.2 copy.112
  69.5 0.2 copy.113
  69.7 2.4 %fusion.3 = (f32[8,32,16]{1,2,0:T(8,128)S(1)}, f32[8,32,16]{1,2,0:T(8,128)S(1)}) fusion(f32[32,32,16]{1,2,0:T(8,128)S(1)} %copy.113, f32[32,32,16]{1,2,0:T(8,128)S(1)} %copy.112, bf16[2,32,8,32,16]{3,4,2,1,0:T(8,128)(2,1)} %param.26), kind=kLoop, calls=%fused_computation.8 | loop fusion | flops 1302528 | bytes 688128 | tf_op jit(solution)/shard_map/reduce_sum | solution.py:249
  72.1 0.6 fusion.76
  72.7 0.7 fusion.66
  73.4 0.7 convolution_subtract_fusion.2
  74.0 0.7 convolution_add_fusion.2
  74.8 0.6 convolution_multiply_fusion
  75.4 0.3 fusion.6
  75.7 1.8 %fusion.34 = bf16[1,16,8,1024]{3,2,1,0:T(8,128)(2,1)} fusion(f32[16,8,1024]{2,1,0:T(8,128)S(1)} %fusion.6), kind=kLoop, calls=%fused_computation.73 | loop fusion | flops 8519680 | bytes 786432 | tf_op jit(solution)/shard_map/broadcast_in_dim | solution.py:393
  77.5 0.3 fusion.35
  78.0 0.3 fusion.71
  78.4 0.3 fusion.73
  78.8 0.3 fusion.12
  79.1 0.3 fusion.14
  79.4 0.2 collective-permute-start.10
  79.7 0.2 constant_dynamic-slice_fusion
  79.8 0.2 constant_dynamic-slice_fusion.1
  80.2 0.7 collective-permute-done.10
  81.5 2.4 %collective-permute-start.13 = (f32[48,8,16]{0,1,2:T(8,128)S(1)}, f32[48,8,16]{0,1,2:T(8,128)S(1)}, u32[]{:S(2)}, u32[]{:S(2)}) collective-permute-start(f32[48,8,16]{0,1,2:T(8,128)S(1)} %pad_maximum_fusion.6), channel_id=1, source_target_pairs={{0,24},{8,0},{16,8},{24,16},{1,25},{9,1},{17,9},{25,17},{2,26},{10... | collective-permute-start | bytes 73736 | tf_op jit(solution)/shard_map/ppermute | solution.py:295
  84.2 0.5 collective-permute-start.12
  85.0 0.8 collective-permute-start.11
  85.9 0.2 add_bitcast_fusion.3
  86.3 2.9 %collective-permute-done.12 = f32[48,8,16]{0,1,2:T(8,128)S(1)} collective-permute-done((f32[48,8,16]{0,1,2:T(8,128)S(1)}, f32[48,8,16]{0,1,2:T(8,128)S(1)}, u32[]{:S(2)}, u32[]{:S(2)}) %collective-permute-start.12) | collective-permute-done | bytes 24608 | tf_op jit(solution)/shard_map/ppermute | solution.py:295
  90.8 0.1 add_bitcast_fusion
  91.0 0.1 add_bitcast_fusion.1
  91.1 0.1 add_bitcast_fusion.2
  91.3 1.4 %fusion.17 = f32[2,16,8,8,16]{4,3,2,1,0:T(8,128)} fusion(f32[1,16,8,8,16]{4,3,2,1,0:T(8,128)S(1)} %get-tuple-element.28, f32[1,16,8,8,16]{4,3,2,1,0:T(8,128)S(1)} %get-tuple-element.27, f32[1,16,8,8,16]{4,3,2,1,0:T(8,128)S(1)} %get-tuple-element.26, f32[1,16,8,8,16]{4,3,2,1,0:T(8,128)S(1)} %get-tuple-element.25, ...), kind=kLoop, calls=%fused_computation.32 | loop fusion | flops 262144 | bytes 655360 | tf_op jit(solution)/shard_map/div | solution.py:407
  (84 shorter events, 4.7 us)
Async XLA Ops:
  0.6 74.8 %copy-start = (bf16[32,8]{0,1:T(8,128)(2,1)S(1)}, bf16[32,8]{0,1:T(8,128)(2,1)}, u32[]{:S(2)}) copy-start(bf16[32,8]{0,1:T(8,128)(2,1)} %param.24) | copy-start | bytes 1540
  2.6 13.4 %collective-permute-start = (bf16[4,1,16384]{2,1,0:T(2,128)(2,1)S(1)}, bf16[4,1,16384]{2,1,0:T(2,128)(2,1)S(1)}, u32[]{:S(2)}, u32[]{:S(2)}) collective-permute-start(bf16[4,1,16384]{2,1,0:T(2,128)(2,1)S(1)} %get-tuple-element.8), channel_id=1, source_target_pairs={{0,1},{1,2},{2,3},{3,4},{4,5},{5,6},{6,7},{7,8},{8,9},{9,10},{10,1... | collective-permute-start | bytes 393224 | tf_op jit(solution)/shard_map/ppermute | solution.py:38
  5.7 13.4 %collective-permute-start.1 = (bf16[4,1,16384]{2,1,0:T(2,128)(2,1)S(1)}, bf16[4,1,16384]{2,1,0:T(2,128)(2,1)S(1)}, u32[]{:S(2)}, u32[]{:S(2)}) collective-permute-start(bf16[4,1,16384]{2,1,0:T(2,128)(2,1)S(1)} %get-tuple-element.7), channel_id=1, source_target_pairs={{1,0},{2,1},{3,2},{4,3},{5,4},{6,5},{7,6},{8,7},{9,8},{10,9},{11,1... | collective-permute-start | bytes 393224 | tf_op jit(solution)/shard_map/ppermute | solution.py:39
  13.0 1.9 %copy-start.6 = (s32[32]{0:T(128)S(1)}, s32[32]{0:T(128)}, u32[]{:S(2)}) copy-start(s32[32]{0:T(128)} %param.20) | copy-start | bytes 388
  16.0 3.0 %copy-start.1 = (bf16[4,1,16384]{2,1,0:T(2,128)(2,1)}, bf16[4,1,16384]{2,1,0:T(2,128)(2,1)S(1)}, u32[]{:S(2)}) copy-start(bf16[4,1,16384]{2,1,0:T(2,128)(2,1)S(1)} %collective-permute-done.above_ref) | copy-start | bytes 393220
  19.1 0.7 copy-start.2
  48.2 15.6 %copy-start.3 = (bf16[1,16,4,1024]{3,2,1,0:T(4,128)(2,1)S(1)}, bf16[1,16,4,1024]{3,2,1,0:T(4,128)(2,1)}, u32[]{:S(2)}) copy-start(bf16[1,16,4,1024]{3,2,1,0:T(4,128)(2,1)} %param.21) | copy-start | bytes 393220
  48.2 15.6 %copy-start.4 = (bf16[4,32]{1,0:T(4,128)(2,1)S(1)}, bf16[4,32]{1,0:T(4,128)(2,1)}, u32[]{:S(2)}) copy-start(bf16[4,32]{1,0:T(4,128)(2,1)} %param.22) | copy-start | bytes 772
  48.2 15.6 %copy-start.5 = (f32[32]{0:T(128)S(1)}, f32[32]{0:T(128)}, u32[]{:S(2)}) copy-start(f32[32]{0:T(128)} %param.23) | copy-start | bytes 388
  48.8 5.5 %collective-permute-start.2 = (bf16[4,1024]{1,0:T(4,128)(2,1)S(1)}, bf16[4,1024]{1,0:T(4,128)(2,1)S(1)}, u32[]{:S(2)}, u32[]{:S(2)}) collective-permute-start(bf16[4,1024]{1,0:T(4,128)(2,1)S(1)} %multiply_convert_fusion), channel_id=1, source_target_pairs={{0,1},{1,2},{2,3},{3,0},{4,5},{5,6},{6,7},{7,4},{8,9},{9,10},{10,1... | collective-permute-start | bytes 24584 | tf_op jit(solution)/shard_map/ppermute | solution.py:283
  48.9 5.5 %collective-permute-start.3 = (bf16[4,1024]{1,0:T(4,128)(2,1)S(1)}, bf16[4,1024]{1,0:T(4,128)(2,1)S(1)}, u32[]{:S(2)}, u32[]{:S(2)}) collective-permute-start(bf16[4,1024]{1,0:T(4,128)(2,1)S(1)} %multiply_convert_fusion), channel_id=1, source_target_pairs={{0,2},{1,3},{2,0},{3,1},{4,6},{5,7},{6,4},{7,5},{8,10},{9,11},{10,... | collective-permute-start | bytes 24584 | tf_op jit(solution)/shard_map/ppermute | solution.py:283
  49.0 5.9 %collective-permute-start.4 = (bf16[4,1024]{1,0:T(4,128)(2,1)S(1)}, bf16[4,1024]{1,0:T(4,128)(2,1)S(1)}, u32[]{:S(2)}, u32[]{:S(2)}) collective-permute-start(bf16[4,1024]{1,0:T(4,128)(2,1)S(1)} %multiply_convert_fusion), channel_id=1, source_target_pairs={{0,3},{1,0},{2,1},{3,2},{4,7},{5,4},{6,5},{7,6},{8,11},{9,8},{10,9... | collective-permute-start | bytes 24584 | tf_op jit(solution)/shard_map/ppermute | solution.py:283
  54.9 1.3 %collective-permute-start.5 = (bf16[4,4,1024]{2,1,0:T(4,128)(2,1)S(1)}, bf16[4,4,1024]{2,1,0:T(4,128)(2,1)S(1)}, u32[]{:S(2)}, u32[]{:S(2)}) collective-permute-start(bf16[4,4,1024]{2,1,0:T(4,128)(2,1)S(1)} %bitcast_dynamic-update-slice_fusion.6), channel_id=1, source_target_pairs={{0,4},{4,0},{1,5},{5,1},{2,6},{6,2},{3,7},{7,3},{8,12},{12,8},{9,1... | collective-permute-start | bytes 98312 | tf_op jit(solution)/shard_map/ppermute | solution.py:283
  56.2 5.2 %collective-permute-start.6 = (bf16[2,4,4,1024]{3,2,1,0:T(4,128)(2,1)S(1)}, bf16[2,4,4,1024]{3,2,1,0:T(4,128)(2,1)S(1)}, u32[]{:S(2)}, u32[]{:S(2)}) collective-permute-start(bf16[2,4,4,1024]{3,2,1,0:T(4,128)(2,1)S(1)} %bitcast_dynamic-update-slice_fusion.4), channel_id=1, source_target_pairs={{0,8},{8,16},{16,24},{24,0},{1,9},{9,17},{17,25},{25,1},{2,10},{10... | collective-permute-start | bytes 196616 | tf_op jit(solution)/shard_map/ppermute | solution.py:283
  58.9 4.3 %collective-permute-start.7 = (bf16[2,4,4,1024]{3,2,1,0:T(4,128)(2,1)S(1)}, bf16[2,4,4,1024]{3,2,1,0:T(4,128)(2,1)S(1)}, u32[]{:S(2)}, u32[]{:S(2)}) collective-permute-start(bf16[2,4,4,1024]{3,2,1,0:T(4,128)(2,1)S(1)} %bitcast_dynamic-update-slice_fusion.4), channel_id=1, source_target_pairs={{0,16},{8,24},{16,0},{24,8},{1,17},{9,25},{17,1},{25,9},{2,18},{10... | collective-permute-start | bytes 196616 | tf_op jit(solution)/shard_map/ppermute | solution.py:283
  59.5 4.3 %collective-permute-start.8 = (bf16[2,4,4,1024]{3,2,1,0:T(4,128)(2,1)S(1)}, bf16[2,4,4,1024]{3,2,1,0:T(4,128)(2,1)S(1)}, u32[]{:S(2)}, u32[]{:S(2)}) collective-permute-start(bf16[2,4,4,1024]{3,2,1,0:T(4,128)(2,1)S(1)} %bitcast_dynamic-update-slice_fusion.4), channel_id=1, source_target_pairs={{0,24},{8,0},{16,8},{24,16},{1,25},{9,1},{17,9},{25,17},{2,26},{10... | collective-permute-start | bytes 196616 | tf_op jit(solution)/shard_map/ppermute | solution.py:283
  67.6 1.6 %collective-permute-start.9 = (f32[64,32,16]{0,1,2:T(8,128)S(1)}, f32[64,32,16]{0,1,2:T(8,128)S(1)}, u32[]{:S(2)}, u32[]{:S(2)}) collective-permute-start(f32[64,32,16]{0,1,2:T(8,128)S(1)} %pad_maximum_fusion.1), channel_id=1, source_target_pairs={{0,4},{4,0},{1,5},{5,1},{2,6},{6,2},{3,7},{7,3},{8,12},{12,8},{9,1... | collective-permute-start | bytes 393224 | tf_op jit(solution)/shard_map/ppermute | solution.py:295
  69.7 5.7 %copy-start.7 = (f32[8]{0:T(128)S(1)}, f32[8]{0:T(128)}, u32[]{:S(2)}) copy-start(f32[8]{0:T(128)} %param.25) | copy-start | bytes 100
  73.4 4.1 %copy-start.8 = (bf16[1,16,8,1024]{3,2,1,0:T(8,128)(2,1)S(1)}, bf16[1,16,8,1024]{3,2,1,0:T(8,128)(2,1)}, u32[]{:S(2)}) copy-start(bf16[1,16,8,1024]{3,2,1,0:T(8,128)(2,1)} %param.27) | copy-start | bytes 786436
  79.4 1.4 %collective-permute-start.10 = (f32[16,32,16]{1,2,0:T(8,128)S(1)}, f32[16,32,16]{1,2,0:T(8,128)S(1)}, u32[]{:S(2)}, u32[]{:S(2)}) collective-permute-start(f32[16,32,16]{1,2,0:T(8,128)S(1)} %pad_maximum_fusion.2), channel_id=1, source_target_pairs={{0,4},{4,0},{1,5},{5,1},{2,6},{6,2},{3,7},{7,3},{8,12},{12,8},{9,1... | collective-permute-start | bytes 98312 | tf_op jit(solution)/shard_map/ppermute | solution.py:295
  81.5 4.6 %collective-permute-start.13 = (f32[48,8,16]{0,1,2:T(8,128)S(1)}, f32[48,8,16]{0,1,2:T(8,128)S(1)}, u32[]{:S(2)}, u32[]{:S(2)}) collective-permute-start(f32[48,8,16]{0,1,2:T(8,128)S(1)} %pad_maximum_fusion.6), channel_id=1, source_target_pairs={{0,24},{8,0},{16,8},{24,16},{1,25},{9,1},{17,9},{25,17},{2,26},{10... | collective-permute-start | bytes 73736 | tf_op jit(solution)/shard_map/ppermute | solution.py:295
  84.2 5.0 %collective-permute-start.12 = (f32[48,8,16]{0,1,2:T(8,128)S(1)}, f32[48,8,16]{0,1,2:T(8,128)S(1)}, u32[]{:S(2)}, u32[]{:S(2)}) collective-permute-start(f32[48,8,16]{0,1,2:T(8,128)S(1)} %pad_maximum_fusion.5), channel_id=1, source_target_pairs={{0,16},{8,24},{16,0},{24,8},{1,17},{9,25},{17,1},{25,9},{2,18},{10... | collective-permute-start | bytes 73736 | tf_op jit(solution)/shard_map/ppermute | solution.py:295
  85.0 5.2 %collective-permute-start.11 = (f32[48,8,16]{0,1,2:T(8,128)S(1)}, f32[48,8,16]{0,1,2:T(8,128)S(1)}, u32[]{:S(2)}, u32[]{:S(2)}) collective-permute-start(f32[48,8,16]{0,1,2:T(8,128)S(1)} %pad_maximum_fusion.4), channel_id=1, source_target_pairs={{0,8},{8,16},{16,24},{24,0},{1,9},{9,17},{17,25},{25,1},{2,10},{10... | collective-permute-start | bytes 73736 | tf_op jit(solution)/shard_map/ppermute | solution.py:295

commit v10 on v9

--- a/solution.py
+++ b/solution.py
@@ -66,7 +66,7 @@
 
 
 CHUNK = 2048
-UNROLL = 4
+UNROLL = 8
 
 
 def solve_kernel(
@@ -84,8 +84,7 @@
             first_ref[tracer, :, cols] = field_ref[tracer, :, cols].astype(jnp.float32)
         return carry
 
-    lax.fori_loop(0, chunks, prepare, 0)
-    step = step_ref[0]
+    lax.fori_loop(0, chunks, prepare, 0, unroll=UNROLL)
     row_ids = lax.broadcasted_iota(jnp.int32, (rows, CHUNK), 0)
 
     def sweep(source_ref, target_ref):
@@ -118,7 +117,7 @@
                     - along * (right_cells - left_cells)
                     - across * (lower_rows - upper_rows)
                 )
-                target_ref[tracer, :, cols] = current + step * change
+                target_ref[tracer, :, cols] = current + change
             return inner
 
         lax.fori_loop(0, chunks, update, 0, unroll=UNROLL)
@@ -138,7 +137,7 @@
             out_ref[tracer, :, cols] = jnp.sum(final_ref[tracer, :, cols], axis=0, keepdims=True)
             return carry
 
-        lax.fori_loop(0, tracers * chunks, store, 0)
+        lax.fori_loop(0, tracers * chunks, store, 0, unroll=UNROLL)
 
     @pl.when(total % 2 == 1)
     def _():
@@ -155,7 +154,7 @@
     step = (window_time / substeps.astype(jnp.float32)).reshape(1)
     kappa_col = kappa_col.astype(jnp.float32)
     drift_col = drift_col.astype(jnp.float32)
-    coefficients = jnp.stack(
+    coefficients = step * jnp.stack(
         [
             kappa_row[:, None] * kappa_col[None, :],
             0.5 * (drift_row[0][:, None] * drift_col[0][None, :]),

time: 93.1 us -> 90.9 us (0.976)
  Pallas kernels: 26.1 us -> 16.8 us
  starting transfers between devices: 19.1 us -> 26.8 us
    pallas_call x1, Pallas kernels: 26.1 us -> 16.8 us  [solve_rows(): pl.pallas_call(solve_kernel, out_shape=jax.ShapeDtypeStruct((tracers, 1,...]
    ppermute x7, starting transfers between devices: 8.63 us -> 16.2 us  [gather_along(): lax.ppermute(block, axis, [(i, (i + shift) % count) for i in range(count)])]
    mul x0 -> x1, other arithmetic: none -> 1.85 us  [solve_rows(): step * jnp.stack([kappa_row[:, None] * kappa_col[None, :], 0.5 * (drift_r...]
    another operation x2 -> x1, other arithmetic: 2.11 us -> 0.27 us  [the longest x1 1.84 us: solve_rows(): jnp.stack([kappa_row[:, None] * kappa_col[None, :], 0.5 * (drift_row[0][:...]
    ppermute x7, waiting for transfers between devices: 5.28 us -> 4.13 us  [gather_along(): lax.ppermute(block, axis, [(i, (i + shift) % count) for i in range(count)])]
  transfers between devices with their start and end apart: 14 -> 14, of which waited for: 11 -> 10; matrix products, arithmetic and copies ran while one was open for 10% -> 11% of each run, Pallas kernels for 0% -> 0%
where the time goes in v10:
time: 90.9 us; the launch traced here: 90.6 us
  starting transfers between devices  26.8 us (29%)
  Pallas kernels  16.8 us (18%)
  other arithmetic  14.4 us (16%)
  waiting for transfers between devices  12.6 us (14%)
  local copies, waits for them, and re-layouts  9.3 us (10%)
  matrix products  8.62 us (9%)
  between operations  2.06 us (2%)
    pallas_call x1, Pallas kernels, solve_rows(): pl.pallas_call(solve_kernel, out_shape=jax.ShapeDtypeStruct((tracers, 1,...  16.8 us
    ppermute x7, starting transfers between devices, gather_along(): lax.ppermute(block, axis, [(i, (i + shift) % count) for i in range(count)])  16.2 us
    ppermute x5, waiting for transfers between devices, packed_ppermute(): packed = lax.ppermute(jnp.concatenate(parts, axis=0), axis, perm)  5.47 us
    ppermute x7, waiting for transfers between devices, gather_along(): lax.ppermute(block, axis, [(i, (i + shift) % count) for i in range(count)])  4.13 us
    ppermute x5, starting transfers between devices, packed_ppermute(): packed = lax.ppermute(jnp.concatenate(parts, axis=0), axis, perm)  4.12 us
    ppermute x1, starting transfers between devices, halo_rows(): below = lax.ppermute(block[:, :1], axis, backward)  3.42 us
    ppermute x1, starting transfers between devices, halo_rows(): above = lax.ppermute(block[:, -1:], axis, forward)  3.08 us
    ppermute x1, waiting for transfers between devices, halo_rows(): below = lax.ppermute(block[:, :1], axis, backward)  2.99 us
  transfers between devices with their start and end apart: 14, of which 10 were waited for; matrix products, arithmetic and copies ran while one was open for 11% of the time, Pallas kernels for 0%

profile of v10, /device:TPU:0, one launch (start us, length us, event | category | flops | bytes accessed | tf_op | source)
XLA Modules:
  0.0 90.6 jit_solution(9710963501615654087)
XLA Ops:
  0.6 2.0 %fusion.145 = (bf16[4,1,16384]{2,1,0:T(2,128)(2,1)S(1)}, bf16[4,1,16384]{2,1,0:T(2,128)(2,1)S(1)}) fusion(bf16[4,16,16384]{2,1,0:T(8,128)(2,1)} %field_ref.1), kind=kLoop, calls=%fused_computation.240 | loop fusion | bytes 524288 | tf_op jit(solution)/shard_map/slice | solution.py:39
  2.6 3.1 %collective-permute-start = (bf16[4,1,16384]{2,1,0:T(2,128)(2,1)S(1)}, bf16[4,1,16384]{2,1,0:T(2,128)(2,1)S(1)}, u32[]{:S(2)}, u32[]{:S(2)}) collective-permute-start(bf16[4,1,16384]{2,1,0:T(2,128)(2,1)S(1)} %get-tuple-element.8), channel_id=1, source_target_pairs={{0,1},{1,2},{2,3},{3,4},{4,5},{5,6},{6,7},{7,8},{8,9},{9,10},{10,1... | collective-permute-start | bytes 393224 | tf_op jit(solution)/shard_map/ppermute | solution.py:38
  5.7 3.4 %collective-permute-start.1 = (bf16[4,1,16384]{2,1,0:T(2,128)(2,1)S(1)}, bf16[4,1,16384]{2,1,0:T(2,128)(2,1)S(1)}, u32[]{:S(2)}, u32[]{:S(2)}) collective-permute-start(bf16[4,1,16384]{2,1,0:T(2,128)(2,1)S(1)} %get-tuple-element.7), channel_id=1, source_target_pairs={{1,0},{2,1},{3,2},{4,3},{5,4},{6,5},{7,6},{8,7},{9,8},{10,9},{11,1... | collective-permute-start | bytes 393224 | tf_op jit(solution)/shard_map/ppermute | solution.py:39
  9.1 1.0 %fusion.148 = (f32[1,16384]{1,0:T(1,128)S(1)}, f32[1,16384]{1,0:T(1,128)S(1)}) fusion(bf16[2,16384]{1,0:T(2,128)(2,1)} %param.19), kind=kLoop, calls=%fused_computation.243 | loop fusion | bytes 262144 | tf_op jit(solution)/shard_map/slice | solution.py:160
  10.1 0.8 slice_bitcast_fusion.13
  11.6 0.8 convert_element_type.71
  12.3 0.3 cosine_multiply_fusion
  12.6 0.8 broadcast_multiply_fusion
  13.4 0.2 multiply_multiply_fusion
  13.7 1.8 %maximum_multiply_fusion.coef_ref = f32[3,16,16384]{2,1,0:T(8,128)} fusion(f32[1,16,16384]{2,1,0:T(8,128)S(1)} %get-tuple-element.59, f32[1,16,16384]{2,1,0:T(8,128)S(1)} %get-tuple-element.60, f32[1,16,16384]{2,1,0:T(8,128)S(1)} %broadcast_multiply_fusion, f32[]{:T(128)} %bitcast), kind=kLoop, calls=%fused_computation | loop fusion | flops 2359296 | bytes 6291460 | tf_op jit(solution)/shard_map/mul | solution.py:157
  15.8 0.3 negate_convert_fusion
  16.1 3.0 %collective-permute-done.1.below_ref = bf16[4,1,16384]{2,1,0:T(2,128)(2,1)S(1)} collective-permute-done((bf16[4,1,16384]{2,1,0:T(2,128)(2,1)S(1)}, bf16[4,1,16384]{2,1,0:T(2,128)(2,1)S(1)}, u32[]{:S(2)}, u32[]{:S(2)}) %collective-permute-start.1) | collective-permute-done | bytes 131104 | tf_op jit(solution)/shard_map/ppermute | solution.py:39
  19.1 0.7 copy-done.2
  19.8 16.8 %shard_map.157 = f32[4,1,16384]{2,1,0:T(1,128)} custom-call(f32[1]{0:T(128)} %div.12.step_ref, s32[1]{0:T(128)S(6)} %copy.161.count_ref, bf16[4,16,16384]{2,1,0:T(8,128)(2,1)} %field_ref.1, bf16[4,1,16384]{2,1,0:T(2,128)(2,1)} %copy-done.1, bf16[4,1,16384]{2,1,0:T(2,128)(2,1)} %copy-done.2, f32[3,16,16384]{2,1,0:T(8,128)} %maximum_multiply_fusion.coef_ref), custom_call_target="tpu_custom_call" | custom-call | tf_op jit(solution)/shard_map/pallas_call | solution.py:166
  36.6 1.6 %reduce = f32[4,16384]{1,0:T(4,128)S(1)} reduce(f32[4,1,16384]{2,1,0:T(1,128)} %shard_map.157, f32[]{:T(128)} %constant.378), dimensions={1}, to_apply=%pallas_call.3.reduce_sub_computation | reduce | bytes 524292 | tf_op jit(solution)/shard_map/pallas_call | solution.py:166
  38.2 0.7 reshape.218
  38.9 0.6 reduce_sum.27
  39.6 1.6 %collective-permute-start.2 = (bf16[4,1024]{1,0:T(4,128)(2,1)S(1)}, bf16[4,1024]{1,0:T(4,128)(2,1)S(1)}, u32[]{:S(2)}, u32[]{:S(2)}) collective-permute-start(bf16[4,1024]{1,0:T(4,128)(2,1)S(1)} %multiply_convert_fusion), channel_id=1, source_target_pairs={{0,1},{1,2},{2,3},{3,0},{4,5},{5,6},{6,7},{7,4},{8,9},{9,10},{10,1... | collective-permute-start | bytes 24584 | tf_op jit(solution)/shard_map/ppermute | solution.py:282
  41.2 2.4 %collective-permute-start.4 = (bf16[4,1024]{1,0:T(4,128)(2,1)S(1)}, bf16[4,1024]{1,0:T(4,128)(2,1)S(1)}, u32[]{:S(2)}, u32[]{:S(2)}) collective-permute-start(bf16[4,1024]{1,0:T(4,128)(2,1)S(1)} %multiply_convert_fusion), channel_id=1, source_target_pairs={{0,3},{1,0},{2,1},{3,2},{4,7},{5,4},{6,5},{7,6},{8,11},{9,8},{10,9... | collective-permute-start | bytes 24584 | tf_op jit(solution)/shard_map/ppermute | solution.py:282
  43.6 0.6 convert_dynamic-update-slice_fusion
  44.3 0.8 collective-permute-done.2
  45.1 0.7 collective-permute-done.3
  45.8 4.8 %collective-permute-start.5 = (bf16[4,4,1024]{2,1,0:T(4,128)(2,1)S(1)}, bf16[4,4,1024]{2,1,0:T(4,128)(2,1)S(1)}, u32[]{:S(2)}, u32[]{:S(2)}) collective-permute-start(bf16[4,4,1024]{2,1,0:T(4,128)(2,1)S(1)} %bitcast_dynamic-update-slice_fusion.6), channel_id=1, source_target_pairs={{0,4},{4,0},{1,5},{5,1},{2,6},{6,2},{3,7},{7,3},{8,12},{12,8},{9,1... | collective-permute-start | bytes 98312 | tf_op jit(solution)/shard_map/ppermute | solution.py:282
  50.6 0.8 collective-permute-done.5
  51.4 3.4 %collective-permute-start.6 = (bf16[2,4,4,1024]{3,2,1,0:T(4,128)(2,1)S(1)}, bf16[2,4,4,1024]{3,2,1,0:T(4,128)(2,1)S(1)}, u32[]{:S(2)}, u32[]{:S(2)}) collective-permute-start(bf16[2,4,4,1024]{3,2,1,0:T(4,128)(2,1)S(1)} %bitcast_dynamic-update-slice_fusion.4), channel_id=1, source_target_pairs={{0,8},{8,16},{16,24},{24,0},{1,9},{9,17},{17,25},{25,1},{2,10},{10... | collective-permute-start | bytes 196616 | tf_op jit(solution)/shard_map/ppermute | solution.py:282
  54.9 1.1 %collective-permute-start.7 = (bf16[2,4,4,1024]{3,2,1,0:T(4,128)(2,1)S(1)}, bf16[2,4,4,1024]{3,2,1,0:T(4,128)(2,1)S(1)}, u32[]{:S(2)}, u32[]{:S(2)}) collective-permute-start(bf16[2,4,4,1024]{3,2,1,0:T(4,128)(2,1)S(1)} %bitcast_dynamic-update-slice_fusion.4), channel_id=1, source_target_pairs={{0,16},{8,24},{16,0},{24,8},{1,17},{9,25},{17,1},{25,9},{2,18},{10... | collective-permute-start | bytes 196616 | tf_op jit(solution)/shard_map/ppermute | solution.py:282
  55.9 2.8 %collective-permute-start.8 = (bf16[2,4,4,1024]{3,2,1,0:T(4,128)(2,1)S(1)}, bf16[2,4,4,1024]{3,2,1,0:T(4,128)(2,1)S(1)}, u32[]{:S(2)}, u32[]{:S(2)}) collective-permute-start(bf16[2,4,4,1024]{3,2,1,0:T(4,128)(2,1)S(1)} %bitcast_dynamic-update-slice_fusion.4), channel_id=1, source_target_pairs={{0,24},{8,0},{16,8},{24,16},{1,25},{9,1},{17,9},{25,17},{2,26},{10... | collective-permute-start | bytes 196616 | tf_op jit(solution)/shard_map/ppermute | solution.py:282
  59.0 0.2 collective-permute-done.7
  59.2 1.7 %collective-permute-done.8 = bf16[2,4,4,1024]{3,2,1,0:T(4,128)(2,1)S(1)} collective-permute-done((bf16[2,4,4,1024]{3,2,1,0:T(4,128)(2,1)S(1)}, bf16[2,4,4,1024]{3,2,1,0:T(4,128)(2,1)S(1)}, u32[]{:S(2)}, u32[]{:S(2)}) %collective-permute-start.8) | collective-permute-done | bytes 65568 | tf_op jit(solution)/shard_map/ppermute | solution.py:282
  60.9 0.5 fusion.4
  61.5 0.9 %fusion.60 = f32[16,32,32]{1,2,0:T(8,128)S(1)} fusion(bf16[16,32,1024]{2,1,0:T(8,128)(2,1)S(1)} %fusion.4, bf16[1024,16]{0,1:T(8,128)(2,1)S(1)} %get-tuple-element.61, bf16[1024,16]{0,1:T(8,128)(2,1)S(1)} %get-tuple-element.62), kind=kOutput, calls=%fused_computation.138 | convolution fusion | flops 33685504 | bytes 1179648 | tf_op jit(solution)/shard_map/yhx,xk->yhk/dot_general | solution.py:368
  62.4 0.5 fusion.41
  62.9 0.5 fusion.45
  63.5 0.5 fusion.8
  64.0 0.5 fusion.10
  64.8 0.3 sine_multiply_fusion
  65.1 1.3 %collective-permute-done.9 = f32[64,32,16]{0,1,2:T(8,128)S(1)} collective-permute-done((f32[64,32,16]{0,1,2:T(8,128)S(1)}, f32[64,32,16]{0,1,2:T(8,128)S(1)}, u32[]{:S(2)}, u32[]{:S(2)}) %collective-permute-start.9) | collective-permute-done | bytes 131104 | tf_op jit(solution)/shard_map/ppermute | solution.py:294
  66.4 0.2 copy.112
  66.6 0.2 copy.113
  66.8 2.4 %fusion.3 = (f32[8,32,16]{1,2,0:T(8,128)S(1)}, f32[8,32,16]{1,2,0:T(8,128)S(1)}) fusion(f32[32,32,16]{1,2,0:T(8,128)S(1)} %copy.113, f32[32,32,16]{1,2,0:T(8,128)S(1)} %copy.112, bf16[2,32,8,32,16]{3,4,2,1,0:T(8,128)(2,1)} %param.26), kind=kLoop, calls=%fused_computation.8 | loop fusion | flops 1302528 | bytes 688128 | tf_op jit(solution)/shard_map/reduce_sum | solution.py:248
  69.2 0.6 fusion.76
  69.8 0.7 fusion.66
  70.5 0.7 convolution_subtract_fusion.2
  71.2 0.7 convolution_add_fusion.2
  71.9 0.6 convolution_multiply_fusion
  72.5 0.3 fusion.6
  72.8 1.8 %fusion.34 = bf16[1,16,8,1024]{3,2,1,0:T(8,128)(2,1)} fusion(f32[16,8,1024]{2,1,0:T(8,128)S(1)} %fusion.6), kind=kLoop, calls=%fused_computation.73 | loop fusion | flops 8519680 | bytes 786432 | tf_op jit(solution)/shard_map/broadcast_in_dim | solution.py:392
  74.6 0.3 fusion.35
  75.2 0.3 fusion.71
  75.6 0.3 fusion.73
  75.9 0.3 fusion.12
  76.2 0.3 fusion.14
  76.6 0.2 collective-permute-start.10
  76.8 0.2 constant_dynamic-slice_fusion
  76.9 0.2 constant_dynamic-slice_fusion.1
  77.3 0.7 collective-permute-done.10
  78.6 3.1 %collective-permute-start.13 = (f32[48,8,16]{0,1,2:T(8,128)S(1)}, f32[48,8,16]{0,1,2:T(8,128)S(1)}, u32[]{:S(2)}, u32[]{:S(2)}) collective-permute-start(f32[48,8,16]{0,1,2:T(8,128)S(1)} %pad_maximum_fusion.5), channel_id=1, source_target_pairs={{0,24},{8,0},{16,8},{24,16},{1,25},{9,1},{17,9},{25,17},{2,26},{10... | collective-permute-start | bytes 73736 | tf_op jit(solution)/shard_map/ppermute | solution.py:294
  82.1 0.4 collective-permute-start.12
  82.8 0.3 collective-permute-start.11
  83.2 0.2 add_bitcast_fusion.3
  83.4 0.6 collective-permute-done.13
  84.2 2.9 %collective-permute-done.12 = f32[48,8,16]{0,1,2:T(8,128)S(1)} collective-permute-done((f32[48,8,16]{0,1,2:T(8,128)S(1)}, f32[48,8,16]{0,1,2:T(8,128)S(1)}, u32[]{:S(2)}, u32[]{:S(2)}) %collective-permute-start.12) | collective-permute-done | bytes 24608 | tf_op jit(solution)/shard_map/ppermute | solution.py:294
  88.7 0.1 add_bitcast_fusion
  89.1 1.4 %fusion.17 = f32[2,16,8,8,16]{4,3,2,1,0:T(8,128)} fusion(f32[1,16,8,8,16]{4,3,2,1,0:T(8,128)S(1)} %get-tuple-element.28, f32[1,16,8,8,16]{4,3,2,1,0:T(8,128)S(1)} %get-tuple-element.27, f32[1,16,8,8,16]{4,3,2,1,0:T(8,128)S(1)} %get-tuple-element.26, f32[1,16,8,8,16]{4,3,2,1,0:T(8,128)S(1)} %get-tuple-element.25, ...), kind=kLoop, calls=%fused_computation.32 | loop fusion | flops 262144 | bytes 655360 | tf_op jit(solution)/shard_map/div | solution.py:406
  (84 shorter events, 4.8 us)
Async XLA Ops:
  0.6 71.9 %copy-start = (bf16[32,8]{0,1:T(8,128)(2,1)S(1)}, bf16[32,8]{0,1:T(8,128)(2,1)}, u32[]{:S(2)}) copy-start(bf16[32,8]{0,1:T(8,128)(2,1)} %param.24) | copy-start | bytes 1540
  2.6 13.5 %collective-permute-start = (bf16[4,1,16384]{2,1,0:T(2,128)(2,1)S(1)}, bf16[4,1,16384]{2,1,0:T(2,128)(2,1)S(1)}, u32[]{:S(2)}, u32[]{:S(2)}) collective-permute-start(bf16[4,1,16384]{2,1,0:T(2,128)(2,1)S(1)} %get-tuple-element.8), channel_id=1, source_target_pairs={{0,1},{1,2},{2,3},{3,4},{4,5},{5,6},{6,7},{7,8},{8,9},{9,10},{10,1... | collective-permute-start | bytes 393224 | tf_op jit(solution)/shard_map/ppermute | solution.py:38
  5.7 13.4 %collective-permute-start.1 = (bf16[4,1,16384]{2,1,0:T(2,128)(2,1)S(1)}, bf16[4,1,16384]{2,1,0:T(2,128)(2,1)S(1)}, u32[]{:S(2)}, u32[]{:S(2)}) collective-permute-start(bf16[4,1,16384]{2,1,0:T(2,128)(2,1)S(1)} %get-tuple-element.7), channel_id=1, source_target_pairs={{1,0},{2,1},{3,2},{4,3},{5,4},{6,5},{7,6},{8,7},{9,8},{10,9},{11,1... | collective-permute-start | bytes 393224 | tf_op jit(solution)/shard_map/ppermute | solution.py:39
  13.7 1.9 %copy-start.6 = (s32[32]{0:T(128)S(1)}, s32[32]{0:T(128)}, u32[]{:S(2)}) copy-start(s32[32]{0:T(128)} %param.20) | copy-start | bytes 388
  16.1 3.0 %copy-start.1 = (bf16[4,1,16384]{2,1,0:T(2,128)(2,1)}, bf16[4,1,16384]{2,1,0:T(2,128)(2,1)S(1)}, u32[]{:S(2)}) copy-start(bf16[4,1,16384]{2,1,0:T(2,128)(2,1)S(1)} %collective-permute-done.above_ref) | copy-start | bytes 393220
  19.1 0.7 copy-start.2
  38.9 22.0 %copy-start.3 = (bf16[1,16,4,1024]{3,2,1,0:T(4,128)(2,1)S(1)}, bf16[1,16,4,1024]{3,2,1,0:T(4,128)(2,1)}, u32[]{:S(2)}) copy-start(bf16[1,16,4,1024]{3,2,1,0:T(4,128)(2,1)} %param.21) | copy-start | bytes 393220
  38.9 22.0 %copy-start.4 = (bf16[4,32]{1,0:T(4,128)(2,1)S(1)}, bf16[4,32]{1,0:T(4,128)(2,1)}, u32[]{:S(2)}) copy-start(bf16[4,32]{1,0:T(4,128)(2,1)} %param.22) | copy-start | bytes 772
  38.9 22.0 %copy-start.5 = (f32[32]{0:T(128)S(1)}, f32[32]{0:T(128)}, u32[]{:S(2)}) copy-start(f32[32]{0:T(128)} %param.23) | copy-start | bytes 388
  39.6 5.5 %collective-permute-start.2 = (bf16[4,1024]{1,0:T(4,128)(2,1)S(1)}, bf16[4,1024]{1,0:T(4,128)(2,1)S(1)}, u32[]{:S(2)}, u32[]{:S(2)}) collective-permute-start(bf16[4,1024]{1,0:T(4,128)(2,1)S(1)} %multiply_convert_fusion), channel_id=1, source_target_pairs={{0,1},{1,2},{2,3},{3,0},{4,5},{5,6},{6,7},{7,4},{8,9},{9,10},{10,1... | collective-permute-start | bytes 24584 | tf_op jit(solution)/shard_map/ppermute | solution.py:282
  41.2 4.5 %collective-permute-start.3 = (bf16[4,1024]{1,0:T(4,128)(2,1)S(1)}, bf16[4,1024]{1,0:T(4,128)(2,1)S(1)}, u32[]{:S(2)}, u32[]{:S(2)}) collective-permute-start(bf16[4,1024]{1,0:T(4,128)(2,1)S(1)} %multiply_convert_fusion), channel_id=1, source_target_pairs={{0,2},{1,3},{2,0},{3,1},{4,6},{5,7},{6,4},{7,5},{8,10},{9,11},{10,... | collective-permute-start | bytes 24584 | tf_op jit(solution)/shard_map/ppermute | solution.py:282
  41.2 4.6 %collective-permute-start.4 = (bf16[4,1024]{1,0:T(4,128)(2,1)S(1)}, bf16[4,1024]{1,0:T(4,128)(2,1)S(1)}, u32[]{:S(2)}, u32[]{:S(2)}) collective-permute-start(bf16[4,1024]{1,0:T(4,128)(2,1)S(1)} %multiply_convert_fusion), channel_id=1, source_target_pairs={{0,3},{1,0},{2,1},{3,2},{4,7},{5,4},{6,5},{7,6},{8,11},{9,8},{10,9... | collective-permute-start | bytes 24584 | tf_op jit(solution)/shard_map/ppermute | solution.py:282
  45.8 5.6 %collective-permute-start.5 = (bf16[4,4,1024]{2,1,0:T(4,128)(2,1)S(1)}, bf16[4,4,1024]{2,1,0:T(4,128)(2,1)S(1)}, u32[]{:S(2)}, u32[]{:S(2)}) collective-permute-start(bf16[4,4,1024]{2,1,0:T(4,128)(2,1)S(1)} %bitcast_dynamic-update-slice_fusion.6), channel_id=1, source_target_pairs={{0,4},{4,0},{1,5},{5,1},{2,6},{6,2},{3,7},{7,3},{8,12},{12,8},{9,1... | collective-permute-start | bytes 98312 | tf_op jit(solution)/shard_map/ppermute | solution.py:282
  51.4 7.5 %collective-permute-start.6 = (bf16[2,4,4,1024]{3,2,1,0:T(4,128)(2,1)S(1)}, bf16[2,4,4,1024]{3,2,1,0:T(4,128)(2,1)S(1)}, u32[]{:S(2)}, u32[]{:S(2)}) collective-permute-start(bf16[2,4,4,1024]{3,2,1,0:T(4,128)(2,1)S(1)} %bitcast_dynamic-update-slice_fusion.4), channel_id=1, source_target_pairs={{0,8},{8,16},{16,24},{24,0},{1,9},{9,17},{17,25},{25,1},{2,10},{10... | collective-permute-start | bytes 196616 | tf_op jit(solution)/shard_map/ppermute | solution.py:282
  54.9 4.3 %collective-permute-start.7 = (bf16[2,4,4,1024]{3,2,1,0:T(4,128)(2,1)S(1)}, bf16[2,4,4,1024]{3,2,1,0:T(4,128)(2,1)S(1)}, u32[]{:S(2)}, u32[]{:S(2)}) collective-permute-start(bf16[2,4,4,1024]{3,2,1,0:T(4,128)(2,1)S(1)} %bitcast_dynamic-update-slice_fusion.4), channel_id=1, source_target_pairs={{0,16},{8,24},{16,0},{24,8},{1,17},{9,25},{17,1},{25,9},{2,18},{10... | collective-permute-start | bytes 196616 | tf_op jit(solution)/shard_map/ppermute | solution.py:282
  55.9 4.9 %collective-permute-start.8 = (bf16[2,4,4,1024]{3,2,1,0:T(4,128)(2,1)S(1)}, bf16[2,4,4,1024]{3,2,1,0:T(4,128)(2,1)S(1)}, u32[]{:S(2)}, u32[]{:S(2)}) collective-permute-start(bf16[2,4,4,1024]{3,2,1,0:T(4,128)(2,1)S(1)} %bitcast_dynamic-update-slice_fusion.4), channel_id=1, source_target_pairs={{0,24},{8,0},{16,8},{24,16},{1,25},{9,1},{17,9},{25,17},{2,26},{10... | collective-permute-start | bytes 196616 | tf_op jit(solution)/shard_map/ppermute | solution.py:282
  64.7 1.6 %collective-permute-start.9 = (f32[64,32,16]{0,1,2:T(8,128)S(1)}, f32[64,32,16]{0,1,2:T(8,128)S(1)}, u32[]{:S(2)}, u32[]{:S(2)}) collective-permute-start(f32[64,32,16]{0,1,2:T(8,128)S(1)} %pad_maximum_fusion), channel_id=1, source_target_pairs={{0,4},{4,0},{1,5},{5,1},{2,6},{6,2},{3,7},{7,3},{8,12},{12,8},{9,1... | collective-permute-start | bytes 393224 | tf_op jit(solution)/shard_map/ppermute | solution.py:294
  66.8 5.7 %copy-start.7 = (f32[8]{0:T(128)S(1)}, f32[8]{0:T(128)}, u32[]{:S(2)}) copy-start(f32[8]{0:T(128)} %param.25) | copy-start | bytes 100
  70.5 4.1 %copy-start.8 = (bf16[1,16,8,1024]{3,2,1,0:T(8,128)(2,1)S(1)}, bf16[1,16,8,1024]{3,2,1,0:T(8,128)(2,1)}, u32[]{:S(2)}) copy-start(bf16[1,16,8,1024]{3,2,1,0:T(8,128)(2,1)} %param.27) | copy-start | bytes 786436
  76.6 1.4 %collective-permute-start.10 = (f32[16,32,16]{1,2,0:T(8,128)S(1)}, f32[16,32,16]{1,2,0:T(8,128)S(1)}, u32[]{:S(2)}, u32[]{:S(2)}) collective-permute-start(f32[16,32,16]{1,2,0:T(8,128)S(1)} %pad_maximum_fusion.1), channel_id=1, source_target_pairs={{0,4},{4,0},{1,5},{5,1},{2,6},{6,2},{3,7},{7,3},{8,12},{12,8},{9,1... | collective-permute-start | bytes 98312 | tf_op jit(solution)/shard_map/ppermute | solution.py:294
  78.6 5.4 %collective-permute-start.13 = (f32[48,8,16]{0,1,2:T(8,128)S(1)}, f32[48,8,16]{0,1,2:T(8,128)S(1)}, u32[]{:S(2)}, u32[]{:S(2)}) collective-permute-start(f32[48,8,16]{0,1,2:T(8,128)S(1)} %pad_maximum_fusion.5), channel_id=1, source_target_pairs={{0,24},{8,0},{16,8},{24,16},{1,25},{9,1},{17,9},{25,17},{2,26},{10... | collective-permute-start | bytes 73736 | tf_op jit(solution)/shard_map/ppermute | solution.py:294
  82.1 5.0 %collective-permute-start.12 = (f32[48,8,16]{0,1,2:T(8,128)S(1)}, f32[48,8,16]{0,1,2:T(8,128)S(1)}, u32[]{:S(2)}, u32[]{:S(2)}) collective-permute-start(f32[48,8,16]{0,1,2:T(8,128)S(1)} %pad_maximum_fusion.4), channel_id=1, source_target_pairs={{0,16},{8,24},{16,0},{24,8},{1,17},{9,25},{17,1},{25,9},{2,18},{10... | collective-permute-start | bytes 73736 | tf_op jit(solution)/shard_map/ppermute | solution.py:294
  82.8 5.3 %collective-permute-start.11 = (f32[48,8,16]{0,1,2:T(8,128)S(1)}, f32[48,8,16]{0,1,2:T(8,128)S(1)}, u32[]{:S(2)}, u32[]{:S(2)}) collective-permute-start(f32[48,8,16]{0,1,2:T(8,128)S(1)} %pad_maximum_fusion.3), channel_id=1, source_target_pairs={{0,8},{8,16},{16,24},{24,0},{1,9},{9,17},{17,25},{25,1},{2,10},{10... | collective-permute-start | bytes 73736 | tf_op jit(solution)/shard_map/ppermute | solution.py:294

commit v11 on v10

--- a/solution.py
+++ b/solution.py
@@ -132,12 +132,14 @@
 
     def collect(final_ref):
         def store(index, carry):
-            tracer = index // chunks
-            cols = chunk_at(index % chunks)
-            out_ref[tracer, :, cols] = jnp.sum(final_ref[tracer, :, cols], axis=0, keepdims=True)
+            cols = chunk_at(index)
+            for tracer in range(tracers):
+                out_ref[tracer : tracer + 1, cols] = jnp.sum(
+                    final_ref[tracer, :, cols], axis=0, keepdims=True
+                )
             return carry
 
-        lax.fori_loop(0, tracers * chunks, store, 0, unroll=UNROLL)
+        lax.fori_loop(0, chunks, store, 0, unroll=UNROLL)
 
     @pl.when(total % 2 == 1)
     def _():
@@ -165,7 +167,7 @@
     vmem = pl.BlockSpec(memory_space=pltpu.VMEM)
     return pl.pallas_call(
         solve_kernel,
-        out_shape=jax.ShapeDtypeStruct((tracers, 1, width), jnp.float32),
+        out_shape=jax.ShapeDtypeStruct((tracers, width), jnp.float32),
         in_specs=[smem, smem] + [vmem] * 4,
         out_specs=vmem,
         scratch_shapes=[

time: 90.9 us -> 89.6 us (0.986)
  Pallas kernels: 16.8 us -> 7.51 us
  starting transfers between devices: 26.8 us -> 32.8 us
  waiting for transfers between devices: 12.6 us -> 15.8 us
  other arithmetic: 14.4 us -> 12.7 us
    pallas_call x1, Pallas kernels: 16.8 us -> 7.51 us  [solve_rows(): pl.pallas_call(solve_kernel, out_shape=jax.ShapeDtypeStruct((tracers, wid...]
    ppermute x7, starting transfers between devices: 16.2 us -> 22 us  [gather_along(): lax.ppermute(block, axis, [(i, (i + shift) % count) for i in range(count)])]
    ppermute x7, waiting for transfers between devices: 4.13 us -> 7.26 us  [gather_along(): lax.ppermute(block, axis, [(i, (i + shift) % count) for i in range(count)])]
    pallas_call x1 -> x0, other arithmetic: 1.63 us -> none  [solve_rows(): pl.pallas_call(solve_kernel, out_shape=jax.ShapeDtypeStruct((tracers, 1,...]
    reshape x1, local copies, waits for them, and re-layouts: 0.67 us -> 1.62 us  [body(): row_sums.reshape(C, SW, FACTOR).sum(axis=2) * (1.0 / (FACTOR * FACTOR))]
  transfers between devices with their start and end apart: 14 -> 14, of which waited for: 10 -> 11; matrix products, arithmetic and copies ran while one was open for 11% -> 11% of each run, Pallas kernels for 0% -> 0%
where the time goes in v11:
time: 89.6 us; the launch traced here: 89.9 us
  starting transfers between devices  32.8 us (37%)
  waiting for transfers between devices  15.8 us (18%)
  other arithmetic  12.7 us (14%)
  local copies, waits for them, and re-layouts  10.2 us (11%)
  matrix products  8.62 us (10%)
  Pallas kernels  7.51 us (8%)
  between operations  2.08 us (2%)
    ppermute x7, starting transfers between devices, gather_along(): lax.ppermute(block, axis, [(i, (i + shift) % count) for i in range(count)])  22 us
    pallas_call x1, Pallas kernels, solve_rows(): pl.pallas_call(solve_kernel, out_shape=jax.ShapeDtypeStruct((tracers, wid...  7.51 us
    ppermute x7, waiting for transfers between devices, gather_along(): lax.ppermute(block, axis, [(i, (i + shift) % count) for i in range(count)])  7.26 us
    ppermute x5, waiting for transfers between devices, packed_ppermute(): packed = lax.ppermute(jnp.concatenate(parts, axis=0), axis, perm)  5.59 us
    ppermute x5, starting transfers between devices, packed_ppermute(): packed = lax.ppermute(jnp.concatenate(parts, axis=0), axis, perm)  4.3 us
    ppermute x1, starting transfers between devices, halo_rows(): below = lax.ppermute(block[:, :1], axis, backward)  3.42 us
    ppermute x1, starting transfers between devices, halo_rows(): above = lax.ppermute(block[:, -1:], axis, forward)  3.08 us
    ppermute x1, waiting for transfers between devices, halo_rows(): below = lax.ppermute(block[:, :1], axis, backward)  2.99 us
  transfers between devices with their start and end apart: 14, of which 11 were waited for; matrix products, arithmetic and copies ran while one was open for 11% of the time, Pallas kernels for 0%

profile of v11, /device:TPU:0, one launch (start us, length us, event | category | flops | bytes accessed | tf_op | source)
XLA Modules:
  0.0 89.9 jit_solution(5257217834578297646)
XLA Ops:
  0.6 2.0 %fusion.145 = (bf16[4,1,16384]{2,1,0:T(2,128)(2,1)S(1)}, bf16[4,1,16384]{2,1,0:T(2,128)(2,1)S(1)}) fusion(bf16[4,16,16384]{2,1,0:T(8,128)(2,1)} %field_ref.1), kind=kLoop, calls=%fused_computation.240 | loop fusion | bytes 524288 | tf_op jit(solution)/shard_map/slice | solution.py:39
  2.6 3.1 %collective-permute-start = (bf16[4,1,16384]{2,1,0:T(2,128)(2,1)S(1)}, bf16[4,1,16384]{2,1,0:T(2,128)(2,1)S(1)}, u32[]{:S(2)}, u32[]{:S(2)}) collective-permute-start(bf16[4,1,16384]{2,1,0:T(2,128)(2,1)S(1)} %get-tuple-element.8), channel_id=1, source_target_pairs={{0,1},{1,2},{2,3},{3,4},{4,5},{5,6},{6,7},{7,8},{8,9},{9,10},{10,1... | collective-permute-start | bytes 393224 | tf_op jit(solution)/shard_map/ppermute | solution.py:38
  5.7 3.4 %collective-permute-start.1 = (bf16[4,1,16384]{2,1,0:T(2,128)(2,1)S(1)}, bf16[4,1,16384]{2,1,0:T(2,128)(2,1)S(1)}, u32[]{:S(2)}, u32[]{:S(2)}) collective-permute-start(bf16[4,1,16384]{2,1,0:T(2,128)(2,1)S(1)} %get-tuple-element.7), channel_id=1, source_target_pairs={{1,0},{2,1},{3,2},{4,3},{5,4},{6,5},{7,6},{8,7},{9,8},{10,9},{11,1... | collective-permute-start | bytes 393224 | tf_op jit(solution)/shard_map/ppermute | solution.py:39
  9.1 1.0 %fusion.148 = (f32[1,16384]{1,0:T(1,128)S(1)}, f32[1,16384]{1,0:T(1,128)S(1)}) fusion(bf16[2,16384]{1,0:T(2,128)(2,1)} %param.19), kind=kLoop, calls=%fused_computation.243 | loop fusion | bytes 262144 | tf_op jit(solution)/shard_map/slice | solution.py:162
  10.1 0.8 slice_bitcast_fusion.13
  11.6 0.8 convert_element_type.71
  12.3 0.3 cosine_multiply_fusion
  12.6 0.8 broadcast_multiply_fusion
  13.4 0.2 multiply_multiply_fusion
  13.7 1.8 %maximum_multiply_fusion.coef_ref = f32[3,16,16384]{2,1,0:T(8,128)} fusion(f32[1,16,16384]{2,1,0:T(8,128)S(1)} %get-tuple-element.59, f32[1,16,16384]{2,1,0:T(8,128)S(1)} %get-tuple-element.60, f32[1,16,16384]{2,1,0:T(8,128)S(1)} %broadcast_multiply_fusion, f32[]{:T(128)} %bitcast), kind=kLoop, calls=%fused_computation | loop fusion | flops 2359296 | bytes 6291460 | tf_op jit(solution)/shard_map/mul | solution.py:159
  15.8 0.3 negate_convert_fusion
  16.1 3.0 %collective-permute-done.1.below_ref = bf16[4,1,16384]{2,1,0:T(2,128)(2,1)S(1)} collective-permute-done((bf16[4,1,16384]{2,1,0:T(2,128)(2,1)S(1)}, bf16[4,1,16384]{2,1,0:T(2,128)(2,1)S(1)}, u32[]{:S(2)}, u32[]{:S(2)}) %collective-permute-start.1) | collective-permute-done | bytes 131104 | tf_op jit(solution)/shard_map/ppermute | solution.py:39
  19.1 0.7 copy-done.2
  19.8 7.5 %shard_map.157 = f32[4,16384]{1,0:T(4,128)} custom-call(f32[1]{0:T(128)} %div.12.step_ref, s32[1]{0:T(128)S(6)} %copy.161.count_ref, bf16[4,16,16384]{2,1,0:T(8,128)(2,1)} %field_ref.1, bf16[4,1,16384]{2,1,0:T(2,128)(2,1)} %copy-done.1, bf16[4,1,16384]{2,1,0:T(2,128)(2,1)} %copy-done.2, f32[3,16,16384]{2,1,0:T(8,128)} %maximum_multiply_fusion.coef_ref), custom_call_target="tpu_custom_call" | custom-call | tf_op jit(solution)/shard_map/pallas_call | solution.py:168
  27.3 1.6 %reshape.218 = f32[4,1024,16]{2,1,0:T(8,128)S(1)} reshape(f32[4,16384]{1,0:T(4,128)} %shard_map.157) | data formatting | bytes 524288 | tf_op jit(solution)/shard_map/reshape | solution.py:357
  29.0 0.6 reduce_sum.27
  29.6 1.6 %collective-permute-start.2 = (bf16[4,1024]{1,0:T(4,128)(2,1)S(1)}, bf16[4,1024]{1,0:T(4,128)(2,1)S(1)}, u32[]{:S(2)}, u32[]{:S(2)}) collective-permute-start(bf16[4,1024]{1,0:T(4,128)(2,1)S(1)} %multiply_convert_fusion), channel_id=1, source_target_pairs={{0,1},{1,2},{2,3},{3,0},{4,5},{5,6},{6,7},{7,4},{8,9},{9,10},{10,1... | collective-permute-start | bytes 24584 | tf_op jit(solution)/shard_map/ppermute | solution.py:284
  31.2 17.4 %collective-permute-start.3 = (bf16[4,1024]{1,0:T(4,128)(2,1)S(1)}, bf16[4,1024]{1,0:T(4,128)(2,1)S(1)}, u32[]{:S(2)}, u32[]{:S(2)}) collective-permute-start(bf16[4,1024]{1,0:T(4,128)(2,1)S(1)} %multiply_convert_fusion), channel_id=1, source_target_pairs={{0,2},{1,3},{2,0},{3,1},{4,6},{5,7},{6,4},{7,5},{8,10},{9,11},{10,... | collective-permute-start | bytes 24584 | tf_op jit(solution)/shard_map/ppermute | solution.py:284
  48.6 0.6 convert_dynamic-update-slice_fusion
  49.2 0.4 collective-permute-done.2
  49.7 0.6 collective-permute-done.3
  50.3 2.0 %collective-permute-done.4 = bf16[4,1024]{1,0:T(4,128)(2,1)S(1)} collective-permute-done((bf16[4,1024]{1,0:T(4,128)(2,1)S(1)}, bf16[4,1024]{1,0:T(4,128)(2,1)S(1)}, u32[]{:S(2)}, u32[]{:S(2)}) %collective-permute-start.4) | collective-permute-done | bytes 8224 | tf_op jit(solution)/shard_map/ppermute | solution.py:284
  52.4 1.1 %collective-permute-done.5 = bf16[4,4,1024]{2,1,0:T(4,128)(2,1)S(1)} collective-permute-done((bf16[4,4,1024]{2,1,0:T(4,128)(2,1)S(1)}, bf16[4,4,1024]{2,1,0:T(4,128)(2,1)S(1)}, u32[]{:S(2)}, u32[]{:S(2)}) %collective-permute-start.5) | collective-permute-done | bytes 32800 | tf_op jit(solution)/shard_map/ppermute | solution.py:284
  53.6 2.0 %collective-permute-start.7 = (bf16[2,4,4,1024]{3,2,1,0:T(4,128)(2,1)S(1)}, bf16[2,4,4,1024]{3,2,1,0:T(4,128)(2,1)S(1)}, u32[]{:S(2)}, u32[]{:S(2)}) collective-permute-start(bf16[2,4,4,1024]{3,2,1,0:T(4,128)(2,1)S(1)} %bitcast_dynamic-update-slice_fusion.4), channel_id=1, source_target_pairs={{0,16},{8,24},{16,0},{24,8},{1,17},{9,25},{17,1},{25,9},{2,18},{10... | collective-permute-start | bytes 196616 | tf_op jit(solution)/shard_map/ppermute | solution.py:284
  55.6 0.9 %collective-permute-start.8 = (bf16[2,4,4,1024]{3,2,1,0:T(4,128)(2,1)S(1)}, bf16[2,4,4,1024]{3,2,1,0:T(4,128)(2,1)S(1)}, u32[]{:S(2)}, u32[]{:S(2)}) collective-permute-start(bf16[2,4,4,1024]{3,2,1,0:T(4,128)(2,1)S(1)} %bitcast_dynamic-update-slice_fusion.4), channel_id=1, source_target_pairs={{0,24},{8,0},{16,8},{24,16},{1,25},{9,1},{17,9},{25,17},{2,26},{10... | collective-permute-start | bytes 196616 | tf_op jit(solution)/shard_map/ppermute | solution.py:284
  56.7 2.7 %collective-permute-done.6 = bf16[2,4,4,1024]{3,2,1,0:T(4,128)(2,1)S(1)} collective-permute-done((bf16[2,4,4,1024]{3,2,1,0:T(4,128)(2,1)S(1)}, bf16[2,4,4,1024]{3,2,1,0:T(4,128)(2,1)S(1)}, u32[]{:S(2)}, u32[]{:S(2)}) %collective-permute-start.6) | collective-permute-done | bytes 65568 | tf_op jit(solution)/shard_map/ppermute | solution.py:284
  59.4 0.4 collective-permute-done.8
  59.9 0.5 fusion.4
  60.5 0.9 %fusion.60 = f32[16,32,32]{1,2,0:T(8,128)S(1)} fusion(bf16[16,32,1024]{2,1,0:T(8,128)(2,1)S(1)} %fusion.4, bf16[1024,16]{0,1:T(8,128)(2,1)S(1)} %get-tuple-element.61, bf16[1024,16]{0,1:T(8,128)(2,1)S(1)} %get-tuple-element.62), kind=kOutput, calls=%fused_computation.138 | convolution fusion | flops 33685504 | bytes 1179648 | tf_op jit(solution)/shard_map/yhx,xk->yhk/dot_general | solution.py:370
  61.4 0.5 fusion.41
  61.9 0.5 fusion.45
  62.5 0.5 fusion.8
  63.0 0.5 fusion.10
  63.8 0.3 sine_multiply_fusion
  64.1 1.3 %collective-permute-done.9 = f32[64,32,16]{0,1,2:T(8,128)S(1)} collective-permute-done((f32[64,32,16]{0,1,2:T(8,128)S(1)}, f32[64,32,16]{0,1,2:T(8,128)S(1)}, u32[]{:S(2)}, u32[]{:S(2)}) %collective-permute-start.9) | collective-permute-done | bytes 131104 | tf_op jit(solution)/shard_map/ppermute | solution.py:296
  65.5 0.2 copy.112
  65.6 0.2 copy.113
  65.8 2.4 %fusion.3 = (f32[8,32,16]{1,2,0:T(8,128)S(1)}, f32[8,32,16]{1,2,0:T(8,128)S(1)}) fusion(f32[32,32,16]{1,2,0:T(8,128)S(1)} %copy.113, f32[32,32,16]{1,2,0:T(8,128)S(1)} %copy.112, bf16[2,32,8,32,16]{3,4,2,1,0:T(8,128)(2,1)} %param.26), kind=kLoop, calls=%fused_computation.8 | loop fusion | flops 1302528 | bytes 688128 | tf_op jit(solution)/shard_map/reduce_sum | solution.py:250
  68.2 0.6 fusion.76
  68.8 0.7 fusion.66
  69.5 0.7 convolution_subtract_fusion.2
  70.2 0.7 convolution_add_fusion.2
  71.0 0.6 convolution_multiply_fusion
  71.5 0.3 fusion.6
  71.8 1.8 %fusion.34 = bf16[1,16,8,1024]{3,2,1,0:T(8,128)(2,1)} fusion(f32[16,8,1024]{2,1,0:T(8,128)S(1)} %fusion.6), kind=kLoop, calls=%fused_computation.73 | loop fusion | flops 8519680 | bytes 786432 | tf_op jit(solution)/shard_map/broadcast_in_dim | solution.py:394
  73.6 0.3 fusion.35
  74.2 0.3 fusion.71
  74.6 0.3 fusion.73
  74.9 0.3 fusion.12
  75.2 0.3 fusion.14
  75.6 0.2 collective-permute-start.10
  75.8 0.2 constant_dynamic-slice_fusion
  76.0 0.2 constant_dynamic-slice_fusion.1
  76.3 0.7 collective-permute-done.10
  77.0 0.1 constant_dynamic-slice_fusion.3
  77.6 2.2 %collective-permute-start.13 = (f32[48,8,16]{0,1,2:T(8,128)S(1)}, f32[48,8,16]{0,1,2:T(8,128)S(1)}, u32[]{:S(2)}, u32[]{:S(2)}) collective-permute-start(f32[48,8,16]{0,1,2:T(8,128)S(1)} %pad_maximum_fusion.5), channel_id=1, source_target_pairs={{0,24},{8,0},{16,8},{24,16},{1,25},{9,1},{17,9},{25,17},{2,26},{10... | collective-permute-start | bytes 73736 | tf_op jit(solution)/shard_map/ppermute | solution.py:296
  80.2 1.7 %collective-permute-start.12 = (f32[48,8,16]{0,1,2:T(8,128)S(1)}, f32[48,8,16]{0,1,2:T(8,128)S(1)}, u32[]{:S(2)}, u32[]{:S(2)}) collective-permute-start(f32[48,8,16]{0,1,2:T(8,128)S(1)} %pad_maximum_fusion.4), channel_id=1, source_target_pairs={{0,16},{8,24},{16,0},{24,8},{1,17},{9,25},{17,1},{25,9},{2,18},{10... | collective-permute-start | bytes 73736 | tf_op jit(solution)/shard_map/ppermute | solution.py:296
  82.4 0.2 add_bitcast_fusion.3
  82.8 1.7 %collective-permute-done.12 = f32[48,8,16]{0,1,2:T(8,128)S(1)} collective-permute-done((f32[48,8,16]{0,1,2:T(8,128)S(1)}, f32[48,8,16]{0,1,2:T(8,128)S(1)}, u32[]{:S(2)}, u32[]{:S(2)}) %collective-permute-start.12) | collective-permute-done | bytes 24608 | tf_op jit(solution)/shard_map/ppermute | solution.py:296
  85.5 1.9 %collective-permute-done.11 = f32[48,8,16]{0,1,2:T(8,128)S(1)} collective-permute-done((f32[48,8,16]{0,1,2:T(8,128)S(1)}, f32[48,8,16]{0,1,2:T(8,128)S(1)}, u32[]{:S(2)}, u32[]{:S(2)}) %collective-permute-start.11) | collective-permute-done | bytes 24608 | tf_op jit(solution)/shard_map/ppermute | solution.py:296
  88.0 0.1 add_bitcast_fusion
  88.1 0.1 add_bitcast_fusion.1
  88.3 0.1 add_bitcast_fusion.2
  88.4 1.4 %fusion.17 = f32[2,16,8,8,16]{4,3,2,1,0:T(8,128)} fusion(f32[1,16,8,8,16]{4,3,2,1,0:T(8,128)S(1)} %get-tuple-element.28, f32[1,16,8,8,16]{4,3,2,1,0:T(8,128)S(1)} %get-tuple-element.27, f32[1,16,8,8,16]{4,3,2,1,0:T(8,128)S(1)} %get-tuple-element.26, f32[1,16,8,8,16]{4,3,2,1,0:T(8,128)S(1)} %get-tuple-element.25, ...), kind=kLoop, calls=%fused_computation.32 | loop fusion | flops 262144 | bytes 655360 | tf_op jit(solution)/shard_map/div | solution.py:408
  (83 shorter events, 4.5 us)
Async XLA Ops:
  0.6 70.9 %copy-start = (bf16[32,8]{0,1:T(8,128)(2,1)S(1)}, bf16[32,8]{0,1:T(8,128)(2,1)}, u32[]{:S(2)}) copy-start(bf16[32,8]{0,1:T(8,128)(2,1)} %param.24) | copy-start | bytes 1540
  2.6 13.5 %collective-permute-start = (bf16[4,1,16384]{2,1,0:T(2,128)(2,1)S(1)}, bf16[4,1,16384]{2,1,0:T(2,128)(2,1)S(1)}, u32[]{:S(2)}, u32[]{:S(2)}) collective-permute-start(bf16[4,1,16384]{2,1,0:T(2,128)(2,1)S(1)} %get-tuple-element.8), channel_id=1, source_target_pairs={{0,1},{1,2},{2,3},{3,4},{4,5},{5,6},{6,7},{7,8},{8,9},{9,10},{10,1... | collective-permute-start | bytes 393224 | tf_op jit(solution)/shard_map/ppermute | solution.py:38
  5.7 13.4 %collective-permute-start.1 = (bf16[4,1,16384]{2,1,0:T(2,128)(2,1)S(1)}, bf16[4,1,16384]{2,1,0:T(2,128)(2,1)S(1)}, u32[]{:S(2)}, u32[]{:S(2)}) collective-permute-start(bf16[4,1,16384]{2,1,0:T(2,128)(2,1)S(1)} %get-tuple-element.7), channel_id=1, source_target_pairs={{1,0},{2,1},{3,2},{4,3},{5,4},{6,5},{7,6},{8,7},{9,8},{10,9},{11,1... | collective-permute-start | bytes 393224 | tf_op jit(solution)/shard_map/ppermute | solution.py:39
  13.7 1.9 %copy-start.6 = (s32[32]{0:T(128)S(1)}, s32[32]{0:T(128)}, u32[]{:S(2)}) copy-start(s32[32]{0:T(128)} %param.20) | copy-start | bytes 388
  16.1 3.0 %copy-start.1 = (bf16[4,1,16384]{2,1,0:T(2,128)(2,1)}, bf16[4,1,16384]{2,1,0:T(2,128)(2,1)S(1)}, u32[]{:S(2)}) copy-start(bf16[4,1,16384]{2,1,0:T(2,128)(2,1)S(1)} %collective-permute-done.above_ref) | copy-start | bytes 393220
  19.1 0.7 copy-start.2
  28.9 31.0 %copy-start.3 = (bf16[1,16,4,1024]{3,2,1,0:T(4,128)(2,1)S(1)}, bf16[1,16,4,1024]{3,2,1,0:T(4,128)(2,1)}, u32[]{:S(2)}) copy-start(bf16[1,16,4,1024]{3,2,1,0:T(4,128)(2,1)} %param.21) | copy-start | bytes 393220
  28.9 31.0 %copy-start.4 = (bf16[4,32]{1,0:T(4,128)(2,1)S(1)}, bf16[4,32]{1,0:T(4,128)(2,1)}, u32[]{:S(2)}) copy-start(bf16[4,32]{1,0:T(4,128)(2,1)} %param.22) | copy-start | bytes 772
  28.9 31.0 %copy-start.5 = (f32[32]{0:T(128)S(1)}, f32[32]{0:T(128)}, u32[]{:S(2)}) copy-start(f32[32]{0:T(128)} %param.23) | copy-start | bytes 388
  29.6 20.1 %collective-permute-start.2 = (bf16[4,1024]{1,0:T(4,128)(2,1)S(1)}, bf16[4,1024]{1,0:T(4,128)(2,1)S(1)}, u32[]{:S(2)}, u32[]{:S(2)}) collective-permute-start(bf16[4,1024]{1,0:T(4,128)(2,1)S(1)} %multiply_convert_fusion), channel_id=1, source_target_pairs={{0,1},{1,2},{2,3},{3,0},{4,5},{5,6},{6,7},{7,4},{8,9},{9,10},{10,1... | collective-permute-start | bytes 24584 | tf_op jit(solution)/shard_map/ppermute | solution.py:284
  31.2 19.0 %collective-permute-start.3 = (bf16[4,1024]{1,0:T(4,128)(2,1)S(1)}, bf16[4,1024]{1,0:T(4,128)(2,1)S(1)}, u32[]{:S(2)}, u32[]{:S(2)}) collective-permute-start(bf16[4,1024]{1,0:T(4,128)(2,1)S(1)} %multiply_convert_fusion), channel_id=1, source_target_pairs={{0,2},{1,3},{2,0},{3,1},{4,6},{5,7},{6,4},{7,5},{8,10},{9,11},{10,... | collective-permute-start | bytes 24584 | tf_op jit(solution)/shard_map/ppermute | solution.py:284
  48.6 3.7 %collective-permute-start.4 = (bf16[4,1024]{1,0:T(4,128)(2,1)S(1)}, bf16[4,1024]{1,0:T(4,128)(2,1)S(1)}, u32[]{:S(2)}, u32[]{:S(2)}) collective-permute-start(bf16[4,1024]{1,0:T(4,128)(2,1)S(1)} %multiply_convert_fusion), channel_id=1, source_target_pairs={{0,3},{1,0},{2,1},{3,2},{4,7},{5,4},{6,5},{7,6},{8,11},{9,8},{10,9... | collective-permute-start | bytes 24584 | tf_op jit(solution)/shard_map/ppermute | solution.py:284
  52.2 1.3 %collective-permute-start.5 = (bf16[4,4,1024]{2,1,0:T(4,128)(2,1)S(1)}, bf16[4,4,1024]{2,1,0:T(4,128)(2,1)S(1)}, u32[]{:S(2)}, u32[]{:S(2)}) collective-permute-start(bf16[4,4,1024]{2,1,0:T(4,128)(2,1)S(1)} %bitcast_dynamic-update-slice_fusion.6), channel_id=1, source_target_pairs={{0,4},{4,0},{1,5},{5,1},{2,6},{6,2},{3,7},{7,3},{8,12},{12,8},{9,1... | collective-permute-start | bytes 98312 | tf_op jit(solution)/shard_map/ppermute | solution.py:284
  53.5 5.8 %collective-permute-start.6 = (bf16[2,4,4,1024]{3,2,1,0:T(4,128)(2,1)S(1)}, bf16[2,4,4,1024]{3,2,1,0:T(4,128)(2,1)S(1)}, u32[]{:S(2)}, u32[]{:S(2)}) collective-permute-start(bf16[2,4,4,1024]{3,2,1,0:T(4,128)(2,1)S(1)} %bitcast_dynamic-update-slice_fusion.4), channel_id=1, source_target_pairs={{0,8},{8,16},{16,24},{24,0},{1,9},{9,17},{17,25},{25,1},{2,10},{10... | collective-permute-start | bytes 196616 | tf_op jit(solution)/shard_map/ppermute | solution.py:284
  53.6 5.8 %collective-permute-start.7 = (bf16[2,4,4,1024]{3,2,1,0:T(4,128)(2,1)S(1)}, bf16[2,4,4,1024]{3,2,1,0:T(4,128)(2,1)S(1)}, u32[]{:S(2)}, u32[]{:S(2)}) collective-permute-start(bf16[2,4,4,1024]{3,2,1,0:T(4,128)(2,1)S(1)} %bitcast_dynamic-update-slice_fusion.4), channel_id=1, source_target_pairs={{0,16},{8,24},{16,0},{24,8},{1,17},{9,25},{17,1},{25,9},{2,18},{10... | collective-permute-start | bytes 196616 | tf_op jit(solution)/shard_map/ppermute | solution.py:284
  55.6 4.3 %collective-permute-start.8 = (bf16[2,4,4,1024]{3,2,1,0:T(4,128)(2,1)S(1)}, bf16[2,4,4,1024]{3,2,1,0:T(4,128)(2,1)S(1)}, u32[]{:S(2)}, u32[]{:S(2)}) collective-permute-start(bf16[2,4,4,1024]{3,2,1,0:T(4,128)(2,1)S(1)} %bitcast_dynamic-update-slice_fusion.4), channel_id=1, source_target_pairs={{0,24},{8,0},{16,8},{24,16},{1,25},{9,1},{17,9},{25,17},{2,26},{10... | collective-permute-start | bytes 196616 | tf_op jit(solution)/shard_map/ppermute | solution.py:284
  63.7 1.6 %collective-permute-start.9 = (f32[64,32,16]{0,1,2:T(8,128)S(1)}, f32[64,32,16]{0,1,2:T(8,128)S(1)}, u32[]{:S(2)}, u32[]{:S(2)}) collective-permute-start(f32[64,32,16]{0,1,2:T(8,128)S(1)} %pad_maximum_fusion), channel_id=1, source_target_pairs={{0,4},{4,0},{1,5},{5,1},{2,6},{6,2},{3,7},{7,3},{8,12},{12,8},{9,1... | collective-permute-start | bytes 393224 | tf_op jit(solution)/shard_map/ppermute | solution.py:296
  65.8 5.7 %copy-start.7 = (f32[8]{0:T(128)S(1)}, f32[8]{0:T(128)}, u32[]{:S(2)}) copy-start(f32[8]{0:T(128)} %param.25) | copy-start | bytes 100
  69.5 4.1 %copy-start.8 = (bf16[1,16,8,1024]{3,2,1,0:T(8,128)(2,1)S(1)}, bf16[1,16,8,1024]{3,2,1,0:T(8,128)(2,1)}, u32[]{:S(2)}) copy-start(bf16[1,16,8,1024]{3,2,1,0:T(8,128)(2,1)} %param.27) | copy-start | bytes 786436
  75.6 1.4 %collective-permute-start.10 = (f32[16,32,16]{1,2,0:T(8,128)S(1)}, f32[16,32,16]{1,2,0:T(8,128)S(1)}, u32[]{:S(2)}, u32[]{:S(2)}) collective-permute-start(f32[16,32,16]{1,2,0:T(8,128)S(1)} %pad_maximum_fusion.1), channel_id=1, source_target_pairs={{0,4},{4,0},{1,5},{5,1},{2,6},{6,2},{3,7},{7,3},{8,12},{12,8},{9,1... | collective-permute-start | bytes 98312 | tf_op jit(solution)/shard_map/ppermute | solution.py:296
  77.6 5.0 %collective-permute-start.13 = (f32[48,8,16]{0,1,2:T(8,128)S(1)}, f32[48,8,16]{0,1,2:T(8,128)S(1)}, u32[]{:S(2)}, u32[]{:S(2)}) collective-permute-start(f32[48,8,16]{0,1,2:T(8,128)S(1)} %pad_maximum_fusion.5), channel_id=1, source_target_pairs={{0,24},{8,0},{16,8},{24,16},{1,25},{9,1},{17,9},{25,17},{2,26},{10... | collective-permute-start | bytes 73736 | tf_op jit(solution)/shard_map/ppermute | solution.py:296
  80.2 4.3 %collective-permute-start.12 = (f32[48,8,16]{0,1,2:T(8,128)S(1)}, f32[48,8,16]{0,1,2:T(8,128)S(1)}, u32[]{:S(2)}, u32[]{:S(2)}) collective-permute-start(f32[48,8,16]{0,1,2:T(8,128)S(1)} %pad_maximum_fusion.4), channel_id=1, source_target_pairs={{0,16},{8,24},{16,0},{24,8},{1,17},{9,25},{17,1},{25,9},{2,18},{10... | collective-permute-start | bytes 73736 | tf_op jit(solution)/shard_map/ppermute | solution.py:296
  82.2 5.2 %collective-permute-start.11 = (f32[48,8,16]{0,1,2:T(8,128)S(1)}, f32[48,8,16]{0,1,2:T(8,128)S(1)}, u32[]{:S(2)}, u32[]{:S(2)}) collective-permute-start(f32[48,8,16]{0,1,2:T(8,128)S(1)} %pad_maximum_fusion.3), channel_id=1, source_target_pairs={{0,8},{8,16},{16,24},{24,0},{1,9},{9,17},{17,25},{25,1},{2,10},{10... | collective-permute-start | bytes 73736 | tf_op jit(solution)/shard_map/ppermute | solution.py:296

commit v12 on v11

--- a/solution.py
+++ b/solution.py
@@ -78,13 +78,6 @@
     def chunk_at(index):
         return pl.ds(pl.multiple_of(index * CHUNK, CHUNK), CHUNK)
 
-    def prepare(index, carry):
-        cols = chunk_at(index)
-        for tracer in range(tracers):
-            first_ref[tracer, :, cols] = field_ref[tracer, :, cols].astype(jnp.float32)
-        return carry
-
-    lax.fori_loop(0, chunks, prepare, 0, unroll=UNROLL)
     row_ids = lax.broadcasted_iota(jnp.int32, (rows, CHUNK), 0)
 
     def sweep(source_ref, target_ref):
@@ -96,9 +89,14 @@
             along = coef_ref[1, :, cols]
             across = coef_ref[2, :, cols]
             for tracer in range(tracers):
-                current = source_ref[tracer, :, cols]
+                current = source_ref[tracer, :, cols].astype(jnp.float32)
                 extended = jnp.concatenate(
-                    [source_ref[tracer, :, before], current, source_ref[tracer, :, after]], axis=1
+                    [
+                        source_ref[tracer, :, before].astype(jnp.float32),
+                        current,
+                        source_ref[tracer, :, after].astype(jnp.float32),
+                    ],
+                    axis=1,
                 )
                 span = CHUNK + 256
                 right_cells = pltpu.roll(extended, span - 1, 1)[:, 128 : 128 + CHUNK]
@@ -123,12 +121,13 @@
         lax.fori_loop(0, chunks, update, 0, unroll=UNROLL)
 
     def two_steps(number, carry):
+        sweep(second_ref, first_ref)
         sweep(first_ref, second_ref)
-        sweep(second_ref, first_ref)
         return carry
 
     total = count_ref[0]
-    lax.fori_loop(0, total // 2, two_steps, 0)
+    sweep(field_ref, second_ref)
+    lax.fori_loop(0, (total - 1) // 2, two_steps, 0)
 
     def collect(final_ref):
         def store(index, carry):
@@ -141,14 +140,14 @@
 
         lax.fori_loop(0, chunks, store, 0, unroll=UNROLL)
 
+    @pl.when(total % 2 == 0)
+    def _():
+        sweep(second_ref, first_ref)
+        collect(first_ref)
+
     @pl.when(total % 2 == 1)
     def _():
-        sweep(first_ref, second_ref)
         collect(second_ref)
-
-    @pl.when(total % 2 == 0)
-    def _():
-        collect(first_ref)
 
 
 def solve_rows(field, above_row, below_row, substeps, kappa_row, drift_row, kappa_col, drift_col):

time: 89.6 us -> 90 us (level)
  Pallas kernels: 7.51 us -> 11.1 us
  starting transfers between devices: 32.8 us -> 30.1 us
    pallas_call x1, Pallas kernels: 7.51 us -> 11.1 us  [solve_rows(): pl.pallas_call(solve_kernel, out_shape=jax.ShapeDtypeStruct((tracers, wid...]
    ppermute x5, starting transfers between devices: 4.3 us -> 2.89 us  [packed_ppermute(): packed = lax.ppermute(jnp.concatenate(parts, axis=0), axis, perm)]
    ppermute x7, starting transfers between devices: 22 us -> 20.7 us  [gather_along(): lax.ppermute(block, axis, [(i, (i + shift) % count) for i in range(count)])]
where the time goes in v12:
time: 90 us
  starting transfers between devices  30.1 us (33%)
  waiting for transfers between devices  15.1 us (17%)
  other arithmetic  12.7 us (14%)
  Pallas kernels  11.1 us (12%)
  local copies, waits for them, and re-layouts  10.2 us (11%)
  matrix products  8.62 us (10%)
  between operations  2.06 us (2%)
    ppermute x7, starting transfers between devices, gather_along(): lax.ppermute(block, axis, [(i, (i + shift) % count) for i in range(count)])  20.7 us
    pallas_call x1, Pallas kernels, solve_rows(): pl.pallas_call(solve_kernel, out_shape=jax.ShapeDtypeStruct((tracers, wid...  11.1 us
    ppermute x7, waiting for transfers between devices, gather_along(): lax.ppermute(block, axis, [(i, (i + shift) % count) for i in range(count)])  6.5 us
    ppermute x5, waiting for transfers between devices, packed_ppermute(): packed = lax.ppermute(jnp.concatenate(parts, axis=0), axis, perm)  5.6 us
    ppermute x1, starting transfers between devices, halo_rows(): below = lax.ppermute(block[:, :1], axis, backward)  3.42 us
    ppermute x1, starting transfers between devices, halo_rows(): above = lax.ppermute(block[:, -1:], axis, forward)  3.08 us
    ppermute x1, waiting for transfers between devices, halo_rows(): below = lax.ppermute(block[:, :1], axis, backward)  2.99 us
    ppermute x5, starting transfers between devices, packed_ppermute(): packed = lax.ppermute(jnp.concatenate(parts, axis=0), axis, perm)  2.89 us
  transfers between devices with their start and end apart: 14, of which 11 were waited for; matrix products, arithmetic and copies ran while one was open for 11% of the time, Pallas kernels for 0%

profile of v12, /device:TPU:0, one launch (start us, length us, event | category | flops | bytes accessed | tf_op | source)
XLA Modules:
  0.0 90.0 jit_solution(9893760315953163015)
XLA Ops:
  0.6 2.0 %fusion.145 = (bf16[4,1,16384]{2,1,0:T(2,128)(2,1)S(1)}, bf16[4,1,16384]{2,1,0:T(2,128)(2,1)S(1)}) fusion(bf16[4,16,16384]{2,1,0:T(8,128)(2,1)} %field_ref.1), kind=kLoop, calls=%fused_computation.240 | loop fusion | bytes 524288 | tf_op jit(solution)/shard_map/slice | solution.py:39
  2.6 3.1 %collective-permute-start = (bf16[4,1,16384]{2,1,0:T(2,128)(2,1)S(1)}, bf16[4,1,16384]{2,1,0:T(2,128)(2,1)S(1)}, u32[]{:S(2)}, u32[]{:S(2)}) collective-permute-start(bf16[4,1,16384]{2,1,0:T(2,128)(2,1)S(1)} %get-tuple-element.8), channel_id=1, source_target_pairs={{0,1},{1,2},{2,3},{3,4},{4,5},{5,6},{6,7},{7,8},{8,9},{9,10},{10,1... | collective-permute-start | bytes 393224 | tf_op jit(solution)/shard_map/ppermute | solution.py:38
  5.7 3.4 %collective-permute-start.1 = (bf16[4,1,16384]{2,1,0:T(2,128)(2,1)S(1)}, bf16[4,1,16384]{2,1,0:T(2,128)(2,1)S(1)}, u32[]{:S(2)}, u32[]{:S(2)}) collective-permute-start(bf16[4,1,16384]{2,1,0:T(2,128)(2,1)S(1)} %get-tuple-element.7), channel_id=1, source_target_pairs={{1,0},{2,1},{3,2},{4,3},{5,4},{6,5},{7,6},{8,7},{9,8},{10,9},{11,1... | collective-permute-start | bytes 393224 | tf_op jit(solution)/shard_map/ppermute | solution.py:39
  9.1 1.0 %fusion.148 = (f32[1,16384]{1,0:T(1,128)S(1)}, f32[1,16384]{1,0:T(1,128)S(1)}) fusion(bf16[2,16384]{1,0:T(2,128)(2,1)} %param.19), kind=kLoop, calls=%fused_computation.243 | loop fusion | bytes 262144 | tf_op jit(solution)/shard_map/slice | solution.py:161
  10.1 0.8 slice_bitcast_fusion.13
  11.6 0.8 convert_element_type.71
  12.3 0.3 cosine_multiply_fusion
  12.6 0.8 broadcast_multiply_fusion
  13.4 0.2 multiply_multiply_fusion
  13.7 1.8 %maximum_multiply_fusion.coef_ref = f32[3,16,16384]{2,1,0:T(8,128)} fusion(f32[1,16,16384]{2,1,0:T(8,128)S(1)} %get-tuple-element.59, f32[1,16,16384]{2,1,0:T(8,128)S(1)} %get-tuple-element.60, f32[1,16,16384]{2,1,0:T(8,128)S(1)} %broadcast_multiply_fusion, f32[]{:T(128)} %bitcast), kind=kLoop, calls=%fused_computation | loop fusion | flops 2359296 | bytes 6291460 | tf_op jit(solution)/shard_map/mul | solution.py:158
  15.8 0.3 negate_convert_fusion
  16.1 3.0 %collective-permute-done.1.below_ref = bf16[4,1,16384]{2,1,0:T(2,128)(2,1)S(1)} collective-permute-done((bf16[4,1,16384]{2,1,0:T(2,128)(2,1)S(1)}, bf16[4,1,16384]{2,1,0:T(2,128)(2,1)S(1)}, u32[]{:S(2)}, u32[]{:S(2)}) %collective-permute-start.1) | collective-permute-done | bytes 131104 | tf_op jit(solution)/shard_map/ppermute | solution.py:39
  19.1 0.7 copy-done.2
  19.8 11.1 %shard_map.157 = f32[4,16384]{1,0:T(4,128)} custom-call(f32[1]{0:T(128)} %div.12.step_ref, s32[1]{0:T(128)S(6)} %copy.161.count_ref, bf16[4,16,16384]{2,1,0:T(8,128)(2,1)} %field_ref.1, bf16[4,1,16384]{2,1,0:T(2,128)(2,1)} %copy-done.1, bf16[4,1,16384]{2,1,0:T(2,128)(2,1)} %copy-done.2, f32[3,16,16384]{2,1,0:T(8,128)} %maximum_multiply_fusion.coef_ref), custom_call_target="tpu_custom_call" | custom-call | tf_op jit(solution)/shard_map/pallas_call | solution.py:167
  30.9 1.6 %reshape.218 = f32[4,1024,16]{2,1,0:T(8,128)S(1)} reshape(f32[4,16384]{1,0:T(4,128)} %shard_map.157) | data formatting | bytes 524288 | tf_op jit(solution)/shard_map/reshape | solution.py:356
  32.5 0.6 reduce_sum.27
  33.2 3.6 %collective-permute-start.3 = (bf16[4,1024]{1,0:T(4,128)(2,1)S(1)}, bf16[4,1024]{1,0:T(4,128)(2,1)S(1)}, u32[]{:S(2)}, u32[]{:S(2)}) collective-permute-start(bf16[4,1024]{1,0:T(4,128)(2,1)S(1)} %multiply_convert_fusion), channel_id=1, source_target_pairs={{0,2},{1,3},{2,0},{3,1},{4,6},{5,7},{6,4},{7,5},{8,10},{9,11},{10,... | collective-permute-start | bytes 24584 | tf_op jit(solution)/shard_map/ppermute | solution.py:283
  36.8 1.3 %collective-permute-start.4 = (bf16[4,1024]{1,0:T(4,128)(2,1)S(1)}, bf16[4,1024]{1,0:T(4,128)(2,1)S(1)}, u32[]{:S(2)}, u32[]{:S(2)}) collective-permute-start(bf16[4,1024]{1,0:T(4,128)(2,1)S(1)} %multiply_convert_fusion), channel_id=1, source_target_pairs={{0,3},{1,0},{2,1},{3,2},{4,7},{5,4},{6,5},{7,6},{8,11},{9,8},{10,9... | collective-permute-start | bytes 24584 | tf_op jit(solution)/shard_map/ppermute | solution.py:283
  38.1 0.6 convert_dynamic-update-slice_fusion
  38.8 1.6 %collective-permute-done.4 = bf16[4,1024]{1,0:T(4,128)(2,1)S(1)} collective-permute-done((bf16[4,1024]{1,0:T(4,128)(2,1)S(1)}, bf16[4,1024]{1,0:T(4,128)(2,1)S(1)}, u32[]{:S(2)}, u32[]{:S(2)}) %collective-permute-start.4) | collective-permute-done | bytes 8224 | tf_op jit(solution)/shard_map/ppermute | solution.py:283
  40.4 10.6 %collective-permute-start.5 = (bf16[4,4,1024]{2,1,0:T(4,128)(2,1)S(1)}, bf16[4,4,1024]{2,1,0:T(4,128)(2,1)S(1)}, u32[]{:S(2)}, u32[]{:S(2)}) collective-permute-start(bf16[4,4,1024]{2,1,0:T(4,128)(2,1)S(1)} %bitcast_dynamic-update-slice_fusion.6), channel_id=1, source_target_pairs={{0,4},{4,0},{1,5},{5,1},{2,6},{6,2},{3,7},{7,3},{8,12},{12,8},{9,1... | collective-permute-start | bytes 98312 | tf_op jit(solution)/shard_map/ppermute | solution.py:283
  51.1 0.8 collective-permute-done.5
  52.0 2.4 %collective-permute-start.6 = (bf16[2,4,4,1024]{3,2,1,0:T(4,128)(2,1)S(1)}, bf16[2,4,4,1024]{3,2,1,0:T(4,128)(2,1)S(1)}, u32[]{:S(2)}, u32[]{:S(2)}) collective-permute-start(bf16[2,4,4,1024]{3,2,1,0:T(4,128)(2,1)S(1)} %bitcast_dynamic-update-slice_fusion.4), channel_id=1, source_target_pairs={{0,8},{8,16},{16,24},{24,0},{1,9},{9,17},{17,25},{25,1},{2,10},{10... | collective-permute-start | bytes 196616 | tf_op jit(solution)/shard_map/ppermute | solution.py:283
  54.4 2.7 %collective-permute-start.7 = (bf16[2,4,4,1024]{3,2,1,0:T(4,128)(2,1)S(1)}, bf16[2,4,4,1024]{3,2,1,0:T(4,128)(2,1)S(1)}, u32[]{:S(2)}, u32[]{:S(2)}) collective-permute-start(bf16[2,4,4,1024]{3,2,1,0:T(4,128)(2,1)S(1)} %bitcast_dynamic-update-slice_fusion.4), channel_id=1, source_target_pairs={{0,16},{8,24},{16,0},{24,8},{1,17},{9,25},{17,1},{25,9},{2,18},{10... | collective-permute-start | bytes 196616 | tf_op jit(solution)/shard_map/ppermute | solution.py:283
  57.2 1.8 %collective-permute-done.6 = bf16[2,4,4,1024]{3,2,1,0:T(4,128)(2,1)S(1)} collective-permute-done((bf16[2,4,4,1024]{3,2,1,0:T(4,128)(2,1)S(1)}, bf16[2,4,4,1024]{3,2,1,0:T(4,128)(2,1)S(1)}, u32[]{:S(2)}, u32[]{:S(2)}) %collective-permute-start.6) | collective-permute-done | bytes 65568 | tf_op jit(solution)/shard_map/ppermute | solution.py:283
  59.1 1.3 %collective-permute-done.7 = bf16[2,4,4,1024]{3,2,1,0:T(4,128)(2,1)S(1)} collective-permute-done((bf16[2,4,4,1024]{3,2,1,0:T(4,128)(2,1)S(1)}, bf16[2,4,4,1024]{3,2,1,0:T(4,128)(2,1)S(1)}, u32[]{:S(2)}, u32[]{:S(2)}) %collective-permute-start.7) | collective-permute-done | bytes 65568 | tf_op jit(solution)/shard_map/ppermute | solution.py:283
  60.4 1.0 %collective-permute-done.8 = bf16[2,4,4,1024]{3,2,1,0:T(4,128)(2,1)S(1)} collective-permute-done((bf16[2,4,4,1024]{3,2,1,0:T(4,128)(2,1)S(1)}, bf16[2,4,4,1024]{3,2,1,0:T(4,128)(2,1)S(1)}, u32[]{:S(2)}, u32[]{:S(2)}) %collective-permute-start.8) | collective-permute-done | bytes 65568 | tf_op jit(solution)/shard_map/ppermute | solution.py:283
  61.4 0.5 fusion.4
  62.0 0.9 %fusion.60 = f32[16,32,32]{1,2,0:T(8,128)S(1)} fusion(bf16[16,32,1024]{2,1,0:T(8,128)(2,1)S(1)} %fusion.4, bf16[1024,16]{0,1:T(8,128)(2,1)S(1)} %get-tuple-element.61, bf16[1024,16]{0,1:T(8,128)(2,1)S(1)} %get-tuple-element.62), kind=kOutput, calls=%fused_computation.138 | convolution fusion | flops 33685504 | bytes 1179648 | tf_op jit(solution)/shard_map/yhx,xk->yhk/dot_general | solution.py:369
  62.9 0.5 fusion.41
  63.5 0.5 fusion.45
  64.0 0.5 fusion.8
  64.5 0.5 fusion.10
  65.3 0.3 sine_multiply_fusion
  65.6 1.3 %collective-permute-done.9 = f32[64,32,16]{0,1,2:T(8,128)S(1)} collective-permute-done((f32[64,32,16]{0,1,2:T(8,128)S(1)}, f32[64,32,16]{0,1,2:T(8,128)S(1)}, u32[]{:S(2)}, u32[]{:S(2)}) %collective-permute-start.9) | collective-permute-done | bytes 131104 | tf_op jit(solution)/shard_map/ppermute | solution.py:295
  67.0 0.2 copy.112
  67.1 0.2 copy.113
  67.3 2.4 %fusion.3 = (f32[8,32,16]{1,2,0:T(8,128)S(1)}, f32[8,32,16]{1,2,0:T(8,128)S(1)}) fusion(f32[32,32,16]{1,2,0:T(8,128)S(1)} %copy.113, f32[32,32,16]{1,2,0:T(8,128)S(1)} %copy.112, bf16[2,32,8,32,16]{3,4,2,1,0:T(8,128)(2,1)} %param.26), kind=kLoop, calls=%fused_computation.8 | loop fusion | flops 1302528 | bytes 688128 | tf_op jit(solution)/shard_map/reduce_sum | solution.py:249
  69.7 0.6 fusion.76
  70.3 0.7 fusion.66
  71.0 0.7 convolution_subtract_fusion.2
  71.7 0.7 convolution_add_fusion.2
  72.5 0.6 convolution_multiply_fusion
  73.0 0.3 fusion.6
  73.3 1.8 %fusion.34 = bf16[1,16,8,1024]{3,2,1,0:T(8,128)(2,1)} fusion(f32[16,8,1024]{2,1,0:T(8,128)S(1)} %fusion.6), kind=kLoop, calls=%fused_computation.73 | loop fusion | flops 8519680 | bytes 786432 | tf_op jit(solution)/shard_map/broadcast_in_dim | solution.py:393
  75.1 0.3 fusion.35
  75.7 0.3 fusion.71
  76.1 0.3 fusion.73
  76.4 0.3 fusion.12
  76.7 0.3 fusion.14
  77.1 0.2 collective-permute-start.10
  77.3 0.2 constant_dynamic-slice_fusion
  77.4 0.2 constant_dynamic-slice_fusion.1
  77.8 0.7 collective-permute-done.10
  79.1 1.0 %collective-permute-start.13 = (f32[48,8,16]{0,1,2:T(8,128)S(1)}, f32[48,8,16]{0,1,2:T(8,128)S(1)}, u32[]{:S(2)}, u32[]{:S(2)}) collective-permute-start(f32[48,8,16]{0,1,2:T(8,128)S(1)} %pad_maximum_fusion.5), channel_id=1, source_target_pairs={{0,24},{8,0},{16,8},{24,16},{1,25},{9,1},{17,9},{25,17},{2,26},{10... | collective-permute-start | bytes 73736 | tf_op jit(solution)/shard_map/ppermute | solution.py:295
  80.4 1.6 %collective-permute-start.12 = (f32[48,8,16]{0,1,2:T(8,128)S(1)}, f32[48,8,16]{0,1,2:T(8,128)S(1)}, u32[]{:S(2)}, u32[]{:S(2)}) collective-permute-start(f32[48,8,16]{0,1,2:T(8,128)S(1)} %pad_maximum_fusion.4), channel_id=1, source_target_pairs={{0,16},{8,24},{16,0},{24,8},{1,17},{9,25},{17,1},{25,9},{2,18},{10... | collective-permute-start | bytes 73736 | tf_op jit(solution)/shard_map/ppermute | solution.py:295
  82.5 0.2 add_bitcast_fusion.3
  82.6 0.8 collective-permute-done.13
  83.6 1.1 %collective-permute-done.12 = f32[48,8,16]{0,1,2:T(8,128)S(1)} collective-permute-done((f32[48,8,16]{0,1,2:T(8,128)S(1)}, f32[48,8,16]{0,1,2:T(8,128)S(1)}, u32[]{:S(2)}, u32[]{:S(2)}) %collective-permute-start.12) | collective-permute-done | bytes 24608 | tf_op jit(solution)/shard_map/ppermute | solution.py:295
  85.7 1.8 %collective-permute-done.11 = f32[48,8,16]{0,1,2:T(8,128)S(1)} collective-permute-done((f32[48,8,16]{0,1,2:T(8,128)S(1)}, f32[48,8,16]{0,1,2:T(8,128)S(1)}, u32[]{:S(2)}, u32[]{:S(2)}) %collective-permute-start.11) | collective-permute-done | bytes 24608 | tf_op jit(solution)/shard_map/ppermute | solution.py:295
  88.1 0.1 add_bitcast_fusion
  88.2 0.1 add_bitcast_fusion.1
  88.4 0.1 add_bitcast_fusion.2
  88.5 1.4 %fusion.17 = f32[2,16,8,8,16]{4,3,2,1,0:T(8,128)} fusion(f32[1,16,8,8,16]{4,3,2,1,0:T(8,128)S(1)} %get-tuple-element.28, f32[1,16,8,8,16]{4,3,2,1,0:T(8,128)S(1)} %get-tuple-element.27, f32[1,16,8,8,16]{4,3,2,1,0:T(8,128)S(1)} %get-tuple-element.26, f32[1,16,8,8,16]{4,3,2,1,0:T(8,128)S(1)} %get-tuple-element.25, ...), kind=kLoop, calls=%fused_computation.32 | loop fusion | flops 262144 | bytes 655360 | tf_op jit(solution)/shard_map/div | solution.py:407
  (83 shorter events, 4.6 us)
Async XLA Ops:
  0.6 72.4 %copy-start = (bf16[32,8]{0,1:T(8,128)(2,1)S(1)}, bf16[32,8]{0,1:T(8,128)(2,1)}, u32[]{:S(2)}) copy-start(bf16[32,8]{0,1:T(8,128)(2,1)} %param.24) | copy-start | bytes 1540
  2.6 13.5 %collective-permute-start = (bf16[4,1,16384]{2,1,0:T(2,128)(2,1)S(1)}, bf16[4,1,16384]{2,1,0:T(2,128)(2,1)S(1)}, u32[]{:S(2)}, u32[]{:S(2)}) collective-permute-start(bf16[4,1,16384]{2,1,0:T(2,128)(2,1)S(1)} %get-tuple-element.8), channel_id=1, source_target_pairs={{0,1},{1,2},{2,3},{3,4},{4,5},{5,6},{6,7},{7,8},{8,9},{9,10},{10,1... | collective-permute-start | bytes 393224 | tf_op jit(solution)/shard_map/ppermute | solution.py:38
  5.7 13.4 %collective-permute-start.1 = (bf16[4,1,16384]{2,1,0:T(2,128)(2,1)S(1)}, bf16[4,1,16384]{2,1,0:T(2,128)(2,1)S(1)}, u32[]{:S(2)}, u32[]{:S(2)}) collective-permute-start(bf16[4,1,16384]{2,1,0:T(2,128)(2,1)S(1)} %get-tuple-element.7), channel_id=1, source_target_pairs={{1,0},{2,1},{3,2},{4,3},{5,4},{6,5},{7,6},{8,7},{9,8},{10,9},{11,1... | collective-permute-start | bytes 393224 | tf_op jit(solution)/shard_map/ppermute | solution.py:39
  13.7 1.9 %copy-start.6 = (s32[32]{0:T(128)S(1)}, s32[32]{0:T(128)}, u32[]{:S(2)}) copy-start(s32[32]{0:T(128)} %param.20) | copy-start | bytes 388
  16.1 3.0 %copy-start.1 = (bf16[4,1,16384]{2,1,0:T(2,128)(2,1)}, bf16[4,1,16384]{2,1,0:T(2,128)(2,1)S(1)}, u32[]{:S(2)}) copy-start(bf16[4,1,16384]{2,1,0:T(2,128)(2,1)S(1)} %collective-permute-done.above_ref) | copy-start | bytes 393220
  19.1 0.7 copy-start.2
  32.5 28.9 %copy-start.3 = (bf16[1,16,4,1024]{3,2,1,0:T(4,128)(2,1)S(1)}, bf16[1,16,4,1024]{3,2,1,0:T(4,128)(2,1)}, u32[]{:S(2)}) copy-start(bf16[1,16,4,1024]{3,2,1,0:T(4,128)(2,1)} %param.21) | copy-start | bytes 393220
  32.5 28.9 %copy-start.4 = (bf16[4,32]{1,0:T(4,128)(2,1)S(1)}, bf16[4,32]{1,0:T(4,128)(2,1)}, u32[]{:S(2)}) copy-start(bf16[4,32]{1,0:T(4,128)(2,1)} %param.22) | copy-start | bytes 772
  32.5 28.9 %copy-start.5 = (f32[32]{0:T(128)S(1)}, f32[32]{0:T(128)}, u32[]{:S(2)}) copy-start(f32[32]{0:T(128)} %param.23) | copy-start | bytes 388
  33.2 5.6 %collective-permute-start.2 = (bf16[4,1024]{1,0:T(4,128)(2,1)S(1)}, bf16[4,1024]{1,0:T(4,128)(2,1)S(1)}, u32[]{:S(2)}, u32[]{:S(2)}) collective-permute-start(bf16[4,1024]{1,0:T(4,128)(2,1)S(1)} %multiply_convert_fusion), channel_id=1, source_target_pairs={{0,1},{1,2},{2,3},{3,0},{4,5},{5,6},{6,7},{7,4},{8,9},{9,10},{10,1... | collective-permute-start | bytes 24584 | tf_op jit(solution)/shard_map/ppermute | solution.py:283
  33.2 5.5 %collective-permute-start.3 = (bf16[4,1024]{1,0:T(4,128)(2,1)S(1)}, bf16[4,1024]{1,0:T(4,128)(2,1)S(1)}, u32[]{:S(2)}, u32[]{:S(2)}) collective-permute-start(bf16[4,1024]{1,0:T(4,128)(2,1)S(1)} %multiply_convert_fusion), channel_id=1, source_target_pairs={{0,2},{1,3},{2,0},{3,1},{4,6},{5,7},{6,4},{7,5},{8,10},{9,11},{10,... | collective-permute-start | bytes 24584 | tf_op jit(solution)/shard_map/ppermute | solution.py:283
  36.8 3.7 %collective-permute-start.4 = (bf16[4,1024]{1,0:T(4,128)(2,1)S(1)}, bf16[4,1024]{1,0:T(4,128)(2,1)S(1)}, u32[]{:S(2)}, u32[]{:S(2)}) collective-permute-start(bf16[4,1024]{1,0:T(4,128)(2,1)S(1)} %multiply_convert_fusion), channel_id=1, source_target_pairs={{0,3},{1,0},{2,1},{3,2},{4,7},{5,4},{6,5},{7,6},{8,11},{9,8},{10,9... | collective-permute-start | bytes 24584 | tf_op jit(solution)/shard_map/ppermute | solution.py:283
  40.4 11.5 %collective-permute-start.5 = (bf16[4,4,1024]{2,1,0:T(4,128)(2,1)S(1)}, bf16[4,4,1024]{2,1,0:T(4,128)(2,1)S(1)}, u32[]{:S(2)}, u32[]{:S(2)}) collective-permute-start(bf16[4,4,1024]{2,1,0:T(4,128)(2,1)S(1)} %bitcast_dynamic-update-slice_fusion.6), channel_id=1, source_target_pairs={{0,4},{4,0},{1,5},{5,1},{2,6},{6,2},{3,7},{7,3},{8,12},{12,8},{9,1... | collective-permute-start | bytes 98312 | tf_op jit(solution)/shard_map/ppermute | solution.py:283
  52.0 7.1 %collective-permute-start.6 = (bf16[2,4,4,1024]{3,2,1,0:T(4,128)(2,1)S(1)}, bf16[2,4,4,1024]{3,2,1,0:T(4,128)(2,1)S(1)}, u32[]{:S(2)}, u32[]{:S(2)}) collective-permute-start(bf16[2,4,4,1024]{3,2,1,0:T(4,128)(2,1)S(1)} %bitcast_dynamic-update-slice_fusion.4), channel_id=1, source_target_pairs={{0,8},{8,16},{16,24},{24,0},{1,9},{9,17},{17,25},{25,1},{2,10},{10... | collective-permute-start | bytes 196616 | tf_op jit(solution)/shard_map/ppermute | solution.py:283
  54.4 6.0 %collective-permute-start.7 = (bf16[2,4,4,1024]{3,2,1,0:T(4,128)(2,1)S(1)}, bf16[2,4,4,1024]{3,2,1,0:T(4,128)(2,1)S(1)}, u32[]{:S(2)}, u32[]{:S(2)}) collective-permute-start(bf16[2,4,4,1024]{3,2,1,0:T(4,128)(2,1)S(1)} %bitcast_dynamic-update-slice_fusion.4), channel_id=1, source_target_pairs={{0,16},{8,24},{16,0},{24,8},{1,17},{9,25},{17,1},{25,9},{2,18},{10... | collective-permute-start | bytes 196616 | tf_op jit(solution)/shard_map/ppermute | solution.py:283
  57.1 4.3 %collective-permute-start.8 = (bf16[2,4,4,1024]{3,2,1,0:T(4,128)(2,1)S(1)}, bf16[2,4,4,1024]{3,2,1,0:T(4,128)(2,1)S(1)}, u32[]{:S(2)}, u32[]{:S(2)}) collective-permute-start(bf16[2,4,4,1024]{3,2,1,0:T(4,128)(2,1)S(1)} %bitcast_dynamic-update-slice_fusion.4), channel_id=1, source_target_pairs={{0,24},{8,0},{16,8},{24,16},{1,25},{9,1},{17,9},{25,17},{2,26},{10... | collective-permute-start | bytes 196616 | tf_op jit(solution)/shard_map/ppermute | solution.py:283
  65.2 1.6 %collective-permute-start.9 = (f32[64,32,16]{0,1,2:T(8,128)S(1)}, f32[64,32,16]{0,1,2:T(8,128)S(1)}, u32[]{:S(2)}, u32[]{:S(2)}) collective-permute-start(f32[64,32,16]{0,1,2:T(8,128)S(1)} %pad_maximum_fusion), channel_id=1, source_target_pairs={{0,4},{4,0},{1,5},{5,1},{2,6},{6,2},{3,7},{7,3},{8,12},{12,8},{9,1... | collective-permute-start | bytes 393224 | tf_op jit(solution)/shard_map/ppermute | solution.py:295
  67.3 5.7 %copy-start.7 = (f32[8]{0:T(128)S(1)}, f32[8]{0:T(128)}, u32[]{:S(2)}) copy-start(f32[8]{0:T(128)} %param.25) | copy-start | bytes 100
  71.0 4.1 %copy-start.8 = (bf16[1,16,8,1024]{3,2,1,0:T(8,128)(2,1)S(1)}, bf16[1,16,8,1024]{3,2,1,0:T(8,128)(2,1)}, u32[]{:S(2)}) copy-start(bf16[1,16,8,1024]{3,2,1,0:T(8,128)(2,1)} %param.27) | copy-start | bytes 786436
  77.1 1.4 %collective-permute-start.10 = (f32[16,32,16]{1,2,0:T(8,128)S(1)}, f32[16,32,16]{1,2,0:T(8,128)S(1)}, u32[]{:S(2)}, u32[]{:S(2)}) collective-permute-start(f32[16,32,16]{1,2,0:T(8,128)S(1)} %pad_maximum_fusion.1), channel_id=1, source_target_pairs={{0,4},{4,0},{1,5},{5,1},{2,6},{6,2},{3,7},{7,3},{8,12},{12,8},{9,1... | collective-permute-start | bytes 98312 | tf_op jit(solution)/shard_map/ppermute | solution.py:295
  79.1 4.3 %collective-permute-start.13 = (f32[48,8,16]{0,1,2:T(8,128)S(1)}, f32[48,8,16]{0,1,2:T(8,128)S(1)}, u32[]{:S(2)}, u32[]{:S(2)}) collective-permute-start(f32[48,8,16]{0,1,2:T(8,128)S(1)} %pad_maximum_fusion.5), channel_id=1, source_target_pairs={{0,24},{8,0},{16,8},{24,16},{1,25},{9,1},{17,9},{25,17},{2,26},{10... | collective-permute-start | bytes 73736 | tf_op jit(solution)/shard_map/ppermute | solution.py:295
  80.4 4.3 %collective-permute-start.12 = (f32[48,8,16]{0,1,2:T(8,128)S(1)}, f32[48,8,16]{0,1,2:T(8,128)S(1)}, u32[]{:S(2)}, u32[]{:S(2)}) collective-permute-start(f32[48,8,16]{0,1,2:T(8,128)S(1)} %pad_maximum_fusion.4), channel_id=1, source_target_pairs={{0,16},{8,24},{16,0},{24,8},{1,17},{9,25},{17,1},{25,9},{2,18},{10... | collective-permute-start | bytes 73736 | tf_op jit(solution)/shard_map/ppermute | solution.py:295
  82.3 5.2 %collective-permute-start.11 = (f32[48,8,16]{0,1,2:T(8,128)S(1)}, f32[48,8,16]{0,1,2:T(8,128)S(1)}, u32[]{:S(2)}, u32[]{:S(2)}) collective-permute-start(f32[48,8,16]{0,1,2:T(8,128)S(1)} %pad_maximum_fusion.3), channel_id=1, source_target_pairs={{0,8},{8,16},{16,24},{24,0},{1,9},{9,17},{17,25},{25,1},{2,10},{10... | collective-permute-start | bytes 73736 | tf_op jit(solution)/shard_map/ppermute | solution.py:295

commit v13 on v11

--- a/solution.py
+++ b/solution.py
@@ -354,7 +354,15 @@
         kappa_cols,
         drift_cols,
     )
-    coarse_rows = (row_sums.reshape(C, SW, FACTOR).sum(axis=2) * (1.0 / (FACTOR * FACTOR)))[None]
+    lanes = 128
+    grouping = (
+        jnp.arange(lanes, dtype=jnp.int32)[:, None] // FACTOR
+        == jnp.arange(lanes // FACTOR, dtype=jnp.int32)[None, :]
+    ).astype(jnp.float32)
+    grouped = jnp.dot(
+        row_sums.reshape(-1, lanes), grouping, precision=lax.Precision.HIGHEST
+    )
+    coarse_rows = (grouped.reshape(C, SW) * (1.0 / (FACTOR * FACTOR)))[None]
     coarse_low = coarse_rows.astype(jnp.bfloat16)
     member = lax.axis_index("mem")
     member_rows = buffer.shape[1]

time: 89.6 us -> 89.3 us (level)
  Pallas kernels: 7.51 us -> 10.6 us
  starting transfers between devices: 32.8 us -> 30.3 us
  other arithmetic: 12.7 us -> 11.5 us
    pallas_call x1, Pallas kernels: 7.51 us -> 10.6 us  [solve_rows(): pl.pallas_call(solve_kernel, out_shape=jax.ShapeDtypeStruct((tracers, wid...]
    ppermute x7, starting transfers between devices: 22 us -> 20.5 us  [gather_along(): lax.ppermute(block, axis, [(i, (i + shift) % count) for i in range(count)])]
    ppermute x5, starting transfers between devices: 4.3 us -> 3.34 us  [packed_ppermute(): packed = lax.ppermute(jnp.concatenate(parts, axis=0), axis, perm)]
  transfers between devices with their start and end apart: 14 -> 14, of which waited for: 11 -> 13; matrix products, arithmetic and copies ran while one was open for 11% -> 10% of each run, Pallas kernels for 0% -> 0%
where the time goes in v13:
time: 89.3 us; the launch traced here: 89.5 us
  starting transfers between devices  30.3 us (34%)
  waiting for transfers between devices  15.6 us (17%)
  other arithmetic  11.5 us (13%)
  Pallas kernels  10.6 us (12%)
  local copies, waits for them, and re-layouts  10.4 us (12%)
  matrix products  8.92 us (10%)
  between operations  2.06 us (2%)
    ppermute x7, starting transfers between devices, gather_along(): lax.ppermute(block, axis, [(i, (i + shift) % count) for i in range(count)])  20.5 us
    pallas_call x1, Pallas kernels, solve_rows(): pl.pallas_call(solve_kernel, out_shape=jax.ShapeDtypeStruct((tracers, wid...  10.6 us
    ppermute x7, waiting for transfers between devices, gather_along(): lax.ppermute(block, axis, [(i, (i + shift) % count) for i in range(count)])  7.05 us
    ppermute x5, waiting for transfers between devices, packed_ppermute(): packed = lax.ppermute(jnp.concatenate(parts, axis=0), axis, perm)  5.56 us
    ppermute x1, starting transfers between devices, halo_rows(): below = lax.ppermute(block[:, :1], axis, backward)  3.42 us
    ppermute x5, starting transfers between devices, packed_ppermute(): packed = lax.ppermute(jnp.concatenate(parts, axis=0), axis, perm)  3.34 us
    ppermute x1, starting transfers between devices, halo_rows(): above = lax.ppermute(block[:, -1:], axis, forward)  3.08 us
    ppermute x1, waiting for transfers between devices, halo_rows(): below = lax.ppermute(block[:, :1], axis, backward)  2.98 us
  transfers between devices with their start and end apart: 14, of which 13 were waited for; matrix products, arithmetic and copies ran while one was open for 10% of the time, Pallas kernels for 0%

profile of v13, /device:TPU:0, one launch (start us, length us, event | category | flops | bytes accessed | tf_op | source)
XLA Modules:
  0.0 89.5 jit_solution(4455762821063879084)
XLA Ops:
  0.6 2.0 %fusion.146 = (bf16[4,1,16384]{2,1,0:T(2,128)(2,1)S(1)}, bf16[4,1,16384]{2,1,0:T(2,128)(2,1)S(1)}) fusion(bf16[4,16,16384]{2,1,0:T(8,128)(2,1)} %field_ref.1), kind=kLoop, calls=%fused_computation.245 | loop fusion | bytes 524288 | tf_op jit(solution)/shard_map/slice | solution.py:39
  2.6 3.1 %collective-permute-start = (bf16[4,1,16384]{2,1,0:T(2,128)(2,1)S(1)}, bf16[4,1,16384]{2,1,0:T(2,128)(2,1)S(1)}, u32[]{:S(2)}, u32[]{:S(2)}) collective-permute-start(bf16[4,1,16384]{2,1,0:T(2,128)(2,1)S(1)} %get-tuple-element.6), channel_id=1, source_target_pairs={{0,1},{1,2},{2,3},{3,4},{4,5},{5,6},{6,7},{7,8},{8,9},{9,10},{10,1... | collective-permute-start | bytes 393224 | tf_op jit(solution)/shard_map/ppermute | solution.py:38
  5.7 3.4 %collective-permute-start.1 = (bf16[4,1,16384]{2,1,0:T(2,128)(2,1)S(1)}, bf16[4,1,16384]{2,1,0:T(2,128)(2,1)S(1)}, u32[]{:S(2)}, u32[]{:S(2)}) collective-permute-start(bf16[4,1,16384]{2,1,0:T(2,128)(2,1)S(1)} %get-tuple-element.5), channel_id=1, source_target_pairs={{1,0},{2,1},{3,2},{4,3},{5,4},{6,5},{7,6},{8,7},{9,8},{10,9},{11,1... | collective-permute-start | bytes 393224 | tf_op jit(solution)/shard_map/ppermute | solution.py:39
  9.1 1.0 %fusion.149 = (f32[1,16384]{1,0:T(1,128)S(1)}, f32[1,16384]{1,0:T(1,128)S(1)}) fusion(bf16[2,16384]{1,0:T(2,128)(2,1)} %param.19), kind=kLoop, calls=%fused_computation.248 | loop fusion | bytes 262144 | tf_op jit(solution)/shard_map/slice | solution.py:162
  10.1 0.8 slice_bitcast_fusion.13
  11.6 0.8 convert_element_type.75
  12.3 0.3 cosine_multiply_fusion
  12.6 0.8 broadcast_multiply_fusion
  13.4 0.2 multiply_multiply_fusion
  13.7 1.8 %maximum_multiply_fusion.coef_ref = f32[3,16,16384]{2,1,0:T(8,128)} fusion(f32[1,16,16384]{2,1,0:T(8,128)S(1)} %get-tuple-element.57, f32[1,16,16384]{2,1,0:T(8,128)S(1)} %get-tuple-element.58, f32[1,16,16384]{2,1,0:T(8,128)S(1)} %broadcast_multiply_fusion, f32[]{:T(128)} %bitcast), kind=kLoop, calls=%fused_computation | loop fusion | flops 2359296 | bytes 6291460 | tf_op jit(solution)/shard_map/mul | solution.py:159
  15.8 0.3 negate_convert_fusion
  16.1 3.0 %collective-permute-done.1.below_ref = bf16[4,1,16384]{2,1,0:T(2,128)(2,1)S(1)} collective-permute-done((bf16[4,1,16384]{2,1,0:T(2,128)(2,1)S(1)}, bf16[4,1,16384]{2,1,0:T(2,128)(2,1)S(1)}, u32[]{:S(2)}, u32[]{:S(2)}) %collective-permute-start.1) | collective-permute-done | bytes 131104 | tf_op jit(solution)/shard_map/ppermute | solution.py:39
  19.1 0.7 copy-done.2
  19.8 10.6 %shard_map.157 = f32[4,16384]{1,0:T(4,128)} custom-call(f32[1]{0:T(128)} %div.20.step_ref, s32[1]{0:T(128)S(6)} %copy.167.count_ref, bf16[4,16,16384]{2,1,0:T(8,128)(2,1)} %field_ref.1, bf16[4,1,16384]{2,1,0:T(2,128)(2,1)} %copy-done.1, bf16[4,1,16384]{2,1,0:T(2,128)(2,1)} %copy-done.2, f32[3,16,16384]{2,1,0:T(8,128)} %maximum_multiply_fusion.coef_ref), custom_call_target="tpu_custom_call" | custom-call | tf_op jit(solution)/shard_map/pallas_call | solution.py:168
  30.4 1.2 %reshape.263 = f32[512,128]{1,0:T(8,128)S(1)} reshape(f32[4,16384]{1,0:T(4,128)} %shard_map.157) | data formatting | bytes 524288 | tf_op jit(solution)/shard_map/reshape | solution.py:363
  31.6 0.3 fusion.150
  31.9 0.2 copy.113
  32.1 0.2 convert_element_type.82
  32.2 4.7 %collective-permute-start.2 = (bf16[4,1024]{1,0:T(4,128)(2,1)S(1)}, bf16[4,1024]{1,0:T(4,128)(2,1)S(1)}, u32[]{:S(2)}, u32[]{:S(2)}) collective-permute-start(bf16[4,1024]{1,0:T(4,128)(2,1)S(1)} %convert_element_type.82), channel_id=1, source_target_pairs={{0,1},{1,2},{2,3},{3,0},{4,5},{5,6},{6,7},{7,4},{8,9},{9,10},{10,1... | collective-permute-start | bytes 24584 | tf_op jit(solution)/shard_map/ppermute | solution.py:284
  36.9 11.2 %collective-permute-start.3 = (bf16[4,1024]{1,0:T(4,128)(2,1)S(1)}, bf16[4,1024]{1,0:T(4,128)(2,1)S(1)}, u32[]{:S(2)}, u32[]{:S(2)}) collective-permute-start(bf16[4,1024]{1,0:T(4,128)(2,1)S(1)} %convert_element_type.82), channel_id=1, source_target_pairs={{0,2},{1,3},{2,0},{3,1},{4,6},{5,7},{6,4},{7,5},{8,10},{9,11},{10,... | collective-permute-start | bytes 24584 | tf_op jit(solution)/shard_map/ppermute | solution.py:284
  48.3 0.2 mul.364
  48.5 0.7 collective-permute-done.2
  49.2 0.5 collective-permute-done.3
  49.8 2.0 %collective-permute-done.4 = bf16[4,1024]{1,0:T(4,128)(2,1)S(1)} collective-permute-done((bf16[4,1024]{1,0:T(4,128)(2,1)S(1)}, bf16[4,1024]{1,0:T(4,128)(2,1)S(1)}, u32[]{:S(2)}, u32[]{:S(2)}) %collective-permute-start.4) | collective-permute-done | bytes 8224 | tf_op jit(solution)/shard_map/ppermute | solution.py:284
  52.0 1.1 %collective-permute-done.5 = bf16[4,4,1024]{2,1,0:T(4,128)(2,1)S(1)} collective-permute-done((bf16[4,4,1024]{2,1,0:T(4,128)(2,1)S(1)}, bf16[4,4,1024]{2,1,0:T(4,128)(2,1)S(1)}, u32[]{:S(2)}, u32[]{:S(2)}) %collective-permute-start.5) | collective-permute-done | bytes 32800 | tf_op jit(solution)/shard_map/ppermute | solution.py:284
  53.2 3.0 %collective-permute-start.7 = (bf16[2,4,4,1024]{3,2,1,0:T(4,128)(2,1)S(1)}, bf16[2,4,4,1024]{3,2,1,0:T(4,128)(2,1)S(1)}, u32[]{:S(2)}, u32[]{:S(2)}) collective-permute-start(bf16[2,4,4,1024]{3,2,1,0:T(4,128)(2,1)S(1)} %bitcast_dynamic-update-slice_fusion.4), channel_id=1, source_target_pairs={{0,16},{8,24},{16,0},{24,8},{1,17},{9,25},{17,1},{25,9},{2,18},{10... | collective-permute-start | bytes 196616 | tf_op jit(solution)/shard_map/ppermute | solution.py:284
  56.2 1.4 %collective-permute-start.8 = (bf16[2,4,4,1024]{3,2,1,0:T(4,128)(2,1)S(1)}, bf16[2,4,4,1024]{3,2,1,0:T(4,128)(2,1)S(1)}, u32[]{:S(2)}, u32[]{:S(2)}) collective-permute-start(bf16[2,4,4,1024]{3,2,1,0:T(4,128)(2,1)S(1)} %bitcast_dynamic-update-slice_fusion.4), channel_id=1, source_target_pairs={{0,24},{8,0},{16,8},{24,16},{1,25},{9,1},{17,9},{25,17},{2,26},{10... | collective-permute-start | bytes 196616 | tf_op jit(solution)/shard_map/ppermute | solution.py:284
  57.7 0.9 %collective-permute-done.6 = bf16[2,4,4,1024]{3,2,1,0:T(4,128)(2,1)S(1)} collective-permute-done((bf16[2,4,4,1024]{3,2,1,0:T(4,128)(2,1)S(1)}, bf16[2,4,4,1024]{3,2,1,0:T(4,128)(2,1)S(1)}, u32[]{:S(2)}, u32[]{:S(2)}) %collective-permute-start.6) | collective-permute-done | bytes 65568 | tf_op jit(solution)/shard_map/ppermute | solution.py:284
  58.7 0.9 %collective-permute-done.7 = bf16[2,4,4,1024]{3,2,1,0:T(4,128)(2,1)S(1)} collective-permute-done((bf16[2,4,4,1024]{3,2,1,0:T(4,128)(2,1)S(1)}, bf16[2,4,4,1024]{3,2,1,0:T(4,128)(2,1)S(1)}, u32[]{:S(2)}, u32[]{:S(2)}) %collective-permute-start.7) | collective-permute-done | bytes 65568 | tf_op jit(solution)/shard_map/ppermute | solution.py:284
  59.7 0.8 collective-permute-done.8
  60.5 0.5 fusion.4
  61.0 0.9 %fusion.60 = f32[16,32,32]{1,2,0:T(8,128)S(1)} fusion(bf16[16,32,1024]{2,1,0:T(8,128)(2,1)S(1)} %fusion.4, bf16[1024,16]{0,1:T(8,128)(2,1)S(1)} %get-tuple-element.61, bf16[1024,16]{0,1:T(8,128)(2,1)S(1)} %get-tuple-element.62), kind=kOutput, calls=%fused_computation.140 | convolution fusion | flops 33685504 | bytes 1179648 | tf_op jit(solution)/shard_map/yhx,xk->yhk/dot_general | solution.py:378
  62.0 0.5 fusion.41
  62.5 0.5 fusion.45
  63.1 0.5 fusion.8
  63.6 0.5 fusion.10
  64.4 0.3 sine_multiply_fusion
  64.6 1.3 %collective-permute-done.9 = f32[64,32,16]{0,1,2:T(8,128)S(1)} collective-permute-done((f32[64,32,16]{0,1,2:T(8,128)S(1)}, f32[64,32,16]{0,1,2:T(8,128)S(1)}, u32[]{:S(2)}, u32[]{:S(2)}) %collective-permute-start.9) | collective-permute-done | bytes 131104 | tf_op jit(solution)/shard_map/ppermute | solution.py:296
  66.0 0.2 copy.118
  66.2 0.2 copy.119
  66.4 2.4 %fusion.3 = (f32[8,32,16]{1,2,0:T(8,128)S(1)}, f32[8,32,16]{1,2,0:T(8,128)S(1)}) fusion(f32[32,32,16]{1,2,0:T(8,128)S(1)} %copy.119, f32[32,32,16]{1,2,0:T(8,128)S(1)} %copy.118, bf16[2,32,8,32,16]{3,4,2,1,0:T(8,128)(2,1)} %param.26), kind=kLoop, calls=%fused_computation.8 | loop fusion | flops 1302528 | bytes 688128 | tf_op jit(solution)/shard_map/reduce_sum | solution.py:250
  68.8 0.6 fusion.77
  69.4 0.7 fusion.67
  70.1 0.7 convolution_subtract_fusion.2
  70.8 0.7 convolution_add_fusion.2
  71.5 0.6 convolution_multiply_fusion
  72.1 0.3 fusion.6
  72.4 1.8 %fusion.34 = bf16[1,16,8,1024]{3,2,1,0:T(8,128)(2,1)} fusion(f32[16,8,1024]{2,1,0:T(8,128)S(1)} %fusion.6), kind=kLoop, calls=%fused_computation.74 | loop fusion | flops 8519680 | bytes 786432 | tf_op jit(solution)/shard_map/broadcast_in_dim | solution.py:402
  74.2 0.3 fusion.35
  74.8 0.3 fusion.72
  75.2 0.3 fusion.74
  75.5 0.3 fusion.12
  75.8 0.3 fusion.14
  76.2 0.2 collective-permute-start.10
  76.4 0.2 constant_dynamic-slice_fusion
  76.5 0.2 constant_dynamic-slice_fusion.1
  76.9 0.7 collective-permute-done.10
  78.2 2.4 %collective-permute-start.13 = (f32[48,8,16]{0,1,2:T(8,128)S(1)}, f32[48,8,16]{0,1,2:T(8,128)S(1)}, u32[]{:S(2)}, u32[]{:S(2)}) collective-permute-start(f32[48,8,16]{0,1,2:T(8,128)S(1)} %pad_maximum_fusion.5), channel_id=1, source_target_pairs={{0,24},{8,0},{16,8},{24,16},{1,25},{9,1},{17,9},{25,17},{2,26},{10... | collective-permute-start | bytes 73736 | tf_op jit(solution)/shard_map/ppermute | solution.py:296
  80.9 0.6 collective-permute-start.12
  82.0 0.2 add_bitcast_fusion.3
  82.2 0.6 collective-permute-done.13
  83.0 2.9 %collective-permute-done.12 = f32[48,8,16]{0,1,2:T(8,128)S(1)} collective-permute-done((f32[48,8,16]{0,1,2:T(8,128)S(1)}, f32[48,8,16]{0,1,2:T(8,128)S(1)}, u32[]{:S(2)}, u32[]{:S(2)}) %collective-permute-start.12) | collective-permute-done | bytes 24608 | tf_op jit(solution)/shard_map/ppermute | solution.py:296
  87.6 0.1 add_bitcast_fusion
  88.0 1.4 %fusion.17 = f32[2,16,8,8,16]{4,3,2,1,0:T(8,128)} fusion(f32[1,16,8,8,16]{4,3,2,1,0:T(8,128)S(1)} %get-tuple-element.26, f32[1,16,8,8,16]{4,3,2,1,0:T(8,128)S(1)} %get-tuple-element.25, f32[1,16,8,8,16]{4,3,2,1,0:T(8,128)S(1)} %get-tuple-element.24, f32[1,16,8,8,16]{4,3,2,1,0:T(8,128)S(1)} %get-tuple-element.23, ...), kind=kLoop, calls=%fused_computation.33 | loop fusion | flops 262144 | bytes 655360 | tf_op jit(solution)/shard_map/div | solution.py:416
  (89 shorter events, 5.2 us)
Async XLA Ops:
  0.6 71.5 %copy-start = (bf16[32,8]{0,1:T(8,128)(2,1)S(1)}, bf16[32,8]{0,1:T(8,128)(2,1)}, u32[]{:S(2)}) copy-start(bf16[32,8]{0,1:T(8,128)(2,1)} %param.24) | copy-start | bytes 1540
  2.6 13.5 %collective-permute-start = (bf16[4,1,16384]{2,1,0:T(2,128)(2,1)S(1)}, bf16[4,1,16384]{2,1,0:T(2,128)(2,1)S(1)}, u32[]{:S(2)}, u32[]{:S(2)}) collective-permute-start(bf16[4,1,16384]{2,1,0:T(2,128)(2,1)S(1)} %get-tuple-element.6), channel_id=1, source_target_pairs={{0,1},{1,2},{2,3},{3,4},{4,5},{5,6},{6,7},{7,8},{8,9},{9,10},{10,1... | collective-permute-start | bytes 393224 | tf_op jit(solution)/shard_map/ppermute | solution.py:38
  5.7 13.4 %collective-permute-start.1 = (bf16[4,1,16384]{2,1,0:T(2,128)(2,1)S(1)}, bf16[4,1,16384]{2,1,0:T(2,128)(2,1)S(1)}, u32[]{:S(2)}, u32[]{:S(2)}) collective-permute-start(bf16[4,1,16384]{2,1,0:T(2,128)(2,1)S(1)} %get-tuple-element.5), channel_id=1, source_target_pairs={{1,0},{2,1},{3,2},{4,3},{5,4},{6,5},{7,6},{8,7},{9,8},{10,9},{11,1... | collective-permute-start | bytes 393224 | tf_op jit(solution)/shard_map/ppermute | solution.py:39
  13.7 1.9 %copy-start.7 = (s32[32]{0:T(128)S(1)}, s32[32]{0:T(128)}, u32[]{:S(2)}) copy-start(s32[32]{0:T(128)} %param.20) | copy-start | bytes 388
  16.1 3.0 %copy-start.1 = (bf16[4,1,16384]{2,1,0:T(2,128)(2,1)}, bf16[4,1,16384]{2,1,0:T(2,128)(2,1)S(1)}, u32[]{:S(2)}) copy-start(bf16[4,1,16384]{2,1,0:T(2,128)(2,1)S(1)} %collective-permute-done.above_ref) | copy-start | bytes 393220
  19.1 0.7 copy-start.2
  30.4 30.1 %copy-start.3 = (bf16[1,16,4,1024]{3,2,1,0:T(4,128)(2,1)S(1)}, bf16[1,16,4,1024]{3,2,1,0:T(4,128)(2,1)}, u32[]{:S(2)}) copy-start(bf16[1,16,4,1024]{3,2,1,0:T(4,128)(2,1)} %param.21) | copy-start | bytes 393220
  30.4 30.1 %copy-start.5 = (bf16[4,32]{1,0:T(4,128)(2,1)S(1)}, bf16[4,32]{1,0:T(4,128)(2,1)}, u32[]{:S(2)}) copy-start(bf16[4,32]{1,0:T(4,128)(2,1)} %param.22) | copy-start | bytes 772
  30.4 30.1 %copy-start.6 = (f32[32]{0:T(128)S(1)}, f32[32]{0:T(128)}, u32[]{:S(2)}) copy-start(f32[32]{0:T(128)} %param.23) | copy-start | bytes 388
  32.2 17.0 %collective-permute-start.2 = (bf16[4,1024]{1,0:T(4,128)(2,1)S(1)}, bf16[4,1024]{1,0:T(4,128)(2,1)S(1)}, u32[]{:S(2)}, u32[]{:S(2)}) collective-permute-start(bf16[4,1024]{1,0:T(4,128)(2,1)S(1)} %convert_element_type.82), channel_id=1, source_target_pairs={{0,1},{1,2},{2,3},{3,0},{4,5},{5,6},{6,7},{7,4},{8,9},{9,10},{10,1... | collective-permute-start | bytes 24584 | tf_op jit(solution)/shard_map/ppermute | solution.py:284
  36.9 12.8 %collective-permute-start.3 = (bf16[4,1024]{1,0:T(4,128)(2,1)S(1)}, bf16[4,1024]{1,0:T(4,128)(2,1)S(1)}, u32[]{:S(2)}, u32[]{:S(2)}) collective-permute-start(bf16[4,1024]{1,0:T(4,128)(2,1)S(1)} %convert_element_type.82), channel_id=1, source_target_pairs={{0,2},{1,3},{2,0},{3,1},{4,6},{5,7},{6,4},{7,5},{8,10},{9,11},{10,... | collective-permute-start | bytes 24584 | tf_op jit(solution)/shard_map/ppermute | solution.py:284
  48.2 3.7 %collective-permute-start.4 = (bf16[4,1024]{1,0:T(4,128)(2,1)S(1)}, bf16[4,1024]{1,0:T(4,128)(2,1)S(1)}, u32[]{:S(2)}, u32[]{:S(2)}) collective-permute-start(bf16[4,1024]{1,0:T(4,128)(2,1)S(1)} %convert_element_type.82), channel_id=1, source_target_pairs={{0,3},{1,0},{2,1},{3,2},{4,7},{5,4},{6,5},{7,6},{8,11},{9,8},{10,9... | collective-permute-start | bytes 24584 | tf_op jit(solution)/shard_map/ppermute | solution.py:284
  48.5 13.5 %copy-start.4 = (f32[1,4,1024]{2,1,0:T(4,128)}, f32[1,4,1024]{2,1,0:T(4,128)S(1)}, u32[]{:S(2)}) copy-start(f32[1,4,1024]{2,1,0:T(4,128)S(1)} %mul.364) | copy-start | bytes 49156
  51.8 1.3 %collective-permute-start.5 = (bf16[4,4,1024]{2,1,0:T(4,128)(2,1)S(1)}, bf16[4,4,1024]{2,1,0:T(4,128)(2,1)S(1)}, u32[]{:S(2)}, u32[]{:S(2)}) collective-permute-start(bf16[4,4,1024]{2,1,0:T(4,128)(2,1)S(1)} %bitcast_dynamic-update-slice_fusion.6), channel_id=1, source_target_pairs={{0,4},{4,0},{1,5},{5,1},{2,6},{6,2},{3,7},{7,3},{8,12},{12,8},{9,1... | collective-permute-start | bytes 98312 | tf_op jit(solution)/shard_map/ppermute | solution.py:284
  53.1 5.5 %collective-permute-start.6 = (bf16[2,4,4,1024]{3,2,1,0:T(4,128)(2,1)S(1)}, bf16[2,4,4,1024]{3,2,1,0:T(4,128)(2,1)S(1)}, u32[]{:S(2)}, u32[]{:S(2)}) collective-permute-start(bf16[2,4,4,1024]{3,2,1,0:T(4,128)(2,1)S(1)} %bitcast_dynamic-update-slice_fusion.4), channel_id=1, source_target_pairs={{0,8},{8,16},{16,24},{24,0},{1,9},{9,17},{17,25},{25,1},{2,10},{10... | collective-permute-start | bytes 196616 | tf_op jit(solution)/shard_map/ppermute | solution.py:284
  53.2 6.4 %collective-permute-start.7 = (bf16[2,4,4,1024]{3,2,1,0:T(4,128)(2,1)S(1)}, bf16[2,4,4,1024]{3,2,1,0:T(4,128)(2,1)S(1)}, u32[]{:S(2)}, u32[]{:S(2)}) collective-permute-start(bf16[2,4,4,1024]{3,2,1,0:T(4,128)(2,1)S(1)} %bitcast_dynamic-update-slice_fusion.4), channel_id=1, source_target_pairs={{0,16},{8,24},{16,0},{24,8},{1,17},{9,25},{17,1},{25,9},{2,18},{10... | collective-permute-start | bytes 196616 | tf_op jit(solution)/shard_map/ppermute | solution.py:284
  56.2 4.3 %collective-permute-start.8 = (bf16[2,4,4,1024]{3,2,1,0:T(4,128)(2,1)S(1)}, bf16[2,4,4,1024]{3,2,1,0:T(4,128)(2,1)S(1)}, u32[]{:S(2)}, u32[]{:S(2)}) collective-permute-start(bf16[2,4,4,1024]{3,2,1,0:T(4,128)(2,1)S(1)} %bitcast_dynamic-update-slice_fusion.4), channel_id=1, source_target_pairs={{0,24},{8,0},{16,8},{24,16},{1,25},{9,1},{17,9},{25,17},{2,26},{10... | collective-permute-start | bytes 196616 | tf_op jit(solution)/shard_map/ppermute | solution.py:284
  64.3 1.6 %collective-permute-start.9 = (f32[64,32,16]{0,1,2:T(8,128)S(1)}, f32[64,32,16]{0,1,2:T(8,128)S(1)}, u32[]{:S(2)}, u32[]{:S(2)}) collective-permute-start(f32[64,32,16]{0,1,2:T(8,128)S(1)} %pad_maximum_fusion), channel_id=1, source_target_pairs={{0,4},{4,0},{1,5},{5,1},{2,6},{6,2},{3,7},{7,3},{8,12},{12,8},{9,1... | collective-permute-start | bytes 393224 | tf_op jit(solution)/shard_map/ppermute | solution.py:296
  66.4 5.7 %copy-start.8 = (f32[8]{0:T(128)S(1)}, f32[8]{0:T(128)}, u32[]{:S(2)}) copy-start(f32[8]{0:T(128)} %param.25) | copy-start | bytes 100
  70.1 4.1 %copy-start.9 = (bf16[1,16,8,1024]{3,2,1,0:T(8,128)(2,1)S(1)}, bf16[1,16,8,1024]{3,2,1,0:T(8,128)(2,1)}, u32[]{:S(2)}) copy-start(bf16[1,16,8,1024]{3,2,1,0:T(8,128)(2,1)} %param.27) | copy-start | bytes 786436
  76.2 1.4 %collective-permute-start.10 = (f32[16,32,16]{1,2,0:T(8,128)S(1)}, f32[16,32,16]{1,2,0:T(8,128)S(1)}, u32[]{:S(2)}, u32[]{:S(2)}) collective-permute-start(f32[16,32,16]{1,2,0:T(8,128)S(1)} %pad_maximum_fusion.1), channel_id=1, source_target_pairs={{0,4},{4,0},{1,5},{5,1},{2,6},{6,2},{3,7},{7,3},{8,12},{12,8},{9,1... | collective-permute-start | bytes 98312 | tf_op jit(solution)/shard_map/ppermute | solution.py:296
  78.2 4.7 %collective-permute-start.13 = (f32[48,8,16]{0,1,2:T(8,128)S(1)}, f32[48,8,16]{0,1,2:T(8,128)S(1)}, u32[]{:S(2)}, u32[]{:S(2)}) collective-permute-start(f32[48,8,16]{0,1,2:T(8,128)S(1)} %pad_maximum_fusion.5), channel_id=1, source_target_pairs={{0,24},{8,0},{16,8},{24,16},{1,25},{9,1},{17,9},{25,17},{2,26},{10... | collective-permute-start | bytes 73736 | tf_op jit(solution)/shard_map/ppermute | solution.py:296
  80.9 5.0 %collective-permute-start.12 = (f32[48,8,16]{0,1,2:T(8,128)S(1)}, f32[48,8,16]{0,1,2:T(8,128)S(1)}, u32[]{:S(2)}, u32[]{:S(2)}) collective-permute-start(f32[48,8,16]{0,1,2:T(8,128)S(1)} %pad_maximum_fusion.4), channel_id=1, source_target_pairs={{0,16},{8,24},{16,0},{24,8},{1,17},{9,25},{17,1},{25,9},{2,18},{10... | collective-permute-start | bytes 73736 | tf_op jit(solution)/shard_map/ppermute | solution.py:296
  81.8 5.2 %collective-permute-start.11 = (f32[48,8,16]{0,1,2:T(8,128)S(1)}, f32[48,8,16]{0,1,2:T(8,128)S(1)}, u32[]{:S(2)}, u32[]{:S(2)}) collective-permute-start(f32[48,8,16]{0,1,2:T(8,128)S(1)} %pad_maximum_fusion.3), channel_id=1, source_target_pairs={{0,8},{8,16},{16,24},{24,0},{1,9},{9,17},{17,25},{25,1},{2,10},{10... | collective-permute-start | bytes 73736 | tf_op jit(solution)/shard_map/ppermute | solution.py:296

commit v14 on v13

--- a/solution.py
+++ b/solution.py
@@ -35,8 +35,8 @@
     count = lax.axis_size(axis)
     forward = [(i, (i + 1) % count) for i in range(count)]
     backward = [((i + 1) % count, i) for i in range(count)]
-    above = lax.ppermute(block[:, -1:], axis, forward)
-    below = lax.ppermute(block[:, :1], axis, backward)
+    above = lax.ppermute(block[:, -1], axis, forward)
+    below = lax.ppermute(block[:, 0], axis, backward)
     return above, below
 
 
@@ -104,10 +104,10 @@
                 right_cells = pltpu.roll(extended, span - 1, 1)[:, 128 : 128 + CHUNK]
                 left_cells = pltpu.roll(extended, 1, 1)[:, 128 : 128 + CHUNK]
                 upper_rows = jnp.where(
-                    row_ids == 0, above_ref[tracer, :, cols].astype(jnp.float32), pltpu.roll(current, 1, 0)
+                    row_ids == 0, above_ref[tracer : tracer + 1, cols].astype(jnp.float32), pltpu.roll(current, 1, 0)
                 )
                 lower_rows = jnp.where(
-                    row_ids == rows - 1, below_ref[tracer, :, cols].astype(jnp.float32), pltpu.roll(current, rows - 1, 0)
+                    row_ids == rows - 1, below_ref[tracer : tracer + 1, cols].astype(jnp.float32), pltpu.roll(current, rows - 1, 0)
                 )
                 change = diffusion * (
                     right_cells + left_cells + upper_rows + lower_rows - 4.0 * current

time: 89.3 us -> 84.4 us (0.945)
  Pallas kernels: 10.6 us -> 23.4 us
  starting transfers between devices: 30.3 us -> 18.5 us
  waiting for transfers between devices: 15.6 us -> 10.9 us
  other arithmetic: 11.5 us -> 10.1 us
    ppermute x7, starting transfers between devices: 20.5 us -> 7.31 us  [gather_along(): lax.ppermute(block, axis, [(i, (i + shift) % count) for i in range(count)])]
    pallas_call x1, Pallas kernels: 10.6 us -> 23.4 us  [solve_rows(): pl.pallas_call(solve_kernel, out_shape=jax.ShapeDtypeStruct((tracers, wid...]
    ppermute x2, waiting for transfers between devices: 2.98 us -> 0.01 us  [the longest x1 0.01 us: halo_rows(): above = lax.ppermute(block[:, -1], axis, forward)]
    ppermute x7, waiting for transfers between devices: 7.05 us -> 5.25 us  [gather_along(): lax.ppermute(block, axis, [(i, (i + shift) % count) for i in range(count)])]
    ppermute x5, starting transfers between devices: 3.34 us -> 4.69 us  [packed_ppermute(): packed = lax.ppermute(jnp.concatenate(parts, axis=0), axis, perm)]
    unnamed x20 -> x28, local copies, waits for them, and re-layouts: 0.75 us -> 1.68 us
  transfers between devices with their start and end apart: 14 -> 14, of which waited for: 13 -> 8; matrix products, arithmetic and copies ran while one was open for 10% -> 9% of each run, Pallas kernels for 0% -> 0%
where the time goes in v14:
time: 84.4 us; the launch traced here: 84.6 us
  Pallas kernels  23.4 us (28%)
  starting transfers between devices  18.5 us (22%)
  waiting for transfers between devices  10.9 us (13%)
  local copies, waits for them, and re-layouts  10.6 us (13%)
  other arithmetic  10.1 us (12%)
  matrix products  8.91 us (11%)
  between operations  2.21 us (3%)
    pallas_call x1, Pallas kernels, solve_rows(): pl.pallas_call(solve_kernel, out_shape=jax.ShapeDtypeStruct((tracers, wid...  23.4 us
    ppermute x7, starting transfers between devices, gather_along(): lax.ppermute(block, axis, [(i, (i + shift) % count) for i in range(count)])  7.31 us
    ppermute x5, waiting for transfers between devices, packed_ppermute(): packed = lax.ppermute(jnp.concatenate(parts, axis=0), axis, perm)  5.61 us
    ppermute x7, waiting for transfers between devices, gather_along(): lax.ppermute(block, axis, [(i, (i + shift) % count) for i in range(count)])  5.25 us
    ppermute x5, starting transfers between devices, packed_ppermute(): packed = lax.ppermute(jnp.concatenate(parts, axis=0), axis, perm)  4.69 us
    ppermute x1, starting transfers between devices, halo_rows(): below = lax.ppermute(block[:, 0], axis, backward)  3.42 us
    ppermute x1, starting transfers between devices, halo_rows(): above = lax.ppermute(block[:, -1], axis, forward)  3.08 us
    reduce_sum x1, other arithmetic, mix_modes(): jnp.sum(real_weight * mode_imag + imag_weight * mode_real, axis=0)  2.4 us
  transfers between devices with their start and end apart: 14, of which 8 were waited for; matrix products, arithmetic and copies ran while one was open for 9% of the time, Pallas kernels for 0%

profile of v14, /device:TPU:0, one launch (start us, length us, event | category | flops | bytes accessed | tf_op | source)
XLA Modules:
  0.0 84.6 jit_solution(9283292204761095984)
XLA Ops:
  0.7 2.0 %fusion.146 = (bf16[4,1,16384]{2,1,0:T(2,128)(2,1)S(1)}, bf16[4,1,16384]{2,1,0:T(2,128)(2,1)S(1)}) fusion(bf16[4,16,16384]{2,1,0:T(8,128)(2,1)} %field_ref.1), kind=kLoop, calls=%fused_computation.247 | loop fusion | bytes 524288 | tf_op jit(solution)/shard_map/slice | solution.py:39
  2.7 0.2 copy.170
  2.8 3.1 %collective-permute-start = (bf16[4,16384]{1,0:T(4,128)(2,1)S(1)}, bf16[4,16384]{1,0:T(4,128)(2,1)S(1)}, u32[]{:S(2)}, u32[]{:S(2)}) collective-permute-start(bf16[4,16384]{1,0:T(4,128)(2,1)S(1)} %bitcast.182), channel_id=1, source_target_pairs={{0,1},{1,2},{2,3},{3,4},{4,5},{5,6},{6,7},{7,8},{8,9},{9,10},{10,1... | collective-permute-start | bytes 393224 | tf_op jit(solution)/shard_map/ppermute | solution.py:38
  5.9 0.2 copy.169
  6.1 3.4 %collective-permute-start.1 = (bf16[4,16384]{1,0:T(4,128)(2,1)S(1)}, bf16[4,16384]{1,0:T(4,128)(2,1)S(1)}, u32[]{:S(2)}, u32[]{:S(2)}) collective-permute-start(bf16[4,16384]{1,0:T(4,128)(2,1)S(1)} %bitcast.183), channel_id=1, source_target_pairs={{1,0},{2,1},{3,2},{4,3},{5,4},{6,5},{7,6},{8,7},{9,8},{10,9},{11,1... | collective-permute-start | bytes 393224 | tf_op jit(solution)/shard_map/ppermute | solution.py:39
  9.5 1.0 %fusion.149 = (f32[1,16384]{1,0:T(1,128)S(1)}, f32[1,16384]{1,0:T(1,128)S(1)}) fusion(bf16[2,16384]{1,0:T(2,128)(2,1)} %param.19), kind=kLoop, calls=%fused_computation.250 | loop fusion | bytes 262144 | tf_op jit(solution)/shard_map/slice | solution.py:162
  11.3 0.3 cosine_multiply_fusion
  11.6 0.1 broadcast_multiply_fusion
  11.7 0.2 multiply_multiply_fusion
  12.0 1.9 %maximum_multiply_fusion.coef_ref = f32[3,16,16384]{2,1,0:T(8,128)} fusion(f32[1,16,16384]{2,1,0:T(8,128)S(1)} %get-tuple-element.57, f32[1,16,16384]{2,1,0:T(8,128)S(1)} %get-tuple-element.58, f32[1,16,16384]{2,1,0:T(8,128)S(1)} %broadcast_multiply_fusion, f32[]{:T(128)} %bitcast.2), kind=kLoop, calls=%fused_computation | loop fusion | flops 2359296 | bytes 6291460 | tf_op jit(solution)/shard_map/mul | solution.py:159
  14.1 0.3 negate_convert_fusion
  14.4 0.6 copy-done.2
  15.0 0.6 copy-done.3
  15.7 23.4 %shard_map.157 = f32[4,16384]{1,0:T(4,128)} custom-call(f32[1]{0:T(128)} %div.20.step_ref, s32[1]{0:T(128)S(6)} %copy.181.count_ref, bf16[4,16,16384]{2,1,0:T(8,128)(2,1)} %field_ref.1, bf16[4,16384]{1,0:T(4,128)(2,1)} %copy-done.2, bf16[4,16384]{1,0:T(4,128)(2,1)} %copy-done.3, f32[3,16,16384]{2,1,0:T(8,128)} %maximum_multiply_fusion.coef_ref), custom_call_target="tpu_custom_call" | custom-call | tf_op jit(solution)/shard_map/pallas_call | solution.py:168
  39.1 1.2 %reshape.263 = f32[512,128]{1,0:T(8,128)S(1)} reshape(f32[4,16384]{1,0:T(4,128)} %shard_map.157) | data formatting | bytes 524288 | tf_op jit(solution)/shard_map/reshape | solution.py:363
  40.2 0.3 fusion.150
  40.6 0.2 copy.121
  40.7 0.2 convert_element_type.82
  41.0 1.2 %collective-permute-start.3 = (bf16[4,1024]{1,0:T(4,128)(2,1)S(1)}, bf16[4,1024]{1,0:T(4,128)(2,1)S(1)}, u32[]{:S(2)}, u32[]{:S(2)}) collective-permute-start(bf16[4,1024]{1,0:T(4,128)(2,1)S(1)} %convert_element_type.82), channel_id=1, source_target_pairs={{0,2},{1,3},{2,0},{3,1},{4,6},{5,7},{6,4},{7,5},{8,10},{9,11},{10,... | collective-permute-start | bytes 24584 | tf_op jit(solution)/shard_map/ppermute | solution.py:284
  42.2 2.6 %collective-permute-start.4 = (bf16[4,1024]{1,0:T(4,128)(2,1)S(1)}, bf16[4,1024]{1,0:T(4,128)(2,1)S(1)}, u32[]{:S(2)}, u32[]{:S(2)}) collective-permute-start(bf16[4,1024]{1,0:T(4,128)(2,1)S(1)} %convert_element_type.82), channel_id=1, source_target_pairs={{0,3},{1,0},{2,1},{3,2},{4,7},{5,4},{6,5},{7,6},{8,11},{9,8},{10,9... | collective-permute-start | bytes 24584 | tf_op jit(solution)/shard_map/ppermute | solution.py:284
  44.9 0.2 mul.364
  45.1 1.3 %collective-permute-done.2 = bf16[4,1024]{1,0:T(4,128)(2,1)S(1)} collective-permute-done((bf16[4,1024]{1,0:T(4,128)(2,1)S(1)}, bf16[4,1024]{1,0:T(4,128)(2,1)S(1)}, u32[]{:S(2)}, u32[]{:S(2)}) %collective-permute-start.2) | collective-permute-done | bytes 8224 | tf_op jit(solution)/shard_map/ppermute | solution.py:284
  46.5 0.5 collective-permute-done.4
  47.1 1.1 %collective-permute-done.5 = bf16[4,4,1024]{2,1,0:T(4,128)(2,1)S(1)} collective-permute-done((bf16[4,4,1024]{2,1,0:T(4,128)(2,1)S(1)}, bf16[4,4,1024]{2,1,0:T(4,128)(2,1)S(1)}, u32[]{:S(2)}, u32[]{:S(2)}) %collective-permute-start.5) | collective-permute-done | bytes 32800 | tf_op jit(solution)/shard_map/ppermute | solution.py:284
  48.4 1.0 %collective-permute-start.7 = (bf16[2,4,4,1024]{3,2,1,0:T(4,128)(2,1)S(1)}, bf16[2,4,4,1024]{3,2,1,0:T(4,128)(2,1)S(1)}, u32[]{:S(2)}, u32[]{:S(2)}) collective-permute-start(bf16[2,4,4,1024]{3,2,1,0:T(4,128)(2,1)S(1)} %bitcast_dynamic-update-slice_fusion.4), channel_id=1, source_target_pairs={{0,16},{8,24},{16,0},{24,8},{1,17},{9,25},{17,1},{25,9},{2,18},{10... | collective-permute-start | bytes 196616 | tf_op jit(solution)/shard_map/ppermute | solution.py:284
  49.3 2.3 %collective-permute-start.8 = (bf16[2,4,4,1024]{3,2,1,0:T(4,128)(2,1)S(1)}, bf16[2,4,4,1024]{3,2,1,0:T(4,128)(2,1)S(1)}, u32[]{:S(2)}, u32[]{:S(2)}) collective-permute-start(bf16[2,4,4,1024]{3,2,1,0:T(4,128)(2,1)S(1)} %bitcast_dynamic-update-slice_fusion.4), channel_id=1, source_target_pairs={{0,24},{8,0},{16,8},{24,16},{1,25},{9,1},{17,9},{25,17},{2,26},{10... | collective-permute-start | bytes 196616 | tf_op jit(solution)/shard_map/ppermute | solution.py:284
  51.8 2.3 %collective-permute-done.6 = bf16[2,4,4,1024]{3,2,1,0:T(4,128)(2,1)S(1)} collective-permute-done((bf16[2,4,4,1024]{3,2,1,0:T(4,128)(2,1)S(1)}, bf16[2,4,4,1024]{3,2,1,0:T(4,128)(2,1)S(1)}, u32[]{:S(2)}, u32[]{:S(2)}) %collective-permute-start.6) | collective-permute-done | bytes 65568 | tf_op jit(solution)/shard_map/ppermute | solution.py:284
  54.3 0.5 fusion.4
  54.8 0.9 %fusion.60 = f32[16,32,32]{1,2,0:T(8,128)S(1)} fusion(bf16[16,32,1024]{2,1,0:T(8,128)(2,1)S(1)} %fusion.4, bf16[1024,16]{0,1:T(8,128)(2,1)S(1)} %get-tuple-element.61, bf16[1024,16]{0,1:T(8,128)(2,1)S(1)} %get-tuple-element.62), kind=kOutput, calls=%fused_computation.142 | convolution fusion | flops 33685504 | bytes 1179648 | tf_op jit(solution)/shard_map/yhx,xk->yhk/dot_general | solution.py:378
  55.8 0.5 fusion.41
  56.3 0.5 fusion.45
  56.8 0.5 fusion.8
  57.4 0.5 fusion.10
  58.1 0.3 sine_multiply_fusion
  58.4 1.3 %collective-permute-done.9 = f32[64,32,16]{0,1,2:T(8,128)S(1)} collective-permute-done((f32[64,32,16]{0,1,2:T(8,128)S(1)}, f32[64,32,16]{0,1,2:T(8,128)S(1)}, u32[]{:S(2)}, u32[]{:S(2)}) %collective-permute-start.9) | collective-permute-done | bytes 131104 | tf_op jit(solution)/shard_map/ppermute | solution.py:296
  59.8 0.2 copy.126
  60.0 0.2 copy.127
  60.1 2.4 %fusion.3 = (f32[8,32,16]{1,2,0:T(8,128)S(1)}, f32[8,32,16]{1,2,0:T(8,128)S(1)}) fusion(f32[32,32,16]{1,2,0:T(8,128)S(1)} %copy.127, f32[32,32,16]{1,2,0:T(8,128)S(1)} %copy.126, bf16[2,32,8,32,16]{3,4,2,1,0:T(8,128)(2,1)} %param.26), kind=kLoop, calls=%fused_computation.8 | loop fusion | flops 1302528 | bytes 688128 | tf_op jit(solution)/shard_map/reduce_sum | solution.py:250
  62.5 0.6 fusion.77
  63.2 0.7 fusion.67
  63.8 0.7 convolution_subtract_fusion.2
  64.5 0.7 convolution_add_fusion.2
  65.3 0.6 convolution_multiply_fusion
  65.9 0.3 fusion.6
  66.2 1.8 %fusion.34 = bf16[1,16,8,1024]{3,2,1,0:T(8,128)(2,1)} fusion(f32[16,8,1024]{2,1,0:T(8,128)S(1)} %fusion.6), kind=kLoop, calls=%fused_computation.74 | loop fusion | flops 8519680 | bytes 786432 | tf_op jit(solution)/shard_map/broadcast_in_dim | solution.py:402
  68.0 0.3 fusion.35
  68.5 0.3 fusion.72
  68.9 0.3 fusion.74
  69.2 0.3 fusion.12
  69.6 0.3 fusion.14
  69.9 0.2 collective-permute-start.10
  70.1 0.2 constant_dynamic-slice_fusion
  70.3 0.2 constant_dynamic-slice_fusion.1
  70.6 0.7 collective-permute-done.10
  71.4 0.1 constant_dynamic-slice_fusion.3
  71.9 2.7 %collective-permute-start.13 = (f32[48,8,16]{0,1,2:T(8,128)S(1)}, f32[48,8,16]{0,1,2:T(8,128)S(1)}, u32[]{:S(2)}, u32[]{:S(2)}) collective-permute-start(f32[48,8,16]{0,1,2:T(8,128)S(1)} %pad_maximum_fusion.5), channel_id=1, source_target_pairs={{0,24},{8,0},{16,8},{24,16},{1,25},{9,1},{17,9},{25,17},{2,26},{10... | collective-permute-start | bytes 73736 | tf_op jit(solution)/shard_map/ppermute | solution.py:296
  75.0 1.7 %collective-permute-start.12 = (f32[48,8,16]{0,1,2:T(8,128)S(1)}, f32[48,8,16]{0,1,2:T(8,128)S(1)}, u32[]{:S(2)}, u32[]{:S(2)}) collective-permute-start(f32[48,8,16]{0,1,2:T(8,128)S(1)} %pad_maximum_fusion.4), channel_id=1, source_target_pairs={{0,16},{8,24},{16,0},{24,8},{1,17},{9,25},{17,1},{25,9},{2,18},{10... | collective-permute-start | bytes 73736 | tf_op jit(solution)/shard_map/ppermute | solution.py:296
  77.1 0.2 add_bitcast_fusion.3
  77.5 1.8 %collective-permute-done.12 = f32[48,8,16]{0,1,2:T(8,128)S(1)} collective-permute-done((f32[48,8,16]{0,1,2:T(8,128)S(1)}, f32[48,8,16]{0,1,2:T(8,128)S(1)}, u32[]{:S(2)}, u32[]{:S(2)}) %collective-permute-start.12) | collective-permute-done | bytes 24608 | tf_op jit(solution)/shard_map/ppermute | solution.py:296
  80.3 1.9 %collective-permute-done.11 = f32[48,8,16]{0,1,2:T(8,128)S(1)} collective-permute-done((f32[48,8,16]{0,1,2:T(8,128)S(1)}, f32[48,8,16]{0,1,2:T(8,128)S(1)}, u32[]{:S(2)}, u32[]{:S(2)}) %collective-permute-start.11) | collective-permute-done | bytes 24608 | tf_op jit(solution)/shard_map/ppermute | solution.py:296
  82.7 0.1 add_bitcast_fusion
  82.9 0.1 add_bitcast_fusion.1
  83.0 0.1 add_bitcast_fusion.2
  83.2 1.4 %fusion.17 = f32[2,16,8,8,16]{4,3,2,1,0:T(8,128)} fusion(f32[1,16,8,8,16]{4,3,2,1,0:T(8,128)S(1)} %get-tuple-element.26, f32[1,16,8,8,16]{4,3,2,1,0:T(8,128)S(1)} %get-tuple-element.25, f32[1,16,8,8,16]{4,3,2,1,0:T(8,128)S(1)} %get-tuple-element.24, f32[1,16,8,8,16]{4,3,2,1,0:T(8,128)S(1)} %get-tuple-element.23, ...), kind=kLoop, calls=%fused_computation.33 | loop fusion | flops 262144 | bytes 655360 | tf_op jit(solution)/shard_map/div | solution.py:416
  (97 shorter events, 4.7 us)
Async XLA Ops:
  0.6 65.2 %copy-start = (bf16[32,8]{0,1:T(8,128)(2,1)S(1)}, bf16[32,8]{0,1:T(8,128)(2,1)}, u32[]{:S(2)}) copy-start(bf16[32,8]{0,1:T(8,128)(2,1)} %param.24) | copy-start | bytes 1540
  0.6 9.9 %copy-start.7 = (f32[2,16]{1,0:T(2,128)S(1)}, f32[2,16]{1,0:T(2,128)}, u32[]{:S(2)}) copy-start(f32[2,16]{1,0:T(2,128)} %param.18) | copy-start | bytes 388
  0.7 10.6 %copy-start.5 = (bf16[16384]{0:T(1024)(128)(2,1)S(1)}, bf16[16384]{0:T(1024)(128)(2,1)}, u32[]{:S(2)}) copy-start(bf16[16384]{0:T(1024)(128)(2,1)} %param.17) | copy-start | bytes 98308
  0.7 10.9 %copy-start.8 = (f32[16]{0:T(128)S(1)}, f32[16]{0:T(128)}, u32[]{:S(2)}) copy-start(f32[16]{0:T(128)} %param.16) | copy-start | bytes 196
  2.8 11.5 %collective-permute-start = (bf16[4,16384]{1,0:T(4,128)(2,1)S(1)}, bf16[4,16384]{1,0:T(4,128)(2,1)S(1)}, u32[]{:S(2)}, u32[]{:S(2)}) collective-permute-start(bf16[4,16384]{1,0:T(4,128)(2,1)S(1)} %bitcast.182), channel_id=1, source_target_pairs={{0,1},{1,2},{2,3},{3,4},{4,5},{5,6},{6,7},{7,8},{8,9},{9,10},{10,1... | collective-permute-start | bytes 393224 | tf_op jit(solution)/shard_map/ppermute | solution.py:38
  6.1 8.3 %collective-permute-start.1 = (bf16[4,16384]{1,0:T(4,128)(2,1)S(1)}, bf16[4,16384]{1,0:T(4,128)(2,1)S(1)}, u32[]{:S(2)}, u32[]{:S(2)}) collective-permute-start(bf16[4,16384]{1,0:T(4,128)(2,1)S(1)} %bitcast.183), channel_id=1, source_target_pairs={{1,0},{2,1},{3,2},{4,3},{5,4},{6,5},{7,6},{8,7},{9,8},{10,9},{11,1... | collective-permute-start | bytes 393224 | tf_op jit(solution)/shard_map/ppermute | solution.py:39
  12.0 1.9 %copy-start.10 = (s32[32]{0:T(128)S(1)}, s32[32]{0:T(128)}, u32[]{:S(2)}) copy-start(s32[32]{0:T(128)} %param.20) | copy-start | bytes 388
  14.4 0.7 copy-start.2
  15.0 0.6 copy-start.3
  39.1 15.2 %copy-start.1 = (bf16[1,16,4,1024]{3,2,1,0:T(4,128)(2,1)S(1)}, bf16[1,16,4,1024]{3,2,1,0:T(4,128)(2,1)}, u32[]{:S(2)}) copy-start(bf16[1,16,4,1024]{3,2,1,0:T(4,128)(2,1)} %param.21) | copy-start | bytes 393220
  39.1 15.2 %copy-start.6 = (bf16[4,32]{1,0:T(4,128)(2,1)S(1)}, bf16[4,32]{1,0:T(4,128)(2,1)}, u32[]{:S(2)}) copy-start(bf16[4,32]{1,0:T(4,128)(2,1)} %param.22) | copy-start | bytes 772
  39.1 15.2 %copy-start.9 = (f32[32]{0:T(128)S(1)}, f32[32]{0:T(128)}, u32[]{:S(2)}) copy-start(f32[32]{0:T(128)} %param.23) | copy-start | bytes 388
  40.9 5.5 %collective-permute-start.2 = (bf16[4,1024]{1,0:T(4,128)(2,1)S(1)}, bf16[4,1024]{1,0:T(4,128)(2,1)S(1)}, u32[]{:S(2)}, u32[]{:S(2)}) collective-permute-start(bf16[4,1024]{1,0:T(4,128)(2,1)S(1)} %convert_element_type.82), channel_id=1, source_target_pairs={{0,1},{1,2},{2,3},{3,0},{4,5},{5,6},{6,7},{7,4},{8,9},{9,10},{10,1... | collective-permute-start | bytes 24584 | tf_op jit(solution)/shard_map/ppermute | solution.py:284
  41.0 5.5 %collective-permute-start.3 = (bf16[4,1024]{1,0:T(4,128)(2,1)S(1)}, bf16[4,1024]{1,0:T(4,128)(2,1)S(1)}, u32[]{:S(2)}, u32[]{:S(2)}) collective-permute-start(bf16[4,1024]{1,0:T(4,128)(2,1)S(1)} %convert_element_type.82), channel_id=1, source_target_pairs={{0,2},{1,3},{2,0},{3,1},{4,6},{5,7},{6,4},{7,5},{8,10},{9,11},{10,... | collective-permute-start | bytes 24584 | tf_op jit(solution)/shard_map/ppermute | solution.py:284
  42.2 4.8 %collective-permute-start.4 = (bf16[4,1024]{1,0:T(4,128)(2,1)S(1)}, bf16[4,1024]{1,0:T(4,128)(2,1)S(1)}, u32[]{:S(2)}, u32[]{:S(2)}) collective-permute-start(bf16[4,1024]{1,0:T(4,128)(2,1)S(1)} %convert_element_type.82), channel_id=1, source_target_pairs={{0,3},{1,0},{2,1},{3,2},{4,7},{5,4},{6,5},{7,6},{8,11},{9,8},{10,9... | collective-permute-start | bytes 24584 | tf_op jit(solution)/shard_map/ppermute | solution.py:284
  45.1 10.7 %copy-start.4 = (f32[1,4,1024]{2,1,0:T(4,128)}, f32[1,4,1024]{2,1,0:T(4,128)S(1)}, u32[]{:S(2)}) copy-start(f32[1,4,1024]{2,1,0:T(4,128)S(1)} %mul.364) | copy-start | bytes 49156
  47.0 1.3 %collective-permute-start.5 = (bf16[4,4,1024]{2,1,0:T(4,128)(2,1)S(1)}, bf16[4,4,1024]{2,1,0:T(4,128)(2,1)S(1)}, u32[]{:S(2)}, u32[]{:S(2)}) collective-permute-start(bf16[4,4,1024]{2,1,0:T(4,128)(2,1)S(1)} %bitcast_dynamic-update-slice_fusion.6), channel_id=1, source_target_pairs={{0,4},{4,0},{1,5},{5,1},{2,6},{6,2},{3,7},{7,3},{8,12},{12,8},{9,1... | collective-permute-start | bytes 98312 | tf_op jit(solution)/shard_map/ppermute | solution.py:284
  48.3 5.8 %collective-permute-start.6 = (bf16[2,4,4,1024]{3,2,1,0:T(4,128)(2,1)S(1)}, bf16[2,4,4,1024]{3,2,1,0:T(4,128)(2,1)S(1)}, u32[]{:S(2)}, u32[]{:S(2)}) collective-permute-start(bf16[2,4,4,1024]{3,2,1,0:T(4,128)(2,1)S(1)} %bitcast_dynamic-update-slice_fusion.4), channel_id=1, source_target_pairs={{0,8},{8,16},{16,24},{24,0},{1,9},{9,17},{17,25},{25,1},{2,10},{10... | collective-permute-start | bytes 196616 | tf_op jit(solution)/shard_map/ppermute | solution.py:284
  48.4 5.8 %collective-permute-start.7 = (bf16[2,4,4,1024]{3,2,1,0:T(4,128)(2,1)S(1)}, bf16[2,4,4,1024]{3,2,1,0:T(4,128)(2,1)S(1)}, u32[]{:S(2)}, u32[]{:S(2)}) collective-permute-start(bf16[2,4,4,1024]{3,2,1,0:T(4,128)(2,1)S(1)} %bitcast_dynamic-update-slice_fusion.4), channel_id=1, source_target_pairs={{0,16},{8,24},{16,0},{24,8},{1,17},{9,25},{17,1},{25,9},{2,18},{10... | collective-permute-start | bytes 196616 | tf_op jit(solution)/shard_map/ppermute | solution.py:284
  49.3 4.8 %collective-permute-start.8 = (bf16[2,4,4,1024]{3,2,1,0:T(4,128)(2,1)S(1)}, bf16[2,4,4,1024]{3,2,1,0:T(4,128)(2,1)S(1)}, u32[]{:S(2)}, u32[]{:S(2)}) collective-permute-start(bf16[2,4,4,1024]{3,2,1,0:T(4,128)(2,1)S(1)} %bitcast_dynamic-update-slice_fusion.4), channel_id=1, source_target_pairs={{0,24},{8,0},{16,8},{24,16},{1,25},{9,1},{17,9},{25,17},{2,26},{10... | collective-permute-start | bytes 196616 | tf_op jit(solution)/shard_map/ppermute | solution.py:284
  58.0 1.6 %collective-permute-start.9 = (f32[64,32,16]{0,1,2:T(8,128)S(1)}, f32[64,32,16]{0,1,2:T(8,128)S(1)}, u32[]{:S(2)}, u32[]{:S(2)}) collective-permute-start(f32[64,32,16]{0,1,2:T(8,128)S(1)} %pad_maximum_fusion), channel_id=1, source_target_pairs={{0,4},{4,0},{1,5},{5,1},{2,6},{6,2},{3,7},{7,3},{8,12},{12,8},{9,1... | collective-permute-start | bytes 393224 | tf_op jit(solution)/shard_map/ppermute | solution.py:296
  60.1 5.7 %copy-start.11 = (f32[8]{0:T(128)S(1)}, f32[8]{0:T(128)}, u32[]{:S(2)}) copy-start(f32[8]{0:T(128)} %param.25) | copy-start | bytes 100
  63.8 4.1 %copy-start.12 = (bf16[1,16,8,1024]{3,2,1,0:T(8,128)(2,1)S(1)}, bf16[1,16,8,1024]{3,2,1,0:T(8,128)(2,1)}, u32[]{:S(2)}) copy-start(bf16[1,16,8,1024]{3,2,1,0:T(8,128)(2,1)} %param.27) | copy-start | bytes 786436
  69.9 1.4 %collective-permute-start.10 = (f32[16,32,16]{1,2,0:T(8,128)S(1)}, f32[16,32,16]{1,2,0:T(8,128)S(1)}, u32[]{:S(2)}, u32[]{:S(2)}) collective-permute-start(f32[16,32,16]{1,2,0:T(8,128)S(1)} %pad_maximum_fusion.1), channel_id=1, source_target_pairs={{0,4},{4,0},{1,5},{5,1},{2,6},{6,2},{3,7},{7,3},{8,12},{12,8},{9,1... | collective-permute-start | bytes 98312 | tf_op jit(solution)/shard_map/ppermute | solution.py:296
  71.9 5.4 %collective-permute-start.13 = (f32[48,8,16]{0,1,2:T(8,128)S(1)}, f32[48,8,16]{0,1,2:T(8,128)S(1)}, u32[]{:S(2)}, u32[]{:S(2)}) collective-permute-start(f32[48,8,16]{0,1,2:T(8,128)S(1)} %pad_maximum_fusion.5), channel_id=1, source_target_pairs={{0,24},{8,0},{16,8},{24,16},{1,25},{9,1},{17,9},{25,17},{2,26},{10... | collective-permute-start | bytes 73736 | tf_op jit(solution)/shard_map/ppermute | solution.py:296
  75.0 4.3 %collective-permute-start.12 = (f32[48,8,16]{0,1,2:T(8,128)S(1)}, f32[48,8,16]{0,1,2:T(8,128)S(1)}, u32[]{:S(2)}, u32[]{:S(2)}) collective-permute-start(f32[48,8,16]{0,1,2:T(8,128)S(1)} %pad_maximum_fusion.4), channel_id=1, source_target_pairs={{0,16},{8,24},{16,0},{24,8},{1,17},{9,25},{17,1},{25,9},{2,18},{10... | collective-permute-start | bytes 73736 | tf_op jit(solution)/shard_map/ppermute | solution.py:296
  76.9 5.2 %collective-permute-start.11 = (f32[48,8,16]{0,1,2:T(8,128)S(1)}, f32[48,8,16]{0,1,2:T(8,128)S(1)}, u32[]{:S(2)}, u32[]{:S(2)}) collective-permute-start(f32[48,8,16]{0,1,2:T(8,128)S(1)} %pad_maximum_fusion.3), channel_id=1, source_target_pairs={{0,8},{8,16},{16,24},{24,0},{1,9},{9,17},{17,25},{25,1},{2,10},{10... | collective-permute-start | bytes 73736 | tf_op jit(solution)/shard_map/ppermute | solution.py:296
